TPU v7x, 1024 devices: a whole 4x4x32 slice. The times are simulated.
1024 devices in a mesh: seq: 32 (over z_lo, y), head: 32 (over z_hi, x, core).
Axes of the slice: x: 4, y: 4, z: 32 (z_hi: 4, z_lo: 8; z = z_hi * 8 + z_lo), core: 2. Of those that a mesh axis runs over, the one named last changes fastest.
Arguments:
- query: bfloat16 [8192, 4096], P('seq', 'head'), may hold values from -131 to 131
- keys: bfloat16 [8192, 4096], P('seq', 'head'), may hold values from -5 to 5, as said below
- values: bfloat16 [8192, 4096], P('seq', 'head'), may hold values from -5 to 5, as said below
- d_out: bfloat16 [8192, 5376], P('seq', 'head'), may hold values from -6 to 6
- w_out: bfloat16 [4096, 5376], P('head'), may hold values from -0.09375 to 0.09375
- w_query: bfloat16 [5376, 4096], P(None, 'head'), may hold values from -0.078125 to 0.078125
- w_key: bfloat16 [5376, 4096], P(None, 'head'), as said below
- w_value: bfloat16 [5376, 4096], P(None, 'head'), as said below
Outputs:
- grad_input: bfloat16 [8192, 5376], P('seq', 'head')
Inputs may be any that keep to these rules, and one draw needn't show every extreme that they name: `keys`: the columns of query heads 2i and 2i + 1 are equal: both read key head i. `values`: the columns of query heads 2i and 2i + 1 are equal: both read value head i. `w_key`: the columns of query heads 2i and 2i + 1 are equal; every entry lies within 5 / sqrt(5376) in magnitude. `w_value`: the columns of query heads 2i and 2i + 1 are equal; every entry lies within 5 / sqrt(5376) in magnitude.
All inputs are finite; a program needn't handle non-finite values.
Results may differ from a plain program's by a relative error of at most 0.03.
Values may be sent and summed in bfloat16 or wider, within the bound.
No kernel may reach another device: no remote copies, remote signals or barrier semaphores. Data moves between devices by JAX's collectives and lax.ppermute only.
A program may use at most 32 MiB of HBM per device.

v0:
```python
import jax
import jax.numpy as jnp
from jax import lax
from jax.sharding import PartitionSpec as P

WINDOW = 1024
NBR = 4


score_scale = 168.0 ** (-0.5)


def from_behind(block, axis, distance):
    devices = range(lax.axis_size(axis))
    route = [(i - distance, i) for i in devices if i - distance in devices]
    return lax.ppermute(block, axis, route)


def dot_rows(left, right):
    return lax.dot_general(
        left, right, (((1,), (1,)), ((), ())), preferred_element_type=jnp.float32
    )


def dot_cols(left, right):
    return lax.dot_general(
        left, right, (((0,), (0,)), ((), ())), preferred_element_type=jnp.float32
    )


def band_backward(query_block, key_band, value_band, grad_block, query_start, key_start):
    length = query_block.shape[0]
    span = key_band.shape[0]
    query_pos = query_start + jnp.arange(length, dtype=jnp.int32)
    key_pos = key_start + jnp.arange(span, dtype=jnp.int32)
    offset = query_pos[:, None] - key_pos[None, :]
    allowed = (key_pos[None, :] >= 0) & (offset >= 0) & (offset < WINDOW)
    scores = dot_rows(query_block, key_band) * score_scale
    masked = jnp.where(allowed, scores, -1e30)
    top = jnp.max(masked, axis=1, keepdims=True)
    weights = jnp.where(allowed, jnp.exp(masked - top), 0.0)
    probs = weights / jnp.sum(weights, axis=1, keepdims=True)
    probs_low = probs.astype(jnp.bfloat16)
    grad_probs = dot_rows(grad_block, value_band)
    delta = jnp.sum(probs * grad_probs, axis=1, keepdims=True)
    grad_scores = (probs * (grad_probs - delta)).astype(jnp.bfloat16)
    grad_query = (
        jnp.dot(grad_scores, key_band, preferred_element_type=jnp.float32) * score_scale
    ).astype(jnp.bfloat16)
    grad_keys = (dot_cols(grad_scores, query_block) * score_scale).astype(jnp.bfloat16)
    grad_values = dot_cols(probs_low, grad_block).astype(jnp.bfloat16)
    return (grad_query, grad_keys, grad_values)


def body(query, keys, values, d_out, w_out, w_query, w_key, w_value):
    length = query.shape[0]
    seq_index = lax.axis_index("seq")
    gathered = lax.all_gather(d_out, "head", axis=1, tiled=True)
    grad_heads = dot_rows(gathered, w_out).astype(jnp.bfloat16)
    reach = NBR
    key_blocks = []
    value_blocks = []
    for distance in range(reach, 0, -1):
        far_keys, far_values = from_behind((keys, values), "seq", distance)
        key_blocks.append(far_keys)
        value_blocks.append(far_values)
    key_band = jnp.concatenate(key_blocks + [keys], axis=0)
    value_band = jnp.concatenate(value_blocks + [values], axis=0)
    query_start = seq_index * length
    grad_query, key_parts, value_parts = band_backward(
        query, key_band, value_band, grad_heads, query_start, query_start - reach * length
    )
    key_total = key_parts[reach * length :].astype(jnp.float32)
    value_total = value_parts[reach * length :].astype(jnp.float32)
    for distance in range(1, reach + 1):
        first = (reach - distance) * length
        outgoing = (key_parts[first : first + length], value_parts[first : first + length])
        back_keys, back_values = from_behind((outgoing[0], outgoing[1]), "seq", -distance)
        key_total = key_total + back_keys.astype(jnp.float32)
        value_total = value_total + back_values.astype(jnp.float32)
    grad_keys = key_total.astype(jnp.bfloat16)
    grad_values = value_total.astype(jnp.bfloat16)
    summed = dot_rows(w_query, grad_query)
    summed = summed + dot_rows(w_key, grad_keys)
    summed = summed + dot_rows(w_value, grad_values)
    reduced = lax.psum_scatter(
        summed.astype(jnp.bfloat16), "head", scatter_dimension=0, tiled=True
    ).astype(jnp.float32)
    return reduced.T.astype(jnp.bfloat16)


def solution(mesh):
    in_specs = (
        P("seq", "head"),
        P("seq", "head"),
        P("seq", "head"),
        P("seq", "head"),
        P("head", None),
        P(None, "head"),
        P(None, "head"),
        P(None, "head"),
    )
    out_specs = P("seq", "head")
    return jax.shard_map(body, mesh=mesh, in_specs=in_specs, out_specs=out_specs, check_vma=False)
```

profile of v0, /device:TPU:1, one launch (start us, length us, event | category | flops | bytes accessed | tf_op | source)
XLA Modules:
  0.0 399.1 jit_solution(1865463319904127898)
XLA Ops:
  7.3 5.7 %collective-permute-start.2 = (bf16[256,128]{1,0:T(8,128)(2,1)}, bf16[256,128]{1,0:T(8,128)(2,1)S(1)}, u32[]{:S(2)}, u32[]{:S(2)}) collective-permute-start(bf16[256,128]{1,0:T(8,128)(2,1)} %param.9), channel_id=1, source_target_pairs={{0,64},{32,96},{64,128},{96,160},{128,192},{160,224},{192,256},{22... | collective-permute-start | bytes 196616 | tf_op jit(solution)/shard_map/ppermute | solution.py:16
  13.0 4.0 %collective-permute-start.1 = (bf16[256,128]{1,0:T(8,128)(2,1)}, bf16[256,128]{1,0:T(8,128)(2,1)S(1)}, u32[]{:S(2)}, u32[]{:S(2)}) collective-permute-start(bf16[256,128]{1,0:T(8,128)(2,1)} %param.9), channel_id=1, source_target_pairs={{0,96},{32,128},{64,160},{96,192},{128,224},{160,256},{192,288},{2... | collective-permute-start | bytes 196616 | tf_op jit(solution)/shard_map/ppermute | solution.py:16
  17.0 3.5 collective-permute-start
  20.6 2.6 collective-permute-start.3
  23.2 3.5 collective-permute-start.4
  26.8 1.6 collective-permute-done.4
  28.4 6.4 %collective-permute-start.5 = (bf16[256,128]{1,0:T(8,128)(2,1)}, bf16[256,128]{1,0:T(8,128)(2,1)S(1)}, u32[]{:S(2)}, u32[]{:S(2)}) collective-permute-start(bf16[256,128]{1,0:T(8,128)(2,1)} %param.10), channel_id=1, source_target_pairs={{0,96},{32,128},{64,160},{96,192},{128,224},{160,256},{192,288},{2... | collective-permute-start | bytes 196616 | tf_op jit(solution)/shard_map/ppermute | solution.py:16
  34.8 1.6 collective-permute-done.5
  36.4 2.1 collective-permute-start.6
  38.6 1.6 collective-permute-done.6
  40.2 5.2 %collective-permute-start.7 = (bf16[256,128]{1,0:T(8,128)(2,1)}, bf16[256,128]{1,0:T(8,128)(2,1)S(1)}, u32[]{:S(2)}, u32[]{:S(2)}) collective-permute-start(bf16[256,128]{1,0:T(8,128)(2,1)} %param.10), channel_id=1, source_target_pairs={{0,32},{32,64},{64,96},{96,128},{128,160},{160,192},{192,224},{224... | collective-permute-start | bytes 196616 | tf_op jit(solution)/shard_map/ppermute | solution.py:16
  45.4 1.6 collective-permute-done.7
  49.6 112.0 %all-gather.2.cloned.1.call-done = bf16[256,5376]{0,1:T(8,128)(2,1)} async-done(((bf16[256,168]{0,1:T(8,128)(2,1)}), bf16[256,5376]{0,1:T(8,128)(2,1)}) %all-gather.2.cloned.1.call-update) | async-done | bytes 2752528 | tf_op jit(solution)/shard_map/all_gather | solution.py:58
  161.6 3.1 convolution_convert_fusion.1
  168.8 1.7 multiply_convert_fusion
  170.9 1.3 collective-permute-start.8
  174.8 1.4 collective-permute-start.9
  176.3 3.6 fusion.8
  182.5 1.4 collective-permute-start.13
  184.2 3.9 convolution_add_fusion.1
  188.1 2.4 collective-permute-done.15
  191.4 3.3 fusion.1
  194.6 4.6 %copy.16 = bf16[5376,256]{1,0:T(8,128)(2,1)} copy(bf16[5376,256]{0,1:T(8,128)(2,1)} %fusion.1) | data formatting | bytes 5505024
  199.3 193.0 %reduce-scatter.4.cloned.1.call-done = bf16[168,256]{1,0:T(8,128)(2,1)} async-done(((bf16[5376,256]{1,0:T(8,128)(2,1)}), bf16[168,256]{1,0:T(8,128)(2,1)}) %reduce-scatter.4.cloned.1.call-update) | async-done | bytes 86032
  (62 shorter events, 14.1 us)
Async XLA Ops:
  6.5 169.7 %copy-start = (bf16[5376,128]{1,0:T(8,128)(2,1)S(1)}, bf16[5376,128]{1,0:T(8,128)(2,1)}, u32[]{:S(2)}) copy-start(bf16[5376,128]{1,0:T(8,128)(2,1)} %param.13) | copy-start | bytes 4128772
  6.5 41.4 %copy-start.6 = (bf16[256,128]{1,0:T(8,128)(2,1)S(1)}, bf16[256,128]{1,0:T(8,128)(2,1)}, u32[]{:S(2)}) copy-start(bf16[256,128]{1,0:T(8,128)(2,1)} %param.9) | copy-start | bytes 196612
  6.5 41.4 %copy-start.5 = (bf16[256,128]{1,0:T(8,128)(2,1)S(1)}, bf16[256,128]{1,0:T(8,128)(2,1)}, u32[]{:S(2)}) copy-start(bf16[256,128]{1,0:T(8,128)(2,1)} %param.8) | copy-start | bytes 196612
  6.5 155.0 %all-gather.2.cloned.1.call-start = ((), (), s32[]{:S(2)}) async-start(), calls=%async_computation.1 | async-start | bytes 2838528 | tf_op jit(solution)/shard_map/all_gather | solution.py:58
  7.3 385.0 %reduce-scatter.4.cloned.1.call-start = ((), (), s32[]{:S(2)}) async-start(), calls=%async_computation.2 | async-start | bytes 2838528
  7.3 40.6 %collective-permute-start.2 = (bf16[256,128]{1,0:T(8,128)(2,1)}, bf16[256,128]{1,0:T(8,128)(2,1)S(1)}, u32[]{:S(2)}, u32[]{:S(2)}) collective-permute-start(bf16[256,128]{1,0:T(8,128)(2,1)} %param.9), channel_id=1, source_target_pairs={{0,64},{32,96},{64,128},{96,160},{128,192},{160,224},{192,256},{22... | collective-permute-start | bytes 196616 | tf_op jit(solution)/shard_map/ppermute | solution.py:16
  13.0 34.9 %collective-permute-start.1 = (bf16[256,128]{1,0:T(8,128)(2,1)}, bf16[256,128]{1,0:T(8,128)(2,1)S(1)}, u32[]{:S(2)}, u32[]{:S(2)}) collective-permute-start(bf16[256,128]{1,0:T(8,128)(2,1)} %param.9), channel_id=1, source_target_pairs={{0,96},{32,128},{64,160},{96,192},{128,224},{160,256},{192,288},{2... | collective-permute-start | bytes 196616 | tf_op jit(solution)/shard_map/ppermute | solution.py:16
  17.0 30.8 %collective-permute-start = (bf16[256,128]{1,0:T(8,128)(2,1)}, bf16[256,128]{1,0:T(8,128)(2,1)S(1)}, u32[]{:S(2)}, u32[]{:S(2)}) collective-permute-start(bf16[256,128]{1,0:T(8,128)(2,1)} %param.9), channel_id=1, source_target_pairs={{0,128},{32,160},{64,192},{96,224},{128,256},{160,288},{192,320},{... | collective-permute-start | bytes 196616 | tf_op jit(solution)/shard_map/ppermute | solution.py:16
  20.6 27.4 %collective-permute-start.3 = (bf16[256,128]{1,0:T(8,128)(2,1)}, bf16[256,128]{1,0:T(8,128)(2,1)S(1)}, u32[]{:S(2)}, u32[]{:S(2)}) collective-permute-start(bf16[256,128]{1,0:T(8,128)(2,1)} %param.9), channel_id=1, source_target_pairs={{0,32},{32,64},{64,96},{96,128},{128,160},{160,192},{192,224},{224... | collective-permute-start | bytes 196616 | tf_op jit(solution)/shard_map/ppermute | solution.py:16
  23.2 5.2 %collective-permute-start.4 = (bf16[256,128]{1,0:T(8,128)(2,1)}, bf16[256,128]{1,0:T(8,128)(2,1)S(1)}, u32[]{:S(2)}, u32[]{:S(2)}) collective-permute-start(bf16[256,128]{1,0:T(8,128)(2,1)} %param.10), channel_id=1, source_target_pairs={{0,128},{32,160},{64,192},{96,224},{128,256},{160,288},{192,320},{... | collective-permute-start | bytes 196616 | tf_op jit(solution)/shard_map/ppermute | solution.py:16
  28.4 8.1 %collective-permute-start.5 = (bf16[256,128]{1,0:T(8,128)(2,1)}, bf16[256,128]{1,0:T(8,128)(2,1)S(1)}, u32[]{:S(2)}, u32[]{:S(2)}) collective-permute-start(bf16[256,128]{1,0:T(8,128)(2,1)} %param.10), channel_id=1, source_target_pairs={{0,96},{32,128},{64,160},{96,192},{128,224},{160,256},{192,288},{2... | collective-permute-start | bytes 196616 | tf_op jit(solution)/shard_map/ppermute | solution.py:16
  36.4 3.7 collective-permute-start.6
  40.2 6.8 %collective-permute-start.7 = (bf16[256,128]{1,0:T(8,128)(2,1)}, bf16[256,128]{1,0:T(8,128)(2,1)S(1)}, u32[]{:S(2)}, u32[]{:S(2)}) collective-permute-start(bf16[256,128]{1,0:T(8,128)(2,1)} %param.10), channel_id=1, source_target_pairs={{0,32},{32,64},{64,96},{96,128},{128,160},{160,192},{192,224},{224... | collective-permute-start | bytes 196616 | tf_op jit(solution)/shard_map/ppermute | solution.py:16
  48.7 119.3 %copy-start.9 = (f32[256]{0:T(256)}, f32[256]{0:T(256)S(1)}, u32[]{:S(2)}) copy-start(f32[256]{0:T(256)S(1)} %get-tuple-element.13) | copy-start | bytes 3076
  49.6 118.4 %copy-start.10 = (f32[256]{0:T(256)}, f32[256]{0:T(256)S(1)}, u32[]{:S(2)}) copy-start(f32[256]{0:T(256)S(1)} %fusion.10) | copy-start | bytes 3076
  166.7 21.4 %collective-permute-start.12 = (bf16[256,128]{1,0:T(8,128)(2,1)}, bf16[256,128]{1,0:T(8,128)(2,1)S(1)}, u32[]{:S(2)}, u32[]{:S(2)}) collective-permute-start(bf16[256,128]{1,0:T(8,128)(2,1)} %get-tuple-element.5), channel_id=1, source_target_pairs={{32,0},{64,32},{96,64},{128,96},{160,128},{192,160},{224,192},{256... | collective-permute-start | bytes 196616 | tf_op jit(solution)/shard_map/ppermute | solution.py:16
  170.9 9.0 %collective-permute-start.8 = (bf16[256,128]{1,0:T(8,128)(2,1)S(1)}, bf16[256,128]{1,0:T(8,128)(2,1)S(1)}, u32[]{:S(2)}, u32[]{:S(2)}) collective-permute-start(bf16[256,128]{1,0:T(8,128)(2,1)S(1)} %get-tuple-element.9), channel_id=1, source_target_pairs={{32,0},{64,32},{96,64},{128,96},{160,128},{192,160},{224,192},{256... | collective-permute-start | bytes 196616 | tf_op jit(solution)/shard_map/ppermute | solution.py:16
  172.2 9.0 %collective-permute-start.11 = (bf16[256,128]{1,0:T(8,128)(2,1)S(1)}, bf16[256,128]{1,0:T(8,128)(2,1)S(1)}, u32[]{:S(2)}, u32[]{:S(2)}) collective-permute-start(bf16[256,128]{1,0:T(8,128)(2,1)S(1)} %get-tuple-element.10), channel_id=1, source_target_pairs={{128,0},{160,32},{192,64},{224,96},{256,128},{288,160},{320,192},{... | collective-permute-start | bytes 196616 | tf_op jit(solution)/shard_map/ppermute | solution.py:16
  173.5 9.0 %collective-permute-start.10 = (bf16[256,128]{1,0:T(8,128)(2,1)S(1)}, bf16[256,128]{1,0:T(8,128)(2,1)S(1)}, u32[]{:S(2)}, u32[]{:S(2)}) collective-permute-start(bf16[256,128]{1,0:T(8,128)(2,1)S(1)} %get-tuple-element.11), channel_id=1, source_target_pairs={{96,0},{128,32},{160,64},{192,96},{224,128},{256,160},{288,192},{3... | collective-permute-start | bytes 196616 | tf_op jit(solution)/shard_map/ppermute | solution.py:16
  174.8 9.4 %collective-permute-start.9 = (bf16[256,128]{1,0:T(8,128)(2,1)S(1)}, bf16[256,128]{1,0:T(8,128)(2,1)S(1)}, u32[]{:S(2)}, u32[]{:S(2)}) collective-permute-start(bf16[256,128]{1,0:T(8,128)(2,1)S(1)} %get-tuple-element.12), channel_id=1, source_target_pairs={{64,0},{96,32},{128,64},{160,96},{192,128},{224,160},{256,192},{28... | collective-permute-start | bytes 196616 | tf_op jit(solution)/shard_map/ppermute | solution.py:16
  179.9 10.7 %collective-permute-start.15 = (bf16[256,128]{1,0:T(8,128)(2,1)S(1)}, bf16[256,128]{1,0:T(8,128)(2,1)S(1)}, u32[]{:S(2)}, u32[]{:S(2)}) collective-permute-start(bf16[256,128]{1,0:T(8,128)(2,1)S(1)} %copy-done.8), channel_id=1, source_target_pairs={{128,0},{160,32},{192,64},{224,96},{256,128},{288,160},{320,192},{... | collective-permute-start | bytes 196616 | tf_op jit(solution)/shard_map/ppermute | solution.py:16
  181.2 9.4 %collective-permute-start.14 = (bf16[256,128]{1,0:T(8,128)(2,1)S(1)}, bf16[256,128]{1,0:T(8,128)(2,1)S(1)}, u32[]{:S(2)}, u32[]{:S(2)}) collective-permute-start(bf16[256,128]{1,0:T(8,128)(2,1)S(1)} %copy-done.7), channel_id=1, source_target_pairs={{96,0},{128,32},{160,64},{192,96},{224,128},{256,160},{288,192},{3... | collective-permute-start | bytes 196616 | tf_op jit(solution)/shard_map/ppermute | solution.py:16
  182.5 8.9 %copy-start.1 = (bf16[5376,128]{1,0:T(8,128)(2,1)S(1)}, bf16[5376,128]{1,0:T(8,128)(2,1)}, u32[]{:S(2)}) copy-start(bf16[5376,128]{1,0:T(8,128)(2,1)} %param.15) | copy-start | bytes 4128772
  182.5 8.9 %collective-permute-start.13 = (bf16[256,128]{1,0:T(8,128)(2,1)S(1)}, bf16[256,128]{1,0:T(8,128)(2,1)S(1)}, u32[]{:S(2)}, u32[]{:S(2)}) collective-permute-start(bf16[256,128]{1,0:T(8,128)(2,1)S(1)} %get-tuple-element.8), channel_id=1, source_target_pairs={{64,0},{96,32},{128,64},{160,96},{192,128},{224,160},{256,192},{28... | collective-permute-start | bytes 196616 | tf_op jit(solution)/shard_map/ppermute | solution.py:16
  (5 other events, 18.7 us)
Sparse Core Ops, SparseCore 0:
  11.7 149.8 all-gather.1
  199.4 192.7 reduce-scatter.3
where the time goes:
time: 400 us; the launch traced here: 399 us
  waiting for transfers between devices  316 us (79%)
  starting transfers between devices  43.7 us (11%)
  matrix products  16.7 us (4%)
  between operations  13.8 us (3%)
  local copies, waits for them, and re-layouts  6.55 us (2%)
    unnamed x3, waiting for transfers between devices  194 us
    all_gather x1, waiting for transfers between devices, body(): gathered = lax.all_gather(d_out, 'head', axis=1, tiled=True)  112 us
    ppermute x16, starting transfers between devices, from_behind(): return lax.ppermute(block, axis, route)  43.7 us
    dot_general x6, matrix products, dot_rows(): lax.dot_general(left, right, (((1,), (1,)), ((), ())), preferred_element_...  15.2 us
    ppermute x16, waiting for transfers between devices, from_behind(): return lax.ppermute(block, axis, route)  9.97 us
  transfers between devices with their start and end apart: 18, of which 9 were waited for; matrix products, arithmetic and copies ran while one was open for 3% of the time, Pallas kernels for 0%

commit v1 on v0

v1 whole, which is shorter than its diff:
```python
import jax
import jax.numpy as jnp
from jax import lax
from jax.sharding import Mesh
from jax.sharding import PartitionSpec as P

WINDOW = 1024
NBR = 4


score_scale = 168.0 ** (-0.5)


def from_behind(block, axis, distance):
    devices = range(lax.axis_size(axis))
    route = [(i - distance, i) for i in devices if i - distance in devices]
    return lax.ppermute(block, axis, route)


def shift(block, axis, size, step):
    return lax.ppermute(block, axis, [(i, (i + step) % size) for i in range(size)])


def gather_axis(block, axis, size):
    me = lax.axis_index(axis)
    buf = jnp.zeros((size,) + block.shape, block.dtype)
    buf = lax.dynamic_update_index_in_dim(buf, block, me, 0)
    for step in range(1, size):
        got = shift(block, axis, size, step)
        buf = lax.dynamic_update_index_in_dim(buf, got, (me - step) % size, 0)
    return buf


def scatter_axis(parts, axis, size, dim):
    me = lax.axis_index(axis)
    acc = lax.dynamic_index_in_dim(parts, me, dim, keepdims=False).astype(jnp.float32)
    for step in range(1, size):
        out = lax.dynamic_index_in_dim(parts, (me + step) % size, dim, keepdims=False)
        acc = acc + shift(out.astype(jnp.bfloat16), axis, size, step).astype(jnp.float32)
    return acc


def dot_rows(left, right):
    return lax.dot_general(
        left, right, (((1,), (1,)), ((), ())), preferred_element_type=jnp.float32
    )


def dot_cols(left, right):
    return lax.dot_general(
        left, right, (((0,), (0,)), ((), ())), preferred_element_type=jnp.float32
    )


def band_backward(query_block, key_band, value_band, grad_block, query_start, key_start):
    length = query_block.shape[0]
    span = key_band.shape[0]
    query_pos = query_start + jnp.arange(length, dtype=jnp.int32)
    key_pos = key_start + jnp.arange(span, dtype=jnp.int32)
    offset = query_pos[:, None] - key_pos[None, :]
    allowed = (key_pos[None, :] >= 0) & (offset >= 0) & (offset < WINDOW)
    scores = dot_rows(query_block, key_band) * score_scale
    masked = jnp.where(allowed, scores, -1e30)
    top = jnp.max(masked, axis=1, keepdims=True)
    weights = jnp.where(allowed, jnp.exp(masked - top), 0.0)
    probs = weights / jnp.sum(weights, axis=1, keepdims=True)
    probs_low = probs.astype(jnp.bfloat16)
    grad_probs = dot_rows(grad_block, value_band)
    delta = jnp.sum(probs * grad_probs, axis=1, keepdims=True)
    grad_scores = (probs * (grad_probs - delta)).astype(jnp.bfloat16)
    grad_query = (
        jnp.dot(grad_scores, key_band, preferred_element_type=jnp.float32) * score_scale
    ).astype(jnp.bfloat16)
    grad_keys = (dot_cols(grad_scores, query_block) * score_scale).astype(jnp.bfloat16)
    grad_values = dot_cols(probs_low, grad_block).astype(jnp.bfloat16)
    return (grad_query, grad_keys, grad_values)


def make_body(n_zhi, n_x, n_core):
    def body(query, keys, values, d_out, w_out, w_query, w_key, w_value):
        length, dim = query.shape
        width = d_out.shape[1]
        seq_index = lax.axis_index("seq")
        stacked = gather_axis(d_out, "zhi", n_zhi)
        stacked = gather_axis(stacked, "x", n_x)
        stacked = gather_axis(stacked, "core", n_core)
        out_rows = w_out.reshape(w_out.shape[0], n_zhi, n_x, n_core, width)
        grad_heads = jnp.einsum(
            "cxzti,hzxci->th", stacked, out_rows, preferred_element_type=jnp.float32
        ).astype(jnp.bfloat16)
        reach = NBR
        kv = jnp.concatenate([keys, values], axis=1)
        kv_blocks = [from_behind(kv, "seq", distance) for distance in range(reach, 0, -1)]
        kv_band = jnp.concatenate(kv_blocks + [kv], axis=0)
        key_band = kv_band[:, :dim]
        value_band = kv_band[:, dim:]
        query_start = seq_index * length
        grad_query, key_parts, value_parts = band_backward(
            query, key_band, value_band, grad_heads, query_start, query_start - reach * length
        )
        kv_parts = jnp.concatenate([key_parts, value_parts], axis=1)
        kv_total = kv_parts[reach * length :].astype(jnp.float32)
        for distance in range(1, reach + 1):
            first = (reach - distance) * length
            back = from_behind(kv_parts[first : first + length], "seq", -distance)
            kv_total = kv_total + back.astype(jnp.float32)
        kv_total = kv_total.astype(jnp.bfloat16)
        grad_keys = kv_total[:, :dim]
        grad_values = kv_total[:, dim:]
        summed = dot_rows(w_query, grad_query)
        summed = summed + dot_rows(w_key, grad_keys)
        summed = summed + dot_rows(w_value, grad_values)
        term = summed.astype(jnp.bfloat16).reshape(n_zhi, n_x, n_core, width, length)
        part = scatter_axis(term, "core", n_core, 2)
        part = scatter_axis(part, "x", n_x, 1)
        part = scatter_axis(part, "zhi", n_zhi, 0)
        return part.T.astype(jnp.bfloat16)

    return body


def solution(mesh):
    n_seq, n_head = mesh.devices.shape
    n_core = 2
    n_x = len({d.coords[0] for d in mesh.devices[0]})
    n_zhi = n_head // (n_x * n_core)
    fine = Mesh(mesh.devices.reshape(n_seq, n_zhi, n_x, n_core), ("seq", "zhi", "x", "core"))
    head = ("zhi", "x", "core")
    in_specs = (
        P("seq", head),
        P("seq", head),
        P("seq", head),
        P("seq", head),
        P(head, None),
        P(None, head),
        P(None, head),
        P(None, head),
    )
    out_specs = P("seq", head)
    return jax.shard_map(
        make_body(n_zhi, n_x, n_core),
        mesh=fine,
        in_specs=in_specs,
        out_specs=out_specs,
        check_vma=False,
    )
```

time: 400 us -> 224 us (0.56)
  waiting for transfers between devices: 316 us -> 62.8 us
  starting transfers between devices: 43.7 us -> 121 us
  between operations: 13.8 us -> 0.84 us
  local copies, waits for them, and re-layouts: 6.55 us -> 16.2 us
  other arithmetic: 2.65 us -> 7.49 us
    unnamed x3 -> x0, waiting for transfers between devices: 194 us -> none
    all_gather x1 -> x0, waiting for transfers between devices: 112 us -> none  [body(): gathered = lax.all_gather(d_out, 'head', axis=1, tiled=True)]
    ppermute x0 -> x14, starting transfers between devices: none -> 103 us  [shift(): lax.ppermute(block, axis, [(i, (i + step) % size) for i in range(size)])]
    ppermute x0 -> x14, waiting for transfers between devices: none -> 54.5 us  [shift(): lax.ppermute(block, axis, [(i, (i + step) % size) for i in range(size)])]
    ppermute x16 -> x8, starting transfers between devices: 43.7 us -> 18.4 us  [from_behind(): return lax.ppermute(block, axis, route)]
    convert_element_type x0 -> x3, local copies, waits for them, and re-layouts: none -> 4.75 us  [the longest x1 4.57 us: body(): summed.astype(jnp.bfloat16).reshape(n_zhi, n_x, n_core, width, length)]
    dot_general x6 -> x5, matrix products: 15.2 us -> 11.4 us  [dot_rows(): lax.dot_general(left, right, (((1,), (1,)), ((), ())), preferred_element_...]
    ppermute x16 -> x8, waiting for transfers between devices: 9.97 us -> 8.31 us  [from_behind(): return lax.ppermute(block, axis, route)]
  transfers between devices with their start and end apart: 18 -> 22, of which waited for: 9 -> 12; matrix products, arithmetic and copies ran while one was open for 3% -> 6% of each run, Pallas kernels for 0% -> 0%
where the time goes in v1:
time: 224 us; the launch traced here: 223 us
  starting transfers between devices  121 us (54%)
  waiting for transfers between devices  62.8 us (28%)
  local copies, waits for them, and re-layouts  16.2 us (7%)
  matrix products  14.1 us (6%)
  other arithmetic  7.49 us (3%)
    ppermute x14, starting transfers between devices, shift(): lax.ppermute(block, axis, [(i, (i + step) % size) for i in range(size)])  103 us
    ppermute x14, waiting for transfers between devices, shift(): lax.ppermute(block, axis, [(i, (i + step) % size) for i in range(size)])  54.5 us
    ppermute x8, starting transfers between devices, from_behind(): return lax.ppermute(block, axis, route)  18.4 us
    dot_general x5, matrix products, dot_rows(): lax.dot_general(left, right, (((1,), (1,)), ((), ())), preferred_element_...  11.4 us
    ppermute x8, waiting for transfers between devices, from_behind(): return lax.ppermute(block, axis, route)  8.31 us
    unnamed x21, local copies, waits for them, and re-layouts  5.84 us
    convert_element_type x1, local copies, waits for them, and re-layouts, body(): summed.astype(jnp.bfloat16).reshape(n_zhi, n_x, n_core, width, length)  4.57 us
  transfers between devices with their start and end apart: 22, of which 12 were waited for; matrix products, arithmetic and copies ran while one was open for 6% of the time, Pallas kernels for 0%

profile of v1, /device:TPU:1, one launch (start us, length us, event | category | flops | bytes accessed | tf_op | source)
XLA Modules:
  0.0 222.5 jit_solution(11489169905297969305)
XLA Ops:
  0.0 16.4 %collective-permute-start.4 = (bf16[256,168]{0,1:T(8,128)(2,1)}, bf16[256,168]{0,1:T(8,128)(2,1)}, u32[]{:S(2)}, u32[]{:S(2)}) collective-permute-start(bf16[256,168]{0,1:T(8,128)(2,1)} %param.11), channel_id=1, source_target_pairs={{0,8},{8,16},{16,24},{24,0},{1,9},{9,17},{17,25},{25,1},{2,10},{10... | collective-permute-start | bytes 258056 | tf_op jit(solution)/shard_map/ppermute | solution.py:21
  16.4 19.1 %collective-permute-start.5 = (bf16[256,168]{0,1:T(8,128)(2,1)}, bf16[256,168]{0,1:T(8,128)(2,1)S(1)}, u32[]{:S(2)}, u32[]{:S(2)}) collective-permute-start(bf16[256,168]{0,1:T(8,128)(2,1)} %param.11), channel_id=1, source_target_pairs={{0,16},{8,24},{16,0},{24,8},{1,17},{9,25},{17,1},{25,9},{2,18},{10... | collective-permute-start | bytes 258056 | tf_op jit(solution)/shard_map/ppermute | solution.py:21
  35.5 8.2 %collective-permute-start.6 = (bf16[256,168]{0,1:T(8,128)(2,1)}, bf16[256,168]{0,1:T(8,128)(2,1)S(1)}, u32[]{:S(2)}, u32[]{:S(2)}) collective-permute-start(bf16[256,168]{0,1:T(8,128)(2,1)} %param.11), channel_id=1, source_target_pairs={{0,24},{8,0},{16,8},{24,16},{1,25},{9,1},{17,9},{25,17},{2,26},{10... | collective-permute-start | bytes 258056 | tf_op jit(solution)/shard_map/ppermute | solution.py:21
  46.6 3.3 %collective-permute-start = (bf16[256,256]{1,0:T(8,128)(2,1)}, bf16[256,256]{1,0:T(8,128)(2,1)}, u32[]{:S(2)}, u32[]{:S(2)}) collective-permute-start(bf16[256,256]{1,0:T(8,128)(2,1)} %constant_dynamic-update-slice_fusion), channel_id=1, source_target_pairs={{0,128},{32,160},{64,192},{96,224},{128,256},{160,288},{192,320},{... | collective-permute-start | bytes 393224 | tf_op jit(solution)/shard_map/ppermute | solution.py:17
  49.9 4.6 %collective-permute-start.1 = (bf16[256,256]{1,0:T(8,128)(2,1)}, bf16[256,256]{1,0:T(8,128)(2,1)S(1)}, u32[]{:S(2)}, u32[]{:S(2)}) collective-permute-start(bf16[256,256]{1,0:T(8,128)(2,1)} %constant_dynamic-update-slice_fusion), channel_id=1, source_target_pairs={{0,96},{32,128},{64,160},{96,192},{128,224},{160,256},{192,288},{2... | collective-permute-start | bytes 393224 | tf_op jit(solution)/shard_map/ppermute | solution.py:17
  59.7 6.0 %collective-permute-done.6 = bf16[256,168]{0,1:T(8,128)(2,1)S(1)} collective-permute-done((bf16[256,168]{0,1:T(8,128)(2,1)}, bf16[256,168]{0,1:T(8,128)(2,1)S(1)}, u32[]{:S(2)}, u32[]{:S(2)}) %collective-permute-start.6) | collective-permute-done | bytes 86048 | tf_op jit(solution)/shard_map/ppermute | solution.py:21
  68.9 4.4 %collective-permute-start.8 = (bf16[4,256,168]{1,2,0:T(8,128)(2,1)S(1)}, bf16[4,256,168]{1,2,0:T(8,128)(2,1)S(1)}, u32[]{:S(2)}, u32[]{:S(2)}) collective-permute-start(bf16[4,256,168]{1,2,0:T(8,128)(2,1)S(1)} %bitcast_dynamic-update-slice_fusion.6), channel_id=1, source_target_pairs={{0,4},{2,6},{4,0},{6,2},{1,5},{3,7},{5,1},{7,3},{8,12},{10,14},{12... | collective-permute-start | bytes 1032200 | tf_op jit(solution)/shard_map/ppermute | solution.py:21
  73.4 4.6 %collective-permute-done.7 = bf16[4,256,168]{1,2,0:T(8,128)(2,1)S(1)} collective-permute-done((bf16[4,256,168]{1,2,0:T(8,128)(2,1)S(1)}, bf16[4,256,168]{1,2,0:T(8,128)(2,1)S(1)}, u32[]{:S(2)}, u32[]{:S(2)}) %collective-permute-start.7) | collective-permute-done | bytes 344096 | tf_op jit(solution)/shard_map/ppermute | solution.py:21
  77.9 3.2 %collective-permute-start.9 = (bf16[4,256,168]{1,2,0:T(8,128)(2,1)S(1)}, bf16[4,256,168]{1,2,0:T(8,128)(2,1)S(1)}, u32[]{:S(2)}, u32[]{:S(2)}) collective-permute-start(bf16[4,256,168]{1,2,0:T(8,128)(2,1)S(1)} %bitcast_dynamic-update-slice_fusion.6), channel_id=1, source_target_pairs={{0,6},{2,0},{4,2},{6,4},{1,7},{3,1},{5,3},{7,5},{8,14},{10,8},{12,... | collective-permute-start | bytes 1032200 | tf_op jit(solution)/shard_map/ppermute | solution.py:21
  81.2 5.1 %collective-permute-done.8 = bf16[4,256,168]{1,2,0:T(8,128)(2,1)S(1)} collective-permute-done((bf16[4,256,168]{1,2,0:T(8,128)(2,1)S(1)}, bf16[4,256,168]{1,2,0:T(8,128)(2,1)S(1)}, u32[]{:S(2)}, u32[]{:S(2)}) %collective-permute-start.8) | collective-permute-done | bytes 344096 | tf_op jit(solution)/shard_map/ppermute | solution.py:21
  86.3 3.2 %collective-permute-start.3 = (bf16[256,256]{1,0:T(8,128)(2,1)}, bf16[256,256]{1,0:T(8,128)(2,1)S(1)}, u32[]{:S(2)}, u32[]{:S(2)}) collective-permute-start(bf16[256,256]{1,0:T(8,128)(2,1)} %constant_dynamic-update-slice_fusion), channel_id=1, source_target_pairs={{0,32},{32,64},{64,96},{96,128},{128,160},{160,192},{192,224},{224... | collective-permute-start | bytes 393224 | tf_op jit(solution)/shard_map/ppermute | solution.py:17
  89.6 3.6 %collective-permute-start.10 = (bf16[4,4,256,168]{2,3,1,0:T(8,128)(2,1)S(1)}, bf16[4,4,256,168]{2,3,1,0:T(8,128)(2,1)S(1)}, u32[]{:S(2)}, u32[]{:S(2)}) collective-permute-start(bf16[4,4,256,168]{2,3,1,0:T(8,128)(2,1)S(1)} %bitcast_dynamic-update-slice_fusion.2), channel_id=1, source_target_pairs={{0,1},{1,0},{2,3},{3,2},{4,5},{5,4},{6,7},{7,6},{8,9},{9,8},{10,11... | collective-permute-start | bytes 4128776 | tf_op jit(solution)/shard_map/ppermute | solution.py:21
  106.8 3.6 %fusion.16 = f32[256,5376]{1,0:T(8,128)} fusion(bf16[5376,128]{1,0:T(8,128)(2,1)S(1)} %copy-done, bf16[256,1280]{0,1:T(8,128)(2,1)S(1)} %multiply_convert_fusion, bf16[1280,256]{1,0:T(8,128)(2,1)S(1)} %constant_dynamic-update-slice_fusion.7), kind=kOutput, calls=%fused_computation.27 | convolution fusion | flops 436273152 | bytes 7864320 | tf_op jit(solution)/shard_map/dot_general | solution.py:44
  114.9 3.8 %collective-permute-done.14 = bf16[256,256]{0,1:T(8,128)(2,1)} collective-permute-done((bf16[256,256]{0,1:T(8,128)(2,1)}, bf16[256,256]{0,1:T(8,128)(2,1)}, u32[]{:S(2)}, u32[]{:S(2)}) %collective-permute-start.14) | collective-permute-done | bytes 131104 | tf_op jit(solution)/shard_map/ppermute | solution.py:17
  119.8 4.0 %convolution_add_fusion.1 = f32[256,5376]{1,0:T(8,128)S(1)} fusion(f32[256,5376]{1,0:T(8,128)} %fusion.16, bf16[5376,128]{1,0:T(8,128)(2,1)} %param.14, bf16[256,256]{0,1:T(8,128)(2,1)S(1)} %add_convert_fusion), kind=kOutput, calls=%fused_computation.1 | convolution fusion | flops 353697792 | bytes 12451840 | tf_op jit(solution)/shard_map/dot_general | solution.py:44
  126.3 4.6 %copy.18 = bf16[5376,256]{1,0:T(8,128)(2,1)} copy(bf16[5376,256]{0,1:T(8,128)(2,1)} %fusion.1) | data formatting | bytes 5505024 | tf_op jit(solution)/shard_map/convert_element_type | solution.py:113
  133.4 3.4 %collective-permute-start.15 = (bf16[4,4,168,256]{3,2,1,0:T(8,128)(2,1)}, bf16[4,4,168,256]{3,2,1,0:T(8,128)(2,1)S(1)}, u32[]{:S(2)}, u32[]{:S(2)}) collective-permute-start(bf16[4,4,168,256]{3,2,1,0:T(8,128)(2,1)} %dynamic-slice_bitcast_fusion), channel_id=1, source_target_pairs={{0,1},{1,0},{2,3},{3,2},{4,5},{5,4},{6,7},{7,6},{8,9},{9,8},{10,11... | collective-permute-start | bytes 4128776 | tf_op jit(solution)/shard_map/ppermute | solution.py:21
  145.5 4.5 %collective-permute-start.17 = (bf16[4,168,256]{2,1,0:T(8,128)(2,1)S(1)}, bf16[4,168,256]{2,1,0:T(8,128)(2,1)S(1)}, u32[]{:S(2)}, u32[]{:S(2)}) collective-permute-start(bf16[4,168,256]{2,1,0:T(8,128)(2,1)S(1)} %get-tuple-element.7), channel_id=1, source_target_pairs={{0,4},{2,6},{4,0},{6,2},{1,5},{3,7},{5,1},{7,3},{8,12},{10,14},{12... | collective-permute-start | bytes 1032200 | tf_op jit(solution)/shard_map/ppermute | solution.py:21
  152.1 3.3 %collective-permute-done.16 = bf16[4,168,256]{2,1,0:T(8,128)(2,1)S(1)} collective-permute-done((bf16[4,168,256]{2,1,0:T(8,128)(2,1)S(1)}, bf16[4,168,256]{2,1,0:T(8,128)(2,1)S(1)}, u32[]{:S(2)}, u32[]{:S(2)}) %collective-permute-start.16) | collective-permute-done | bytes 344096 | tf_op jit(solution)/shard_map/ppermute | solution.py:21
  155.4 7.9 %collective-permute-done.17 = bf16[4,168,256]{2,1,0:T(8,128)(2,1)S(1)} collective-permute-done((bf16[4,168,256]{2,1,0:T(8,128)(2,1)S(1)}, bf16[4,168,256]{2,1,0:T(8,128)(2,1)S(1)}, u32[]{:S(2)}, u32[]{:S(2)}) %collective-permute-start.17) | collective-permute-done | bytes 344096 | tf_op jit(solution)/shard_map/ppermute | solution.py:21
  166.3 9.6 %collective-permute-start.19 = (bf16[168,256]{1,0:T(8,128)(2,1)S(1)}, bf16[168,256]{1,0:T(8,128)(2,1)S(1)}, u32[]{:S(2)}, u32[]{:S(2)}) collective-permute-start(bf16[168,256]{1,0:T(8,128)(2,1)S(1)} %get-tuple-element.8), channel_id=1, source_target_pairs={{0,8},{8,16},{16,24},{24,0},{1,9},{9,17},{17,25},{25,1},{2,10},{10... | collective-permute-start | bytes 258056 | tf_op jit(solution)/shard_map/ppermute | solution.py:21
  175.9 13.9 %collective-permute-start.20 = (bf16[168,256]{1,0:T(8,128)(2,1)S(1)}, bf16[168,256]{1,0:T(8,128)(2,1)S(1)}, u32[]{:S(2)}, u32[]{:S(2)}) collective-permute-start(bf16[168,256]{1,0:T(8,128)(2,1)S(1)} %get-tuple-element.10), channel_id=1, source_target_pairs={{0,16},{8,24},{16,0},{24,8},{1,17},{9,25},{17,1},{25,9},{2,18},{10... | collective-permute-start | bytes 258056 | tf_op jit(solution)/shard_map/ppermute | solution.py:21
  189.8 9.0 %collective-permute-start.21 = (bf16[168,256]{1,0:T(8,128)(2,1)S(1)}, bf16[168,256]{1,0:T(8,128)(2,1)S(1)}, u32[]{:S(2)}, u32[]{:S(2)}) collective-permute-start(bf16[168,256]{1,0:T(8,128)(2,1)S(1)} %get-tuple-element.9), channel_id=1, source_target_pairs={{0,24},{8,0},{16,8},{24,16},{1,25},{9,1},{17,9},{25,17},{2,26},{10... | collective-permute-start | bytes 258056 | tf_op jit(solution)/shard_map/ppermute | solution.py:21
  200.4 21.5 %collective-permute-done.21 = bf16[168,256]{1,0:T(8,128)(2,1)S(1)} collective-permute-done((bf16[168,256]{1,0:T(8,128)(2,1)S(1)}, bf16[168,256]{1,0:T(8,128)(2,1)S(1)}, u32[]{:S(2)}, u32[]{:S(2)}) %collective-permute-start.21) | collective-permute-done | bytes 86048 | tf_op jit(solution)/shard_map/ppermute | solution.py:21
  (78 shorter events, 51.1 us)
Async XLA Ops:
  0.0 106.7 %copy-start = (bf16[5376,128]{1,0:T(8,128)(2,1)S(1)}, bf16[5376,128]{1,0:T(8,128)(2,1)}, u32[]{:S(2)}) copy-start(bf16[5376,128]{1,0:T(8,128)(2,1)} %param.13) | copy-start | bytes 4128772
  0.0 56.7 %collective-permute-start.4 = (bf16[256,168]{0,1:T(8,128)(2,1)}, bf16[256,168]{0,1:T(8,128)(2,1)}, u32[]{:S(2)}, u32[]{:S(2)}) collective-permute-start(bf16[256,168]{0,1:T(8,128)(2,1)} %param.11), channel_id=1, source_target_pairs={{0,8},{8,16},{16,24},{24,0},{1,9},{9,17},{17,25},{25,1},{2,10},{10... | collective-permute-start | bytes 258056 | tf_op jit(solution)/shard_map/ppermute | solution.py:21
  16.4 43.3 %collective-permute-start.5 = (bf16[256,168]{0,1:T(8,128)(2,1)}, bf16[256,168]{0,1:T(8,128)(2,1)S(1)}, u32[]{:S(2)}, u32[]{:S(2)}) collective-permute-start(bf16[256,168]{0,1:T(8,128)(2,1)} %param.11), channel_id=1, source_target_pairs={{0,16},{8,24},{16,0},{24,8},{1,17},{9,25},{17,1},{25,9},{2,18},{10... | collective-permute-start | bytes 258056 | tf_op jit(solution)/shard_map/ppermute | solution.py:21
  35.5 30.2 %collective-permute-start.6 = (bf16[256,168]{0,1:T(8,128)(2,1)}, bf16[256,168]{0,1:T(8,128)(2,1)S(1)}, u32[]{:S(2)}, u32[]{:S(2)}) collective-permute-start(bf16[256,168]{0,1:T(8,128)(2,1)} %param.11), channel_id=1, source_target_pairs={{0,24},{8,0},{16,8},{24,16},{1,25},{9,1},{17,9},{25,17},{2,26},{10... | collective-permute-start | bytes 258056 | tf_op jit(solution)/shard_map/ppermute | solution.py:21
  46.6 46.5 %collective-permute-start = (bf16[256,256]{1,0:T(8,128)(2,1)}, bf16[256,256]{1,0:T(8,128)(2,1)}, u32[]{:S(2)}, u32[]{:S(2)}) collective-permute-start(bf16[256,256]{1,0:T(8,128)(2,1)} %constant_dynamic-update-slice_fusion), channel_id=1, source_target_pairs={{0,128},{32,160},{64,192},{96,224},{128,256},{160,288},{192,320},{... | collective-permute-start | bytes 393224 | tf_op jit(solution)/shard_map/ppermute | solution.py:17
  49.9 44.2 %collective-permute-start.1 = (bf16[256,256]{1,0:T(8,128)(2,1)}, bf16[256,256]{1,0:T(8,128)(2,1)S(1)}, u32[]{:S(2)}, u32[]{:S(2)}) collective-permute-start(bf16[256,256]{1,0:T(8,128)(2,1)} %constant_dynamic-update-slice_fusion), channel_id=1, source_target_pairs={{0,96},{32,128},{64,160},{96,192},{128,224},{160,256},{192,288},{2... | collective-permute-start | bytes 393224 | tf_op jit(solution)/shard_map/ppermute | solution.py:17
  56.7 37.4 %collective-permute-start.2 = (bf16[256,256]{1,0:T(8,128)(2,1)}, bf16[256,256]{1,0:T(8,128)(2,1)S(1)}, u32[]{:S(2)}, u32[]{:S(2)}) collective-permute-start(bf16[256,256]{1,0:T(8,128)(2,1)} %constant_dynamic-update-slice_fusion), channel_id=1, source_target_pairs={{0,64},{32,96},{64,128},{96,160},{128,192},{160,224},{192,256},{22... | collective-permute-start | bytes 393224 | tf_op jit(solution)/shard_map/ppermute | solution.py:17
  65.7 12.2 %collective-permute-start.7 = (bf16[4,256,168]{1,2,0:T(8,128)(2,1)S(1)}, bf16[4,256,168]{1,2,0:T(8,128)(2,1)S(1)}, u32[]{:S(2)}, u32[]{:S(2)}) collective-permute-start(bf16[4,256,168]{1,2,0:T(8,128)(2,1)S(1)} %bitcast_dynamic-update-slice_fusion.6), channel_id=1, source_target_pairs={{0,2},{2,4},{4,6},{6,0},{1,3},{3,5},{5,7},{7,1},{8,10},{10,12},{12... | collective-permute-start | bytes 1032200 | tf_op jit(solution)/shard_map/ppermute | solution.py:21
  68.9 17.4 %collective-permute-start.8 = (bf16[4,256,168]{1,2,0:T(8,128)(2,1)S(1)}, bf16[4,256,168]{1,2,0:T(8,128)(2,1)S(1)}, u32[]{:S(2)}, u32[]{:S(2)}) collective-permute-start(bf16[4,256,168]{1,2,0:T(8,128)(2,1)S(1)} %bitcast_dynamic-update-slice_fusion.6), channel_id=1, source_target_pairs={{0,4},{2,6},{4,0},{6,2},{1,5},{3,7},{5,1},{7,3},{8,12},{10,14},{12... | collective-permute-start | bytes 1032200 | tf_op jit(solution)/shard_map/ppermute | solution.py:21
  77.9 11.6 %collective-permute-start.9 = (bf16[4,256,168]{1,2,0:T(8,128)(2,1)S(1)}, bf16[4,256,168]{1,2,0:T(8,128)(2,1)S(1)}, u32[]{:S(2)}, u32[]{:S(2)}) collective-permute-start(bf16[4,256,168]{1,2,0:T(8,128)(2,1)S(1)} %bitcast_dynamic-update-slice_fusion.6), channel_id=1, source_target_pairs={{0,6},{2,0},{4,2},{6,4},{1,7},{3,1},{5,3},{7,5},{8,14},{10,8},{12,... | collective-permute-start | bytes 1032200 | tf_op jit(solution)/shard_map/ppermute | solution.py:21
  81.2 13.1 %copy-start.6 = (bf16[256,128]{1,0:T(8,128)(2,1)S(1)}, bf16[256,128]{1,0:T(8,128)(2,1)}, u32[]{:S(2)}) copy-start(bf16[256,128]{1,0:T(8,128)(2,1)} %param.8) | copy-start | bytes 196612
  86.3 7.9 %collective-permute-start.3 = (bf16[256,256]{1,0:T(8,128)(2,1)}, bf16[256,256]{1,0:T(8,128)(2,1)S(1)}, u32[]{:S(2)}, u32[]{:S(2)}) collective-permute-start(bf16[256,256]{1,0:T(8,128)(2,1)} %constant_dynamic-update-slice_fusion), channel_id=1, source_target_pairs={{0,32},{32,64},{64,96},{96,128},{128,160},{160,192},{192,224},{224... | collective-permute-start | bytes 393224 | tf_op jit(solution)/shard_map/ppermute | solution.py:17
  89.6 6.5 %collective-permute-start.10 = (bf16[4,4,256,168]{2,3,1,0:T(8,128)(2,1)S(1)}, bf16[4,4,256,168]{2,3,1,0:T(8,128)(2,1)S(1)}, u32[]{:S(2)}, u32[]{:S(2)}) collective-permute-start(bf16[4,4,256,168]{2,3,1,0:T(8,128)(2,1)S(1)} %bitcast_dynamic-update-slice_fusion.2), channel_id=1, source_target_pairs={{0,1},{1,0},{2,3},{3,2},{4,5},{5,4},{6,7},{7,6},{8,9},{9,8},{10,11... | collective-permute-start | bytes 4128776 | tf_op jit(solution)/shard_map/ppermute | solution.py:21
  101.6 8.8 %collective-permute-start.11 = (bf16[256,256]{0,1:T(8,128)(2,1)}, bf16[256,256]{0,1:T(8,128)(2,1)S(1)}, u32[]{:S(2)}, u32[]{:S(2)}) collective-permute-start(bf16[256,256]{0,1:T(8,128)(2,1)} %get-tuple-element.11), channel_id=1, source_target_pairs={{32,0},{64,32},{96,64},{128,96},{160,128},{192,160},{224,192},{256... | collective-permute-start | bytes 393224 | tf_op jit(solution)/shard_map/ppermute | solution.py:17
  102.8 8.9 %collective-permute-start.12 = (bf16[256,256]{0,1:T(8,128)(2,1)}, bf16[256,256]{0,1:T(8,128)(2,1)}, u32[]{:S(2)}, u32[]{:S(2)}) collective-permute-start(bf16[256,256]{0,1:T(8,128)(2,1)} %get-tuple-element.12), channel_id=1, source_target_pairs={{64,0},{96,32},{128,64},{160,96},{192,128},{224,160},{256,192},{28... | collective-permute-start | bytes 393224 | tf_op jit(solution)/shard_map/ppermute | solution.py:17
  104.1 10.7 %collective-permute-start.13 = (bf16[256,256]{0,1:T(8,128)(2,1)}, bf16[256,256]{0,1:T(8,128)(2,1)}, u32[]{:S(2)}, u32[]{:S(2)}) collective-permute-start(bf16[256,256]{0,1:T(8,128)(2,1)} %get-tuple-element.14), channel_id=1, source_target_pairs={{96,0},{128,32},{160,64},{192,96},{224,128},{256,160},{288,192},{3... | collective-permute-start | bytes 393224 | tf_op jit(solution)/shard_map/ppermute | solution.py:17
  105.4 13.2 %collective-permute-start.14 = (bf16[256,256]{0,1:T(8,128)(2,1)}, bf16[256,256]{0,1:T(8,128)(2,1)}, u32[]{:S(2)}, u32[]{:S(2)}) collective-permute-start(bf16[256,256]{0,1:T(8,128)(2,1)} %get-tuple-element.13), channel_id=1, source_target_pairs={{128,0},{160,32},{192,64},{224,96},{256,128},{288,160},{320,192},{... | collective-permute-start | bytes 393224 | tf_op jit(solution)/shard_map/ppermute | solution.py:17
  133.4 6.3 %collective-permute-start.15 = (bf16[4,4,168,256]{3,2,1,0:T(8,128)(2,1)}, bf16[4,4,168,256]{3,2,1,0:T(8,128)(2,1)S(1)}, u32[]{:S(2)}, u32[]{:S(2)}) collective-permute-start(bf16[4,4,168,256]{3,2,1,0:T(8,128)(2,1)} %dynamic-slice_bitcast_fusion), channel_id=1, source_target_pairs={{0,1},{1,0},{2,3},{3,2},{4,5},{5,4},{6,7},{7,6},{8,9},{9,8},{10,11... | collective-permute-start | bytes 4128776 | tf_op jit(solution)/shard_map/ppermute | solution.py:21
  143.0 12.4 %collective-permute-start.16 = (bf16[4,168,256]{2,1,0:T(8,128)(2,1)S(1)}, bf16[4,168,256]{2,1,0:T(8,128)(2,1)S(1)}, u32[]{:S(2)}, u32[]{:S(2)}) collective-permute-start(bf16[4,168,256]{2,1,0:T(8,128)(2,1)S(1)} %get-tuple-element.5), channel_id=1, source_target_pairs={{0,2},{2,4},{4,6},{6,0},{1,3},{3,5},{5,7},{7,1},{8,10},{10,12},{12... | collective-permute-start | bytes 1032200 | tf_op jit(solution)/shard_map/ppermute | solution.py:21
  145.5 17.8 %collective-permute-start.17 = (bf16[4,168,256]{2,1,0:T(8,128)(2,1)S(1)}, bf16[4,168,256]{2,1,0:T(8,128)(2,1)S(1)}, u32[]{:S(2)}, u32[]{:S(2)}) collective-permute-start(bf16[4,168,256]{2,1,0:T(8,128)(2,1)S(1)} %get-tuple-element.7), channel_id=1, source_target_pairs={{0,4},{2,6},{4,0},{6,2},{1,5},{3,7},{5,1},{7,3},{8,12},{10,14},{12... | collective-permute-start | bytes 1032200 | tf_op jit(solution)/shard_map/ppermute | solution.py:21
  150.1 14.9 %collective-permute-start.18 = (bf16[4,168,256]{2,1,0:T(8,128)(2,1)S(1)}, bf16[4,168,256]{2,1,0:T(8,128)(2,1)S(1)}, u32[]{:S(2)}, u32[]{:S(2)}) collective-permute-start(bf16[4,168,256]{2,1,0:T(8,128)(2,1)S(1)} %get-tuple-element.6), channel_id=1, source_target_pairs={{0,6},{2,0},{4,2},{6,4},{1,7},{3,1},{5,3},{7,5},{8,14},{10,8},{12,... | collective-permute-start | bytes 1032200 | tf_op jit(solution)/shard_map/ppermute | solution.py:21
  166.3 32.5 %collective-permute-start.19 = (bf16[168,256]{1,0:T(8,128)(2,1)S(1)}, bf16[168,256]{1,0:T(8,128)(2,1)S(1)}, u32[]{:S(2)}, u32[]{:S(2)}) collective-permute-start(bf16[168,256]{1,0:T(8,128)(2,1)S(1)} %get-tuple-element.8), channel_id=1, source_target_pairs={{0,8},{8,16},{16,24},{24,0},{1,9},{9,17},{17,25},{25,1},{2,10},{10... | collective-permute-start | bytes 258056 | tf_op jit(solution)/shard_map/ppermute | solution.py:21
  175.9 24.5 %collective-permute-start.20 = (bf16[168,256]{1,0:T(8,128)(2,1)S(1)}, bf16[168,256]{1,0:T(8,128)(2,1)S(1)}, u32[]{:S(2)}, u32[]{:S(2)}) collective-permute-start(bf16[168,256]{1,0:T(8,128)(2,1)S(1)} %get-tuple-element.10), channel_id=1, source_target_pairs={{0,16},{8,24},{16,0},{24,8},{1,17},{9,25},{17,1},{25,9},{2,18},{10... | collective-permute-start | bytes 258056 | tf_op jit(solution)/shard_map/ppermute | solution.py:21
  189.8 32.0 %collective-permute-start.21 = (bf16[168,256]{1,0:T(8,128)(2,1)S(1)}, bf16[168,256]{1,0:T(8,128)(2,1)S(1)}, u32[]{:S(2)}, u32[]{:S(2)}) collective-permute-start(bf16[168,256]{1,0:T(8,128)(2,1)S(1)} %get-tuple-element.9), channel_id=1, source_target_pairs={{0,24},{8,0},{16,8},{24,16},{1,25},{9,1},{17,9},{25,17},{2,26},{10... | collective-permute-start | bytes 258056 | tf_op jit(solution)/shard_map/ppermute | solution.py:21
  (5 other events, 33.6 us)

commit v2 on v1

--- a/solution.py
+++ b/solution.py
@@ -22,6 +22,8 @@
 
 
 def gather_axis(block, axis, size):
+    if size == 4:
+        return ring_gather(block, axis)
     me = lax.axis_index(axis)
     buf = jnp.zeros((size,) + block.shape, block.dtype)
     buf = lax.dynamic_update_index_in_dim(buf, block, me, 0)
@@ -31,7 +33,43 @@
     return buf
 
 
+def ring_gather(block, axis):
+    me = lax.axis_index(axis)
+    half = block.shape[0] // 2
+    ahead = shift(block, axis, 4, 1)
+    behind = shift(block, axis, 4, -1)
+    far = jnp.concatenate(
+        [shift(ahead[:half], axis, 4, 1), shift(behind[half:], axis, 4, -1)], axis=0
+    )
+    buf = jnp.zeros((4,) + block.shape, block.dtype)
+    buf = lax.dynamic_update_index_in_dim(buf, block, me, 0)
+    buf = lax.dynamic_update_index_in_dim(buf, ahead, (me + 3) % 4, 0)
+    buf = lax.dynamic_update_index_in_dim(buf, behind, (me + 1) % 4, 0)
+    return lax.dynamic_update_index_in_dim(buf, far, (me + 2) % 4, 0)
+
+
+def ring_scatter(parts, axis, dim):
+    me = lax.axis_index(axis)
+
+    def piece(k):
+        return lax.dynamic_index_in_dim(parts, k % 4, dim, keepdims=False).astype(jnp.float32)
+
+    far = piece(me + 2)
+    half = far.shape[0] // 2
+    got_a = shift(far[:half].astype(jnp.bfloat16), axis, 4, 1).astype(jnp.float32)
+    got_b = shift(far[half:].astype(jnp.bfloat16), axis, 4, -1).astype(jnp.float32)
+    up = piece(me + 1)
+    up = jnp.concatenate([up[:half] + got_a, up[half:]], axis=0)
+    down = piece(me + 3)
+    down = jnp.concatenate([down[:half], down[half:] + got_b], axis=0)
+    acc = piece(me)
+    acc = acc + shift(up.astype(jnp.bfloat16), axis, 4, 1).astype(jnp.float32)
+    return acc + shift(down.astype(jnp.bfloat16), axis, 4, -1).astype(jnp.float32)
+
+
 def scatter_axis(parts, axis, size, dim):
+    if size == 4:
+        return ring_scatter(parts, axis, dim)
     me = lax.axis_index(axis)
     acc = lax.dynamic_index_in_dim(parts, me, dim, keepdims=False).astype(jnp.float32)
     for step in range(1, size):

time: 224 us -> 228 us (1.018)
  starting transfers between devices: 121 us -> 127 us
    ppermute x14 -> x18, starting transfers between devices: 103 us -> 109 us  [shift(): lax.ppermute(block, axis, [(i, (i + step) % size) for i in range(size)])]
    ppermute x14 -> x18, waiting for transfers between devices: 54.5 us -> 51.7 us  [shift(): lax.ppermute(block, axis, [(i, (i + step) % size) for i in range(size)])]
    unnamed x21 -> x22, local copies, waits for them, and re-layouts: 5.84 us -> 5.29 us
  transfers between devices with their start and end apart: 22 -> 26, of which waited for: 12 -> 14; matrix products, arithmetic and copies ran while one was open for 6% -> 6% of each run, Pallas kernels for 0% -> 0%
where the time goes in v2:
time: 228 us; the launch traced here: 226 us
  starting transfers between devices  127 us (56%)
  waiting for transfers between devices  61.3 us (27%)
  local copies, waits for them, and re-layouts  14.8 us (6%)
  matrix products  14.1 us (6%)
  other arithmetic  7.72 us (3%)
    ppermute x18, starting transfers between devices, shift(): lax.ppermute(block, axis, [(i, (i + step) % size) for i in range(size)])  109 us
    ppermute x18, waiting for transfers between devices, shift(): lax.ppermute(block, axis, [(i, (i + step) % size) for i in range(size)])  51.7 us
    ppermute x8, starting transfers between devices, from_behind(): return lax.ppermute(block, axis, route)  17.7 us
    dot_general x5, matrix products, dot_rows(): lax.dot_general(left, right, (((1,), (1,)), ((), ())), preferred_element_...  11.5 us
    ppermute x8, waiting for transfers between devices, from_behind(): return lax.ppermute(block, axis, route)  9.59 us
    unnamed x22, local copies, waits for them, and re-layouts  5.29 us
    convert_element_type x1, local copies, waits for them, and re-layouts, body(): summed.astype(jnp.bfloat16).reshape(n_zhi, n_x, n_core, width, length)  4.59 us
  transfers between devices with their start and end apart: 26, of which 14 were waited for; matrix products, arithmetic and copies ran while one was open for 6% of the time, Pallas kernels for 0%

profile of v2, /device:TPU:1, one launch (start us, length us, event | category | flops | bytes accessed | tf_op | source)
XLA Modules:
  0.0 225.9 jit_solution(4040046061470165136)
XLA Ops:
  0.0 16.4 %collective-permute-start.4 = (bf16[256,168]{0,1:T(8,128)(2,1)}, bf16[256,168]{0,1:T(8,128)(2,1)S(1)}, u32[]{:S(2)}, u32[]{:S(2)}) collective-permute-start(bf16[256,168]{0,1:T(8,128)(2,1)} %param.11), channel_id=1, source_target_pairs={{0,8},{8,16},{16,24},{24,0},{1,9},{9,17},{17,25},{25,1},{2,10},{10... | collective-permute-start | bytes 258056 | tf_op jit(solution)/shard_map/ppermute | solution.py:21
  16.4 9.2 %collective-permute-start.5 = (bf16[256,168]{0,1:T(8,128)(2,1)}, bf16[256,168]{0,1:T(8,128)(2,1)S(1)}, u32[]{:S(2)}, u32[]{:S(2)}) collective-permute-start(bf16[256,168]{0,1:T(8,128)(2,1)} %param.11), channel_id=1, source_target_pairs={{0,24},{8,0},{16,8},{24,16},{1,25},{9,1},{17,9},{25,17},{2,26},{10... | collective-permute-start | bytes 258056 | tf_op jit(solution)/shard_map/ppermute | solution.py:21
  28.6 3.3 %collective-permute-start = (bf16[256,256]{1,0:T(8,128)(2,1)}, bf16[256,256]{1,0:T(8,128)(2,1)}, u32[]{:S(2)}, u32[]{:S(2)}) collective-permute-start(bf16[256,256]{1,0:T(8,128)(2,1)} %constant_dynamic-update-slice_fusion), channel_id=1, source_target_pairs={{0,128},{32,160},{64,192},{96,224},{128,256},{160,288},{192,320},{... | collective-permute-start | bytes 393224 | tf_op jit(solution)/shard_map/ppermute | solution.py:17
  31.9 5.3 %collective-permute-start.1 = (bf16[256,256]{1,0:T(8,128)(2,1)}, bf16[256,256]{1,0:T(8,128)(2,1)}, u32[]{:S(2)}, u32[]{:S(2)}) collective-permute-start(bf16[256,256]{1,0:T(8,128)(2,1)} %constant_dynamic-update-slice_fusion), channel_id=1, source_target_pairs={{0,96},{32,128},{64,160},{96,192},{128,224},{160,256},{192,288},{2... | collective-permute-start | bytes 393224 | tf_op jit(solution)/shard_map/ppermute | solution.py:17
  41.4 8.2 %collective-permute-start.6 = (bf16[128,168]{0,1:T(8,128)(2,1)S(1)}, bf16[128,168]{0,1:T(8,128)(2,1)S(1)}, u32[]{:S(2)}, u32[]{:S(2)}) collective-permute-start(bf16[128,168]{0,1:T(8,128)(2,1)S(1)} %slice.145), channel_id=1, source_target_pairs={{0,8},{8,16},{16,24},{24,0},{1,9},{9,17},{17,25},{25,1},{2,10},{10... | collective-permute-start | bytes 129032 | tf_op jit(solution)/shard_map/ppermute | solution.py:21
  49.6 5.8 %collective-permute-start.7 = (bf16[128,168]{0,1:T(8,128)(2,1)S(1)}, bf16[128,168]{0,1:T(8,128)(2,1)S(1)}, u32[]{:S(2)}, u32[]{:S(2)}) collective-permute-start(bf16[128,168]{0,1:T(8,128)(2,1)S(1)} %slice.146), channel_id=1, source_target_pairs={{0,24},{8,0},{16,8},{24,16},{1,25},{9,1},{17,9},{25,17},{2,26},{10... | collective-permute-start | bytes 129032 | tf_op jit(solution)/shard_map/ppermute | solution.py:21
  55.5 7.9 %collective-permute-done.7 = bf16[128,168]{0,1:T(8,128)(2,1)S(1)} collective-permute-done((bf16[128,168]{0,1:T(8,128)(2,1)S(1)}, bf16[128,168]{0,1:T(8,128)(2,1)S(1)}, u32[]{:S(2)}, u32[]{:S(2)}) %collective-permute-start.7) | collective-permute-done | bytes 43040 | tf_op jit(solution)/shard_map/ppermute | solution.py:21
  63.4 3.1 %collective-permute-start.8 = (bf16[4,256,168]{1,2,0:T(8,128)(2,1)S(1)}, bf16[4,256,168]{1,2,0:T(8,128)(2,1)S(1)}, u32[]{:S(2)}, u32[]{:S(2)}) collective-permute-start(bf16[4,256,168]{1,2,0:T(8,128)(2,1)S(1)} %fusion.44), channel_id=1, source_target_pairs={{0,2},{2,4},{4,6},{6,0},{1,3},{3,5},{5,7},{7,1},{8,10},{10,12},{12... | collective-permute-start | bytes 1032200 | tf_op jit(solution)/shard_map/ppermute | solution.py:21
  66.5 3.4 %collective-permute-start.9 = (bf16[4,256,168]{1,2,0:T(8,128)(2,1)S(1)}, bf16[4,256,168]{1,2,0:T(8,128)(2,1)S(1)}, u32[]{:S(2)}, u32[]{:S(2)}) collective-permute-start(bf16[4,256,168]{1,2,0:T(8,128)(2,1)S(1)} %fusion.44), channel_id=1, source_target_pairs={{0,6},{2,0},{4,2},{6,4},{1,7},{3,1},{5,3},{7,5},{8,14},{10,8},{12,... | collective-permute-start | bytes 1032200 | tf_op jit(solution)/shard_map/ppermute | solution.py:21
  74.8 4.3 %collective-permute-start.11 = (bf16[2,256,168]{1,2,0:T(8,128)(2,1)S(1)}, bf16[2,256,168]{1,2,0:T(8,128)(2,1)S(1)}, u32[]{:S(2)}, u32[]{:S(2)}) collective-permute-start(bf16[2,256,168]{1,2,0:T(8,128)(2,1)S(1)} %slice.148), channel_id=1, source_target_pairs={{0,6},{2,0},{4,2},{6,4},{1,7},{3,1},{5,3},{7,5},{8,14},{10,8},{12,... | collective-permute-start | bytes 516104 | tf_op jit(solution)/shard_map/ppermute | solution.py:21
  81.9 8.7 %collective-permute-start.12 = (bf16[4,4,256,168]{2,3,1,0:T(8,128)(2,1)S(1)}, bf16[4,4,256,168]{2,3,1,0:T(8,128)(2,1)S(1)}, u32[]{:S(2)}, u32[]{:S(2)}) collective-permute-start(bf16[4,4,256,168]{2,3,1,0:T(8,128)(2,1)S(1)} %fusion.25), channel_id=1, source_target_pairs={{0,1},{1,0},{2,3},{3,2},{4,5},{5,4},{6,7},{7,6},{8,9},{9,8},{10,11... | collective-permute-start | bytes 4128776 | tf_op jit(solution)/shard_map/ppermute | solution.py:21
  105.1 3.6 %fusion.16 = f32[256,5376]{1,0:T(8,128)} fusion(bf16[5376,128]{1,0:T(8,128)(2,1)S(1)} %copy-done, bf16[256,1280]{0,1:T(8,128)(2,1)S(1)} %multiply_convert_fusion, bf16[1280,256]{1,0:T(8,128)(2,1)S(1)} %constant_dynamic-update-slice_fusion.7), kind=kOutput, calls=%fused_computation.27 | convolution fusion | flops 436273152 | bytes 7864320 | tf_op jit(solution)/shard_map/dot_general | solution.py:82
  111.5 3.0 %collective-permute-done.15 = bf16[256,256]{0,1:T(8,128)(2,1)} collective-permute-done((bf16[256,256]{0,1:T(8,128)(2,1)}, bf16[256,256]{0,1:T(8,128)(2,1)}, u32[]{:S(2)}, u32[]{:S(2)}) %collective-permute-start.15) | collective-permute-done | bytes 131104 | tf_op jit(solution)/shard_map/ppermute | solution.py:17
  114.5 3.8 %collective-permute-done.16 = bf16[256,256]{0,1:T(8,128)(2,1)} collective-permute-done((bf16[256,256]{0,1:T(8,128)(2,1)}, bf16[256,256]{0,1:T(8,128)(2,1)}, u32[]{:S(2)}, u32[]{:S(2)}) %collective-permute-start.16) | collective-permute-done | bytes 131104 | tf_op jit(solution)/shard_map/ppermute | solution.py:17
  119.4 4.0 %convolution_add_fusion.1 = f32[256,5376]{1,0:T(8,128)S(1)} fusion(f32[256,5376]{1,0:T(8,128)} %fusion.16, bf16[5376,128]{1,0:T(8,128)(2,1)} %param.14, bf16[256,256]{0,1:T(8,128)(2,1)S(1)} %add_convert_fusion), kind=kOutput, calls=%fused_computation.1 | convolution fusion | flops 353697792 | bytes 12451840 | tf_op jit(solution)/shard_map/dot_general | solution.py:82
  125.9 4.6 %copy.18 = bf16[5376,256]{1,0:T(8,128)(2,1)} copy(bf16[5376,256]{0,1:T(8,128)(2,1)} %fusion.1) | data formatting | bytes 5505024 | tf_op jit(solution)/shard_map/convert_element_type | solution.py:151
  133.0 3.0 %collective-permute-start.17 = (bf16[4,4,168,256]{3,2,1,0:T(8,128)(2,1)}, bf16[4,4,168,256]{3,2,1,0:T(8,128)(2,1)S(1)}, u32[]{:S(2)}, u32[]{:S(2)}) collective-permute-start(bf16[4,4,168,256]{3,2,1,0:T(8,128)(2,1)} %dynamic-slice_bitcast_fusion), channel_id=1, source_target_pairs={{0,1},{1,0},{2,3},{3,2},{4,5},{5,4},{6,7},{7,6},{8,9},{9,8},{10,11... | collective-permute-start | bytes 4128776 | tf_op jit(solution)/shard_map/ppermute | solution.py:21
  142.8 4.6 %collective-permute-start.20 = (bf16[2,168,256]{2,1,0:T(8,128)(2,1)S(1)}, bf16[2,168,256]{2,1,0:T(8,128)(2,1)S(1)}, u32[]{:S(2)}, u32[]{:S(2)}) collective-permute-start(bf16[2,168,256]{2,1,0:T(8,128)(2,1)S(1)} %get-tuple-element.16), channel_id=1, source_target_pairs={{0,6},{2,0},{4,2},{6,4},{1,7},{3,1},{5,3},{7,5},{8,14},{10,8},{12,... | collective-permute-start | bytes 516104 | tf_op jit(solution)/shard_map/ppermute | solution.py:21
  151.6 4.6 %collective-permute-start.21 = (bf16[4,168,256]{2,1,0:T(8,128)(2,1)S(1)}, bf16[4,168,256]{2,1,0:T(8,128)(2,1)S(1)}, u32[]{:S(2)}, u32[]{:S(2)}) collective-permute-start(bf16[4,168,256]{2,1,0:T(8,128)(2,1)S(1)} %pad_maximum_fusion.1), channel_id=1, source_target_pairs={{0,6},{2,0},{4,2},{6,4},{1,7},{3,1},{5,3},{7,5},{8,14},{10,8},{12,... | collective-permute-start | bytes 1032200 | tf_op jit(solution)/shard_map/ppermute | solution.py:21
  156.2 4.8 %collective-permute-done.19 = bf16[4,168,256]{2,1,0:T(8,128)(2,1)S(1)} collective-permute-done((bf16[4,168,256]{2,1,0:T(8,128)(2,1)S(1)}, bf16[4,168,256]{2,1,0:T(8,128)(2,1)S(1)}, u32[]{:S(2)}, u32[]{:S(2)}) %collective-permute-start.19) | collective-permute-done | bytes 344096 | tf_op jit(solution)/shard_map/ppermute | solution.py:21
  163.3 15.4 %collective-permute-start.22 = (bf16[84,256]{1,0:T(8,128)(2,1)S(1)}, bf16[84,256]{1,0:T(8,128)(2,1)S(1)}, u32[]{:S(2)}, u32[]{:S(2)}) collective-permute-start(bf16[84,256]{1,0:T(8,128)(2,1)S(1)} %get-tuple-element.17), channel_id=1, source_target_pairs={{0,8},{8,16},{16,24},{24,0},{1,9},{9,17},{17,25},{25,1},{2,10},{10... | collective-permute-start | bytes 129032 | tf_op jit(solution)/shard_map/ppermute | solution.py:21
  180.7 11.6 %collective-permute-done.24 = bf16[84,256]{1,0:T(8,128)(2,1)S(1)} collective-permute-done((bf16[84,256]{1,0:T(8,128)(2,1)S(1)}, bf16[84,256]{1,0:T(8,128)(2,1)S(1)}, u32[]{:S(2)}, u32[]{:S(2)}) %collective-permute-start.24) | collective-permute-done | bytes 43040 | tf_op jit(solution)/shard_map/ppermute | solution.py:21
  192.3 13.1 %collective-permute-start.23 = (bf16[168,256]{1,0:T(8,128)(2,1)S(1)}, bf16[168,256]{1,0:T(8,128)(2,1)S(1)}, u32[]{:S(2)}, u32[]{:S(2)}) collective-permute-start(bf16[168,256]{1,0:T(8,128)(2,1)S(1)} %pad_maximum_fusion.3), channel_id=1, source_target_pairs={{0,8},{8,16},{16,24},{24,0},{1,9},{9,17},{17,25},{25,1},{2,10},{10... | collective-permute-start | bytes 258056 | tf_op jit(solution)/shard_map/ppermute | solution.py:21
  210.3 15.0 %collective-permute-done.25 = bf16[168,256]{1,0:T(8,128)(2,1)S(1)} collective-permute-done((bf16[168,256]{1,0:T(8,128)(2,1)S(1)}, bf16[168,256]{1,0:T(8,128)(2,1)S(1)}, u32[]{:S(2)}, u32[]{:S(2)}) %collective-permute-start.25) | collective-permute-done | bytes 86048 | tf_op jit(solution)/shard_map/ppermute | solution.py:21
  (103 shorter events, 58.5 us)
Async XLA Ops:
  0.0 41.4 %collective-permute-start.4 = (bf16[256,168]{0,1:T(8,128)(2,1)}, bf16[256,168]{0,1:T(8,128)(2,1)S(1)}, u32[]{:S(2)}, u32[]{:S(2)}) collective-permute-start(bf16[256,168]{0,1:T(8,128)(2,1)} %param.11), channel_id=1, source_target_pairs={{0,8},{8,16},{16,24},{24,0},{1,9},{9,17},{17,25},{25,1},{2,10},{10... | collective-permute-start | bytes 258056 | tf_op jit(solution)/shard_map/ppermute | solution.py:21
  16.4 33.2 %collective-permute-start.5 = (bf16[256,168]{0,1:T(8,128)(2,1)}, bf16[256,168]{0,1:T(8,128)(2,1)S(1)}, u32[]{:S(2)}, u32[]{:S(2)}) collective-permute-start(bf16[256,168]{0,1:T(8,128)(2,1)} %param.11), channel_id=1, source_target_pairs={{0,24},{8,0},{16,8},{24,16},{1,25},{9,1},{17,9},{25,17},{2,26},{10... | collective-permute-start | bytes 258056 | tf_op jit(solution)/shard_map/ppermute | solution.py:21
  28.6 62.0 %collective-permute-start = (bf16[256,256]{1,0:T(8,128)(2,1)}, bf16[256,256]{1,0:T(8,128)(2,1)}, u32[]{:S(2)}, u32[]{:S(2)}) collective-permute-start(bf16[256,256]{1,0:T(8,128)(2,1)} %constant_dynamic-update-slice_fusion), channel_id=1, source_target_pairs={{0,128},{32,160},{64,192},{96,224},{128,256},{160,288},{192,320},{... | collective-permute-start | bytes 393224 | tf_op jit(solution)/shard_map/ppermute | solution.py:17
  31.9 59.7 %collective-permute-start.1 = (bf16[256,256]{1,0:T(8,128)(2,1)}, bf16[256,256]{1,0:T(8,128)(2,1)}, u32[]{:S(2)}, u32[]{:S(2)}) collective-permute-start(bf16[256,256]{1,0:T(8,128)(2,1)} %constant_dynamic-update-slice_fusion), channel_id=1, source_target_pairs={{0,96},{32,128},{64,160},{96,192},{128,224},{160,256},{192,288},{2... | collective-permute-start | bytes 393224 | tf_op jit(solution)/shard_map/ppermute | solution.py:17
  37.2 55.3 %collective-permute-start.2 = (bf16[256,256]{1,0:T(8,128)(2,1)}, bf16[256,256]{1,0:T(8,128)(2,1)S(1)}, u32[]{:S(2)}, u32[]{:S(2)}) collective-permute-start(bf16[256,256]{1,0:T(8,128)(2,1)} %constant_dynamic-update-slice_fusion), channel_id=1, source_target_pairs={{0,64},{32,96},{64,128},{96,160},{128,192},{160,224},{192,256},{22... | collective-permute-start | bytes 393224 | tf_op jit(solution)/shard_map/ppermute | solution.py:17
  41.4 14.1 %collective-permute-start.6 = (bf16[128,168]{0,1:T(8,128)(2,1)S(1)}, bf16[128,168]{0,1:T(8,128)(2,1)S(1)}, u32[]{:S(2)}, u32[]{:S(2)}) collective-permute-start(bf16[128,168]{0,1:T(8,128)(2,1)S(1)} %slice.145), channel_id=1, source_target_pairs={{0,8},{8,16},{16,24},{24,0},{1,9},{9,17},{17,25},{25,1},{2,10},{10... | collective-permute-start | bytes 129032 | tf_op jit(solution)/shard_map/ppermute | solution.py:21
  49.6 13.7 %collective-permute-start.7 = (bf16[128,168]{0,1:T(8,128)(2,1)S(1)}, bf16[128,168]{0,1:T(8,128)(2,1)S(1)}, u32[]{:S(2)}, u32[]{:S(2)}) collective-permute-start(bf16[128,168]{0,1:T(8,128)(2,1)S(1)} %slice.146), channel_id=1, source_target_pairs={{0,24},{8,0},{16,8},{24,16},{1,25},{9,1},{17,9},{25,17},{2,26},{10... | collective-permute-start | bytes 129032 | tf_op jit(solution)/shard_map/ppermute | solution.py:21
  63.4 9.2 %collective-permute-start.8 = (bf16[4,256,168]{1,2,0:T(8,128)(2,1)S(1)}, bf16[4,256,168]{1,2,0:T(8,128)(2,1)S(1)}, u32[]{:S(2)}, u32[]{:S(2)}) collective-permute-start(bf16[4,256,168]{1,2,0:T(8,128)(2,1)S(1)} %fusion.44), channel_id=1, source_target_pairs={{0,2},{2,4},{4,6},{6,0},{1,3},{3,5},{5,7},{7,1},{8,10},{10,12},{12... | collective-permute-start | bytes 1032200 | tf_op jit(solution)/shard_map/ppermute | solution.py:21
  66.5 8.3 %collective-permute-start.9 = (bf16[4,256,168]{1,2,0:T(8,128)(2,1)S(1)}, bf16[4,256,168]{1,2,0:T(8,128)(2,1)S(1)}, u32[]{:S(2)}, u32[]{:S(2)}) collective-permute-start(bf16[4,256,168]{1,2,0:T(8,128)(2,1)S(1)} %fusion.44), channel_id=1, source_target_pairs={{0,6},{2,0},{4,2},{6,4},{1,7},{3,1},{5,3},{7,5},{8,14},{10,8},{12,... | collective-permute-start | bytes 1032200 | tf_op jit(solution)/shard_map/ppermute | solution.py:21
  72.6 7.4 %collective-permute-start.10 = (bf16[2,256,168]{1,2,0:T(8,128)(2,1)S(1)}, bf16[2,256,168]{1,2,0:T(8,128)(2,1)S(1)}, u32[]{:S(2)}, u32[]{:S(2)}) collective-permute-start(bf16[2,256,168]{1,2,0:T(8,128)(2,1)S(1)} %slice.147), channel_id=1, source_target_pairs={{0,2},{2,4},{4,6},{6,0},{1,3},{3,5},{5,7},{7,1},{8,10},{10,12},{12... | collective-permute-start | bytes 516104 | tf_op jit(solution)/shard_map/ppermute | solution.py:21
  79.9 12.5 %collective-permute-start.3 = (bf16[256,256]{1,0:T(8,128)(2,1)}, bf16[256,256]{1,0:T(8,128)(2,1)S(1)}, u32[]{:S(2)}, u32[]{:S(2)}) collective-permute-start(bf16[256,256]{1,0:T(8,128)(2,1)} %constant_dynamic-update-slice_fusion), channel_id=1, source_target_pairs={{0,32},{32,64},{64,96},{96,128},{128,160},{160,192},{192,224},{224... | collective-permute-start | bytes 393224 | tf_op jit(solution)/shard_map/ppermute | solution.py:17
  81.9 12.6 %collective-permute-start.12 = (bf16[4,4,256,168]{2,3,1,0:T(8,128)(2,1)S(1)}, bf16[4,4,256,168]{2,3,1,0:T(8,128)(2,1)S(1)}, u32[]{:S(2)}, u32[]{:S(2)}) collective-permute-start(bf16[4,4,256,168]{2,3,1,0:T(8,128)(2,1)S(1)} %fusion.25), channel_id=1, source_target_pairs={{0,1},{1,0},{2,3},{3,2},{4,5},{5,4},{6,7},{7,6},{8,9},{9,8},{10,11... | collective-permute-start | bytes 4128776 | tf_op jit(solution)/shard_map/ppermute | solution.py:21
  99.9 8.8 %collective-permute-start.13 = (bf16[256,256]{0,1:T(8,128)(2,1)}, bf16[256,256]{0,1:T(8,128)(2,1)S(1)}, u32[]{:S(2)}, u32[]{:S(2)}) collective-permute-start(bf16[256,256]{0,1:T(8,128)(2,1)} %get-tuple-element.11), channel_id=1, source_target_pairs={{32,0},{64,32},{96,64},{128,96},{160,128},{192,160},{224,192},{256... | collective-permute-start | bytes 393224 | tf_op jit(solution)/shard_map/ppermute | solution.py:17
  101.2 10.4 %collective-permute-start.14 = (bf16[256,256]{0,1:T(8,128)(2,1)}, bf16[256,256]{0,1:T(8,128)(2,1)}, u32[]{:S(2)}, u32[]{:S(2)}) collective-permute-start(bf16[256,256]{0,1:T(8,128)(2,1)} %get-tuple-element.12), channel_id=1, source_target_pairs={{64,0},{96,32},{128,64},{160,96},{192,128},{224,160},{256,192},{28... | collective-permute-start | bytes 393224 | tf_op jit(solution)/shard_map/ppermute | solution.py:17
  102.5 12.1 %collective-permute-start.15 = (bf16[256,256]{0,1:T(8,128)(2,1)}, bf16[256,256]{0,1:T(8,128)(2,1)}, u32[]{:S(2)}, u32[]{:S(2)}) collective-permute-start(bf16[256,256]{0,1:T(8,128)(2,1)} %get-tuple-element.14), channel_id=1, source_target_pairs={{96,0},{128,32},{160,64},{192,96},{224,128},{256,160},{288,192},{3... | collective-permute-start | bytes 393224 | tf_op jit(solution)/shard_map/ppermute | solution.py:17
  103.8 14.5 %collective-permute-start.16 = (bf16[256,256]{0,1:T(8,128)(2,1)}, bf16[256,256]{0,1:T(8,128)(2,1)}, u32[]{:S(2)}, u32[]{:S(2)}) collective-permute-start(bf16[256,256]{0,1:T(8,128)(2,1)} %get-tuple-element.13), channel_id=1, source_target_pairs={{128,0},{160,32},{192,64},{224,96},{256,128},{288,160},{320,192},{... | collective-permute-start | bytes 393224 | tf_op jit(solution)/shard_map/ppermute | solution.py:17
  140.8 8.7 %collective-permute-start.18 = (bf16[2,168,256]{2,1,0:T(8,128)(2,1)S(1)}, bf16[2,168,256]{2,1,0:T(8,128)(2,1)S(1)}, u32[]{:S(2)}, u32[]{:S(2)}) collective-permute-start(bf16[2,168,256]{2,1,0:T(8,128)(2,1)S(1)} %get-tuple-element.15), channel_id=1, source_target_pairs={{0,2},{2,4},{4,6},{6,0},{1,3},{3,5},{5,7},{7,1},{8,10},{10,12},{12... | collective-permute-start | bytes 516104 | tf_op jit(solution)/shard_map/ppermute | solution.py:21
  142.8 8.8 %collective-permute-start.20 = (bf16[2,168,256]{2,1,0:T(8,128)(2,1)S(1)}, bf16[2,168,256]{2,1,0:T(8,128)(2,1)S(1)}, u32[]{:S(2)}, u32[]{:S(2)}) collective-permute-start(bf16[2,168,256]{2,1,0:T(8,128)(2,1)S(1)} %get-tuple-element.16), channel_id=1, source_target_pairs={{0,6},{2,0},{4,2},{6,4},{1,7},{3,1},{5,3},{7,5},{8,14},{10,8},{12,... | collective-permute-start | bytes 516104 | tf_op jit(solution)/shard_map/ppermute | solution.py:21
  149.6 11.5 %collective-permute-start.19 = (bf16[4,168,256]{2,1,0:T(8,128)(2,1)S(1)}, bf16[4,168,256]{2,1,0:T(8,128)(2,1)S(1)}, u32[]{:S(2)}, u32[]{:S(2)}) collective-permute-start(bf16[4,168,256]{2,1,0:T(8,128)(2,1)S(1)} %pad_maximum_fusion), channel_id=1, source_target_pairs={{0,2},{2,4},{4,6},{6,0},{1,3},{3,5},{5,7},{7,1},{8,10},{10,12},{12... | collective-permute-start | bytes 1032200 | tf_op jit(solution)/shard_map/ppermute | solution.py:21
  151.6 10.4 %collective-permute-start.21 = (bf16[4,168,256]{2,1,0:T(8,128)(2,1)S(1)}, bf16[4,168,256]{2,1,0:T(8,128)(2,1)S(1)}, u32[]{:S(2)}, u32[]{:S(2)}) collective-permute-start(bf16[4,168,256]{2,1,0:T(8,128)(2,1)S(1)} %pad_maximum_fusion.1), channel_id=1, source_target_pairs={{0,6},{2,0},{4,2},{6,4},{1,7},{3,1},{5,3},{7,5},{8,14},{10,8},{12,... | collective-permute-start | bytes 1032200 | tf_op jit(solution)/shard_map/ppermute | solution.py:21
  163.3 17.4 %collective-permute-start.22 = (bf16[84,256]{1,0:T(8,128)(2,1)S(1)}, bf16[84,256]{1,0:T(8,128)(2,1)S(1)}, u32[]{:S(2)}, u32[]{:S(2)}) collective-permute-start(bf16[84,256]{1,0:T(8,128)(2,1)S(1)} %get-tuple-element.17), channel_id=1, source_target_pairs={{0,8},{8,16},{16,24},{24,0},{1,9},{9,17},{17,25},{25,1},{2,10},{10... | collective-permute-start | bytes 129032 | tf_op jit(solution)/shard_map/ppermute | solution.py:21
  178.7 13.6 %collective-permute-start.24 = (bf16[84,256]{1,0:T(8,128)(2,1)S(1)}, bf16[84,256]{1,0:T(8,128)(2,1)S(1)}, u32[]{:S(2)}, u32[]{:S(2)}) collective-permute-start(bf16[84,256]{1,0:T(8,128)(2,1)S(1)} %get-tuple-element.18), channel_id=1, source_target_pairs={{0,24},{8,0},{16,8},{24,16},{1,25},{9,1},{17,9},{25,17},{2,26},{10... | collective-permute-start | bytes 129032 | tf_op jit(solution)/shard_map/ppermute | solution.py:21
  192.3 18.0 %collective-permute-start.23 = (bf16[168,256]{1,0:T(8,128)(2,1)S(1)}, bf16[168,256]{1,0:T(8,128)(2,1)S(1)}, u32[]{:S(2)}, u32[]{:S(2)}) collective-permute-start(bf16[168,256]{1,0:T(8,128)(2,1)S(1)} %pad_maximum_fusion.3), channel_id=1, source_target_pairs={{0,8},{8,16},{16,24},{24,0},{1,9},{9,17},{17,25},{25,1},{2,10},{10... | collective-permute-start | bytes 258056 | tf_op jit(solution)/shard_map/ppermute | solution.py:21
  205.5 19.8 %collective-permute-start.25 = (bf16[168,256]{1,0:T(8,128)(2,1)S(1)}, bf16[168,256]{1,0:T(8,128)(2,1)S(1)}, u32[]{:S(2)}, u32[]{:S(2)}) collective-permute-start(bf16[168,256]{1,0:T(8,128)(2,1)S(1)} %pad_maximum_fusion.4), channel_id=1, source_target_pairs={{0,24},{8,0},{16,8},{24,16},{1,25},{9,1},{17,9},{25,17},{2,26},{10... | collective-permute-start | bytes 258056 | tf_op jit(solution)/shard_map/ppermute | solution.py:21
  (9 other events, 175.1 us)

commit v3 on v2

--- a/solution.py
+++ b/solution.py
@@ -21,8 +21,8 @@
     return lax.ppermute(block, axis, [(i, (i + step) % size) for i in range(size)])
 
 
-def gather_axis(block, axis, size):
-    if size == 4:
+def gather_axis(block, axis, size, relay=False):
+    if relay and size == 4:
         return ring_gather(block, axis)
     me = lax.axis_index(axis)
     buf = jnp.zeros((size,) + block.shape, block.dtype)
@@ -35,12 +35,9 @@
 
 def ring_gather(block, axis):
     me = lax.axis_index(axis)
-    half = block.shape[0] // 2
     ahead = shift(block, axis, 4, 1)
     behind = shift(block, axis, 4, -1)
-    far = jnp.concatenate(
-        [shift(ahead[:half], axis, 4, 1), shift(behind[half:], axis, 4, -1)], axis=0
-    )
+    far = shift(ahead, axis, 4, 1)
     buf = jnp.zeros((4,) + block.shape, block.dtype)
     buf = lax.dynamic_update_index_in_dim(buf, block, me, 0)
     buf = lax.dynamic_update_index_in_dim(buf, ahead, (me + 3) % 4, 0)
@@ -54,21 +51,16 @@
     def piece(k):
         return lax.dynamic_index_in_dim(parts, k % 4, dim, keepdims=False).astype(jnp.float32)
 
-    far = piece(me + 2)
-    half = far.shape[0] // 2
-    got_a = shift(far[:half].astype(jnp.bfloat16), axis, 4, 1).astype(jnp.float32)
-    got_b = shift(far[half:].astype(jnp.bfloat16), axis, 4, -1).astype(jnp.float32)
-    up = piece(me + 1)
-    up = jnp.concatenate([up[:half] + got_a, up[half:]], axis=0)
-    down = piece(me + 3)
-    down = jnp.concatenate([down[:half], down[half:] + got_b], axis=0)
+    got = shift(piece(me + 2).astype(jnp.bfloat16), axis, 4, 1).astype(jnp.float32)
+    up = (piece(me + 1) + got).astype(jnp.bfloat16)
+    down = piece(me + 3).astype(jnp.bfloat16)
     acc = piece(me)
-    acc = acc + shift(up.astype(jnp.bfloat16), axis, 4, 1).astype(jnp.float32)
-    return acc + shift(down.astype(jnp.bfloat16), axis, 4, -1).astype(jnp.float32)
+    acc = acc + shift(up, axis, 4, 1).astype(jnp.float32)
+    return acc + shift(down, axis, 4, -1).astype(jnp.float32)
 
 
-def scatter_axis(parts, axis, size, dim):
-    if size == 4:
+def scatter_axis(parts, axis, size, dim, relay=False):
+    if relay and size == 4:
         return ring_scatter(parts, axis, dim)
     me = lax.axis_index(axis)
     acc = lax.dynamic_index_in_dim(parts, me, dim, keepdims=False).astype(jnp.float32)
@@ -119,7 +111,7 @@
         length, dim = query.shape
         width = d_out.shape[1]
         seq_index = lax.axis_index("seq")
-        stacked = gather_axis(d_out, "zhi", n_zhi)
+        stacked = gather_axis(d_out, "zhi", n_zhi, relay=True)
         stacked = gather_axis(stacked, "x", n_x)
         stacked = gather_axis(stacked, "core", n_core)
         out_rows = w_out.reshape(w_out.shape[0], n_zhi, n_x, n_core, width)
@@ -151,7 +143,7 @@
         term = summed.astype(jnp.bfloat16).reshape(n_zhi, n_x, n_core, width, length)
         part = scatter_axis(term, "core", n_core, 2)
         part = scatter_axis(part, "x", n_x, 1)
-        part = scatter_axis(part, "zhi", n_zhi, 0)
+        part = scatter_axis(part, "zhi", n_zhi, 0, relay=True)
         return part.T.astype(jnp.bfloat16)
 
     return body

time: 228 us -> 210 us (0.921)
  the two profiles are of different devices: /device:TPU:1 before, /device:TPU:161 now
where the time goes in v3:
time: 210 us; the launch traced here: 209 us
  starting transfers between devices  119 us (57%)
  waiting for transfers between devices  54.7 us (26%)
  local copies, waits for them, and re-layouts  14.7 us (7%)
  matrix products  14.1 us (7%)
  other arithmetic  6.46 us (3%)
    ppermute x14, starting transfers between devices, shift(): lax.ppermute(block, axis, [(i, (i + step) % size) for i in range(size)])  88.1 us
    ppermute x14, waiting for transfers between devices, shift(): lax.ppermute(block, axis, [(i, (i + step) % size) for i in range(size)])  54.7 us
    ppermute x8, starting transfers between devices, from_behind(): return lax.ppermute(block, axis, route)  30.7 us
    dot_general x5, matrix products, dot_rows(): lax.dot_general(left, right, (((1,), (1,)), ((), ())), preferred_element_...  11.4 us
    unnamed x19, local copies, waits for them, and re-layouts  5.21 us
    convert_element_type x1, local copies, waits for them, and re-layouts, body(): summed.astype(jnp.bfloat16).reshape(n_zhi, n_x, n_core, width, length)  4.57 us
  transfers between devices with their start and end apart: 22, of which 11 were waited for; matrix products, arithmetic and copies ran while one was open for 6% of the time, Pallas kernels for 0%

profile of v3, /device:TPU:161, one launch (start us, length us, event | category | flops | bytes accessed | tf_op | source)
XLA Modules:
  0.0 209.5 jit_solution(517246601041838380)
XLA Ops:
  0.0 15.6 %collective-permute-start.4 = (bf16[256,168]{0,1:T(8,128)(2,1)}, bf16[256,168]{0,1:T(8,128)(2,1)S(1)}, u32[]{:S(2)}, u32[]{:S(2)}) collective-permute-start(bf16[256,168]{0,1:T(8,128)(2,1)} %param.11), channel_id=1, source_target_pairs={{0,8},{8,16},{16,24},{24,0},{1,9},{9,17},{17,25},{25,1},{2,10},{10... | collective-permute-start | bytes 258056 | tf_op jit(solution)/shard_map/ppermute | solution.py:21
  15.6 3.5 %collective-permute-start.5 = (bf16[256,168]{0,1:T(8,128)(2,1)}, bf16[256,168]{0,1:T(8,128)(2,1)S(1)}, u32[]{:S(2)}, u32[]{:S(2)}) collective-permute-start(bf16[256,168]{0,1:T(8,128)(2,1)} %param.11), channel_id=1, source_target_pairs={{0,24},{8,0},{16,8},{24,16},{1,25},{9,1},{17,9},{25,17},{2,26},{10... | collective-permute-start | bytes 258056 | tf_op jit(solution)/shard_map/ppermute | solution.py:21
  24.6 4.6 %collective-permute-start.1 = (bf16[256,256]{1,0:T(8,128)(2,1)}, bf16[256,256]{1,0:T(8,128)(2,1)}, u32[]{:S(2)}, u32[]{:S(2)}) collective-permute-start(bf16[256,256]{1,0:T(8,128)(2,1)} %constant_dynamic-update-slice_fusion), channel_id=1, source_target_pairs={{0,96},{32,128},{64,160},{96,192},{128,224},{160,256},{192,288},{2... | collective-permute-start | bytes 393224 | tf_op jit(solution)/shard_map/ppermute | solution.py:17
  34.4 12.1 %collective-permute-start.6 = (bf16[256,168]{0,1:T(8,128)(2,1)S(1)}, bf16[256,168]{0,1:T(8,128)(2,1)S(1)}, u32[]{:S(2)}, u32[]{:S(2)}) collective-permute-start(bf16[256,168]{0,1:T(8,128)(2,1)S(1)} %collective-permute-done.4), channel_id=1, source_target_pairs={{0,8},{8,16},{16,24},{24,0},{1,9},{9,17},{17,25},{25,1},{2,10},{10... | collective-permute-start | bytes 258056 | tf_op jit(solution)/shard_map/ppermute | solution.py:21
  46.5 3.2 %collective-permute-done.6 = bf16[256,168]{0,1:T(8,128)(2,1)S(1)} collective-permute-done((bf16[256,168]{0,1:T(8,128)(2,1)S(1)}, bf16[256,168]{0,1:T(8,128)(2,1)S(1)}, u32[]{:S(2)}, u32[]{:S(2)}) %collective-permute-start.6) | collective-permute-done | bytes 86048 | tf_op jit(solution)/shard_map/ppermute | solution.py:21
  49.8 3.1 %collective-permute-start.7 = (bf16[4,256,168]{1,2,0:T(8,128)(2,1)S(1)}, bf16[4,256,168]{1,2,0:T(8,128)(2,1)S(1)}, u32[]{:S(2)}, u32[]{:S(2)}) collective-permute-start(bf16[4,256,168]{1,2,0:T(8,128)(2,1)S(1)} %bitcast_dynamic-update-slice_fusion.6), channel_id=1, source_target_pairs={{0,2},{2,4},{4,6},{6,0},{1,3},{3,5},{5,7},{7,1},{8,10},{10,12},{12... | collective-permute-start | bytes 1032200 | tf_op jit(solution)/shard_map/ppermute | solution.py:21
  52.9 4.4 %collective-permute-start.8 = (bf16[4,256,168]{1,2,0:T(8,128)(2,1)S(1)}, bf16[4,256,168]{1,2,0:T(8,128)(2,1)S(1)}, u32[]{:S(2)}, u32[]{:S(2)}) collective-permute-start(bf16[4,256,168]{1,2,0:T(8,128)(2,1)S(1)} %bitcast_dynamic-update-slice_fusion.6), channel_id=1, source_target_pairs={{0,4},{2,6},{4,0},{6,2},{1,5},{3,7},{5,1},{7,3},{8,12},{10,14},{12... | collective-permute-start | bytes 1032200 | tf_op jit(solution)/shard_map/ppermute | solution.py:21
  59.3 3.2 %collective-permute-start.9 = (bf16[4,256,168]{1,2,0:T(8,128)(2,1)S(1)}, bf16[4,256,168]{1,2,0:T(8,128)(2,1)S(1)}, u32[]{:S(2)}, u32[]{:S(2)}) collective-permute-start(bf16[4,256,168]{1,2,0:T(8,128)(2,1)S(1)} %bitcast_dynamic-update-slice_fusion.6), channel_id=1, source_target_pairs={{0,6},{2,0},{4,2},{6,4},{1,7},{3,1},{5,3},{7,5},{8,14},{10,8},{12,... | collective-permute-start | bytes 1032200 | tf_op jit(solution)/shard_map/ppermute | solution.py:21
  67.6 13.7 %collective-permute-start.10 = (bf16[4,4,256,168]{2,3,1,0:T(8,128)(2,1)S(1)}, bf16[4,4,256,168]{2,3,1,0:T(8,128)(2,1)S(1)}, u32[]{:S(2)}, u32[]{:S(2)}) collective-permute-start(bf16[4,4,256,168]{2,3,1,0:T(8,128)(2,1)S(1)} %bitcast_dynamic-update-slice_fusion.2), channel_id=1, source_target_pairs={{0,1},{1,0},{2,3},{3,2},{4,5},{5,4},{6,7},{7,6},{8,9},{9,8},{10,11... | collective-permute-start | bytes 4128776 | tf_op jit(solution)/shard_map/ppermute | solution.py:21
  90.6 3.3 %collective-permute-start.11 = (bf16[256,256]{0,1:T(8,128)(2,1)}, bf16[256,256]{0,1:T(8,128)(2,1)S(1)}, u32[]{:S(2)}, u32[]{:S(2)}) collective-permute-start(bf16[256,256]{0,1:T(8,128)(2,1)} %get-tuple-element.10), channel_id=1, source_target_pairs={{32,0},{64,32},{96,64},{128,96},{160,128},{192,160},{224,192},{256... | collective-permute-start | bytes 393224 | tf_op jit(solution)/shard_map/ppermute | solution.py:17
  96.6 8.9 %collective-permute-start.13 = (bf16[256,256]{0,1:T(8,128)(2,1)}, bf16[256,256]{0,1:T(8,128)(2,1)}, u32[]{:S(2)}, u32[]{:S(2)}) collective-permute-start(bf16[256,256]{0,1:T(8,128)(2,1)} %get-tuple-element.13), channel_id=1, source_target_pairs={{96,0},{128,32},{160,64},{192,96},{224,128},{256,160},{288,192},{3... | collective-permute-start | bytes 393224 | tf_op jit(solution)/shard_map/ppermute | solution.py:17
  105.5 3.0 %collective-permute-start.14 = (bf16[256,256]{0,1:T(8,128)(2,1)}, bf16[256,256]{0,1:T(8,128)(2,1)}, u32[]{:S(2)}, u32[]{:S(2)}) collective-permute-start(bf16[256,256]{0,1:T(8,128)(2,1)} %get-tuple-element.12), channel_id=1, source_target_pairs={{128,0},{160,32},{192,64},{224,96},{256,128},{288,160},{320,192},{... | collective-permute-start | bytes 393224 | tf_op jit(solution)/shard_map/ppermute | solution.py:17
  108.5 3.6 %fusion.16 = f32[256,5376]{1,0:T(8,128)} fusion(bf16[5376,128]{1,0:T(8,128)(2,1)S(1)} %copy-done, bf16[256,1280]{0,1:T(8,128)(2,1)S(1)} %multiply_convert_fusion, bf16[1280,256]{1,0:T(8,128)(2,1)S(1)} %constant_dynamic-update-slice_fusion.7), kind=kOutput, calls=%fused_computation.27 | convolution fusion | flops 436273152 | bytes 7864320 | tf_op jit(solution)/shard_map/dot_general | solution.py:74
  113.3 4.0 %convolution_add_fusion.1 = f32[256,5376]{1,0:T(8,128)S(1)} fusion(f32[256,5376]{1,0:T(8,128)} %fusion.16, bf16[5376,128]{1,0:T(8,128)(2,1)} %param.14, bf16[256,256]{0,1:T(8,128)(2,1)S(1)} %add_convert_fusion), kind=kOutput, calls=%fused_computation.1 | convolution fusion | flops 353697792 | bytes 12451840 | tf_op jit(solution)/shard_map/dot_general | solution.py:74
  119.8 4.6 %copy.18 = bf16[5376,256]{1,0:T(8,128)(2,1)} copy(bf16[5376,256]{0,1:T(8,128)(2,1)} %fusion.1) | data formatting | bytes 5505024 | tf_op jit(solution)/shard_map/convert_element_type | solution.py:143
  126.9 4.4 %collective-permute-start.15 = (bf16[4,4,168,256]{3,2,1,0:T(8,128)(2,1)}, bf16[4,4,168,256]{3,2,1,0:T(8,128)(2,1)S(1)}, u32[]{:S(2)}, u32[]{:S(2)}) collective-permute-start(bf16[4,4,168,256]{3,2,1,0:T(8,128)(2,1)} %dynamic-slice_bitcast_fusion), channel_id=1, source_target_pairs={{0,1},{1,0},{2,3},{3,2},{4,5},{5,4},{6,7},{7,6},{8,9},{9,8},{10,11... | collective-permute-start | bytes 4128776 | tf_op jit(solution)/shard_map/ppermute | solution.py:21
  138.5 4.3 %collective-permute-start.17 = (bf16[4,168,256]{2,1,0:T(8,128)(2,1)S(1)}, bf16[4,168,256]{2,1,0:T(8,128)(2,1)S(1)}, u32[]{:S(2)}, u32[]{:S(2)}) collective-permute-start(bf16[4,168,256]{2,1,0:T(8,128)(2,1)S(1)} %get-tuple-element.7), channel_id=1, source_target_pairs={{0,4},{2,6},{4,0},{6,2},{1,5},{3,7},{5,1},{7,3},{8,12},{10,14},{12... | collective-permute-start | bytes 1032200 | tf_op jit(solution)/shard_map/ppermute | solution.py:21
  145.0 3.4 %collective-permute-done.16 = bf16[4,168,256]{2,1,0:T(8,128)(2,1)S(1)} collective-permute-done((bf16[4,168,256]{2,1,0:T(8,128)(2,1)S(1)}, bf16[4,168,256]{2,1,0:T(8,128)(2,1)S(1)}, u32[]{:S(2)}, u32[]{:S(2)}) %collective-permute-start.16) | collective-permute-done | bytes 344096 | tf_op jit(solution)/shard_map/ppermute | solution.py:21
  148.4 7.6 %collective-permute-done.17 = bf16[4,168,256]{2,1,0:T(8,128)(2,1)S(1)} collective-permute-done((bf16[4,168,256]{2,1,0:T(8,128)(2,1)S(1)}, bf16[4,168,256]{2,1,0:T(8,128)(2,1)S(1)}, u32[]{:S(2)}, u32[]{:S(2)}) %collective-permute-start.17) | collective-permute-done | bytes 344096 | tf_op jit(solution)/shard_map/ppermute | solution.py:21
  158.2 10.6 %collective-permute-start.19 = (bf16[168,256]{1,0:T(8,128)(2,1)S(1)}, bf16[168,256]{1,0:T(8,128)(2,1)S(1)}, u32[]{:S(2)}, u32[]{:S(2)}) collective-permute-start(bf16[168,256]{1,0:T(8,128)(2,1)S(1)} %get-tuple-element.8), channel_id=1, source_target_pairs={{0,8},{8,16},{16,24},{24,0},{1,9},{9,17},{17,25},{25,1},{2,10},{10... | collective-permute-start | bytes 258056 | tf_op jit(solution)/shard_map/ppermute | solution.py:21
  168.8 5.6 %collective-permute-start.21 = (bf16[168,256]{1,0:T(8,128)(2,1)S(1)}, bf16[168,256]{1,0:T(8,128)(2,1)S(1)}, u32[]{:S(2)}, u32[]{:S(2)}) collective-permute-start(bf16[168,256]{1,0:T(8,128)(2,1)S(1)} %get-tuple-element.9), channel_id=1, source_target_pairs={{0,24},{8,0},{16,8},{24,16},{1,25},{9,1},{17,9},{25,17},{2,26},{10... | collective-permute-start | bytes 258056 | tf_op jit(solution)/shard_map/ppermute | solution.py:21
  174.4 14.3 %collective-permute-done.19 = bf16[168,256]{1,0:T(8,128)(2,1)S(1)} collective-permute-done((bf16[168,256]{1,0:T(8,128)(2,1)S(1)}, bf16[168,256]{1,0:T(8,128)(2,1)S(1)}, u32[]{:S(2)}, u32[]{:S(2)}) %collective-permute-start.19) | collective-permute-done | bytes 86048 | tf_op jit(solution)/shard_map/ppermute | solution.py:21
  188.6 3.1 %collective-permute-start.20 = (bf16[168,256]{1,0:T(8,128)(2,1)S(1)}, bf16[168,256]{1,0:T(8,128)(2,1)S(1)}, u32[]{:S(2)}, u32[]{:S(2)}) collective-permute-start(bf16[168,256]{1,0:T(8,128)(2,1)S(1)} %fusion.30), channel_id=1, source_target_pairs={{0,8},{8,16},{16,24},{24,0},{1,9},{9,17},{17,25},{25,1},{2,10},{10... | collective-permute-start | bytes 258056 | tf_op jit(solution)/shard_map/ppermute | solution.py:21
  193.0 15.8 %collective-permute-done.20 = bf16[168,256]{1,0:T(8,128)(2,1)S(1)} collective-permute-done((bf16[168,256]{1,0:T(8,128)(2,1)S(1)}, bf16[168,256]{1,0:T(8,128)(2,1)S(1)}, u32[]{:S(2)}, u32[]{:S(2)}) %collective-permute-start.20) | collective-permute-done | bytes 86048 | tf_op jit(solution)/shard_map/ppermute | solution.py:21
  (77 shorter events, 49.0 us)
Async XLA Ops:
  0.0 108.5 %copy-start = (bf16[5376,128]{1,0:T(8,128)(2,1)S(1)}, bf16[5376,128]{1,0:T(8,128)(2,1)}, u32[]{:S(2)}) copy-start(bf16[5376,128]{1,0:T(8,128)(2,1)} %param.13) | copy-start | bytes 4128772
  0.0 34.4 %collective-permute-start.4 = (bf16[256,168]{0,1:T(8,128)(2,1)}, bf16[256,168]{0,1:T(8,128)(2,1)S(1)}, u32[]{:S(2)}, u32[]{:S(2)}) collective-permute-start(bf16[256,168]{0,1:T(8,128)(2,1)} %param.11), channel_id=1, source_target_pairs={{0,8},{8,16},{16,24},{24,0},{1,9},{9,17},{17,25},{25,1},{2,10},{10... | collective-permute-start | bytes 258056 | tf_op jit(solution)/shard_map/ppermute | solution.py:21
  15.6 30.9 %collective-permute-start.5 = (bf16[256,168]{0,1:T(8,128)(2,1)}, bf16[256,168]{0,1:T(8,128)(2,1)S(1)}, u32[]{:S(2)}, u32[]{:S(2)}) collective-permute-start(bf16[256,168]{0,1:T(8,128)(2,1)} %param.11), channel_id=1, source_target_pairs={{0,24},{8,0},{16,8},{24,16},{1,25},{9,1},{17,9},{25,17},{2,26},{10... | collective-permute-start | bytes 258056 | tf_op jit(solution)/shard_map/ppermute | solution.py:21
  22.0 59.3 %collective-permute-start = (bf16[256,256]{1,0:T(8,128)(2,1)}, bf16[256,256]{1,0:T(8,128)(2,1)}, u32[]{:S(2)}, u32[]{:S(2)}) collective-permute-start(bf16[256,256]{1,0:T(8,128)(2,1)} %constant_dynamic-update-slice_fusion), channel_id=1, source_target_pairs={{0,128},{32,160},{64,192},{96,224},{128,256},{160,288},{192,320},{... | collective-permute-start | bytes 393224 | tf_op jit(solution)/shard_map/ppermute | solution.py:17
  24.6 57.5 %collective-permute-start.1 = (bf16[256,256]{1,0:T(8,128)(2,1)}, bf16[256,256]{1,0:T(8,128)(2,1)}, u32[]{:S(2)}, u32[]{:S(2)}) collective-permute-start(bf16[256,256]{1,0:T(8,128)(2,1)} %constant_dynamic-update-slice_fusion), channel_id=1, source_target_pairs={{0,96},{32,128},{64,160},{96,192},{128,224},{160,256},{192,288},{2... | collective-permute-start | bytes 393224 | tf_op jit(solution)/shard_map/ppermute | solution.py:17
  29.3 53.8 %collective-permute-start.2 = (bf16[256,256]{1,0:T(8,128)(2,1)}, bf16[256,256]{1,0:T(8,128)(2,1)S(1)}, u32[]{:S(2)}, u32[]{:S(2)}) collective-permute-start(bf16[256,256]{1,0:T(8,128)(2,1)} %constant_dynamic-update-slice_fusion), channel_id=1, source_target_pairs={{0,64},{32,96},{64,128},{96,160},{128,192},{160,224},{192,256},{22... | collective-permute-start | bytes 393224 | tf_op jit(solution)/shard_map/ppermute | solution.py:17
  34.4 15.4 %collective-permute-start.6 = (bf16[256,168]{0,1:T(8,128)(2,1)S(1)}, bf16[256,168]{0,1:T(8,128)(2,1)S(1)}, u32[]{:S(2)}, u32[]{:S(2)}) collective-permute-start(bf16[256,168]{0,1:T(8,128)(2,1)S(1)} %collective-permute-done.4), channel_id=1, source_target_pairs={{0,8},{8,16},{16,24},{24,0},{1,9},{9,17},{17,25},{25,1},{2,10},{10... | collective-permute-start | bytes 258056 | tf_op jit(solution)/shard_map/ppermute | solution.py:21
  49.8 9.5 %collective-permute-start.7 = (bf16[4,256,168]{1,2,0:T(8,128)(2,1)S(1)}, bf16[4,256,168]{1,2,0:T(8,128)(2,1)S(1)}, u32[]{:S(2)}, u32[]{:S(2)}) collective-permute-start(bf16[4,256,168]{1,2,0:T(8,128)(2,1)S(1)} %bitcast_dynamic-update-slice_fusion.6), channel_id=1, source_target_pairs={{0,2},{2,4},{4,6},{6,0},{1,3},{3,5},{5,7},{7,1},{8,10},{10,12},{12... | collective-permute-start | bytes 1032200 | tf_op jit(solution)/shard_map/ppermute | solution.py:21
  52.9 10.7 %collective-permute-start.8 = (bf16[4,256,168]{1,2,0:T(8,128)(2,1)S(1)}, bf16[4,256,168]{1,2,0:T(8,128)(2,1)S(1)}, u32[]{:S(2)}, u32[]{:S(2)}) collective-permute-start(bf16[4,256,168]{1,2,0:T(8,128)(2,1)S(1)} %bitcast_dynamic-update-slice_fusion.6), channel_id=1, source_target_pairs={{0,4},{2,6},{4,0},{6,2},{1,5},{3,7},{5,1},{7,3},{8,12},{10,14},{12... | collective-permute-start | bytes 1032200 | tf_op jit(solution)/shard_map/ppermute | solution.py:21
  59.3 8.3 %collective-permute-start.9 = (bf16[4,256,168]{1,2,0:T(8,128)(2,1)S(1)}, bf16[4,256,168]{1,2,0:T(8,128)(2,1)S(1)}, u32[]{:S(2)}, u32[]{:S(2)}) collective-permute-start(bf16[4,256,168]{1,2,0:T(8,128)(2,1)S(1)} %bitcast_dynamic-update-slice_fusion.6), channel_id=1, source_target_pairs={{0,6},{2,0},{4,2},{6,4},{1,7},{3,1},{5,3},{7,5},{8,14},{10,8},{12,... | collective-permute-start | bytes 1032200 | tf_op jit(solution)/shard_map/ppermute | solution.py:21
  62.5 20.7 %copy-start.5 = (bf16[256,128]{1,0:T(8,128)(2,1)S(1)}, bf16[256,128]{1,0:T(8,128)(2,1)}, u32[]{:S(2)}) copy-start(bf16[256,128]{1,0:T(8,128)(2,1)} %param.8) | copy-start | bytes 196612
  63.7 19.5 %collective-permute-start.3 = (bf16[256,256]{1,0:T(8,128)(2,1)}, bf16[256,256]{1,0:T(8,128)(2,1)S(1)}, u32[]{:S(2)}, u32[]{:S(2)}) collective-permute-start(bf16[256,256]{1,0:T(8,128)(2,1)} %constant_dynamic-update-slice_fusion), channel_id=1, source_target_pairs={{0,32},{32,64},{64,96},{96,128},{128,160},{160,192},{192,224},{224... | collective-permute-start | bytes 393224 | tf_op jit(solution)/shard_map/ppermute | solution.py:17
  67.6 17.5 %collective-permute-start.10 = (bf16[4,4,256,168]{2,3,1,0:T(8,128)(2,1)S(1)}, bf16[4,4,256,168]{2,3,1,0:T(8,128)(2,1)S(1)}, u32[]{:S(2)}, u32[]{:S(2)}) collective-permute-start(bf16[4,4,256,168]{2,3,1,0:T(8,128)(2,1)S(1)} %bitcast_dynamic-update-slice_fusion.2), channel_id=1, source_target_pairs={{0,1},{1,0},{2,3},{3,2},{4,5},{5,4},{6,7},{7,6},{8,9},{9,8},{10,11... | collective-permute-start | bytes 4128776 | tf_op jit(solution)/shard_map/ppermute | solution.py:21
  90.6 21.6 %collective-permute-start.11 = (bf16[256,256]{0,1:T(8,128)(2,1)}, bf16[256,256]{0,1:T(8,128)(2,1)S(1)}, u32[]{:S(2)}, u32[]{:S(2)}) collective-permute-start(bf16[256,256]{0,1:T(8,128)(2,1)} %get-tuple-element.10), channel_id=1, source_target_pairs={{32,0},{64,32},{96,64},{128,96},{160,128},{192,160},{224,192},{256... | collective-permute-start | bytes 393224 | tf_op jit(solution)/shard_map/ppermute | solution.py:17
  93.8 18.3 %collective-permute-start.12 = (bf16[256,256]{0,1:T(8,128)(2,1)}, bf16[256,256]{0,1:T(8,128)(2,1)}, u32[]{:S(2)}, u32[]{:S(2)}) collective-permute-start(bf16[256,256]{0,1:T(8,128)(2,1)} %get-tuple-element.11), channel_id=1, source_target_pairs={{64,0},{96,32},{128,64},{160,96},{192,128},{224,160},{256,192},{28... | collective-permute-start | bytes 393224 | tf_op jit(solution)/shard_map/ppermute | solution.py:17
  96.6 15.6 %collective-permute-start.13 = (bf16[256,256]{0,1:T(8,128)(2,1)}, bf16[256,256]{0,1:T(8,128)(2,1)}, u32[]{:S(2)}, u32[]{:S(2)}) collective-permute-start(bf16[256,256]{0,1:T(8,128)(2,1)} %get-tuple-element.13), channel_id=1, source_target_pairs={{96,0},{128,32},{160,64},{192,96},{224,128},{256,160},{288,192},{3... | collective-permute-start | bytes 393224 | tf_op jit(solution)/shard_map/ppermute | solution.py:17
  105.5 6.7 %collective-permute-start.14 = (bf16[256,256]{0,1:T(8,128)(2,1)}, bf16[256,256]{0,1:T(8,128)(2,1)}, u32[]{:S(2)}, u32[]{:S(2)}) collective-permute-start(bf16[256,256]{0,1:T(8,128)(2,1)} %get-tuple-element.12), channel_id=1, source_target_pairs={{128,0},{160,32},{192,64},{224,96},{256,128},{288,160},{320,192},{... | collective-permute-start | bytes 393224 | tf_op jit(solution)/shard_map/ppermute | solution.py:17
  126.9 7.4 %collective-permute-start.15 = (bf16[4,4,168,256]{3,2,1,0:T(8,128)(2,1)}, bf16[4,4,168,256]{3,2,1,0:T(8,128)(2,1)S(1)}, u32[]{:S(2)}, u32[]{:S(2)}) collective-permute-start(bf16[4,4,168,256]{3,2,1,0:T(8,128)(2,1)} %dynamic-slice_bitcast_fusion), channel_id=1, source_target_pairs={{0,1},{1,0},{2,3},{3,2},{4,5},{5,4},{6,7},{7,6},{8,9},{9,8},{10,11... | collective-permute-start | bytes 4128776 | tf_op jit(solution)/shard_map/ppermute | solution.py:21
  136.0 12.4 %collective-permute-start.16 = (bf16[4,168,256]{2,1,0:T(8,128)(2,1)S(1)}, bf16[4,168,256]{2,1,0:T(8,128)(2,1)S(1)}, u32[]{:S(2)}, u32[]{:S(2)}) collective-permute-start(bf16[4,168,256]{2,1,0:T(8,128)(2,1)S(1)} %get-tuple-element.5), channel_id=1, source_target_pairs={{0,2},{2,4},{4,6},{6,0},{1,3},{3,5},{5,7},{7,1},{8,10},{10,12},{12... | collective-permute-start | bytes 1032200 | tf_op jit(solution)/shard_map/ppermute | solution.py:21
  138.5 17.5 %collective-permute-start.17 = (bf16[4,168,256]{2,1,0:T(8,128)(2,1)S(1)}, bf16[4,168,256]{2,1,0:T(8,128)(2,1)S(1)}, u32[]{:S(2)}, u32[]{:S(2)}) collective-permute-start(bf16[4,168,256]{2,1,0:T(8,128)(2,1)S(1)} %get-tuple-element.7), channel_id=1, source_target_pairs={{0,4},{2,6},{4,0},{6,2},{1,5},{3,7},{5,1},{7,3},{8,12},{10,14},{12... | collective-permute-start | bytes 1032200 | tf_op jit(solution)/shard_map/ppermute | solution.py:21
  142.7 15.2 %collective-permute-start.18 = (bf16[4,168,256]{2,1,0:T(8,128)(2,1)S(1)}, bf16[4,168,256]{2,1,0:T(8,128)(2,1)S(1)}, u32[]{:S(2)}, u32[]{:S(2)}) collective-permute-start(bf16[4,168,256]{2,1,0:T(8,128)(2,1)S(1)} %get-tuple-element.6), channel_id=1, source_target_pairs={{0,6},{2,0},{4,2},{6,4},{1,7},{3,1},{5,3},{7,5},{8,14},{10,8},{12,... | collective-permute-start | bytes 1032200 | tf_op jit(solution)/shard_map/ppermute | solution.py:21
  158.2 30.4 %collective-permute-start.19 = (bf16[168,256]{1,0:T(8,128)(2,1)S(1)}, bf16[168,256]{1,0:T(8,128)(2,1)S(1)}, u32[]{:S(2)}, u32[]{:S(2)}) collective-permute-start(bf16[168,256]{1,0:T(8,128)(2,1)S(1)} %get-tuple-element.8), channel_id=1, source_target_pairs={{0,8},{8,16},{16,24},{24,0},{1,9},{9,17},{17,25},{25,1},{2,10},{10... | collective-permute-start | bytes 258056 | tf_op jit(solution)/shard_map/ppermute | solution.py:21
  168.8 24.2 %collective-permute-start.21 = (bf16[168,256]{1,0:T(8,128)(2,1)S(1)}, bf16[168,256]{1,0:T(8,128)(2,1)S(1)}, u32[]{:S(2)}, u32[]{:S(2)}) collective-permute-start(bf16[168,256]{1,0:T(8,128)(2,1)S(1)} %get-tuple-element.9), channel_id=1, source_target_pairs={{0,24},{8,0},{16,8},{24,16},{1,25},{9,1},{17,9},{25,17},{2,26},{10... | collective-permute-start | bytes 258056 | tf_op jit(solution)/shard_map/ppermute | solution.py:21
  188.6 20.1 %collective-permute-start.20 = (bf16[168,256]{1,0:T(8,128)(2,1)S(1)}, bf16[168,256]{1,0:T(8,128)(2,1)S(1)}, u32[]{:S(2)}, u32[]{:S(2)}) collective-permute-start(bf16[168,256]{1,0:T(8,128)(2,1)S(1)} %fusion.30), channel_id=1, source_target_pairs={{0,8},{8,16},{16,24},{24,0},{1,9},{9,17},{17,25},{25,1},{2,10},{10... | collective-permute-start | bytes 258056 | tf_op jit(solution)/shard_map/ppermute | solution.py:21
  (4 other events, 47.3 us)

commit v4 on v3

--- a/solution.py
+++ b/solution.py
@@ -112,7 +112,7 @@
         width = d_out.shape[1]
         seq_index = lax.axis_index("seq")
         stacked = gather_axis(d_out, "zhi", n_zhi, relay=True)
-        stacked = gather_axis(stacked, "x", n_x)
+        stacked = gather_axis(stacked, "x", n_x, relay=True)
         stacked = gather_axis(stacked, "core", n_core)
         out_rows = w_out.reshape(w_out.shape[0], n_zhi, n_x, n_core, width)
         grad_heads = jnp.einsum(
@@ -142,7 +142,7 @@
         summed = summed + dot_rows(w_value, grad_values)
         term = summed.astype(jnp.bfloat16).reshape(n_zhi, n_x, n_core, width, length)
         part = scatter_axis(term, "core", n_core, 2)
-        part = scatter_axis(part, "x", n_x, 1)
+        part = scatter_axis(part, "x", n_x, 1, relay=True)
         part = scatter_axis(part, "zhi", n_zhi, 0, relay=True)
         return part.T.astype(jnp.bfloat16)
 

time: 210 us -> 211 us (level)
  the two profiles are of different devices: /device:TPU:161 before, /device:TPU:193 now
where the time goes in v4:
time: 211 us; the launch traced here: 210 us
  starting transfers between devices  114 us (54%)
  waiting for transfers between devices  60.9 us (29%)
  matrix products  14.1 us (7%)
  local copies, waits for them, and re-layouts  13.8 us (7%)
  other arithmetic  6.2 us (3%)
    ppermute x14, starting transfers between devices, shift(): lax.ppermute(block, axis, [(i, (i + step) % size) for i in range(size)])  85.5 us
    ppermute x14, waiting for transfers between devices, shift(): lax.ppermute(block, axis, [(i, (i + step) % size) for i in range(size)])  60.9 us
    ppermute x8, starting transfers between devices, from_behind(): return lax.ppermute(block, axis, route)  28.8 us
    dot_general x5, matrix products, dot_rows(): lax.dot_general(left, right, (((1,), (1,)), ((), ())), preferred_element_...  11.4 us
    unnamed x23, local copies, waits for them, and re-layouts  5.22 us
    convert_element_type x1, local copies, waits for them, and re-layouts, body(): summed.astype(jnp.bfloat16).reshape(n_zhi, n_x, n_core, width, length)  4.63 us
  transfers between devices with their start and end apart: 22, of which 8 were waited for; matrix products, arithmetic and copies ran while one was open for 6% of the time, Pallas kernels for 0%

profile of v4, /device:TPU:193, one launch (start us, length us, event | category | flops | bytes accessed | tf_op | source)
XLA Modules:
  0.0 210.0 jit_solution(4996619347064401799)
XLA Ops:
  0.0 15.6 %collective-permute-start.4 = (bf16[256,168]{0,1:T(8,128)(2,1)}, bf16[256,168]{0,1:T(8,128)(2,1)S(1)}, u32[]{:S(2)}, u32[]{:S(2)}) collective-permute-start(bf16[256,168]{0,1:T(8,128)(2,1)} %param.11), channel_id=1, source_target_pairs={{0,8},{8,16},{16,24},{24,0},{1,9},{9,17},{17,25},{25,1},{2,10},{10... | collective-permute-start | bytes 258056 | tf_op jit(solution)/shard_map/ppermute | solution.py:21
  21.1 2.9 %collective-permute-start = (bf16[256,256]{1,0:T(8,128)(2,1)}, bf16[256,256]{1,0:T(8,128)(2,1)}, u32[]{:S(2)}, u32[]{:S(2)}) collective-permute-start(bf16[256,256]{1,0:T(8,128)(2,1)} %constant_dynamic-update-slice_fusion), channel_id=1, source_target_pairs={{0,128},{32,160},{64,192},{96,224},{128,256},{160,288},{192,320},{... | collective-permute-start | bytes 393224 | tf_op jit(solution)/shard_map/ppermute | solution.py:17
  24.0 4.6 %collective-permute-start.1 = (bf16[256,256]{1,0:T(8,128)(2,1)}, bf16[256,256]{1,0:T(8,128)(2,1)}, u32[]{:S(2)}, u32[]{:S(2)}) collective-permute-start(bf16[256,256]{1,0:T(8,128)(2,1)} %constant_dynamic-update-slice_fusion), channel_id=1, source_target_pairs={{0,96},{32,128},{64,160},{96,192},{128,224},{160,256},{192,288},{2... | collective-permute-start | bytes 393224 | tf_op jit(solution)/shard_map/ppermute | solution.py:17
  32.9 12.1 %collective-permute-start.6 = (bf16[256,168]{0,1:T(8,128)(2,1)S(1)}, bf16[256,168]{0,1:T(8,128)(2,1)S(1)}, u32[]{:S(2)}, u32[]{:S(2)}) collective-permute-start(bf16[256,168]{0,1:T(8,128)(2,1)S(1)} %collective-permute-done.4), channel_id=1, source_target_pairs={{0,8},{8,16},{16,24},{24,0},{1,9},{9,17},{17,25},{25,1},{2,10},{10... | collective-permute-start | bytes 258056 | tf_op jit(solution)/shard_map/ppermute | solution.py:21
  47.0 3.1 %collective-permute-start.7 = (bf16[4,256,168]{1,2,0:T(8,128)(2,1)S(1)}, bf16[4,256,168]{1,2,0:T(8,128)(2,1)S(1)}, u32[]{:S(2)}, u32[]{:S(2)}) collective-permute-start(bf16[4,256,168]{1,2,0:T(8,128)(2,1)S(1)} %bitcast_dynamic-update-slice_fusion.6), channel_id=1, source_target_pairs={{0,2},{2,4},{4,6},{6,0},{1,3},{3,5},{5,7},{7,1},{8,10},{10,12},{12... | collective-permute-start | bytes 1032200 | tf_op jit(solution)/shard_map/ppermute | solution.py:21
  50.2 3.4 %collective-permute-start.8 = (bf16[4,256,168]{1,2,0:T(8,128)(2,1)S(1)}, bf16[4,256,168]{1,2,0:T(8,128)(2,1)S(1)}, u32[]{:S(2)}, u32[]{:S(2)}) collective-permute-start(bf16[4,256,168]{1,2,0:T(8,128)(2,1)S(1)} %bitcast_dynamic-update-slice_fusion.6), channel_id=1, source_target_pairs={{0,6},{2,0},{4,2},{6,4},{1,7},{3,1},{5,3},{7,5},{8,14},{10,8},{12,... | collective-permute-start | bytes 1032200 | tf_op jit(solution)/shard_map/ppermute | solution.py:21
  53.7 2.8 %collective-permute-done.7 = bf16[4,256,168]{1,2,0:T(8,128)(2,1)S(1)} collective-permute-done((bf16[4,256,168]{1,2,0:T(8,128)(2,1)S(1)}, bf16[4,256,168]{1,2,0:T(8,128)(2,1)S(1)}, u32[]{:S(2)}, u32[]{:S(2)}) %collective-permute-start.7) | collective-permute-done | bytes 344096 | tf_op jit(solution)/shard_map/ppermute | solution.py:21
  61.0 7.1 %collective-permute-done.9 = bf16[4,256,168]{1,2,0:T(8,128)(2,1)S(1)} collective-permute-done((bf16[4,256,168]{1,2,0:T(8,128)(2,1)S(1)}, bf16[4,256,168]{1,2,0:T(8,128)(2,1)S(1)}, u32[]{:S(2)}, u32[]{:S(2)}) %collective-permute-start.9) | collective-permute-done | bytes 344096 | tf_op jit(solution)/shard_map/ppermute | solution.py:21
  68.1 14.2 %collective-permute-start.10 = (bf16[4,4,256,168]{2,3,1,0:T(8,128)(2,1)S(1)}, bf16[4,4,256,168]{2,3,1,0:T(8,128)(2,1)S(1)}, u32[]{:S(2)}, u32[]{:S(2)}) collective-permute-start(bf16[4,4,256,168]{2,3,1,0:T(8,128)(2,1)S(1)} %bitcast_dynamic-update-slice_fusion.2), channel_id=1, source_target_pairs={{0,1},{1,0},{2,3},{3,2},{4,5},{5,4},{6,7},{7,6},{8,9},{9,8},{10,11... | collective-permute-start | bytes 4128776 | tf_op jit(solution)/shard_map/ppermute | solution.py:21
  91.7 3.4 %collective-permute-start.11 = (bf16[256,256]{0,1:T(8,128)(2,1)}, bf16[256,256]{0,1:T(8,128)(2,1)S(1)}, u32[]{:S(2)}, u32[]{:S(2)}) collective-permute-start(bf16[256,256]{0,1:T(8,128)(2,1)} %get-tuple-element.9), channel_id=1, source_target_pairs={{32,0},{64,32},{96,64},{128,96},{160,128},{192,160},{224,192},{256... | collective-permute-start | bytes 393224 | tf_op jit(solution)/shard_map/ppermute | solution.py:17
  95.1 5.3 %collective-permute-start.12 = (bf16[256,256]{0,1:T(8,128)(2,1)}, bf16[256,256]{0,1:T(8,128)(2,1)}, u32[]{:S(2)}, u32[]{:S(2)}) collective-permute-start(bf16[256,256]{0,1:T(8,128)(2,1)} %get-tuple-element.10), channel_id=1, source_target_pairs={{64,0},{96,32},{128,64},{160,96},{192,128},{224,160},{256,192},{28... | collective-permute-start | bytes 393224 | tf_op jit(solution)/shard_map/ppermute | solution.py:17
  102.6 5.8 %collective-permute-start.14 = (bf16[256,256]{0,1:T(8,128)(2,1)}, bf16[256,256]{0,1:T(8,128)(2,1)}, u32[]{:S(2)}, u32[]{:S(2)}) collective-permute-start(bf16[256,256]{0,1:T(8,128)(2,1)} %get-tuple-element.11), channel_id=1, source_target_pairs={{128,0},{160,32},{192,64},{224,96},{256,128},{288,160},{320,192},{... | collective-permute-start | bytes 393224 | tf_op jit(solution)/shard_map/ppermute | solution.py:17
  108.4 3.6 %fusion.16 = f32[256,5376]{1,0:T(8,128)} fusion(bf16[5376,128]{1,0:T(8,128)(2,1)S(1)} %copy-done, bf16[256,1280]{0,1:T(8,128)(2,1)S(1)} %multiply_convert_fusion, bf16[1280,256]{1,0:T(8,128)(2,1)S(1)} %constant_dynamic-update-slice_fusion.7), kind=kOutput, calls=%fused_computation.27 | convolution fusion | flops 436273152 | bytes 7864320 | tf_op jit(solution)/shard_map/dot_general | solution.py:74
  113.2 4.0 %convolution_add_fusion.1 = f32[256,5376]{1,0:T(8,128)S(1)} fusion(f32[256,5376]{1,0:T(8,128)} %fusion.16, bf16[5376,128]{1,0:T(8,128)(2,1)} %param.14, bf16[256,256]{0,1:T(8,128)(2,1)S(1)} %add_convert_fusion), kind=kOutput, calls=%fused_computation.1 | convolution fusion | flops 353697792 | bytes 12451840 | tf_op jit(solution)/shard_map/dot_general | solution.py:74
  119.7 4.6 %copy.18 = bf16[5376,256]{1,0:T(8,128)(2,1)} copy(bf16[5376,256]{0,1:T(8,128)(2,1)} %fusion.1) | data formatting | bytes 5505024 | tf_op jit(solution)/shard_map/convert_element_type | solution.py:143
  125.9 3.0 %collective-permute-start.15 = (bf16[4,4,168,256]{3,2,1,0:T(8,128)(2,1)S(1)}, bf16[4,4,168,256]{3,2,1,0:T(8,128)(2,1)S(1)}, u32[]{:S(2)}, u32[]{:S(2)}) collective-permute-start(bf16[4,4,168,256]{3,2,1,0:T(8,128)(2,1)S(1)} %dynamic-slice_bitcast_fusion), channel_id=1, source_target_pairs={{0,1},{1,0},{2,3},{3,2},{4,5},{5,4},{6,7},{7,6},{8,9},{9,8},{10,11... | collective-permute-start | bytes 4128776 | tf_op jit(solution)/shard_map/ppermute | solution.py:21
  134.0 4.6 %collective-permute-start.18 = (bf16[4,168,256]{2,1,0:T(8,128)(2,1)S(1)}, bf16[4,168,256]{2,1,0:T(8,128)(2,1)S(1)}, u32[]{:S(2)}, u32[]{:S(2)}) collective-permute-start(bf16[4,168,256]{2,1,0:T(8,128)(2,1)S(1)} %get-tuple-element.6), channel_id=1, source_target_pairs={{0,6},{2,0},{4,2},{6,4},{1,7},{3,1},{5,3},{7,5},{8,14},{10,8},{12,... | collective-permute-start | bytes 1032200 | tf_op jit(solution)/shard_map/ppermute | solution.py:21
  138.6 5.9 %collective-permute-done.16 = bf16[4,168,256]{2,1,0:T(8,128)(2,1)S(1)} collective-permute-done((bf16[4,168,256]{2,1,0:T(8,128)(2,1)S(1)}, bf16[4,168,256]{2,1,0:T(8,128)(2,1)S(1)}, u32[]{:S(2)}, u32[]{:S(2)}) %collective-permute-start.16) | collective-permute-done | bytes 344096 | tf_op jit(solution)/shard_map/ppermute | solution.py:21
  146.5 9.5 %collective-permute-done.17 = bf16[4,168,256]{2,1,0:T(8,128)(2,1)S(1)} collective-permute-done((bf16[4,168,256]{2,1,0:T(8,128)(2,1)S(1)}, bf16[4,168,256]{2,1,0:T(8,128)(2,1)S(1)}, u32[]{:S(2)}, u32[]{:S(2)}) %collective-permute-start.17) | collective-permute-done | bytes 344096 | tf_op jit(solution)/shard_map/ppermute | solution.py:21
  157.2 10.7 %collective-permute-start.19 = (bf16[168,256]{1,0:T(8,128)(2,1)S(1)}, bf16[168,256]{1,0:T(8,128)(2,1)S(1)}, u32[]{:S(2)}, u32[]{:S(2)}) collective-permute-start(bf16[168,256]{1,0:T(8,128)(2,1)S(1)} %get-tuple-element.7), channel_id=1, source_target_pairs={{0,8},{8,16},{16,24},{24,0},{1,9},{9,17},{17,25},{25,1},{2,10},{10... | collective-permute-start | bytes 258056 | tf_op jit(solution)/shard_map/ppermute | solution.py:21
  167.9 6.0 %collective-permute-start.21 = (bf16[168,256]{1,0:T(8,128)(2,1)S(1)}, bf16[168,256]{1,0:T(8,128)(2,1)S(1)}, u32[]{:S(2)}, u32[]{:S(2)}) collective-permute-start(bf16[168,256]{1,0:T(8,128)(2,1)S(1)} %get-tuple-element.8), channel_id=1, source_target_pairs={{0,24},{8,0},{16,8},{24,16},{1,25},{9,1},{17,9},{25,17},{2,26},{10... | collective-permute-start | bytes 258056 | tf_op jit(solution)/shard_map/ppermute | solution.py:21
  174.0 15.0 %collective-permute-done.19 = bf16[168,256]{1,0:T(8,128)(2,1)S(1)} collective-permute-done((bf16[168,256]{1,0:T(8,128)(2,1)S(1)}, bf16[168,256]{1,0:T(8,128)(2,1)S(1)}, u32[]{:S(2)}, u32[]{:S(2)}) %collective-permute-start.19) | collective-permute-done | bytes 86048 | tf_op jit(solution)/shard_map/ppermute | solution.py:21
  189.0 4.4 %collective-permute-start.20 = (bf16[168,256]{1,0:T(8,128)(2,1)S(1)}, bf16[168,256]{1,0:T(8,128)(2,1)S(1)}, u32[]{:S(2)}, u32[]{:S(2)}) collective-permute-start(bf16[168,256]{1,0:T(8,128)(2,1)S(1)} %fusion.29), channel_id=1, source_target_pairs={{0,8},{8,16},{16,24},{24,0},{1,9},{9,17},{17,25},{25,1},{2,10},{10... | collective-permute-start | bytes 258056 | tf_op jit(solution)/shard_map/ppermute | solution.py:21
  193.5 15.8 %collective-permute-done.20 = bf16[168,256]{1,0:T(8,128)(2,1)S(1)} collective-permute-done((bf16[168,256]{1,0:T(8,128)(2,1)S(1)}, bf16[168,256]{1,0:T(8,128)(2,1)S(1)}, u32[]{:S(2)}, u32[]{:S(2)}) %collective-permute-start.20) | collective-permute-done | bytes 86048 | tf_op jit(solution)/shard_map/ppermute | solution.py:21
  (82 shorter events, 41.6 us)
Async XLA Ops:
  0.0 108.4 %copy-start = (bf16[5376,128]{1,0:T(8,128)(2,1)S(1)}, bf16[5376,128]{1,0:T(8,128)(2,1)}, u32[]{:S(2)}) copy-start(bf16[5376,128]{1,0:T(8,128)(2,1)} %param.13) | copy-start | bytes 4128772
  0.0 32.9 %collective-permute-start.4 = (bf16[256,168]{0,1:T(8,128)(2,1)}, bf16[256,168]{0,1:T(8,128)(2,1)S(1)}, u32[]{:S(2)}, u32[]{:S(2)}) collective-permute-start(bf16[256,168]{0,1:T(8,128)(2,1)} %param.11), channel_id=1, source_target_pairs={{0,8},{8,16},{16,24},{24,0},{1,9},{9,17},{17,25},{25,1},{2,10},{10... | collective-permute-start | bytes 258056 | tf_op jit(solution)/shard_map/ppermute | solution.py:21
  15.6 29.4 %collective-permute-start.5 = (bf16[256,168]{0,1:T(8,128)(2,1)}, bf16[256,168]{0,1:T(8,128)(2,1)S(1)}, u32[]{:S(2)}, u32[]{:S(2)}) collective-permute-start(bf16[256,168]{0,1:T(8,128)(2,1)} %param.11), channel_id=1, source_target_pairs={{0,24},{8,0},{16,8},{24,16},{1,25},{9,1},{17,9},{25,17},{2,26},{10... | collective-permute-start | bytes 258056 | tf_op jit(solution)/shard_map/ppermute | solution.py:21
  21.1 61.3 %collective-permute-start = (bf16[256,256]{1,0:T(8,128)(2,1)}, bf16[256,256]{1,0:T(8,128)(2,1)}, u32[]{:S(2)}, u32[]{:S(2)}) collective-permute-start(bf16[256,256]{1,0:T(8,128)(2,1)} %constant_dynamic-update-slice_fusion), channel_id=1, source_target_pairs={{0,128},{32,160},{64,192},{96,224},{128,256},{160,288},{192,320},{... | collective-permute-start | bytes 393224 | tf_op jit(solution)/shard_map/ppermute | solution.py:17
  24.0 59.3 %collective-permute-start.1 = (bf16[256,256]{1,0:T(8,128)(2,1)}, bf16[256,256]{1,0:T(8,128)(2,1)}, u32[]{:S(2)}, u32[]{:S(2)}) collective-permute-start(bf16[256,256]{1,0:T(8,128)(2,1)} %constant_dynamic-update-slice_fusion), channel_id=1, source_target_pairs={{0,96},{32,128},{64,160},{96,192},{128,224},{160,256},{192,288},{2... | collective-permute-start | bytes 393224 | tf_op jit(solution)/shard_map/ppermute | solution.py:17
  28.7 55.6 %collective-permute-start.2 = (bf16[256,256]{1,0:T(8,128)(2,1)}, bf16[256,256]{1,0:T(8,128)(2,1)S(1)}, u32[]{:S(2)}, u32[]{:S(2)}) collective-permute-start(bf16[256,256]{1,0:T(8,128)(2,1)} %constant_dynamic-update-slice_fusion), channel_id=1, source_target_pairs={{0,64},{32,96},{64,128},{96,160},{128,192},{160,224},{192,256},{22... | collective-permute-start | bytes 393224 | tf_op jit(solution)/shard_map/ppermute | solution.py:17
  32.9 14.1 %collective-permute-start.6 = (bf16[256,168]{0,1:T(8,128)(2,1)S(1)}, bf16[256,168]{0,1:T(8,128)(2,1)S(1)}, u32[]{:S(2)}, u32[]{:S(2)}) collective-permute-start(bf16[256,168]{0,1:T(8,128)(2,1)S(1)} %collective-permute-done.4), channel_id=1, source_target_pairs={{0,8},{8,16},{16,24},{24,0},{1,9},{9,17},{17,25},{25,1},{2,10},{10... | collective-permute-start | bytes 258056 | tf_op jit(solution)/shard_map/ppermute | solution.py:21
  47.0 9.5 %collective-permute-start.7 = (bf16[4,256,168]{1,2,0:T(8,128)(2,1)S(1)}, bf16[4,256,168]{1,2,0:T(8,128)(2,1)S(1)}, u32[]{:S(2)}, u32[]{:S(2)}) collective-permute-start(bf16[4,256,168]{1,2,0:T(8,128)(2,1)S(1)} %bitcast_dynamic-update-slice_fusion.6), channel_id=1, source_target_pairs={{0,2},{2,4},{4,6},{6,0},{1,3},{3,5},{5,7},{7,1},{8,10},{10,12},{12... | collective-permute-start | bytes 1032200 | tf_op jit(solution)/shard_map/ppermute | solution.py:21
  50.2 8.4 %collective-permute-start.8 = (bf16[4,256,168]{1,2,0:T(8,128)(2,1)S(1)}, bf16[4,256,168]{1,2,0:T(8,128)(2,1)S(1)}, u32[]{:S(2)}, u32[]{:S(2)}) collective-permute-start(bf16[4,256,168]{1,2,0:T(8,128)(2,1)S(1)} %bitcast_dynamic-update-slice_fusion.6), channel_id=1, source_target_pairs={{0,6},{2,0},{4,2},{6,4},{1,7},{3,1},{5,3},{7,5},{8,14},{10,8},{12,... | collective-permute-start | bytes 1032200 | tf_op jit(solution)/shard_map/ppermute | solution.py:21
  56.5 11.6 %collective-permute-start.9 = (bf16[4,256,168]{1,2,0:T(8,128)(2,1)S(1)}, bf16[4,256,168]{1,2,0:T(8,128)(2,1)S(1)}, u32[]{:S(2)}, u32[]{:S(2)}) collective-permute-start(bf16[4,256,168]{1,2,0:T(8,128)(2,1)S(1)} %collective-permute-done.7), channel_id=1, source_target_pairs={{0,2},{2,4},{4,6},{6,0},{1,3},{3,5},{5,7},{7,1},{8,10},{10,12},{12... | collective-permute-start | bytes 1032200 | tf_op jit(solution)/shard_map/ppermute | solution.py:21
  58.5 25.9 %copy-start.7 = (bf16[256,128]{1,0:T(8,128)(2,1)S(1)}, bf16[256,128]{1,0:T(8,128)(2,1)}, u32[]{:S(2)}) copy-start(bf16[256,128]{1,0:T(8,128)(2,1)} %param.8) | copy-start | bytes 196612
  58.5 25.7 %collective-permute-start.3 = (bf16[256,256]{1,0:T(8,128)(2,1)}, bf16[256,256]{1,0:T(8,128)(2,1)S(1)}, u32[]{:S(2)}, u32[]{:S(2)}) collective-permute-start(bf16[256,256]{1,0:T(8,128)(2,1)} %constant_dynamic-update-slice_fusion), channel_id=1, source_target_pairs={{0,32},{32,64},{64,96},{96,128},{128,160},{160,192},{192,224},{224... | collective-permute-start | bytes 393224 | tf_op jit(solution)/shard_map/ppermute | solution.py:17
  68.1 18.1 %collective-permute-start.10 = (bf16[4,4,256,168]{2,3,1,0:T(8,128)(2,1)S(1)}, bf16[4,4,256,168]{2,3,1,0:T(8,128)(2,1)S(1)}, u32[]{:S(2)}, u32[]{:S(2)}) collective-permute-start(bf16[4,4,256,168]{2,3,1,0:T(8,128)(2,1)S(1)} %bitcast_dynamic-update-slice_fusion.2), channel_id=1, source_target_pairs={{0,1},{1,0},{2,3},{3,2},{4,5},{5,4},{6,7},{7,6},{8,9},{9,8},{10,11... | collective-permute-start | bytes 4128776 | tf_op jit(solution)/shard_map/ppermute | solution.py:21
  91.7 20.4 %collective-permute-start.11 = (bf16[256,256]{0,1:T(8,128)(2,1)}, bf16[256,256]{0,1:T(8,128)(2,1)S(1)}, u32[]{:S(2)}, u32[]{:S(2)}) collective-permute-start(bf16[256,256]{0,1:T(8,128)(2,1)} %get-tuple-element.9), channel_id=1, source_target_pairs={{32,0},{64,32},{96,64},{128,96},{160,128},{192,160},{224,192},{256... | collective-permute-start | bytes 393224 | tf_op jit(solution)/shard_map/ppermute | solution.py:17
  95.1 17.0 %collective-permute-start.12 = (bf16[256,256]{0,1:T(8,128)(2,1)}, bf16[256,256]{0,1:T(8,128)(2,1)}, u32[]{:S(2)}, u32[]{:S(2)}) collective-permute-start(bf16[256,256]{0,1:T(8,128)(2,1)} %get-tuple-element.10), channel_id=1, source_target_pairs={{64,0},{96,32},{128,64},{160,96},{192,128},{224,160},{256,192},{28... | collective-permute-start | bytes 393224 | tf_op jit(solution)/shard_map/ppermute | solution.py:17
  100.4 11.6 %collective-permute-start.13 = (bf16[256,256]{0,1:T(8,128)(2,1)}, bf16[256,256]{0,1:T(8,128)(2,1)}, u32[]{:S(2)}, u32[]{:S(2)}) collective-permute-start(bf16[256,256]{0,1:T(8,128)(2,1)} %get-tuple-element.12), channel_id=1, source_target_pairs={{96,0},{128,32},{160,64},{192,96},{224,128},{256,160},{288,192},{3... | collective-permute-start | bytes 393224 | tf_op jit(solution)/shard_map/ppermute | solution.py:17
  102.6 9.5 %collective-permute-start.14 = (bf16[256,256]{0,1:T(8,128)(2,1)}, bf16[256,256]{0,1:T(8,128)(2,1)}, u32[]{:S(2)}, u32[]{:S(2)}) collective-permute-start(bf16[256,256]{0,1:T(8,128)(2,1)} %get-tuple-element.11), channel_id=1, source_target_pairs={{128,0},{160,32},{192,64},{224,96},{256,128},{288,160},{320,192},{... | collective-permute-start | bytes 393224 | tf_op jit(solution)/shard_map/ppermute | solution.py:17
  125.9 5.8 %collective-permute-start.15 = (bf16[4,4,168,256]{3,2,1,0:T(8,128)(2,1)S(1)}, bf16[4,4,168,256]{3,2,1,0:T(8,128)(2,1)S(1)}, u32[]{:S(2)}, u32[]{:S(2)}) collective-permute-start(bf16[4,4,168,256]{3,2,1,0:T(8,128)(2,1)S(1)} %dynamic-slice_bitcast_fusion), channel_id=1, source_target_pairs={{0,1},{1,0},{2,3},{3,2},{4,5},{5,4},{6,7},{7,6},{8,9},{9,8},{10,11... | collective-permute-start | bytes 4128776 | tf_op jit(solution)/shard_map/ppermute | solution.py:21
  132.1 12.4 %collective-permute-start.16 = (bf16[4,168,256]{2,1,0:T(8,128)(2,1)S(1)}, bf16[4,168,256]{2,1,0:T(8,128)(2,1)S(1)}, u32[]{:S(2)}, u32[]{:S(2)}) collective-permute-start(bf16[4,168,256]{2,1,0:T(8,128)(2,1)S(1)} %get-tuple-element.5), channel_id=1, source_target_pairs={{0,2},{2,4},{4,6},{6,0},{1,3},{3,5},{5,7},{7,1},{8,10},{10,12},{12... | collective-permute-start | bytes 1032200 | tf_op jit(solution)/shard_map/ppermute | solution.py:21
  134.0 12.5 %collective-permute-start.18 = (bf16[4,168,256]{2,1,0:T(8,128)(2,1)S(1)}, bf16[4,168,256]{2,1,0:T(8,128)(2,1)S(1)}, u32[]{:S(2)}, u32[]{:S(2)}) collective-permute-start(bf16[4,168,256]{2,1,0:T(8,128)(2,1)S(1)} %get-tuple-element.6), channel_id=1, source_target_pairs={{0,6},{2,0},{4,2},{6,4},{1,7},{3,1},{5,3},{7,5},{8,14},{10,8},{12,... | collective-permute-start | bytes 1032200 | tf_op jit(solution)/shard_map/ppermute | solution.py:21
  144.5 11.4 %collective-permute-start.17 = (bf16[4,168,256]{2,1,0:T(8,128)(2,1)S(1)}, bf16[4,168,256]{2,1,0:T(8,128)(2,1)S(1)}, u32[]{:S(2)}, u32[]{:S(2)}) collective-permute-start(bf16[4,168,256]{2,1,0:T(8,128)(2,1)S(1)} %fusion.19), channel_id=1, source_target_pairs={{0,2},{2,4},{4,6},{6,0},{1,3},{3,5},{5,7},{7,1},{8,10},{10,12},{12... | collective-permute-start | bytes 1032200 | tf_op jit(solution)/shard_map/ppermute | solution.py:21
  157.2 31.8 %collective-permute-start.19 = (bf16[168,256]{1,0:T(8,128)(2,1)S(1)}, bf16[168,256]{1,0:T(8,128)(2,1)S(1)}, u32[]{:S(2)}, u32[]{:S(2)}) collective-permute-start(bf16[168,256]{1,0:T(8,128)(2,1)S(1)} %get-tuple-element.7), channel_id=1, source_target_pairs={{0,8},{8,16},{16,24},{24,0},{1,9},{9,17},{17,25},{25,1},{2,10},{10... | collective-permute-start | bytes 258056 | tf_op jit(solution)/shard_map/ppermute | solution.py:21
  167.9 25.5 %collective-permute-start.21 = (bf16[168,256]{1,0:T(8,128)(2,1)S(1)}, bf16[168,256]{1,0:T(8,128)(2,1)S(1)}, u32[]{:S(2)}, u32[]{:S(2)}) collective-permute-start(bf16[168,256]{1,0:T(8,128)(2,1)S(1)} %get-tuple-element.8), channel_id=1, source_target_pairs={{0,24},{8,0},{16,8},{24,16},{1,25},{9,1},{17,9},{25,17},{2,26},{10... | collective-permute-start | bytes 258056 | tf_op jit(solution)/shard_map/ppermute | solution.py:21
  189.0 20.3 %collective-permute-start.20 = (bf16[168,256]{1,0:T(8,128)(2,1)S(1)}, bf16[168,256]{1,0:T(8,128)(2,1)S(1)}, u32[]{:S(2)}, u32[]{:S(2)}) collective-permute-start(bf16[168,256]{1,0:T(8,128)(2,1)S(1)} %fusion.29), channel_id=1, source_target_pairs={{0,8},{8,16},{16,24},{24,0},{1,9},{9,17},{17,25},{25,1},{2,10},{10... | collective-permute-start | bytes 258056 | tf_op jit(solution)/shard_map/ppermute | solution.py:21
  (6 other events, 77.5 us)

commit v5 on v3

--- a/solution.py
+++ b/solution.py
@@ -137,11 +137,21 @@
         kv_total = kv_total.astype(jnp.bfloat16)
         grad_keys = kv_total[:, :dim]
         grad_values = kv_total[:, dim:]
-        summed = dot_rows(w_query, grad_query)
-        summed = summed + dot_rows(w_key, grad_keys)
-        summed = summed + dot_rows(w_value, grad_values)
-        term = summed.astype(jnp.bfloat16).reshape(n_zhi, n_x, n_core, width, length)
-        part = scatter_axis(term, "core", n_core, 2)
+        core_index = lax.axis_index("core")
+
+        def project(index):
+            def rows(w):
+                w = w.reshape(n_zhi, n_x, n_core, width, dim)
+                return lax.dynamic_index_in_dim(w, index, 2, keepdims=False).reshape(-1, dim)
+
+            summed = dot_rows(rows(w_query), grad_query)
+            summed = summed + dot_rows(rows(w_key), grad_keys)
+            summed = summed + dot_rows(rows(w_value), grad_values)
+            return summed.astype(jnp.bfloat16).reshape(n_zhi, n_x, width, length)
+
+        keep = project(core_index)
+        sent = shift(project((core_index + 1) % n_core), "core", n_core, 1)
+        part = keep.astype(jnp.float32) + sent.astype(jnp.float32)
         part = scatter_axis(part, "x", n_x, 1)
         part = scatter_axis(part, "zhi", n_zhi, 0, relay=True)
         return part.T.astype(jnp.bfloat16)

time: 210 us -> 201 us (0.957)
  the two profiles are of different devices: /device:TPU:161 before, /device:TPU:166 now
where the time goes in v5:
time: 201 us; the launch traced here: 200 us
  starting transfers between devices  107 us (53%)
  waiting for transfers between devices  65.4 us (33%)
  local copies, waits for them, and re-layouts  13.3 us (7%)
  matrix products  8.3 us (4%)
  other arithmetic  4.62 us (2%)
    ppermute x14, starting transfers between devices, shift(): lax.ppermute(block, axis, [(i, (i + step) % size) for i in range(size)])  75.7 us
    ppermute x14, waiting for transfers between devices, shift(): lax.ppermute(block, axis, [(i, (i + step) % size) for i in range(size)])  61.4 us
    ppermute x8, starting transfers between devices, from_behind(): return lax.ppermute(block, axis, route)  31.7 us
    unnamed x31, local copies, waits for them, and re-layouts  8.64 us
    dot_general x8, matrix products, dot_rows(): lax.dot_general(left, right, (((1,), (1,)), ((), ())), preferred_element_...  5.28 us
    ppermute x8, waiting for transfers between devices, from_behind(): return lax.ppermute(block, axis, route)  4.03 us
  transfers between devices with their start and end apart: 22, of which 13 were waited for; matrix products, arithmetic and copies ran while one was open for 7% of the time, Pallas kernels for 0%

profile of v5, /device:TPU:166, one launch (start us, length us, event | category | flops | bytes accessed | tf_op | source)
XLA Modules:
  0.0 199.9 jit_solution(13327477846607746186)
XLA Ops:
  0.0 15.8 %collective-permute-start.4 = (bf16[256,168]{0,1:T(8,128)(2,1)}, bf16[256,168]{0,1:T(8,128)(2,1)}, u32[]{:S(2)}, u32[]{:S(2)}) collective-permute-start(bf16[256,168]{0,1:T(8,128)(2,1)} %param.11), channel_id=1, source_target_pairs={{0,8},{8,16},{16,24},{24,0},{1,9},{9,17},{17,25},{25,1},{2,10},{10... | collective-permute-start | bytes 258056 | tf_op jit(solution)/shard_map/ppermute | solution.py:21
  15.9 3.5 %collective-permute-start.5 = (bf16[256,168]{0,1:T(8,128)(2,1)}, bf16[256,168]{0,1:T(8,128)(2,1)}, u32[]{:S(2)}, u32[]{:S(2)}) collective-permute-start(bf16[256,168]{0,1:T(8,128)(2,1)} %param.11), channel_id=1, source_target_pairs={{0,24},{8,0},{16,8},{24,16},{1,25},{9,1},{17,9},{25,17},{2,26},{10... | collective-permute-start | bytes 258056 | tf_op jit(solution)/shard_map/ppermute | solution.py:21
  22.3 2.9 %collective-permute-start = (bf16[256,256]{1,0:T(8,128)(2,1)}, bf16[256,256]{1,0:T(8,128)(2,1)}, u32[]{:S(2)}, u32[]{:S(2)}) collective-permute-start(bf16[256,256]{1,0:T(8,128)(2,1)} %constant_dynamic-update-slice_fusion), channel_id=1, source_target_pairs={{0,128},{32,160},{64,192},{96,224},{128,256},{160,288},{192,320},{... | collective-permute-start | bytes 393224 | tf_op jit(solution)/shard_map/ppermute | solution.py:17
  25.2 4.9 %collective-permute-start.1 = (bf16[256,256]{1,0:T(8,128)(2,1)}, bf16[256,256]{1,0:T(8,128)(2,1)}, u32[]{:S(2)}, u32[]{:S(2)}) collective-permute-start(bf16[256,256]{1,0:T(8,128)(2,1)} %constant_dynamic-update-slice_fusion), channel_id=1, source_target_pairs={{0,96},{32,128},{64,160},{96,192},{128,224},{160,256},{192,288},{2... | collective-permute-start | bytes 393224 | tf_op jit(solution)/shard_map/ppermute | solution.py:17
  30.2 3.2 %collective-permute-start.2 = (bf16[256,256]{1,0:T(8,128)(2,1)}, bf16[256,256]{1,0:T(8,128)(2,1)}, u32[]{:S(2)}, u32[]{:S(2)}) collective-permute-start(bf16[256,256]{1,0:T(8,128)(2,1)} %constant_dynamic-update-slice_fusion), channel_id=1, source_target_pairs={{0,64},{32,96},{64,128},{96,160},{128,192},{160,224},{192,256},{22... | collective-permute-start | bytes 393224 | tf_op jit(solution)/shard_map/ppermute | solution.py:17
  38.3 12.6 %collective-permute-start.6 = (bf16[256,168]{0,1:T(8,128)(2,1)}, bf16[256,168]{0,1:T(8,128)(2,1)S(1)}, u32[]{:S(2)}, u32[]{:S(2)}) collective-permute-start(bf16[256,168]{0,1:T(8,128)(2,1)} %collective-permute-done.4), channel_id=1, source_target_pairs={{0,8},{8,16},{16,24},{24,0},{1,9},{9,17},{17,25},{25,1},{2,10},{10... | collective-permute-start | bytes 258056 | tf_op jit(solution)/shard_map/ppermute | solution.py:21
  52.8 9.3 %collective-permute-done.6 = bf16[256,168]{0,1:T(8,128)(2,1)S(1)} collective-permute-done((bf16[256,168]{0,1:T(8,128)(2,1)}, bf16[256,168]{0,1:T(8,128)(2,1)S(1)}, u32[]{:S(2)}, u32[]{:S(2)}) %collective-permute-start.6) | collective-permute-done | bytes 86048 | tf_op jit(solution)/shard_map/ppermute | solution.py:21
  64.5 4.3 %collective-permute-start.8 = (bf16[4,256,168]{1,2,0:T(8,128)(2,1)S(1)}, bf16[4,256,168]{1,2,0:T(8,128)(2,1)S(1)}, u32[]{:S(2)}, u32[]{:S(2)}) collective-permute-start(bf16[4,256,168]{1,2,0:T(8,128)(2,1)S(1)} %bitcast_dynamic-update-slice_fusion.6), channel_id=1, source_target_pairs={{0,4},{2,6},{4,0},{6,2},{1,5},{3,7},{5,1},{7,3},{8,12},{10,14},{12... | collective-permute-start | bytes 1032200 | tf_op jit(solution)/shard_map/ppermute | solution.py:21
  75.2 2.8 %collective-permute-start.3 = (bf16[256,256]{1,0:T(8,128)(2,1)}, bf16[256,256]{1,0:T(8,128)(2,1)S(1)}, u32[]{:S(2)}, u32[]{:S(2)}) collective-permute-start(bf16[256,256]{1,0:T(8,128)(2,1)} %constant_dynamic-update-slice_fusion), channel_id=1, source_target_pairs={{0,32},{32,64},{64,96},{96,128},{128,160},{160,192},{192,224},{224... | collective-permute-start | bytes 393224 | tf_op jit(solution)/shard_map/ppermute | solution.py:17
  78.0 3.5 %collective-permute-done.9 = bf16[4,256,168]{1,2,0:T(8,128)(2,1)S(1)} collective-permute-done((bf16[4,256,168]{1,2,0:T(8,128)(2,1)S(1)}, bf16[4,256,168]{1,2,0:T(8,128)(2,1)S(1)}, u32[]{:S(2)}, u32[]{:S(2)}) %collective-permute-start.9) | collective-permute-done | bytes 344096 | tf_op jit(solution)/shard_map/ppermute | solution.py:21
  93.4 6.7 %collective-permute-start.11 = (bf16[256,256]{0,1:T(8,128)(2,1)S(1)}, bf16[256,256]{0,1:T(8,128)(2,1)S(1)}, u32[]{:S(2)}, u32[]{:S(2)}) collective-permute-start(bf16[256,256]{0,1:T(8,128)(2,1)S(1)} %get-tuple-element.16), channel_id=1, source_target_pairs={{32,0},{64,32},{96,64},{128,96},{160,128},{192,160},{224,192},{256... | collective-permute-start | bytes 393224 | tf_op jit(solution)/shard_map/ppermute | solution.py:17
  102.0 6.8 %collective-permute-start.13 = (bf16[256,256]{0,1:T(8,128)(2,1)S(1)}, bf16[256,256]{0,1:T(8,128)(2,1)S(1)}, u32[]{:S(2)}, u32[]{:S(2)}) collective-permute-start(bf16[256,256]{0,1:T(8,128)(2,1)S(1)} %get-tuple-element.19), channel_id=1, source_target_pairs={{96,0},{128,32},{160,64},{192,96},{224,128},{256,160},{288,192},{3... | collective-permute-start | bytes 393224 | tf_op jit(solution)/shard_map/ppermute | solution.py:17
  112.0 3.7 %collective-permute-done.14 = bf16[256,256]{0,1:T(8,128)(2,1)S(1)} collective-permute-done((bf16[256,256]{0,1:T(8,128)(2,1)S(1)}, bf16[256,256]{0,1:T(8,128)(2,1)S(1)}, u32[]{:S(2)}, u32[]{:S(2)}) %collective-permute-start.14) | collective-permute-done | bytes 131104 | tf_op jit(solution)/shard_map/ppermute | solution.py:17
  124.0 3.0 %collective-permute-start.16 = (bf16[4,168,256]{2,1,0:T(8,128)(2,1)S(1)}, bf16[4,168,256]{2,1,0:T(8,128)(2,1)S(1)}, u32[]{:S(2)}, u32[]{:S(2)}) collective-permute-start(bf16[4,168,256]{2,1,0:T(8,128)(2,1)S(1)} %get-tuple-element.5), channel_id=1, source_target_pairs={{0,2},{2,4},{4,6},{6,0},{1,3},{3,5},{5,7},{7,1},{8,10},{10,12},{12... | collective-permute-start | bytes 1032200 | tf_op jit(solution)/shard_map/ppermute | solution.py:21
  127.0 2.9 %collective-permute-start.17 = (bf16[4,168,256]{2,1,0:T(8,128)(2,1)S(1)}, bf16[4,168,256]{2,1,0:T(8,128)(2,1)S(1)}, u32[]{:S(2)}, u32[]{:S(2)}) collective-permute-start(bf16[4,168,256]{2,1,0:T(8,128)(2,1)S(1)} %get-tuple-element.7), channel_id=1, source_target_pairs={{0,4},{2,6},{4,0},{6,2},{1,5},{3,7},{5,1},{7,3},{8,12},{10,14},{12... | collective-permute-start | bytes 1032200 | tf_op jit(solution)/shard_map/ppermute | solution.py:21
  129.9 2.8 %collective-permute-start.18 = (bf16[4,168,256]{2,1,0:T(8,128)(2,1)S(1)}, bf16[4,168,256]{2,1,0:T(8,128)(2,1)S(1)}, u32[]{:S(2)}, u32[]{:S(2)}) collective-permute-start(bf16[4,168,256]{2,1,0:T(8,128)(2,1)S(1)} %get-tuple-element.6), channel_id=1, source_target_pairs={{0,6},{2,0},{4,2},{6,4},{1,7},{3,1},{5,3},{7,5},{8,14},{10,8},{12,... | collective-permute-start | bytes 1032200 | tf_op jit(solution)/shard_map/ppermute | solution.py:21
  132.7 4.1 %collective-permute-done.16 = bf16[4,168,256]{2,1,0:T(8,128)(2,1)S(1)} collective-permute-done((bf16[4,168,256]{2,1,0:T(8,128)(2,1)S(1)}, bf16[4,168,256]{2,1,0:T(8,128)(2,1)S(1)}, u32[]{:S(2)}, u32[]{:S(2)}) %collective-permute-start.16) | collective-permute-done | bytes 344096 | tf_op jit(solution)/shard_map/ppermute | solution.py:21
  136.8 4.6 %collective-permute-done.17 = bf16[4,168,256]{2,1,0:T(8,128)(2,1)S(1)} collective-permute-done((bf16[4,168,256]{2,1,0:T(8,128)(2,1)S(1)}, bf16[4,168,256]{2,1,0:T(8,128)(2,1)S(1)}, u32[]{:S(2)}, u32[]{:S(2)}) %collective-permute-start.17) | collective-permute-done | bytes 344096 | tf_op jit(solution)/shard_map/ppermute | solution.py:21
  141.4 6.2 %collective-permute-done.18 = bf16[4,168,256]{2,1,0:T(8,128)(2,1)S(1)} collective-permute-done((bf16[4,168,256]{2,1,0:T(8,128)(2,1)S(1)}, bf16[4,168,256]{2,1,0:T(8,128)(2,1)S(1)}, u32[]{:S(2)}, u32[]{:S(2)}) %collective-permute-start.18) | collective-permute-done | bytes 344096 | tf_op jit(solution)/shard_map/ppermute | solution.py:21
  147.8 10.6 %collective-permute-start.19 = (bf16[168,256]{1,0:T(8,128)(2,1)S(1)}, bf16[168,256]{1,0:T(8,128)(2,1)S(1)}, u32[]{:S(2)}, u32[]{:S(2)}) collective-permute-start(bf16[168,256]{1,0:T(8,128)(2,1)S(1)} %get-tuple-element.14), channel_id=1, source_target_pairs={{0,8},{8,16},{16,24},{24,0},{1,9},{9,17},{17,25},{25,1},{2,10},{10... | collective-permute-start | bytes 258056 | tf_op jit(solution)/shard_map/ppermute | solution.py:21
  158.4 5.2 %collective-permute-start.21 = (bf16[168,256]{1,0:T(8,128)(2,1)S(1)}, bf16[168,256]{1,0:T(8,128)(2,1)S(1)}, u32[]{:S(2)}, u32[]{:S(2)}) collective-permute-start(bf16[168,256]{1,0:T(8,128)(2,1)S(1)} %get-tuple-element.15), channel_id=1, source_target_pairs={{0,24},{8,0},{16,8},{24,16},{1,25},{9,1},{17,9},{25,17},{2,26},{10... | collective-permute-start | bytes 258056 | tf_op jit(solution)/shard_map/ppermute | solution.py:21
  163.6 14.0 %collective-permute-done.19 = bf16[168,256]{1,0:T(8,128)(2,1)S(1)} collective-permute-done((bf16[168,256]{1,0:T(8,128)(2,1)S(1)}, bf16[168,256]{1,0:T(8,128)(2,1)S(1)}, u32[]{:S(2)}, u32[]{:S(2)}) %collective-permute-start.19) | collective-permute-done | bytes 86048 | tf_op jit(solution)/shard_map/ppermute | solution.py:21
  177.6 6.0 %collective-permute-start.20 = (bf16[168,256]{1,0:T(8,128)(2,1)S(1)}, bf16[168,256]{1,0:T(8,128)(2,1)S(1)}, u32[]{:S(2)}, u32[]{:S(2)}) collective-permute-start(bf16[168,256]{1,0:T(8,128)(2,1)S(1)} %fusion.28), channel_id=1, source_target_pairs={{0,8},{8,16},{16,24},{24,0},{1,9},{9,17},{17,25},{25,1},{2,10},{10... | collective-permute-start | bytes 258056 | tf_op jit(solution)/shard_map/ppermute | solution.py:21
  183.6 15.6 %collective-permute-done.20 = bf16[168,256]{1,0:T(8,128)(2,1)S(1)} collective-permute-done((bf16[168,256]{1,0:T(8,128)(2,1)S(1)}, bf16[168,256]{1,0:T(8,128)(2,1)S(1)}, u32[]{:S(2)}, u32[]{:S(2)}) %collective-permute-start.20) | collective-permute-done | bytes 86048 | tf_op jit(solution)/shard_map/ppermute | solution.py:21
  (94 shorter events, 43.9 us)
Async XLA Ops:
  0.0 86.4 %copy-start = (bf16[256,128]{1,0:T(8,128)(2,1)S(1)}, bf16[256,128]{1,0:T(8,128)(2,1)}, u32[]{:S(2)}) copy-start(bf16[256,128]{1,0:T(8,128)(2,1)} %param.8) | copy-start | bytes 196612
  0.0 38.3 %collective-permute-start.4 = (bf16[256,168]{0,1:T(8,128)(2,1)}, bf16[256,168]{0,1:T(8,128)(2,1)}, u32[]{:S(2)}, u32[]{:S(2)}) collective-permute-start(bf16[256,168]{0,1:T(8,128)(2,1)} %param.11), channel_id=1, source_target_pairs={{0,8},{8,16},{16,24},{24,0},{1,9},{9,17},{17,25},{25,1},{2,10},{10... | collective-permute-start | bytes 258056 | tf_op jit(solution)/shard_map/ppermute | solution.py:21
  15.9 36.1 %collective-permute-start.5 = (bf16[256,168]{0,1:T(8,128)(2,1)}, bf16[256,168]{0,1:T(8,128)(2,1)}, u32[]{:S(2)}, u32[]{:S(2)}) collective-permute-start(bf16[256,168]{0,1:T(8,128)(2,1)} %param.11), channel_id=1, source_target_pairs={{0,24},{8,0},{16,8},{24,16},{1,25},{9,1},{17,9},{25,17},{2,26},{10... | collective-permute-start | bytes 258056 | tf_op jit(solution)/shard_map/ppermute | solution.py:21
  22.3 61.3 %collective-permute-start = (bf16[256,256]{1,0:T(8,128)(2,1)}, bf16[256,256]{1,0:T(8,128)(2,1)}, u32[]{:S(2)}, u32[]{:S(2)}) collective-permute-start(bf16[256,256]{1,0:T(8,128)(2,1)} %constant_dynamic-update-slice_fusion), channel_id=1, source_target_pairs={{0,128},{32,160},{64,192},{96,224},{128,256},{160,288},{192,320},{... | collective-permute-start | bytes 393224 | tf_op jit(solution)/shard_map/ppermute | solution.py:17
  25.2 59.3 %collective-permute-start.1 = (bf16[256,256]{1,0:T(8,128)(2,1)}, bf16[256,256]{1,0:T(8,128)(2,1)}, u32[]{:S(2)}, u32[]{:S(2)}) collective-permute-start(bf16[256,256]{1,0:T(8,128)(2,1)} %constant_dynamic-update-slice_fusion), channel_id=1, source_target_pairs={{0,96},{32,128},{64,160},{96,192},{128,224},{160,256},{192,288},{2... | collective-permute-start | bytes 393224 | tf_op jit(solution)/shard_map/ppermute | solution.py:17
  30.2 55.3 %collective-permute-start.2 = (bf16[256,256]{1,0:T(8,128)(2,1)}, bf16[256,256]{1,0:T(8,128)(2,1)}, u32[]{:S(2)}, u32[]{:S(2)}) collective-permute-start(bf16[256,256]{1,0:T(8,128)(2,1)} %constant_dynamic-update-slice_fusion), channel_id=1, source_target_pairs={{0,64},{32,96},{64,128},{96,160},{128,192},{160,224},{192,256},{22... | collective-permute-start | bytes 393224 | tf_op jit(solution)/shard_map/ppermute | solution.py:17
  38.3 23.8 %collective-permute-start.6 = (bf16[256,168]{0,1:T(8,128)(2,1)}, bf16[256,168]{0,1:T(8,128)(2,1)S(1)}, u32[]{:S(2)}, u32[]{:S(2)}) collective-permute-start(bf16[256,168]{0,1:T(8,128)(2,1)} %collective-permute-done.4), channel_id=1, source_target_pairs={{0,8},{8,16},{16,24},{24,0},{1,9},{9,17},{17,25},{25,1},{2,10},{10... | collective-permute-start | bytes 258056 | tf_op jit(solution)/shard_map/ppermute | solution.py:21
  62.1 9.1 %collective-permute-start.7 = (bf16[4,256,168]{1,2,0:T(8,128)(2,1)S(1)}, bf16[4,256,168]{1,2,0:T(8,128)(2,1)S(1)}, u32[]{:S(2)}, u32[]{:S(2)}) collective-permute-start(bf16[4,256,168]{1,2,0:T(8,128)(2,1)S(1)} %bitcast_dynamic-update-slice_fusion.6), channel_id=1, source_target_pairs={{0,2},{2,4},{4,6},{6,0},{1,3},{3,5},{5,7},{7,1},{8,10},{10,12},{12... | collective-permute-start | bytes 1032200 | tf_op jit(solution)/shard_map/ppermute | solution.py:21
  64.5 10.6 %collective-permute-start.8 = (bf16[4,256,168]{1,2,0:T(8,128)(2,1)S(1)}, bf16[4,256,168]{1,2,0:T(8,128)(2,1)S(1)}, u32[]{:S(2)}, u32[]{:S(2)}) collective-permute-start(bf16[4,256,168]{1,2,0:T(8,128)(2,1)S(1)} %bitcast_dynamic-update-slice_fusion.6), channel_id=1, source_target_pairs={{0,4},{2,6},{4,0},{6,2},{1,5},{3,7},{5,1},{7,3},{8,12},{10,14},{12... | collective-permute-start | bytes 1032200 | tf_op jit(solution)/shard_map/ppermute | solution.py:21
  71.2 10.3 %collective-permute-start.9 = (bf16[4,256,168]{1,2,0:T(8,128)(2,1)S(1)}, bf16[4,256,168]{1,2,0:T(8,128)(2,1)S(1)}, u32[]{:S(2)}, u32[]{:S(2)}) collective-permute-start(bf16[4,256,168]{1,2,0:T(8,128)(2,1)S(1)} %bitcast_dynamic-update-slice_fusion.6), channel_id=1, source_target_pairs={{0,6},{2,0},{4,2},{6,4},{1,7},{3,1},{5,3},{7,5},{8,14},{10,8},{12,... | collective-permute-start | bytes 1032200 | tf_op jit(solution)/shard_map/ppermute | solution.py:21
  75.2 11.2 %collective-permute-start.3 = (bf16[256,256]{1,0:T(8,128)(2,1)}, bf16[256,256]{1,0:T(8,128)(2,1)S(1)}, u32[]{:S(2)}, u32[]{:S(2)}) collective-permute-start(bf16[256,256]{1,0:T(8,128)(2,1)} %constant_dynamic-update-slice_fusion), channel_id=1, source_target_pairs={{0,32},{32,64},{64,96},{96,128},{128,160},{160,192},{192,224},{224... | collective-permute-start | bytes 393224 | tf_op jit(solution)/shard_map/ppermute | solution.py:17
  81.6 6.7 %collective-permute-start.10 = (bf16[4,4,256,168]{2,3,1,0:T(8,128)(2,1)S(1)}, bf16[4,4,256,168]{2,3,1,0:T(8,128)(2,1)S(1)}, u32[]{:S(2)}, u32[]{:S(2)}) collective-permute-start(bf16[4,4,256,168]{2,3,1,0:T(8,128)(2,1)S(1)} %bitcast_dynamic-update-slice_fusion.2), channel_id=1, source_target_pairs={{0,1},{1,0},{2,3},{3,2},{4,5},{5,4},{6,7},{7,6},{8,9},{9,8},{10,11... | collective-permute-start | bytes 4128776 | tf_op jit(solution)/shard_map/ppermute | solution.py:21
  93.3 18.4 %copy-start.8 = (bf16[256,128]{1,0:T(8,128)(2,1)}, bf16[256,128]{1,0:T(8,128)(2,1)S(1)}, u32[]{:S(2)}) copy-start(bf16[256,128]{1,0:T(8,128)(2,1)S(1)} %fusion.15) | copy-start | bytes 196612
  93.4 18.3 %collective-permute-start.11 = (bf16[256,256]{0,1:T(8,128)(2,1)S(1)}, bf16[256,256]{0,1:T(8,128)(2,1)S(1)}, u32[]{:S(2)}, u32[]{:S(2)}) collective-permute-start(bf16[256,256]{0,1:T(8,128)(2,1)S(1)} %get-tuple-element.16), channel_id=1, source_target_pairs={{32,0},{64,32},{96,64},{128,96},{160,128},{192,160},{224,192},{256... | collective-permute-start | bytes 393224 | tf_op jit(solution)/shard_map/ppermute | solution.py:17
  100.1 11.8 %collective-permute-start.12 = (bf16[256,256]{0,1:T(8,128)(2,1)S(1)}, bf16[256,256]{0,1:T(8,128)(2,1)S(1)}, u32[]{:S(2)}, u32[]{:S(2)}) collective-permute-start(bf16[256,256]{0,1:T(8,128)(2,1)S(1)} %get-tuple-element.17), channel_id=1, source_target_pairs={{64,0},{96,32},{128,64},{160,96},{192,128},{224,160},{256,192},{28... | collective-permute-start | bytes 393224 | tf_op jit(solution)/shard_map/ppermute | solution.py:17
  102.0 10.0 %collective-permute-start.13 = (bf16[256,256]{0,1:T(8,128)(2,1)S(1)}, bf16[256,256]{0,1:T(8,128)(2,1)S(1)}, u32[]{:S(2)}, u32[]{:S(2)}) collective-permute-start(bf16[256,256]{0,1:T(8,128)(2,1)S(1)} %get-tuple-element.19), channel_id=1, source_target_pairs={{96,0},{128,32},{160,64},{192,96},{224,128},{256,160},{288,192},{3... | collective-permute-start | bytes 393224 | tf_op jit(solution)/shard_map/ppermute | solution.py:17
  108.8 7.0 %collective-permute-start.14 = (bf16[256,256]{0,1:T(8,128)(2,1)S(1)}, bf16[256,256]{0,1:T(8,128)(2,1)S(1)}, u32[]{:S(2)}, u32[]{:S(2)}) collective-permute-start(bf16[256,256]{0,1:T(8,128)(2,1)S(1)} %get-tuple-element.18), channel_id=1, source_target_pairs={{128,0},{160,32},{192,64},{224,96},{256,128},{288,160},{320,192},{... | collective-permute-start | bytes 393224 | tf_op jit(solution)/shard_map/ppermute | solution.py:17
  117.1 5.2 %collective-permute-start.15 = (bf16[4,4,168,256]{3,2,0,1:T(8,128)(2,1)S(1)}, bf16[4,4,168,256]{3,2,0,1:T(8,128)(2,1)}, u32[]{:S(2)}, u32[]{:S(2)}) collective-permute-start(bf16[4,4,168,256]{3,2,0,1:T(8,128)(2,1)S(1)} %copy.18), channel_id=1, source_target_pairs={{0,1},{1,0},{2,3},{3,2},{4,5},{5,4},{6,7},{7,6},{8,9},{9,8},{10,11... | collective-permute-start | bytes 4128776 | tf_op jit(solution)/shard_map/ppermute | solution.py:21
  124.0 12.8 %collective-permute-start.16 = (bf16[4,168,256]{2,1,0:T(8,128)(2,1)S(1)}, bf16[4,168,256]{2,1,0:T(8,128)(2,1)S(1)}, u32[]{:S(2)}, u32[]{:S(2)}) collective-permute-start(bf16[4,168,256]{2,1,0:T(8,128)(2,1)S(1)} %get-tuple-element.5), channel_id=1, source_target_pairs={{0,2},{2,4},{4,6},{6,0},{1,3},{3,5},{5,7},{7,1},{8,10},{10,12},{12... | collective-permute-start | bytes 1032200 | tf_op jit(solution)/shard_map/ppermute | solution.py:21
  127.0 14.4 %collective-permute-start.17 = (bf16[4,168,256]{2,1,0:T(8,128)(2,1)S(1)}, bf16[4,168,256]{2,1,0:T(8,128)(2,1)S(1)}, u32[]{:S(2)}, u32[]{:S(2)}) collective-permute-start(bf16[4,168,256]{2,1,0:T(8,128)(2,1)S(1)} %get-tuple-element.7), channel_id=1, source_target_pairs={{0,4},{2,6},{4,0},{6,2},{1,5},{3,7},{5,1},{7,3},{8,12},{10,14},{12... | collective-permute-start | bytes 1032200 | tf_op jit(solution)/shard_map/ppermute | solution.py:21
  129.9 17.6 %collective-permute-start.18 = (bf16[4,168,256]{2,1,0:T(8,128)(2,1)S(1)}, bf16[4,168,256]{2,1,0:T(8,128)(2,1)S(1)}, u32[]{:S(2)}, u32[]{:S(2)}) collective-permute-start(bf16[4,168,256]{2,1,0:T(8,128)(2,1)S(1)} %get-tuple-element.6), channel_id=1, source_target_pairs={{0,6},{2,0},{4,2},{6,4},{1,7},{3,1},{5,3},{7,5},{8,14},{10,8},{12,... | collective-permute-start | bytes 1032200 | tf_op jit(solution)/shard_map/ppermute | solution.py:21
  147.8 29.8 %collective-permute-start.19 = (bf16[168,256]{1,0:T(8,128)(2,1)S(1)}, bf16[168,256]{1,0:T(8,128)(2,1)S(1)}, u32[]{:S(2)}, u32[]{:S(2)}) collective-permute-start(bf16[168,256]{1,0:T(8,128)(2,1)S(1)} %get-tuple-element.14), channel_id=1, source_target_pairs={{0,8},{8,16},{16,24},{24,0},{1,9},{9,17},{17,25},{25,1},{2,10},{10... | collective-permute-start | bytes 258056 | tf_op jit(solution)/shard_map/ppermute | solution.py:21
  158.4 25.2 %collective-permute-start.21 = (bf16[168,256]{1,0:T(8,128)(2,1)S(1)}, bf16[168,256]{1,0:T(8,128)(2,1)S(1)}, u32[]{:S(2)}, u32[]{:S(2)}) collective-permute-start(bf16[168,256]{1,0:T(8,128)(2,1)S(1)} %get-tuple-element.15), channel_id=1, source_target_pairs={{0,24},{8,0},{16,8},{24,16},{1,25},{9,1},{17,9},{25,17},{2,26},{10... | collective-permute-start | bytes 258056 | tf_op jit(solution)/shard_map/ppermute | solution.py:21
  177.6 21.6 %collective-permute-start.20 = (bf16[168,256]{1,0:T(8,128)(2,1)S(1)}, bf16[168,256]{1,0:T(8,128)(2,1)S(1)}, u32[]{:S(2)}, u32[]{:S(2)}) collective-permute-start(bf16[168,256]{1,0:T(8,128)(2,1)S(1)} %fusion.28), channel_id=1, source_target_pairs={{0,8},{8,16},{16,24},{24,0},{1,9},{9,17},{17,25},{25,1},{2,10},{10... | collective-permute-start | bytes 258056 | tf_op jit(solution)/shard_map/ppermute | solution.py:21
  (10 other events, 48.3 us)

commit v6 on v5

--- a/solution.py
+++ b/solution.py
@@ -112,6 +112,8 @@
         width = d_out.shape[1]
         seq_index = lax.axis_index("seq")
         stacked = gather_axis(d_out, "zhi", n_zhi, relay=True)
+        kv = jnp.concatenate([keys, values], axis=1)
+        stacked, kv = lax.optimization_barrier((stacked, kv))
         stacked = gather_axis(stacked, "x", n_x)
         stacked = gather_axis(stacked, "core", n_core)
         out_rows = w_out.reshape(w_out.shape[0], n_zhi, n_x, n_core, width)
@@ -119,7 +121,6 @@
             "cxzti,hzxci->th", stacked, out_rows, preferred_element_type=jnp.float32
         ).astype(jnp.bfloat16)
         reach = NBR
-        kv = jnp.concatenate([keys, values], axis=1)
         kv_blocks = [from_behind(kv, "seq", distance) for distance in range(reach, 0, -1)]
         kv_band = jnp.concatenate(kv_blocks + [kv], axis=0)
         key_band = kv_band[:, :dim]

time: 201 us -> 210 us (1.045)
  the two profiles are of different devices: /device:TPU:166 before, /device:TPU:131 now
where the time goes in v6:
time: 210 us; the launch traced here: 209 us
  starting transfers between devices  125 us (60%)
  waiting for transfers between devices  51.5 us (25%)
  local copies, waits for them, and re-layouts  16.9 us (8%)
  matrix products  8.29 us (4%)
  other arithmetic  6.2 us (3%)
    ppermute x14, starting transfers between devices, shift(): lax.ppermute(block, axis, [(i, (i + step) % size) for i in range(size)])  88.7 us
    ppermute x14, waiting for transfers between devices, shift(): lax.ppermute(block, axis, [(i, (i + step) % size) for i in range(size)])  44.4 us
    ppermute x8, starting transfers between devices, from_behind(): return lax.ppermute(block, axis, route)  36.5 us
    ppermute x8, waiting for transfers between devices, from_behind(): return lax.ppermute(block, axis, route)  7.11 us
    dot_general x8, matrix products, dot_rows(): lax.dot_general(left, right, (((1,), (1,)), ((), ())), preferred_element_...  5.3 us
    unnamed x25, local copies, waits for them, and re-layouts  4.68 us
  transfers between devices with their start and end apart: 22, of which 10 were waited for; matrix products, arithmetic and copies ran while one was open for 10% of the time, Pallas kernels for 0%

profile of v6, /device:TPU:131, one launch (start us, length us, event | category | flops | bytes accessed | tf_op | source)
XLA Modules:
  0.0 208.7 jit_solution(13008620772467822939)
XLA Ops:
  0.0 15.6 %collective-permute-start = (bf16[256,168]{0,1:T(8,128)(2,1)}, bf16[256,168]{0,1:T(8,128)(2,1)S(1)}, u32[]{:S(2)}, u32[]{:S(2)}) collective-permute-start(bf16[256,168]{0,1:T(8,128)(2,1)} %param.11), channel_id=1, source_target_pairs={{0,8},{8,16},{16,24},{24,0},{1,9},{9,17},{17,25},{25,1},{2,10},{10... | collective-permute-start | bytes 258056 | tf_op jit(solution)/shard_map/ppermute | solution.py:21
  15.6 4.4 %collective-permute-start.1 = (bf16[256,168]{0,1:T(8,128)(2,1)}, bf16[256,168]{0,1:T(8,128)(2,1)S(1)}, u32[]{:S(2)}, u32[]{:S(2)}) collective-permute-start(bf16[256,168]{0,1:T(8,128)(2,1)} %param.11), channel_id=1, source_target_pairs={{0,24},{8,0},{16,8},{24,16},{1,25},{9,1},{17,9},{25,17},{2,26},{10... | collective-permute-start | bytes 258056 | tf_op jit(solution)/shard_map/ppermute | solution.py:21
  27.7 10.6 %collective-permute-start.2 = (bf16[256,168]{0,1:T(8,128)(2,1)S(1)}, bf16[256,168]{0,1:T(8,128)(2,1)S(1)}, u32[]{:S(2)}, u32[]{:S(2)}) collective-permute-start(bf16[256,168]{0,1:T(8,128)(2,1)S(1)} %collective-permute-done), channel_id=1, source_target_pairs={{0,8},{8,16},{16,24},{24,0},{1,9},{9,17},{17,25},{25,1},{2,10},{10... | collective-permute-start | bytes 258056 | tf_op jit(solution)/shard_map/ppermute | solution.py:21
  39.6 6.2 %collective-permute-done.2 = bf16[256,168]{0,1:T(8,128)(2,1)S(1)} collective-permute-done((bf16[256,168]{0,1:T(8,128)(2,1)S(1)}, bf16[256,168]{0,1:T(8,128)(2,1)S(1)}, u32[]{:S(2)}, u32[]{:S(2)}) %collective-permute-start.2) | collective-permute-done | bytes 86048 | tf_op jit(solution)/shard_map/ppermute | solution.py:21
  46.5 3.1 %collective-permute-start.7 = (bf16[4,256,168]{1,2,0:T(8,128)(2,1)}, bf16[4,256,168]{1,2,0:T(8,128)(2,1)S(1)}, u32[]{:S(2)}, u32[]{:S(2)}) collective-permute-start(bf16[4,256,168]{1,2,0:T(8,128)(2,1)} %bitcast_dynamic-update-slice_fusion.6), channel_id=1, source_target_pairs={{0,2},{2,4},{4,6},{6,0},{1,3},{3,5},{5,7},{7,1},{8,10},{10,12},{12... | collective-permute-start | bytes 1032200 | tf_op jit(solution)/shard_map/ppermute | solution.py:21
  49.6 2.7 %collective-permute-start.8 = (bf16[4,256,168]{1,2,0:T(8,128)(2,1)}, bf16[4,256,168]{1,2,0:T(8,128)(2,1)S(1)}, u32[]{:S(2)}, u32[]{:S(2)}) collective-permute-start(bf16[4,256,168]{1,2,0:T(8,128)(2,1)} %bitcast_dynamic-update-slice_fusion.6), channel_id=1, source_target_pairs={{0,4},{2,6},{4,0},{6,2},{1,5},{3,7},{5,1},{7,3},{8,12},{10,14},{12... | collective-permute-start | bytes 1032200 | tf_op jit(solution)/shard_map/ppermute | solution.py:21
  52.3 3.8 %collective-permute-start.9 = (bf16[4,256,168]{1,2,0:T(8,128)(2,1)}, bf16[4,256,168]{1,2,0:T(8,128)(2,1)S(1)}, u32[]{:S(2)}, u32[]{:S(2)}) collective-permute-start(bf16[4,256,168]{1,2,0:T(8,128)(2,1)} %bitcast_dynamic-update-slice_fusion.6), channel_id=1, source_target_pairs={{0,6},{2,0},{4,2},{6,4},{1,7},{3,1},{5,3},{7,5},{8,14},{10,8},{12,... | collective-permute-start | bytes 1032200 | tf_op jit(solution)/shard_map/ppermute | solution.py:21
  56.1 7.8 %collective-permute-start.3 = (bf16[256,256]{1,0:T(8,128)(2,1)}, bf16[256,256]{1,0:T(8,128)(2,1)}, u32[]{:S(2)}, u32[]{:S(2)}) collective-permute-start(bf16[256,256]{1,0:T(8,128)(2,1)} %pad_maximum_fusion.1), channel_id=1, source_target_pairs={{0,128},{32,160},{64,192},{96,224},{128,256},{160,288},{192,320},{... | collective-permute-start | bytes 393224 | tf_op jit(solution)/shard_map/ppermute | solution.py:17
  64.0 4.6 %collective-permute-start.4 = (bf16[256,256]{1,0:T(8,128)(2,1)}, bf16[256,256]{1,0:T(8,128)(2,1)}, u32[]{:S(2)}, u32[]{:S(2)}) collective-permute-start(bf16[256,256]{1,0:T(8,128)(2,1)} %pad_maximum_fusion.1), channel_id=1, source_target_pairs={{0,96},{32,128},{64,160},{96,192},{128,224},{160,256},{192,288},{2... | collective-permute-start | bytes 393224 | tf_op jit(solution)/shard_map/ppermute | solution.py:17
  69.9 5.4 %collective-permute-start.10 = (bf16[4,4,256,168]{2,3,1,0:T(8,128)(2,1)S(1)}, bf16[4,4,256,168]{2,3,1,0:T(8,128)(2,1)}, u32[]{:S(2)}, u32[]{:S(2)}) collective-permute-start(bf16[4,4,256,168]{2,3,1,0:T(8,128)(2,1)S(1)} %bitcast_dynamic-update-slice_fusion.2), channel_id=1, source_target_pairs={{0,1},{1,0},{2,3},{3,2},{4,5},{5,4},{6,7},{7,6},{8,9},{9,8},{10,11... | collective-permute-start | bytes 4128776 | tf_op jit(solution)/shard_map/ppermute | solution.py:21
  77.8 4.9 %collective-permute-start.5 = (bf16[256,256]{1,0:T(8,128)(2,1)}, bf16[256,256]{1,0:T(8,128)(2,1)S(1)}, u32[]{:S(2)}, u32[]{:S(2)}) collective-permute-start(bf16[256,256]{1,0:T(8,128)(2,1)} %pad_maximum_fusion.1), channel_id=1, source_target_pairs={{0,64},{32,96},{64,128},{96,160},{128,192},{160,224},{192,256},{22... | collective-permute-start | bytes 393224 | tf_op jit(solution)/shard_map/ppermute | solution.py:17
  88.6 4.3 %collective-permute-done.6 = bf16[256,256]{1,0:T(8,128)(2,1)S(1)} collective-permute-done((bf16[256,256]{1,0:T(8,128)(2,1)}, bf16[256,256]{1,0:T(8,128)(2,1)S(1)}, u32[]{:S(2)}, u32[]{:S(2)}) %collective-permute-start.6) | collective-permute-done | bytes 131104 | tf_op jit(solution)/shard_map/ppermute | solution.py:17
  104.3 3.2 %collective-permute-start.12 = (bf16[256,256]{0,1:T(8,128)(2,1)S(1)}, bf16[256,256]{0,1:T(8,128)(2,1)S(1)}, u32[]{:S(2)}, u32[]{:S(2)}) collective-permute-start(bf16[256,256]{0,1:T(8,128)(2,1)S(1)} %get-tuple-element.21), channel_id=1, source_target_pairs={{64,0},{96,32},{128,64},{160,96},{192,128},{224,160},{256,192},{28... | collective-permute-start | bytes 393224 | tf_op jit(solution)/shard_map/ppermute | solution.py:17
  107.5 3.8 %collective-permute-start.13 = (bf16[256,256]{0,1:T(8,128)(2,1)S(1)}, bf16[256,256]{0,1:T(8,128)(2,1)S(1)}, u32[]{:S(2)}, u32[]{:S(2)}) collective-permute-start(bf16[256,256]{0,1:T(8,128)(2,1)S(1)} %get-tuple-element.23), channel_id=1, source_target_pairs={{96,0},{128,32},{160,64},{192,96},{224,128},{256,160},{288,192},{3... | collective-permute-start | bytes 393224 | tf_op jit(solution)/shard_map/ppermute | solution.py:17
  111.3 7.6 %collective-permute-start.14 = (bf16[256,256]{0,1:T(8,128)(2,1)S(1)}, bf16[256,256]{0,1:T(8,128)(2,1)S(1)}, u32[]{:S(2)}, u32[]{:S(2)}) collective-permute-start(bf16[256,256]{0,1:T(8,128)(2,1)S(1)} %get-tuple-element.22), channel_id=1, source_target_pairs={{128,0},{160,32},{192,64},{224,96},{256,128},{288,160},{320,192},{... | collective-permute-start | bytes 393224 | tf_op jit(solution)/shard_map/ppermute | solution.py:17
  122.2 4.2 %collective-permute-start.15 = (bf16[4,4,168,256]{3,2,0,1:T(8,128)(2,1)S(1)}, bf16[4,4,168,256]{3,2,0,1:T(8,128)(2,1)}, u32[]{:S(2)}, u32[]{:S(2)}) collective-permute-start(bf16[4,4,168,256]{3,2,0,1:T(8,128)(2,1)S(1)} %copy.18), channel_id=1, source_target_pairs={{0,1},{1,0},{2,3},{3,2},{4,5},{5,4},{6,7},{7,6},{8,9},{9,8},{10,11... | collective-permute-start | bytes 4128776 | tf_op jit(solution)/shard_map/ppermute | solution.py:21
  133.3 2.8 %collective-permute-start.17 = (bf16[4,168,256]{2,1,0:T(8,128)(2,1)S(1)}, bf16[4,168,256]{2,1,0:T(8,128)(2,1)S(1)}, u32[]{:S(2)}, u32[]{:S(2)}) collective-permute-start(bf16[4,168,256]{2,1,0:T(8,128)(2,1)S(1)} %get-tuple-element.11), channel_id=1, source_target_pairs={{0,4},{2,6},{4,0},{6,2},{1,5},{3,7},{5,1},{7,3},{8,12},{10,14},{12... | collective-permute-start | bytes 1032200 | tf_op jit(solution)/shard_map/ppermute | solution.py:21
  136.1 3.7 %collective-permute-start.18 = (bf16[4,168,256]{2,1,0:T(8,128)(2,1)S(1)}, bf16[4,168,256]{2,1,0:T(8,128)(2,1)S(1)}, u32[]{:S(2)}, u32[]{:S(2)}) collective-permute-start(bf16[4,168,256]{2,1,0:T(8,128)(2,1)S(1)} %get-tuple-element.10), channel_id=1, source_target_pairs={{0,6},{2,0},{4,2},{6,4},{1,7},{3,1},{5,3},{7,5},{8,14},{10,8},{12,... | collective-permute-start | bytes 1032200 | tf_op jit(solution)/shard_map/ppermute | solution.py:21
  142.2 3.5 %collective-permute-done.17 = bf16[4,168,256]{2,1,0:T(8,128)(2,1)S(1)} collective-permute-done((bf16[4,168,256]{2,1,0:T(8,128)(2,1)S(1)}, bf16[4,168,256]{2,1,0:T(8,128)(2,1)S(1)}, u32[]{:S(2)}, u32[]{:S(2)}) %collective-permute-start.17) | collective-permute-done | bytes 344096 | tf_op jit(solution)/shard_map/ppermute | solution.py:21
  145.7 8.4 %collective-permute-done.18 = bf16[4,168,256]{2,1,0:T(8,128)(2,1)S(1)} collective-permute-done((bf16[4,168,256]{2,1,0:T(8,128)(2,1)S(1)}, bf16[4,168,256]{2,1,0:T(8,128)(2,1)S(1)}, u32[]{:S(2)}, u32[]{:S(2)}) %collective-permute-start.18) | collective-permute-done | bytes 344096 | tf_op jit(solution)/shard_map/ppermute | solution.py:21
  154.3 12.9 %collective-permute-start.19 = (bf16[168,256]{1,0:T(8,128)(2,1)S(1)}, bf16[168,256]{1,0:T(8,128)(2,1)S(1)}, u32[]{:S(2)}, u32[]{:S(2)}) collective-permute-start(bf16[168,256]{1,0:T(8,128)(2,1)S(1)} %get-tuple-element.18), channel_id=1, source_target_pairs={{0,8},{8,16},{16,24},{24,0},{1,9},{9,17},{17,25},{25,1},{2,10},{10... | collective-permute-start | bytes 258056 | tf_op jit(solution)/shard_map/ppermute | solution.py:21
  167.2 4.7 %collective-permute-start.21 = (bf16[168,256]{1,0:T(8,128)(2,1)S(1)}, bf16[168,256]{1,0:T(8,128)(2,1)S(1)}, u32[]{:S(2)}, u32[]{:S(2)}) collective-permute-start(bf16[168,256]{1,0:T(8,128)(2,1)S(1)} %get-tuple-element.19), channel_id=1, source_target_pairs={{0,24},{8,0},{16,8},{24,16},{1,25},{9,1},{17,9},{25,17},{2,26},{10... | collective-permute-start | bytes 258056 | tf_op jit(solution)/shard_map/ppermute | solution.py:21
  172.6 12.6 %collective-permute-start.20 = (bf16[168,256]{1,0:T(8,128)(2,1)S(1)}, bf16[168,256]{1,0:T(8,128)(2,1)S(1)}, u32[]{:S(2)}, u32[]{:S(2)}) collective-permute-start(bf16[168,256]{1,0:T(8,128)(2,1)S(1)} %fusion.28), channel_id=1, source_target_pairs={{0,8},{8,16},{16,24},{24,0},{1,9},{9,17},{17,25},{25,1},{2,10},{10... | collective-permute-start | bytes 258056 | tf_op jit(solution)/shard_map/ppermute | solution.py:21
  185.3 22.8 %collective-permute-done.20 = bf16[168,256]{1,0:T(8,128)(2,1)S(1)} collective-permute-done((bf16[168,256]{1,0:T(8,128)(2,1)S(1)}, bf16[168,256]{1,0:T(8,128)(2,1)S(1)}, u32[]{:S(2)}, u32[]{:S(2)}) %collective-permute-start.20) | collective-permute-done | bytes 86048 | tf_op jit(solution)/shard_map/ppermute | solution.py:21
  (88 shorter events, 44.5 us)
Async XLA Ops:
  0.0 93.9 %copy-start = (bf16[256,128]{1,0:T(8,128)(2,1)S(1)}, bf16[256,128]{1,0:T(8,128)(2,1)}, u32[]{:S(2)}) copy-start(bf16[256,128]{1,0:T(8,128)(2,1)} %param.8) | copy-start | bytes 196612
  0.0 27.7 %collective-permute-start = (bf16[256,168]{0,1:T(8,128)(2,1)}, bf16[256,168]{0,1:T(8,128)(2,1)S(1)}, u32[]{:S(2)}, u32[]{:S(2)}) collective-permute-start(bf16[256,168]{0,1:T(8,128)(2,1)} %param.11), channel_id=1, source_target_pairs={{0,8},{8,16},{16,24},{24,0},{1,9},{9,17},{17,25},{25,1},{2,10},{10... | collective-permute-start | bytes 258056 | tf_op jit(solution)/shard_map/ppermute | solution.py:21
  15.6 23.4 %collective-permute-start.1 = (bf16[256,168]{0,1:T(8,128)(2,1)}, bf16[256,168]{0,1:T(8,128)(2,1)S(1)}, u32[]{:S(2)}, u32[]{:S(2)}) collective-permute-start(bf16[256,168]{0,1:T(8,128)(2,1)} %param.11), channel_id=1, source_target_pairs={{0,24},{8,0},{16,8},{24,16},{1,25},{9,1},{17,9},{25,17},{2,26},{10... | collective-permute-start | bytes 258056 | tf_op jit(solution)/shard_map/ppermute | solution.py:21
  27.7 18.1 %collective-permute-start.2 = (bf16[256,168]{0,1:T(8,128)(2,1)S(1)}, bf16[256,168]{0,1:T(8,128)(2,1)S(1)}, u32[]{:S(2)}, u32[]{:S(2)}) collective-permute-start(bf16[256,168]{0,1:T(8,128)(2,1)S(1)} %collective-permute-done), channel_id=1, source_target_pairs={{0,8},{8,16},{16,24},{24,0},{1,9},{9,17},{17,25},{25,1},{2,10},{10... | collective-permute-start | bytes 258056 | tf_op jit(solution)/shard_map/ppermute | solution.py:21
  46.5 23.3 %collective-permute-start.7 = (bf16[4,256,168]{1,2,0:T(8,128)(2,1)}, bf16[4,256,168]{1,2,0:T(8,128)(2,1)S(1)}, u32[]{:S(2)}, u32[]{:S(2)}) collective-permute-start(bf16[4,256,168]{1,2,0:T(8,128)(2,1)} %bitcast_dynamic-update-slice_fusion.6), channel_id=1, source_target_pairs={{0,2},{2,4},{4,6},{6,0},{1,3},{3,5},{5,7},{7,1},{8,10},{10,12},{12... | collective-permute-start | bytes 1032200 | tf_op jit(solution)/shard_map/ppermute | solution.py:21
  49.6 20.2 %collective-permute-start.8 = (bf16[4,256,168]{1,2,0:T(8,128)(2,1)}, bf16[4,256,168]{1,2,0:T(8,128)(2,1)S(1)}, u32[]{:S(2)}, u32[]{:S(2)}) collective-permute-start(bf16[4,256,168]{1,2,0:T(8,128)(2,1)} %bitcast_dynamic-update-slice_fusion.6), channel_id=1, source_target_pairs={{0,4},{2,6},{4,0},{6,2},{1,5},{3,7},{5,1},{7,3},{8,12},{10,14},{12... | collective-permute-start | bytes 1032200 | tf_op jit(solution)/shard_map/ppermute | solution.py:21
  52.3 17.5 %collective-permute-start.9 = (bf16[4,256,168]{1,2,0:T(8,128)(2,1)}, bf16[4,256,168]{1,2,0:T(8,128)(2,1)S(1)}, u32[]{:S(2)}, u32[]{:S(2)}) collective-permute-start(bf16[4,256,168]{1,2,0:T(8,128)(2,1)} %bitcast_dynamic-update-slice_fusion.6), channel_id=1, source_target_pairs={{0,6},{2,0},{4,2},{6,4},{1,7},{3,1},{5,3},{7,5},{8,14},{10,8},{12,... | collective-permute-start | bytes 1032200 | tf_op jit(solution)/shard_map/ppermute | solution.py:21
  56.1 29.2 %collective-permute-start.3 = (bf16[256,256]{1,0:T(8,128)(2,1)}, bf16[256,256]{1,0:T(8,128)(2,1)}, u32[]{:S(2)}, u32[]{:S(2)}) collective-permute-start(bf16[256,256]{1,0:T(8,128)(2,1)} %pad_maximum_fusion.1), channel_id=1, source_target_pairs={{0,128},{32,160},{64,192},{96,224},{128,256},{160,288},{192,320},{... | collective-permute-start | bytes 393224 | tf_op jit(solution)/shard_map/ppermute | solution.py:17
  64.0 22.3 %collective-permute-start.4 = (bf16[256,256]{1,0:T(8,128)(2,1)}, bf16[256,256]{1,0:T(8,128)(2,1)}, u32[]{:S(2)}, u32[]{:S(2)}) collective-permute-start(bf16[256,256]{1,0:T(8,128)(2,1)} %pad_maximum_fusion.1), channel_id=1, source_target_pairs={{0,96},{32,128},{64,160},{96,192},{128,224},{160,256},{192,288},{2... | collective-permute-start | bytes 393224 | tf_op jit(solution)/shard_map/ppermute | solution.py:17
  69.9 25.9 %collective-permute-start.10 = (bf16[4,4,256,168]{2,3,1,0:T(8,128)(2,1)S(1)}, bf16[4,4,256,168]{2,3,1,0:T(8,128)(2,1)}, u32[]{:S(2)}, u32[]{:S(2)}) collective-permute-start(bf16[4,4,256,168]{2,3,1,0:T(8,128)(2,1)S(1)} %bitcast_dynamic-update-slice_fusion.2), channel_id=1, source_target_pairs={{0,1},{1,0},{2,3},{3,2},{4,5},{5,4},{6,7},{7,6},{8,9},{9,8},{10,11... | collective-permute-start | bytes 4128776 | tf_op jit(solution)/shard_map/ppermute | solution.py:21
  77.8 10.8 %collective-permute-start.5 = (bf16[256,256]{1,0:T(8,128)(2,1)}, bf16[256,256]{1,0:T(8,128)(2,1)S(1)}, u32[]{:S(2)}, u32[]{:S(2)}) collective-permute-start(bf16[256,256]{1,0:T(8,128)(2,1)} %pad_maximum_fusion.1), channel_id=1, source_target_pairs={{0,64},{32,96},{64,128},{96,160},{128,192},{160,224},{192,256},{22... | collective-permute-start | bytes 393224 | tf_op jit(solution)/shard_map/ppermute | solution.py:17
  82.7 10.2 %collective-permute-start.6 = (bf16[256,256]{1,0:T(8,128)(2,1)}, bf16[256,256]{1,0:T(8,128)(2,1)S(1)}, u32[]{:S(2)}, u32[]{:S(2)}) collective-permute-start(bf16[256,256]{1,0:T(8,128)(2,1)} %pad_maximum_fusion.1), channel_id=1, source_target_pairs={{0,32},{32,64},{64,96},{96,128},{128,160},{160,192},{192,224},{224... | collective-permute-start | bytes 393224 | tf_op jit(solution)/shard_map/ppermute | solution.py:17
  102.3 17.1 %copy-start.9 = (bf16[256,128]{1,0:T(8,128)(2,1)}, bf16[256,128]{1,0:T(8,128)(2,1)S(1)}, u32[]{:S(2)}) copy-start(bf16[256,128]{1,0:T(8,128)(2,1)S(1)} %fusion.15) | copy-start | bytes 196612
  102.4 17.1 %collective-permute-start.11 = (bf16[256,256]{0,1:T(8,128)(2,1)S(1)}, bf16[256,256]{0,1:T(8,128)(2,1)S(1)}, u32[]{:S(2)}, u32[]{:S(2)}) collective-permute-start(bf16[256,256]{0,1:T(8,128)(2,1)S(1)} %get-tuple-element.20), channel_id=1, source_target_pairs={{32,0},{64,32},{96,64},{128,96},{160,128},{192,160},{224,192},{256... | collective-permute-start | bytes 393224 | tf_op jit(solution)/shard_map/ppermute | solution.py:17
  104.3 15.2 %collective-permute-start.12 = (bf16[256,256]{0,1:T(8,128)(2,1)S(1)}, bf16[256,256]{0,1:T(8,128)(2,1)S(1)}, u32[]{:S(2)}, u32[]{:S(2)}) collective-permute-start(bf16[256,256]{0,1:T(8,128)(2,1)S(1)} %get-tuple-element.21), channel_id=1, source_target_pairs={{64,0},{96,32},{128,64},{160,96},{192,128},{224,160},{256,192},{28... | collective-permute-start | bytes 393224 | tf_op jit(solution)/shard_map/ppermute | solution.py:17
  107.5 12.0 %collective-permute-start.13 = (bf16[256,256]{0,1:T(8,128)(2,1)S(1)}, bf16[256,256]{0,1:T(8,128)(2,1)S(1)}, u32[]{:S(2)}, u32[]{:S(2)}) collective-permute-start(bf16[256,256]{0,1:T(8,128)(2,1)S(1)} %get-tuple-element.23), channel_id=1, source_target_pairs={{96,0},{128,32},{160,64},{192,96},{224,128},{256,160},{288,192},{3... | collective-permute-start | bytes 393224 | tf_op jit(solution)/shard_map/ppermute | solution.py:17
  111.3 9.6 %collective-permute-start.14 = (bf16[256,256]{0,1:T(8,128)(2,1)S(1)}, bf16[256,256]{0,1:T(8,128)(2,1)S(1)}, u32[]{:S(2)}, u32[]{:S(2)}) collective-permute-start(bf16[256,256]{0,1:T(8,128)(2,1)S(1)} %get-tuple-element.22), channel_id=1, source_target_pairs={{128,0},{160,32},{192,64},{224,96},{256,128},{288,160},{320,192},{... | collective-permute-start | bytes 393224 | tf_op jit(solution)/shard_map/ppermute | solution.py:17
  122.2 7.0 %collective-permute-start.15 = (bf16[4,4,168,256]{3,2,0,1:T(8,128)(2,1)S(1)}, bf16[4,4,168,256]{3,2,0,1:T(8,128)(2,1)}, u32[]{:S(2)}, u32[]{:S(2)}) collective-permute-start(bf16[4,4,168,256]{3,2,0,1:T(8,128)(2,1)S(1)} %copy.18), channel_id=1, source_target_pairs={{0,1},{1,0},{2,3},{3,2},{4,5},{5,4},{6,7},{7,6},{8,9},{9,8},{10,11... | collective-permute-start | bytes 4128776 | tf_op jit(solution)/shard_map/ppermute | solution.py:21
  131.0 11.2 %collective-permute-start.16 = (bf16[4,168,256]{2,1,0:T(8,128)(2,1)S(1)}, bf16[4,168,256]{2,1,0:T(8,128)(2,1)S(1)}, u32[]{:S(2)}, u32[]{:S(2)}) collective-permute-start(bf16[4,168,256]{2,1,0:T(8,128)(2,1)S(1)} %get-tuple-element.9), channel_id=1, source_target_pairs={{0,2},{2,4},{4,6},{6,0},{1,3},{3,5},{5,7},{7,1},{8,10},{10,12},{12... | collective-permute-start | bytes 1032200 | tf_op jit(solution)/shard_map/ppermute | solution.py:21
  133.3 12.4 %collective-permute-start.17 = (bf16[4,168,256]{2,1,0:T(8,128)(2,1)S(1)}, bf16[4,168,256]{2,1,0:T(8,128)(2,1)S(1)}, u32[]{:S(2)}, u32[]{:S(2)}) collective-permute-start(bf16[4,168,256]{2,1,0:T(8,128)(2,1)S(1)} %get-tuple-element.11), channel_id=1, source_target_pairs={{0,4},{2,6},{4,0},{6,2},{1,5},{3,7},{5,1},{7,3},{8,12},{10,14},{12... | collective-permute-start | bytes 1032200 | tf_op jit(solution)/shard_map/ppermute | solution.py:21
  136.1 18.0 %collective-permute-start.18 = (bf16[4,168,256]{2,1,0:T(8,128)(2,1)S(1)}, bf16[4,168,256]{2,1,0:T(8,128)(2,1)S(1)}, u32[]{:S(2)}, u32[]{:S(2)}) collective-permute-start(bf16[4,168,256]{2,1,0:T(8,128)(2,1)S(1)} %get-tuple-element.10), channel_id=1, source_target_pairs={{0,6},{2,0},{4,2},{6,4},{1,7},{3,1},{5,3},{7,5},{8,14},{10,8},{12,... | collective-permute-start | bytes 1032200 | tf_op jit(solution)/shard_map/ppermute | solution.py:21
  154.3 18.3 %collective-permute-start.19 = (bf16[168,256]{1,0:T(8,128)(2,1)S(1)}, bf16[168,256]{1,0:T(8,128)(2,1)S(1)}, u32[]{:S(2)}, u32[]{:S(2)}) collective-permute-start(bf16[168,256]{1,0:T(8,128)(2,1)S(1)} %get-tuple-element.18), channel_id=1, source_target_pairs={{0,8},{8,16},{16,24},{24,0},{1,9},{9,17},{17,25},{25,1},{2,10},{10... | collective-permute-start | bytes 258056 | tf_op jit(solution)/shard_map/ppermute | solution.py:21
  167.2 18.1 %collective-permute-start.21 = (bf16[168,256]{1,0:T(8,128)(2,1)S(1)}, bf16[168,256]{1,0:T(8,128)(2,1)S(1)}, u32[]{:S(2)}, u32[]{:S(2)}) collective-permute-start(bf16[168,256]{1,0:T(8,128)(2,1)S(1)} %get-tuple-element.19), channel_id=1, source_target_pairs={{0,24},{8,0},{16,8},{24,16},{1,25},{9,1},{17,9},{25,17},{2,26},{10... | collective-permute-start | bytes 258056 | tf_op jit(solution)/shard_map/ppermute | solution.py:21
  172.6 35.4 %collective-permute-start.20 = (bf16[168,256]{1,0:T(8,128)(2,1)S(1)}, bf16[168,256]{1,0:T(8,128)(2,1)S(1)}, u32[]{:S(2)}, u32[]{:S(2)}) collective-permute-start(bf16[168,256]{1,0:T(8,128)(2,1)S(1)} %fusion.28), channel_id=1, source_target_pairs={{0,8},{8,16},{16,24},{24,0},{1,9},{9,17},{17,25},{25,1},{2,10},{10... | collective-permute-start | bytes 258056 | tf_op jit(solution)/shard_map/ppermute | solution.py:21
  (8 other events, 31.9 us)

commit v7 on v5

--- a/solution.py
+++ b/solution.py
@@ -129,14 +129,14 @@
             query, key_band, value_band, grad_heads, query_start, query_start - reach * length
         )
         kv_parts = jnp.concatenate([key_parts, value_parts], axis=1)
-        kv_total = kv_parts[reach * length :].astype(jnp.float32)
+        own = kv_parts[reach * length :]
+        came = None
         for distance in range(1, reach + 1):
             first = (reach - distance) * length
             back = from_behind(kv_parts[first : first + length], "seq", -distance)
-            kv_total = kv_total + back.astype(jnp.float32)
-        kv_total = kv_total.astype(jnp.bfloat16)
-        grad_keys = kv_total[:, :dim]
-        grad_values = kv_total[:, dim:]
+            back = back.astype(jnp.float32)
+            came = back if came is None else came + back
+        came = came.astype(jnp.bfloat16)
         core_index = lax.axis_index("core")
 
         def project(index):
@@ -145,8 +145,10 @@
                 return lax.dynamic_index_in_dim(w, index, 2, keepdims=False).reshape(-1, dim)
 
             summed = dot_rows(rows(w_query), grad_query)
-            summed = summed + dot_rows(rows(w_key), grad_keys)
-            summed = summed + dot_rows(rows(w_value), grad_values)
+            summed = summed + dot_rows(rows(w_key), own[:, :dim])
+            summed = summed + dot_rows(rows(w_value), own[:, dim:])
+            summed = summed + dot_rows(rows(w_key), came[:, :dim])
+            summed = summed + dot_rows(rows(w_value), came[:, dim:])
             return summed.astype(jnp.bfloat16).reshape(n_zhi, n_x, width, length)
 
         keep = project(core_index)

time: 201 us -> 203 us (level)
  the two profiles are of different devices: /device:TPU:166 before, /device:TPU:174 now
where the time goes in v7:
time: 203 us; the launch traced here: 202 us
  starting transfers between devices  110 us (54%)
  waiting for transfers between devices  60.1 us (30%)
  local copies, waits for them, and re-layouts  18.8 us (9%)
  matrix products  9.45 us (5%)
  other arithmetic  3.32 us (2%)
    ppermute x14, starting transfers between devices, shift(): lax.ppermute(block, axis, [(i, (i + step) % size) for i in range(size)])  74.1 us
    ppermute x14, waiting for transfers between devices, shift(): lax.ppermute(block, axis, [(i, (i + step) % size) for i in range(size)])  57.1 us
    ppermute x8, starting transfers between devices, from_behind(): return lax.ppermute(block, axis, route)  35.4 us
    unnamed x25, local copies, waits for them, and re-layouts  9.13 us
    dot_general x12, matrix products, dot_rows(): lax.dot_general(left, right, (((1,), (1,)), ((), ())), preferred_element_...  6.44 us
  transfers between devices with their start and end apart: 22, of which 11 were waited for; matrix products, arithmetic and copies ran while one was open for 11% of the time, Pallas kernels for 0%

profile of v7, /device:TPU:174, one launch (start us, length us, event | category | flops | bytes accessed | tf_op | source)
XLA Modules:
  0.0 202.0 jit_solution(10303920819251500776)
XLA Ops:
  0.0 15.8 %collective-permute-start.4 = (bf16[256,168]{0,1:T(8,128)(2,1)}, bf16[256,168]{0,1:T(8,128)(2,1)}, u32[]{:S(2)}, u32[]{:S(2)}) collective-permute-start(bf16[256,168]{0,1:T(8,128)(2,1)} %param.11), channel_id=1, source_target_pairs={{0,8},{8,16},{16,24},{24,0},{1,9},{9,17},{17,25},{25,1},{2,10},{10... | collective-permute-start | bytes 258056 | tf_op jit(solution)/shard_map/ppermute | solution.py:21
  15.9 3.5 %collective-permute-start.5 = (bf16[256,168]{0,1:T(8,128)(2,1)}, bf16[256,168]{0,1:T(8,128)(2,1)}, u32[]{:S(2)}, u32[]{:S(2)}) collective-permute-start(bf16[256,168]{0,1:T(8,128)(2,1)} %param.11), channel_id=1, source_target_pairs={{0,24},{8,0},{16,8},{24,16},{1,25},{9,1},{17,9},{25,17},{2,26},{10... | collective-permute-start | bytes 258056 | tf_op jit(solution)/shard_map/ppermute | solution.py:21
  22.3 2.9 %collective-permute-start = (bf16[256,256]{1,0:T(8,128)(2,1)}, bf16[256,256]{1,0:T(8,128)(2,1)}, u32[]{:S(2)}, u32[]{:S(2)}) collective-permute-start(bf16[256,256]{1,0:T(8,128)(2,1)} %constant_dynamic-update-slice_fusion), channel_id=1, source_target_pairs={{0,128},{32,160},{64,192},{96,224},{128,256},{160,288},{192,320},{... | collective-permute-start | bytes 393224 | tf_op jit(solution)/shard_map/ppermute | solution.py:17
  25.2 3.0 %collective-permute-start.1 = (bf16[256,256]{1,0:T(8,128)(2,1)}, bf16[256,256]{1,0:T(8,128)(2,1)}, u32[]{:S(2)}, u32[]{:S(2)}) collective-permute-start(bf16[256,256]{1,0:T(8,128)(2,1)} %constant_dynamic-update-slice_fusion), channel_id=1, source_target_pairs={{0,96},{32,128},{64,160},{96,192},{128,224},{160,256},{192,288},{2... | collective-permute-start | bytes 393224 | tf_op jit(solution)/shard_map/ppermute | solution.py:17
  28.3 4.5 %collective-permute-start.2 = (bf16[256,256]{1,0:T(8,128)(2,1)}, bf16[256,256]{1,0:T(8,128)(2,1)}, u32[]{:S(2)}, u32[]{:S(2)}) collective-permute-start(bf16[256,256]{1,0:T(8,128)(2,1)} %constant_dynamic-update-slice_fusion), channel_id=1, source_target_pairs={{0,64},{32,96},{64,128},{96,160},{128,192},{160,224},{192,256},{22... | collective-permute-start | bytes 393224 | tf_op jit(solution)/shard_map/ppermute | solution.py:17
  33.0 2.7 %copy.14 = bf16[128,5376]{0,1:T(8,128)(2,1)} copy(bf16[128,5376]{1,0:T(8,128)(2,1)} %param.12) | data formatting | bytes 2752512 | tf_op args[4]
  39.4 12.6 %collective-permute-start.6 = (bf16[256,168]{0,1:T(8,128)(2,1)}, bf16[256,168]{0,1:T(8,128)(2,1)S(1)}, u32[]{:S(2)}, u32[]{:S(2)}) collective-permute-start(bf16[256,168]{0,1:T(8,128)(2,1)} %collective-permute-done.4), channel_id=1, source_target_pairs={{0,8},{8,16},{16,24},{24,0},{1,9},{9,17},{17,25},{25,1},{2,10},{10... | collective-permute-start | bytes 258056 | tf_op jit(solution)/shard_map/ppermute | solution.py:21
  55.1 8.0 %collective-permute-done.6 = bf16[256,168]{0,1:T(8,128)(2,1)S(1)} collective-permute-done((bf16[256,168]{0,1:T(8,128)(2,1)}, bf16[256,168]{0,1:T(8,128)(2,1)S(1)}, u32[]{:S(2)}, u32[]{:S(2)}) %collective-permute-start.6) | collective-permute-done | bytes 86048 | tf_op jit(solution)/shard_map/ppermute | solution.py:21
  66.1 4.3 %collective-permute-start.8 = (bf16[4,256,168]{1,2,0:T(8,128)(2,1)}, bf16[4,256,168]{1,2,0:T(8,128)(2,1)S(1)}, u32[]{:S(2)}, u32[]{:S(2)}) collective-permute-start(bf16[4,256,168]{1,2,0:T(8,128)(2,1)} %bitcast_dynamic-update-slice_fusion.6), channel_id=1, source_target_pairs={{0,4},{2,6},{4,0},{6,2},{1,5},{3,7},{5,1},{7,3},{8,12},{10,14},{12... | collective-permute-start | bytes 1032200 | tf_op jit(solution)/shard_map/ppermute | solution.py:21
  73.1 2.7 %collective-permute-start.9 = (bf16[4,256,168]{1,2,0:T(8,128)(2,1)}, bf16[4,256,168]{1,2,0:T(8,128)(2,1)S(1)}, u32[]{:S(2)}, u32[]{:S(2)}) collective-permute-start(bf16[4,256,168]{1,2,0:T(8,128)(2,1)} %bitcast_dynamic-update-slice_fusion.6), channel_id=1, source_target_pairs={{0,6},{2,0},{4,2},{6,4},{1,7},{3,1},{5,3},{7,5},{8,14},{10,8},{12,... | collective-permute-start | bytes 1032200 | tf_op jit(solution)/shard_map/ppermute | solution.py:21
  77.0 6.1 %collective-permute-start.3 = (bf16[256,256]{1,0:T(8,128)(2,1)}, bf16[256,256]{1,0:T(8,128)(2,1)S(1)}, u32[]{:S(2)}, u32[]{:S(2)}) collective-permute-start(bf16[256,256]{1,0:T(8,128)(2,1)} %constant_dynamic-update-slice_fusion), channel_id=1, source_target_pairs={{0,32},{32,64},{64,96},{96,128},{128,160},{160,192},{192,224},{224... | collective-permute-start | bytes 393224 | tf_op jit(solution)/shard_map/ppermute | solution.py:17
  96.6 3.1 %collective-permute-start.11 = (bf16[256,256]{0,1:T(8,128)(2,1)S(1)}, bf16[256,256]{0,1:T(8,128)(2,1)S(1)}, u32[]{:S(2)}, u32[]{:S(2)}) collective-permute-start(bf16[256,256]{0,1:T(8,128)(2,1)S(1)} %get-tuple-element.16), channel_id=1, source_target_pairs={{32,0},{64,32},{96,64},{128,96},{160,128},{192,160},{224,192},{256... | collective-permute-start | bytes 393224 | tf_op jit(solution)/shard_map/ppermute | solution.py:17
  99.7 6.0 %collective-permute-start.12 = (bf16[256,256]{0,1:T(8,128)(2,1)S(1)}, bf16[256,256]{0,1:T(8,128)(2,1)S(1)}, u32[]{:S(2)}, u32[]{:S(2)}) collective-permute-start(bf16[256,256]{0,1:T(8,128)(2,1)S(1)} %get-tuple-element.18), channel_id=1, source_target_pairs={{64,0},{96,32},{128,64},{160,96},{192,128},{224,160},{256,192},{28... | collective-permute-start | bytes 393224 | tf_op jit(solution)/shard_map/ppermute | solution.py:17
  105.7 7.8 %collective-permute-start.13 = (bf16[256,256]{0,1:T(8,128)(2,1)S(1)}, bf16[256,256]{0,1:T(8,128)(2,1)S(1)}, u32[]{:S(2)}, u32[]{:S(2)}) collective-permute-start(bf16[256,256]{0,1:T(8,128)(2,1)S(1)} %get-tuple-element.17), channel_id=1, source_target_pairs={{96,0},{128,32},{160,64},{192,96},{224,128},{256,160},{288,192},{3... | collective-permute-start | bytes 393224 | tf_op jit(solution)/shard_map/ppermute | solution.py:17
  117.5 2.9 %collective-permute-done.14 = bf16[256,256]{0,1:T(8,128)(2,1)S(1)} collective-permute-done((bf16[256,256]{0,1:T(8,128)(2,1)S(1)}, bf16[256,256]{0,1:T(8,128)(2,1)S(1)}, u32[]{:S(2)}, u32[]{:S(2)}) %collective-permute-start.14) | collective-permute-done | bytes 131104 | tf_op jit(solution)/shard_map/ppermute | solution.py:17
  129.2 3.4 %collective-permute-start.17 = (bf16[4,168,256]{2,1,0:T(8,128)(2,1)S(1)}, bf16[4,168,256]{2,1,0:T(8,128)(2,1)S(1)}, u32[]{:S(2)}, u32[]{:S(2)}) collective-permute-start(bf16[4,168,256]{2,1,0:T(8,128)(2,1)S(1)} %get-tuple-element.7), channel_id=1, source_target_pairs={{0,4},{2,6},{4,0},{6,2},{1,5},{3,7},{5,1},{7,3},{8,12},{10,14},{12... | collective-permute-start | bytes 1032200 | tf_op jit(solution)/shard_map/ppermute | solution.py:21
  134.9 5.0 %collective-permute-done.16 = bf16[4,168,256]{2,1,0:T(8,128)(2,1)S(1)} collective-permute-done((bf16[4,168,256]{2,1,0:T(8,128)(2,1)S(1)}, bf16[4,168,256]{2,1,0:T(8,128)(2,1)S(1)}, u32[]{:S(2)}, u32[]{:S(2)}) %collective-permute-start.16) | collective-permute-done | bytes 344096 | tf_op jit(solution)/shard_map/ppermute | solution.py:21
  140.0 3.7 %collective-permute-done.17 = bf16[4,168,256]{2,1,0:T(8,128)(2,1)S(1)} collective-permute-done((bf16[4,168,256]{2,1,0:T(8,128)(2,1)S(1)}, bf16[4,168,256]{2,1,0:T(8,128)(2,1)S(1)}, u32[]{:S(2)}, u32[]{:S(2)}) %collective-permute-start.17) | collective-permute-done | bytes 344096 | tf_op jit(solution)/shard_map/ppermute | solution.py:21
  143.6 6.3 %collective-permute-done.18 = bf16[4,168,256]{2,1,0:T(8,128)(2,1)S(1)} collective-permute-done((bf16[4,168,256]{2,1,0:T(8,128)(2,1)S(1)}, bf16[4,168,256]{2,1,0:T(8,128)(2,1)S(1)}, u32[]{:S(2)}, u32[]{:S(2)}) %collective-permute-start.18) | collective-permute-done | bytes 344096 | tf_op jit(solution)/shard_map/ppermute | solution.py:21
  150.2 10.0 %collective-permute-start.19 = (bf16[168,256]{1,0:T(8,128)(2,1)S(1)}, bf16[168,256]{1,0:T(8,128)(2,1)S(1)}, u32[]{:S(2)}, u32[]{:S(2)}) collective-permute-start(bf16[168,256]{1,0:T(8,128)(2,1)S(1)} %get-tuple-element.14), channel_id=1, source_target_pairs={{0,8},{8,16},{16,24},{24,0},{1,9},{9,17},{17,25},{25,1},{2,10},{10... | collective-permute-start | bytes 258056 | tf_op jit(solution)/shard_map/ppermute | solution.py:21
  160.2 5.5 %collective-permute-start.21 = (bf16[168,256]{1,0:T(8,128)(2,1)S(1)}, bf16[168,256]{1,0:T(8,128)(2,1)S(1)}, u32[]{:S(2)}, u32[]{:S(2)}) collective-permute-start(bf16[168,256]{1,0:T(8,128)(2,1)S(1)} %get-tuple-element.15), channel_id=1, source_target_pairs={{0,24},{8,0},{16,8},{24,16},{1,25},{9,1},{17,9},{25,17},{2,26},{10... | collective-permute-start | bytes 258056 | tf_op jit(solution)/shard_map/ppermute | solution.py:21
  165.7 13.9 %collective-permute-done.19 = bf16[168,256]{1,0:T(8,128)(2,1)S(1)} collective-permute-done((bf16[168,256]{1,0:T(8,128)(2,1)S(1)}, bf16[168,256]{1,0:T(8,128)(2,1)S(1)}, u32[]{:S(2)}, u32[]{:S(2)}) %collective-permute-start.19) | collective-permute-done | bytes 86048 | tf_op jit(solution)/shard_map/ppermute | solution.py:21
  179.6 5.4 %collective-permute-start.20 = (bf16[168,256]{1,0:T(8,128)(2,1)S(1)}, bf16[168,256]{1,0:T(8,128)(2,1)S(1)}, u32[]{:S(2)}, u32[]{:S(2)}) collective-permute-start(bf16[168,256]{1,0:T(8,128)(2,1)S(1)} %fusion.28), channel_id=1, source_target_pairs={{0,8},{8,16},{16,24},{24,0},{1,9},{9,17},{17,25},{25,1},{2,10},{10... | collective-permute-start | bytes 258056 | tf_op jit(solution)/shard_map/ppermute | solution.py:21
  185.0 16.3 %collective-permute-done.20 = bf16[168,256]{1,0:T(8,128)(2,1)S(1)} collective-permute-done((bf16[168,256]{1,0:T(8,128)(2,1)S(1)}, bf16[168,256]{1,0:T(8,128)(2,1)S(1)}, u32[]{:S(2)}, u32[]{:S(2)}) %collective-permute-start.20) | collective-permute-done | bytes 86048 | tf_op jit(solution)/shard_map/ppermute | solution.py:21
  (92 shorter events, 45.6 us)
Async XLA Ops:
  0.0 88.5 %copy-start = (bf16[256,128]{1,0:T(8,128)(2,1)S(1)}, bf16[256,128]{1,0:T(8,128)(2,1)}, u32[]{:S(2)}) copy-start(bf16[256,128]{1,0:T(8,128)(2,1)} %param.8) | copy-start | bytes 196612
  0.0 39.4 %collective-permute-start.4 = (bf16[256,168]{0,1:T(8,128)(2,1)}, bf16[256,168]{0,1:T(8,128)(2,1)}, u32[]{:S(2)}, u32[]{:S(2)}) collective-permute-start(bf16[256,168]{0,1:T(8,128)(2,1)} %param.11), channel_id=1, source_target_pairs={{0,8},{8,16},{16,24},{24,0},{1,9},{9,17},{17,25},{25,1},{2,10},{10... | collective-permute-start | bytes 258056 | tf_op jit(solution)/shard_map/ppermute | solution.py:21
  15.9 37.7 %collective-permute-start.5 = (bf16[256,168]{0,1:T(8,128)(2,1)}, bf16[256,168]{0,1:T(8,128)(2,1)}, u32[]{:S(2)}, u32[]{:S(2)}) collective-permute-start(bf16[256,168]{0,1:T(8,128)(2,1)} %param.11), channel_id=1, source_target_pairs={{0,24},{8,0},{16,8},{24,16},{1,25},{9,1},{17,9},{25,17},{2,26},{10... | collective-permute-start | bytes 258056 | tf_op jit(solution)/shard_map/ppermute | solution.py:21
  22.3 63.3 %collective-permute-start = (bf16[256,256]{1,0:T(8,128)(2,1)}, bf16[256,256]{1,0:T(8,128)(2,1)}, u32[]{:S(2)}, u32[]{:S(2)}) collective-permute-start(bf16[256,256]{1,0:T(8,128)(2,1)} %constant_dynamic-update-slice_fusion), channel_id=1, source_target_pairs={{0,128},{32,160},{64,192},{96,224},{128,256},{160,288},{192,320},{... | collective-permute-start | bytes 393224 | tf_op jit(solution)/shard_map/ppermute | solution.py:17
  25.2 61.3 %collective-permute-start.1 = (bf16[256,256]{1,0:T(8,128)(2,1)}, bf16[256,256]{1,0:T(8,128)(2,1)}, u32[]{:S(2)}, u32[]{:S(2)}) collective-permute-start(bf16[256,256]{1,0:T(8,128)(2,1)} %constant_dynamic-update-slice_fusion), channel_id=1, source_target_pairs={{0,96},{32,128},{64,160},{96,192},{128,224},{160,256},{192,288},{2... | collective-permute-start | bytes 393224 | tf_op jit(solution)/shard_map/ppermute | solution.py:17
  28.3 59.2 %collective-permute-start.2 = (bf16[256,256]{1,0:T(8,128)(2,1)}, bf16[256,256]{1,0:T(8,128)(2,1)}, u32[]{:S(2)}, u32[]{:S(2)}) collective-permute-start(bf16[256,256]{1,0:T(8,128)(2,1)} %constant_dynamic-update-slice_fusion), channel_id=1, source_target_pairs={{0,64},{32,96},{64,128},{96,160},{128,192},{160,224},{192,256},{22... | collective-permute-start | bytes 393224 | tf_op jit(solution)/shard_map/ppermute | solution.py:17
  39.4 23.7 %collective-permute-start.6 = (bf16[256,168]{0,1:T(8,128)(2,1)}, bf16[256,168]{0,1:T(8,128)(2,1)S(1)}, u32[]{:S(2)}, u32[]{:S(2)}) collective-permute-start(bf16[256,168]{0,1:T(8,128)(2,1)} %collective-permute-done.4), channel_id=1, source_target_pairs={{0,8},{8,16},{16,24},{24,0},{1,9},{9,17},{17,25},{25,1},{2,10},{10... | collective-permute-start | bytes 258056 | tf_op jit(solution)/shard_map/ppermute | solution.py:21
  63.7 9.3 %collective-permute-start.7 = (bf16[4,256,168]{1,2,0:T(8,128)(2,1)}, bf16[4,256,168]{1,2,0:T(8,128)(2,1)S(1)}, u32[]{:S(2)}, u32[]{:S(2)}) collective-permute-start(bf16[4,256,168]{1,2,0:T(8,128)(2,1)} %bitcast_dynamic-update-slice_fusion.6), channel_id=1, source_target_pairs={{0,2},{2,4},{4,6},{6,0},{1,3},{3,5},{5,7},{7,1},{8,10},{10,12},{12... | collective-permute-start | bytes 1032200 | tf_op jit(solution)/shard_map/ppermute | solution.py:21
  66.1 10.9 %collective-permute-start.8 = (bf16[4,256,168]{1,2,0:T(8,128)(2,1)}, bf16[4,256,168]{1,2,0:T(8,128)(2,1)S(1)}, u32[]{:S(2)}, u32[]{:S(2)}) collective-permute-start(bf16[4,256,168]{1,2,0:T(8,128)(2,1)} %bitcast_dynamic-update-slice_fusion.6), channel_id=1, source_target_pairs={{0,4},{2,6},{4,0},{6,2},{1,5},{3,7},{5,1},{7,3},{8,12},{10,14},{12... | collective-permute-start | bytes 1032200 | tf_op jit(solution)/shard_map/ppermute | solution.py:21
  73.1 10.6 %collective-permute-start.9 = (bf16[4,256,168]{1,2,0:T(8,128)(2,1)}, bf16[4,256,168]{1,2,0:T(8,128)(2,1)S(1)}, u32[]{:S(2)}, u32[]{:S(2)}) collective-permute-start(bf16[4,256,168]{1,2,0:T(8,128)(2,1)} %bitcast_dynamic-update-slice_fusion.6), channel_id=1, source_target_pairs={{0,6},{2,0},{4,2},{6,4},{1,7},{3,1},{5,3},{7,5},{8,14},{10,8},{12,... | collective-permute-start | bytes 1032200 | tf_op jit(solution)/shard_map/ppermute | solution.py:21
  77.0 11.4 %collective-permute-start.3 = (bf16[256,256]{1,0:T(8,128)(2,1)}, bf16[256,256]{1,0:T(8,128)(2,1)S(1)}, u32[]{:S(2)}, u32[]{:S(2)}) collective-permute-start(bf16[256,256]{1,0:T(8,128)(2,1)} %constant_dynamic-update-slice_fusion), channel_id=1, source_target_pairs={{0,32},{32,64},{64,96},{96,128},{128,160},{160,192},{192,224},{224... | collective-permute-start | bytes 393224 | tf_op jit(solution)/shard_map/ppermute | solution.py:17
  83.7 6.7 %collective-permute-start.10 = (bf16[4,4,256,168]{2,3,1,0:T(8,128)(2,1)S(1)}, bf16[4,4,256,168]{2,3,1,0:T(8,128)(2,1)S(1)}, u32[]{:S(2)}, u32[]{:S(2)}) collective-permute-start(bf16[4,4,256,168]{2,3,1,0:T(8,128)(2,1)S(1)} %bitcast_dynamic-update-slice_fusion.2), channel_id=1, source_target_pairs={{0,1},{1,0},{2,3},{3,2},{4,5},{5,4},{6,7},{7,6},{8,9},{9,8},{10,11... | collective-permute-start | bytes 4128776 | tf_op jit(solution)/shard_map/ppermute | solution.py:21
  96.5 18.9 %copy-start.1 = (bf16[4,4,1,168,128]{4,3,2,1,0:T(8,128)(2,1)S(1)}, bf16[4,4,1,168,128]{4,3,2,1,0:T(8,128)(2,1)}, u32[]{:S(2)}) copy-start(bf16[4,4,1,168,128]{4,3,2,1,0:T(8,128)(2,1)} %get-tuple-element.12) | copy-start | bytes 2064388
  96.6 20.9 %collective-permute-start.11 = (bf16[256,256]{0,1:T(8,128)(2,1)S(1)}, bf16[256,256]{0,1:T(8,128)(2,1)S(1)}, u32[]{:S(2)}, u32[]{:S(2)}) collective-permute-start(bf16[256,256]{0,1:T(8,128)(2,1)S(1)} %get-tuple-element.16), channel_id=1, source_target_pairs={{32,0},{64,32},{96,64},{128,96},{160,128},{192,160},{224,192},{256... | collective-permute-start | bytes 393224 | tf_op jit(solution)/shard_map/ppermute | solution.py:17
  99.7 17.8 %collective-permute-start.12 = (bf16[256,256]{0,1:T(8,128)(2,1)S(1)}, bf16[256,256]{0,1:T(8,128)(2,1)S(1)}, u32[]{:S(2)}, u32[]{:S(2)}) collective-permute-start(bf16[256,256]{0,1:T(8,128)(2,1)S(1)} %get-tuple-element.18), channel_id=1, source_target_pairs={{64,0},{96,32},{128,64},{160,96},{192,128},{224,160},{256,192},{28... | collective-permute-start | bytes 393224 | tf_op jit(solution)/shard_map/ppermute | solution.py:17
  105.7 11.9 %collective-permute-start.13 = (bf16[256,256]{0,1:T(8,128)(2,1)S(1)}, bf16[256,256]{0,1:T(8,128)(2,1)S(1)}, u32[]{:S(2)}, u32[]{:S(2)}) collective-permute-start(bf16[256,256]{0,1:T(8,128)(2,1)S(1)} %get-tuple-element.17), channel_id=1, source_target_pairs={{96,0},{128,32},{160,64},{192,96},{224,128},{256,160},{288,192},{3... | collective-permute-start | bytes 393224 | tf_op jit(solution)/shard_map/ppermute | solution.py:17
  113.5 6.9 %collective-permute-start.14 = (bf16[256,256]{0,1:T(8,128)(2,1)S(1)}, bf16[256,256]{0,1:T(8,128)(2,1)S(1)}, u32[]{:S(2)}, u32[]{:S(2)}) collective-permute-start(bf16[256,256]{0,1:T(8,128)(2,1)S(1)} %get-tuple-element.19), channel_id=1, source_target_pairs={{128,0},{160,32},{192,64},{224,96},{256,128},{288,160},{320,192},{... | collective-permute-start | bytes 393224 | tf_op jit(solution)/shard_map/ppermute | solution.py:17
  121.7 5.0 %collective-permute-start.15 = (bf16[4,4,168,256]{3,2,0,1:T(8,128)(2,1)S(1)}, bf16[4,4,168,256]{3,2,0,1:T(8,128)(2,1)S(1)}, u32[]{:S(2)}, u32[]{:S(2)}) collective-permute-start(bf16[4,4,168,256]{3,2,0,1:T(8,128)(2,1)S(1)} %copy.18), channel_id=1, source_target_pairs={{0,1},{1,0},{2,3},{3,2},{4,5},{5,4},{6,7},{7,6},{8,9},{9,8},{10,11... | collective-permute-start | bytes 4128776 | tf_op jit(solution)/shard_map/ppermute | solution.py:21
  127.2 12.8 %collective-permute-start.16 = (bf16[4,168,256]{2,1,0:T(8,128)(2,1)S(1)}, bf16[4,168,256]{2,1,0:T(8,128)(2,1)S(1)}, u32[]{:S(2)}, u32[]{:S(2)}) collective-permute-start(bf16[4,168,256]{2,1,0:T(8,128)(2,1)S(1)} %get-tuple-element.5), channel_id=1, source_target_pairs={{0,2},{2,4},{4,6},{6,0},{1,3},{3,5},{5,7},{7,1},{8,10},{10,12},{12... | collective-permute-start | bytes 1032200 | tf_op jit(solution)/shard_map/ppermute | solution.py:21
  129.2 14.4 %collective-permute-start.17 = (bf16[4,168,256]{2,1,0:T(8,128)(2,1)S(1)}, bf16[4,168,256]{2,1,0:T(8,128)(2,1)S(1)}, u32[]{:S(2)}, u32[]{:S(2)}) collective-permute-start(bf16[4,168,256]{2,1,0:T(8,128)(2,1)S(1)} %get-tuple-element.7), channel_id=1, source_target_pairs={{0,4},{2,6},{4,0},{6,2},{1,5},{3,7},{5,1},{7,3},{8,12},{10,14},{12... | collective-permute-start | bytes 1032200 | tf_op jit(solution)/shard_map/ppermute | solution.py:21
  132.7 17.3 %collective-permute-start.18 = (bf16[4,168,256]{2,1,0:T(8,128)(2,1)S(1)}, bf16[4,168,256]{2,1,0:T(8,128)(2,1)S(1)}, u32[]{:S(2)}, u32[]{:S(2)}) collective-permute-start(bf16[4,168,256]{2,1,0:T(8,128)(2,1)S(1)} %get-tuple-element.6), channel_id=1, source_target_pairs={{0,6},{2,0},{4,2},{6,4},{1,7},{3,1},{5,3},{7,5},{8,14},{10,8},{12,... | collective-permute-start | bytes 1032200 | tf_op jit(solution)/shard_map/ppermute | solution.py:21
  150.2 29.4 %collective-permute-start.19 = (bf16[168,256]{1,0:T(8,128)(2,1)S(1)}, bf16[168,256]{1,0:T(8,128)(2,1)S(1)}, u32[]{:S(2)}, u32[]{:S(2)}) collective-permute-start(bf16[168,256]{1,0:T(8,128)(2,1)S(1)} %get-tuple-element.14), channel_id=1, source_target_pairs={{0,8},{8,16},{16,24},{24,0},{1,9},{9,17},{17,25},{25,1},{2,10},{10... | collective-permute-start | bytes 258056 | tf_op jit(solution)/shard_map/ppermute | solution.py:21
  160.2 24.8 %collective-permute-start.21 = (bf16[168,256]{1,0:T(8,128)(2,1)S(1)}, bf16[168,256]{1,0:T(8,128)(2,1)S(1)}, u32[]{:S(2)}, u32[]{:S(2)}) collective-permute-start(bf16[168,256]{1,0:T(8,128)(2,1)S(1)} %get-tuple-element.15), channel_id=1, source_target_pairs={{0,24},{8,0},{16,8},{24,16},{1,25},{9,1},{17,9},{25,17},{2,26},{10... | collective-permute-start | bytes 258056 | tf_op jit(solution)/shard_map/ppermute | solution.py:21
  179.6 21.7 %collective-permute-start.20 = (bf16[168,256]{1,0:T(8,128)(2,1)S(1)}, bf16[168,256]{1,0:T(8,128)(2,1)S(1)}, u32[]{:S(2)}, u32[]{:S(2)}) collective-permute-start(bf16[168,256]{1,0:T(8,128)(2,1)S(1)} %fusion.28), channel_id=1, source_target_pairs={{0,8},{8,16},{16,24},{24,0},{1,9},{9,17},{17,25},{25,1},{2,10},{10... | collective-permute-start | bytes 258056 | tf_op jit(solution)/shard_map/ppermute | solution.py:21
  (7 other events, 37.6 us)

commit v8 on v5

--- a/solution.py
+++ b/solution.py
@@ -54,6 +54,7 @@
     got = shift(piece(me + 2).astype(jnp.bfloat16), axis, 4, 1).astype(jnp.float32)
     up = (piece(me + 1) + got).astype(jnp.bfloat16)
     down = piece(me + 3).astype(jnp.bfloat16)
+    up, down = lax.optimization_barrier((up, down))
     acc = piece(me)
     acc = acc + shift(up, axis, 4, 1).astype(jnp.float32)
     return acc + shift(down, axis, 4, -1).astype(jnp.float32)

time: 201 us -> 209 us (1.040)
  the two profiles are of different devices: /device:TPU:166 before, /device:TPU:78 now
where the time goes in v8:
time: 209 us; the launch traced here: 208 us
  starting transfers between devices  102 us (49%)
  waiting for transfers between devices  79.1 us (38%)
  local copies, waits for them, and re-layouts  13.3 us (6%)
  matrix products  8.29 us (4%)
  other arithmetic  4.62 us (2%)
    ppermute x14, starting transfers between devices, shift(): lax.ppermute(block, axis, [(i, (i + step) % size) for i in range(size)])  81.6 us
    ppermute x14, waiting for transfers between devices, shift(): lax.ppermute(block, axis, [(i, (i + step) % size) for i in range(size)])  69.4 us
    ppermute x8, starting transfers between devices, from_behind(): return lax.ppermute(block, axis, route)  20.4 us
    ppermute x8, waiting for transfers between devices, from_behind(): return lax.ppermute(block, axis, route)  9.72 us
    unnamed x31, local copies, waits for them, and re-layouts  8.64 us
    dot_general x8, matrix products, dot_rows(): lax.dot_general(left, right, (((1,), (1,)), ((), ())), preferred_element_...  5.28 us
  transfers between devices with their start and end apart: 22, of which 12 were waited for; matrix products, arithmetic and copies ran while one was open for 7% of the time, Pallas kernels for 0%

profile of v8, /device:TPU:78, one launch (start us, length us, event | category | flops | bytes accessed | tf_op | source)
XLA Modules:
  0.0 208.2 jit_solution(1862528627975871303)
XLA Ops:
  0.0 15.8 %collective-permute-start.4 = (bf16[256,168]{0,1:T(8,128)(2,1)}, bf16[256,168]{0,1:T(8,128)(2,1)}, u32[]{:S(2)}, u32[]{:S(2)}) collective-permute-start(bf16[256,168]{0,1:T(8,128)(2,1)} %param.11), channel_id=1, source_target_pairs={{0,8},{8,16},{16,24},{24,0},{1,9},{9,17},{17,25},{25,1},{2,10},{10... | collective-permute-start | bytes 258056 | tf_op jit(solution)/shard_map/ppermute | solution.py:21
  15.9 7.4 %collective-permute-start.5 = (bf16[256,168]{0,1:T(8,128)(2,1)}, bf16[256,168]{0,1:T(8,128)(2,1)}, u32[]{:S(2)}, u32[]{:S(2)}) collective-permute-start(bf16[256,168]{0,1:T(8,128)(2,1)} %param.11), channel_id=1, source_target_pairs={{0,24},{8,0},{16,8},{24,16},{1,25},{9,1},{17,9},{25,17},{2,26},{10... | collective-permute-start | bytes 258056 | tf_op jit(solution)/shard_map/ppermute | solution.py:21
  26.2 2.9 %collective-permute-start = (bf16[256,256]{1,0:T(8,128)(2,1)}, bf16[256,256]{1,0:T(8,128)(2,1)}, u32[]{:S(2)}, u32[]{:S(2)}) collective-permute-start(bf16[256,256]{1,0:T(8,128)(2,1)} %constant_dynamic-update-slice_fusion), channel_id=1, source_target_pairs={{0,128},{32,160},{64,192},{96,224},{128,256},{160,288},{192,320},{... | collective-permute-start | bytes 393224 | tf_op jit(solution)/shard_map/ppermute | solution.py:17
  29.1 2.8 %collective-permute-start.1 = (bf16[256,256]{1,0:T(8,128)(2,1)}, bf16[256,256]{1,0:T(8,128)(2,1)}, u32[]{:S(2)}, u32[]{:S(2)}) collective-permute-start(bf16[256,256]{1,0:T(8,128)(2,1)} %constant_dynamic-update-slice_fusion), channel_id=1, source_target_pairs={{0,96},{32,128},{64,160},{96,192},{128,224},{160,256},{192,288},{2... | collective-permute-start | bytes 393224 | tf_op jit(solution)/shard_map/ppermute | solution.py:17
  32.0 4.5 %collective-permute-start.2 = (bf16[256,256]{1,0:T(8,128)(2,1)}, bf16[256,256]{1,0:T(8,128)(2,1)}, u32[]{:S(2)}, u32[]{:S(2)}) collective-permute-start(bf16[256,256]{1,0:T(8,128)(2,1)} %constant_dynamic-update-slice_fusion), channel_id=1, source_target_pairs={{0,64},{32,96},{64,128},{96,160},{128,192},{160,224},{192,256},{22... | collective-permute-start | bytes 393224 | tf_op jit(solution)/shard_map/ppermute | solution.py:17
  41.4 10.2 %collective-permute-start.6 = (bf16[256,168]{0,1:T(8,128)(2,1)}, bf16[256,168]{0,1:T(8,128)(2,1)S(1)}, u32[]{:S(2)}, u32[]{:S(2)}) collective-permute-start(bf16[256,168]{0,1:T(8,128)(2,1)} %collective-permute-done.4), channel_id=1, source_target_pairs={{0,8},{8,16},{16,24},{24,0},{1,9},{9,17},{17,25},{25,1},{2,10},{10... | collective-permute-start | bytes 258056 | tf_op jit(solution)/shard_map/ppermute | solution.py:21
  53.4 11.0 %collective-permute-done.6 = bf16[256,168]{0,1:T(8,128)(2,1)S(1)} collective-permute-done((bf16[256,168]{0,1:T(8,128)(2,1)}, bf16[256,168]{0,1:T(8,128)(2,1)S(1)}, u32[]{:S(2)}, u32[]{:S(2)}) %collective-permute-start.6) | collective-permute-done | bytes 86048 | tf_op jit(solution)/shard_map/ppermute | solution.py:21
  66.8 4.3 %collective-permute-start.8 = (bf16[4,256,168]{1,2,0:T(8,128)(2,1)S(1)}, bf16[4,256,168]{1,2,0:T(8,128)(2,1)S(1)}, u32[]{:S(2)}, u32[]{:S(2)}) collective-permute-start(bf16[4,256,168]{1,2,0:T(8,128)(2,1)S(1)} %bitcast_dynamic-update-slice_fusion.6), channel_id=1, source_target_pairs={{0,4},{2,6},{4,0},{6,2},{1,5},{3,7},{5,1},{7,3},{8,12},{10,14},{12... | collective-permute-start | bytes 1032200 | tf_op jit(solution)/shard_map/ppermute | solution.py:21
  71.3 6.0 %collective-permute-done.7 = bf16[4,256,168]{1,2,0:T(8,128)(2,1)S(1)} collective-permute-done((bf16[4,256,168]{1,2,0:T(8,128)(2,1)S(1)}, bf16[4,256,168]{1,2,0:T(8,128)(2,1)S(1)}, u32[]{:S(2)}, u32[]{:S(2)}) %collective-permute-start.7) | collective-permute-done | bytes 344096 | tf_op jit(solution)/shard_map/ppermute | solution.py:21
  77.3 2.7 %collective-permute-start.9 = (bf16[4,256,168]{1,2,0:T(8,128)(2,1)S(1)}, bf16[4,256,168]{1,2,0:T(8,128)(2,1)S(1)}, u32[]{:S(2)}, u32[]{:S(2)}) collective-permute-start(bf16[4,256,168]{1,2,0:T(8,128)(2,1)S(1)} %bitcast_dynamic-update-slice_fusion.6), channel_id=1, source_target_pairs={{0,6},{2,0},{4,2},{6,4},{1,7},{3,1},{5,3},{7,5},{8,14},{10,8},{12,... | collective-permute-start | bytes 1032200 | tf_op jit(solution)/shard_map/ppermute | solution.py:21
  80.1 2.5 %collective-permute-start.3 = (bf16[256,256]{1,0:T(8,128)(2,1)}, bf16[256,256]{1,0:T(8,128)(2,1)S(1)}, u32[]{:S(2)}, u32[]{:S(2)}) collective-permute-start(bf16[256,256]{1,0:T(8,128)(2,1)} %constant_dynamic-update-slice_fusion), channel_id=1, source_target_pairs={{0,32},{32,64},{64,96},{96,128},{128,160},{160,192},{192,224},{224... | collective-permute-start | bytes 393224 | tf_op jit(solution)/shard_map/ppermute | solution.py:17
  82.7 5.0 %collective-permute-done.9 = bf16[4,256,168]{1,2,0:T(8,128)(2,1)S(1)} collective-permute-done((bf16[4,256,168]{1,2,0:T(8,128)(2,1)S(1)}, bf16[4,256,168]{1,2,0:T(8,128)(2,1)S(1)}, u32[]{:S(2)}, u32[]{:S(2)}) %collective-permute-start.9) | collective-permute-done | bytes 344096 | tf_op jit(solution)/shard_map/ppermute | solution.py:21
  107.7 3.0 %collective-permute-done.12 = bf16[256,256]{0,1:T(8,128)(2,1)S(1)} collective-permute-done((bf16[256,256]{0,1:T(8,128)(2,1)S(1)}, bf16[256,256]{0,1:T(8,128)(2,1)S(1)}, u32[]{:S(2)}, u32[]{:S(2)}) %collective-permute-start.12) | collective-permute-done | bytes 131104 | tf_op jit(solution)/shard_map/ppermute | solution.py:17
  110.7 4.7 %collective-permute-done.13 = bf16[256,256]{0,1:T(8,128)(2,1)S(1)} collective-permute-done((bf16[256,256]{0,1:T(8,128)(2,1)S(1)}, bf16[256,256]{0,1:T(8,128)(2,1)S(1)}, u32[]{:S(2)}, u32[]{:S(2)}) %collective-permute-start.13) | collective-permute-done | bytes 131104 | tf_op jit(solution)/shard_map/ppermute | solution.py:17
  125.7 5.6 %collective-permute-start.16 = (bf16[4,168,256]{2,1,0:T(8,128)(2,1)S(1)}, bf16[4,168,256]{2,1,0:T(8,128)(2,1)S(1)}, u32[]{:S(2)}, u32[]{:S(2)}) collective-permute-start(bf16[4,168,256]{2,1,0:T(8,128)(2,1)S(1)} %get-tuple-element.9), channel_id=1, source_target_pairs={{0,2},{2,4},{4,6},{6,0},{1,3},{3,5},{5,7},{7,1},{8,10},{10,12},{12... | collective-permute-start | bytes 1032200 | tf_op jit(solution)/shard_map/ppermute | solution.py:21
  133.4 2.6 %collective-permute-start.18 = (bf16[4,168,256]{2,1,0:T(8,128)(2,1)S(1)}, bf16[4,168,256]{2,1,0:T(8,128)(2,1)S(1)}, u32[]{:S(2)}, u32[]{:S(2)}) collective-permute-start(bf16[4,168,256]{2,1,0:T(8,128)(2,1)S(1)} %get-tuple-element.10), channel_id=1, source_target_pairs={{0,6},{2,0},{4,2},{6,4},{1,7},{3,1},{5,3},{7,5},{8,14},{10,8},{12,... | collective-permute-start | bytes 1032200 | tf_op jit(solution)/shard_map/ppermute | solution.py:21
  135.9 10.3 %collective-permute-done.16 = bf16[4,168,256]{2,1,0:T(8,128)(2,1)S(1)} collective-permute-done((bf16[4,168,256]{2,1,0:T(8,128)(2,1)S(1)}, bf16[4,168,256]{2,1,0:T(8,128)(2,1)S(1)}, u32[]{:S(2)}, u32[]{:S(2)}) %collective-permute-start.16) | collective-permute-done | bytes 344096 | tf_op jit(solution)/shard_map/ppermute | solution.py:21
  146.2 5.6 %collective-permute-done.18 = bf16[4,168,256]{2,1,0:T(8,128)(2,1)S(1)} collective-permute-done((bf16[4,168,256]{2,1,0:T(8,128)(2,1)S(1)}, bf16[4,168,256]{2,1,0:T(8,128)(2,1)S(1)}, u32[]{:S(2)}, u32[]{:S(2)}) %collective-permute-start.18) | collective-permute-done | bytes 344096 | tf_op jit(solution)/shard_map/ppermute | solution.py:21
  152.0 10.1 %collective-permute-start.19 = (bf16[168,256]{1,0:T(8,128)(2,1)S(1)}, bf16[168,256]{1,0:T(8,128)(2,1)S(1)}, u32[]{:S(2)}, u32[]{:S(2)}) collective-permute-start(bf16[168,256]{1,0:T(8,128)(2,1)S(1)} %get-tuple-element.19), channel_id=1, source_target_pairs={{0,8},{8,16},{16,24},{24,0},{1,9},{9,17},{17,25},{25,1},{2,10},{10... | collective-permute-start | bytes 258056 | tf_op jit(solution)/shard_map/ppermute | solution.py:21
  162.1 13.2 %collective-permute-done.19 = bf16[168,256]{1,0:T(8,128)(2,1)S(1)} collective-permute-done((bf16[168,256]{1,0:T(8,128)(2,1)S(1)}, bf16[168,256]{1,0:T(8,128)(2,1)S(1)}, u32[]{:S(2)}, u32[]{:S(2)}) %collective-permute-start.19) | collective-permute-done | bytes 86048 | tf_op jit(solution)/shard_map/ppermute | solution.py:21
  175.4 4.5 %collective-permute-start.20 = (bf16[168,256]{1,0:T(8,128)(2,1)S(1)}, bf16[168,256]{1,0:T(8,128)(2,1)S(1)}, u32[]{:S(2)}, u32[]{:S(2)}) collective-permute-start(bf16[168,256]{1,0:T(8,128)(2,1)S(1)} %fusion.28), channel_id=1, source_target_pairs={{0,8},{8,16},{16,24},{24,0},{1,9},{9,17},{17,25},{25,1},{2,10},{10... | collective-permute-start | bytes 258056 | tf_op jit(solution)/shard_map/ppermute | solution.py:21
  179.9 10.0 %collective-permute-start.21 = (bf16[168,256]{1,0:T(8,128)(2,1)S(1)}, bf16[168,256]{1,0:T(8,128)(2,1)S(1)}, u32[]{:S(2)}, u32[]{:S(2)}) collective-permute-start(bf16[168,256]{1,0:T(8,128)(2,1)S(1)} %get-tuple-element.8), channel_id=1, source_target_pairs={{0,24},{8,0},{16,8},{24,16},{1,25},{9,1},{17,9},{25,17},{2,26},{10... | collective-permute-start | bytes 258056 | tf_op jit(solution)/shard_map/ppermute | solution.py:21
  189.9 6.0 %collective-permute-done.20 = bf16[168,256]{1,0:T(8,128)(2,1)S(1)} collective-permute-done((bf16[168,256]{1,0:T(8,128)(2,1)S(1)}, bf16[168,256]{1,0:T(8,128)(2,1)S(1)}, u32[]{:S(2)}, u32[]{:S(2)}) %collective-permute-start.20) | collective-permute-done | bytes 86048 | tf_op jit(solution)/shard_map/ppermute | solution.py:21
  196.0 11.5 %collective-permute-done.21 = bf16[168,256]{1,0:T(8,128)(2,1)S(1)} collective-permute-done((bf16[168,256]{1,0:T(8,128)(2,1)S(1)}, bf16[168,256]{1,0:T(8,128)(2,1)S(1)}, u32[]{:S(2)}, u32[]{:S(2)}) %collective-permute-start.21) | collective-permute-done | bytes 86048 | tf_op jit(solution)/shard_map/ppermute | solution.py:21
  (94 shorter events, 45.1 us)
Async XLA Ops:
  0.0 92.5 %copy-start = (bf16[256,128]{1,0:T(8,128)(2,1)S(1)}, bf16[256,128]{1,0:T(8,128)(2,1)}, u32[]{:S(2)}) copy-start(bf16[256,128]{1,0:T(8,128)(2,1)} %param.8) | copy-start | bytes 196612
  0.0 41.4 %collective-permute-start.4 = (bf16[256,168]{0,1:T(8,128)(2,1)}, bf16[256,168]{0,1:T(8,128)(2,1)}, u32[]{:S(2)}, u32[]{:S(2)}) collective-permute-start(bf16[256,168]{0,1:T(8,128)(2,1)} %param.11), channel_id=1, source_target_pairs={{0,8},{8,16},{16,24},{24,0},{1,9},{9,17},{17,25},{25,1},{2,10},{10... | collective-permute-start | bytes 258056 | tf_op jit(solution)/shard_map/ppermute | solution.py:21
  15.9 36.7 %collective-permute-start.5 = (bf16[256,168]{0,1:T(8,128)(2,1)}, bf16[256,168]{0,1:T(8,128)(2,1)}, u32[]{:S(2)}, u32[]{:S(2)}) collective-permute-start(bf16[256,168]{0,1:T(8,128)(2,1)} %param.11), channel_id=1, source_target_pairs={{0,24},{8,0},{16,8},{24,16},{1,25},{9,1},{17,9},{25,17},{2,26},{10... | collective-permute-start | bytes 258056 | tf_op jit(solution)/shard_map/ppermute | solution.py:21
  26.2 63.4 %collective-permute-start = (bf16[256,256]{1,0:T(8,128)(2,1)}, bf16[256,256]{1,0:T(8,128)(2,1)}, u32[]{:S(2)}, u32[]{:S(2)}) collective-permute-start(bf16[256,256]{1,0:T(8,128)(2,1)} %constant_dynamic-update-slice_fusion), channel_id=1, source_target_pairs={{0,128},{32,160},{64,192},{96,224},{128,256},{160,288},{192,320},{... | collective-permute-start | bytes 393224 | tf_op jit(solution)/shard_map/ppermute | solution.py:17
  29.1 61.4 %collective-permute-start.1 = (bf16[256,256]{1,0:T(8,128)(2,1)}, bf16[256,256]{1,0:T(8,128)(2,1)}, u32[]{:S(2)}, u32[]{:S(2)}) collective-permute-start(bf16[256,256]{1,0:T(8,128)(2,1)} %constant_dynamic-update-slice_fusion), channel_id=1, source_target_pairs={{0,96},{32,128},{64,160},{96,192},{128,224},{160,256},{192,288},{2... | collective-permute-start | bytes 393224 | tf_op jit(solution)/shard_map/ppermute | solution.py:17
  32.0 59.5 %collective-permute-start.2 = (bf16[256,256]{1,0:T(8,128)(2,1)}, bf16[256,256]{1,0:T(8,128)(2,1)}, u32[]{:S(2)}, u32[]{:S(2)}) collective-permute-start(bf16[256,256]{1,0:T(8,128)(2,1)} %constant_dynamic-update-slice_fusion), channel_id=1, source_target_pairs={{0,64},{32,96},{64,128},{96,160},{128,192},{160,224},{192,256},{22... | collective-permute-start | bytes 393224 | tf_op jit(solution)/shard_map/ppermute | solution.py:17
  41.4 23.0 %collective-permute-start.6 = (bf16[256,168]{0,1:T(8,128)(2,1)}, bf16[256,168]{0,1:T(8,128)(2,1)S(1)}, u32[]{:S(2)}, u32[]{:S(2)}) collective-permute-start(bf16[256,168]{0,1:T(8,128)(2,1)} %collective-permute-done.4), channel_id=1, source_target_pairs={{0,8},{8,16},{16,24},{24,0},{1,9},{9,17},{17,25},{25,1},{2,10},{10... | collective-permute-start | bytes 258056 | tf_op jit(solution)/shard_map/ppermute | solution.py:21
  64.4 12.9 %collective-permute-start.7 = (bf16[4,256,168]{1,2,0:T(8,128)(2,1)S(1)}, bf16[4,256,168]{1,2,0:T(8,128)(2,1)S(1)}, u32[]{:S(2)}, u32[]{:S(2)}) collective-permute-start(bf16[4,256,168]{1,2,0:T(8,128)(2,1)S(1)} %bitcast_dynamic-update-slice_fusion.6), channel_id=1, source_target_pairs={{0,2},{2,4},{4,6},{6,0},{1,3},{3,5},{5,7},{7,1},{8,10},{10,12},{12... | collective-permute-start | bytes 1032200 | tf_op jit(solution)/shard_map/ppermute | solution.py:21
  66.8 13.3 %collective-permute-start.8 = (bf16[4,256,168]{1,2,0:T(8,128)(2,1)S(1)}, bf16[4,256,168]{1,2,0:T(8,128)(2,1)S(1)}, u32[]{:S(2)}, u32[]{:S(2)}) collective-permute-start(bf16[4,256,168]{1,2,0:T(8,128)(2,1)S(1)} %bitcast_dynamic-update-slice_fusion.6), channel_id=1, source_target_pairs={{0,4},{2,6},{4,0},{6,2},{1,5},{3,7},{5,1},{7,3},{8,12},{10,14},{12... | collective-permute-start | bytes 1032200 | tf_op jit(solution)/shard_map/ppermute | solution.py:21
  77.3 10.3 %collective-permute-start.9 = (bf16[4,256,168]{1,2,0:T(8,128)(2,1)S(1)}, bf16[4,256,168]{1,2,0:T(8,128)(2,1)S(1)}, u32[]{:S(2)}, u32[]{:S(2)}) collective-permute-start(bf16[4,256,168]{1,2,0:T(8,128)(2,1)S(1)} %bitcast_dynamic-update-slice_fusion.6), channel_id=1, source_target_pairs={{0,6},{2,0},{4,2},{6,4},{1,7},{3,1},{5,3},{7,5},{8,14},{10,8},{12,... | collective-permute-start | bytes 1032200 | tf_op jit(solution)/shard_map/ppermute | solution.py:21
  80.1 12.4 %copy-start.10 = (bf16[256,128]{1,0:T(8,128)(2,1)S(1)}, bf16[256,128]{1,0:T(8,128)(2,1)}, u32[]{:S(2)}) copy-start(bf16[256,128]{1,0:T(8,128)(2,1)} %param.10) | copy-start | bytes 196612
  80.1 12.3 %collective-permute-start.3 = (bf16[256,256]{1,0:T(8,128)(2,1)}, bf16[256,256]{1,0:T(8,128)(2,1)S(1)}, u32[]{:S(2)}, u32[]{:S(2)}) collective-permute-start(bf16[256,256]{1,0:T(8,128)(2,1)} %constant_dynamic-update-slice_fusion), channel_id=1, source_target_pairs={{0,32},{32,64},{64,96},{96,128},{128,160},{160,192},{192,224},{224... | collective-permute-start | bytes 393224 | tf_op jit(solution)/shard_map/ppermute | solution.py:17
  87.7 6.7 %collective-permute-start.10 = (bf16[4,4,256,168]{2,3,1,0:T(8,128)(2,1)S(1)}, bf16[4,4,256,168]{2,3,1,0:T(8,128)(2,1)S(1)}, u32[]{:S(2)}, u32[]{:S(2)}) collective-permute-start(bf16[4,4,256,168]{2,3,1,0:T(8,128)(2,1)S(1)} %bitcast_dynamic-update-slice_fusion.2), channel_id=1, source_target_pairs={{0,1},{1,0},{2,3},{3,2},{4,5},{5,4},{6,7},{7,6},{8,9},{9,8},{10,11... | collective-permute-start | bytes 4128776 | tf_op jit(solution)/shard_map/ppermute | solution.py:21
  99.4 8.2 %collective-permute-start.11 = (bf16[256,256]{0,1:T(8,128)(2,1)S(1)}, bf16[256,256]{0,1:T(8,128)(2,1)S(1)}, u32[]{:S(2)}, u32[]{:S(2)}) collective-permute-start(bf16[256,256]{0,1:T(8,128)(2,1)S(1)} %get-tuple-element.20), channel_id=1, source_target_pairs={{32,0},{64,32},{96,64},{128,96},{160,128},{192,160},{224,192},{256... | collective-permute-start | bytes 393224 | tf_op jit(solution)/shard_map/ppermute | solution.py:17
  101.4 9.3 %collective-permute-start.12 = (bf16[256,256]{0,1:T(8,128)(2,1)S(1)}, bf16[256,256]{0,1:T(8,128)(2,1)S(1)}, u32[]{:S(2)}, u32[]{:S(2)}) collective-permute-start(bf16[256,256]{0,1:T(8,128)(2,1)S(1)} %get-tuple-element.21), channel_id=1, source_target_pairs={{64,0},{96,32},{128,64},{160,96},{192,128},{224,160},{256,192},{28... | collective-permute-start | bytes 393224 | tf_op jit(solution)/shard_map/ppermute | solution.py:17
  103.3 12.1 %collective-permute-start.13 = (bf16[256,256]{0,1:T(8,128)(2,1)S(1)}, bf16[256,256]{0,1:T(8,128)(2,1)S(1)}, u32[]{:S(2)}, u32[]{:S(2)}) collective-permute-start(bf16[256,256]{0,1:T(8,128)(2,1)S(1)} %get-tuple-element.23), channel_id=1, source_target_pairs={{96,0},{128,32},{160,64},{192,96},{224,128},{256,160},{288,192},{3... | collective-permute-start | bytes 393224 | tf_op jit(solution)/shard_map/ppermute | solution.py:17
  105.2 12.2 %collective-permute-start.14 = (bf16[256,256]{0,1:T(8,128)(2,1)S(1)}, bf16[256,256]{0,1:T(8,128)(2,1)S(1)}, u32[]{:S(2)}, u32[]{:S(2)}) collective-permute-start(bf16[256,256]{0,1:T(8,128)(2,1)S(1)} %get-tuple-element.22), channel_id=1, source_target_pairs={{128,0},{160,32},{192,64},{224,96},{256,128},{288,160},{320,192},{... | collective-permute-start | bytes 393224 | tf_op jit(solution)/shard_map/ppermute | solution.py:17
  118.8 5.2 %collective-permute-start.15 = (bf16[4,4,168,256]{3,2,0,1:T(8,128)(2,1)S(1)}, bf16[4,4,168,256]{3,2,0,1:T(8,128)(2,1)}, u32[]{:S(2)}, u32[]{:S(2)}) collective-permute-start(bf16[4,4,168,256]{3,2,0,1:T(8,128)(2,1)S(1)} %copy.18), channel_id=1, source_target_pairs={{0,1},{1,0},{2,3},{3,2},{4,5},{5,4},{6,7},{7,6},{8,9},{9,8},{10,11... | collective-permute-start | bytes 4128776 | tf_op jit(solution)/shard_map/ppermute | solution.py:21
  125.7 20.5 %collective-permute-start.16 = (bf16[4,168,256]{2,1,0:T(8,128)(2,1)S(1)}, bf16[4,168,256]{2,1,0:T(8,128)(2,1)S(1)}, u32[]{:S(2)}, u32[]{:S(2)}) collective-permute-start(bf16[4,168,256]{2,1,0:T(8,128)(2,1)S(1)} %get-tuple-element.9), channel_id=1, source_target_pairs={{0,2},{2,4},{4,6},{6,0},{1,3},{3,5},{5,7},{7,1},{8,10},{10,12},{12... | collective-permute-start | bytes 1032200 | tf_op jit(solution)/shard_map/ppermute | solution.py:21
  131.2 15.0 %collective-permute-start.17 = (bf16[4,168,256]{2,1,0:T(8,128)(2,1)S(1)}, bf16[4,168,256]{2,1,0:T(8,128)(2,1)S(1)}, u32[]{:S(2)}, u32[]{:S(2)}) collective-permute-start(bf16[4,168,256]{2,1,0:T(8,128)(2,1)S(1)} %get-tuple-element.11), channel_id=1, source_target_pairs={{0,4},{2,6},{4,0},{6,2},{1,5},{3,7},{5,1},{7,3},{8,12},{10,14},{12... | collective-permute-start | bytes 1032200 | tf_op jit(solution)/shard_map/ppermute | solution.py:21
  133.4 18.5 %collective-permute-start.18 = (bf16[4,168,256]{2,1,0:T(8,128)(2,1)S(1)}, bf16[4,168,256]{2,1,0:T(8,128)(2,1)S(1)}, u32[]{:S(2)}, u32[]{:S(2)}) collective-permute-start(bf16[4,168,256]{2,1,0:T(8,128)(2,1)S(1)} %get-tuple-element.10), channel_id=1, source_target_pairs={{0,6},{2,0},{4,2},{6,4},{1,7},{3,1},{5,3},{7,5},{8,14},{10,8},{12,... | collective-permute-start | bytes 1032200 | tf_op jit(solution)/shard_map/ppermute | solution.py:21
  152.0 23.3 %collective-permute-start.19 = (bf16[168,256]{1,0:T(8,128)(2,1)S(1)}, bf16[168,256]{1,0:T(8,128)(2,1)S(1)}, u32[]{:S(2)}, u32[]{:S(2)}) collective-permute-start(bf16[168,256]{1,0:T(8,128)(2,1)S(1)} %get-tuple-element.19), channel_id=1, source_target_pairs={{0,8},{8,16},{16,24},{24,0},{1,9},{9,17},{17,25},{25,1},{2,10},{10... | collective-permute-start | bytes 258056 | tf_op jit(solution)/shard_map/ppermute | solution.py:21
  175.4 20.6 %collective-permute-start.20 = (bf16[168,256]{1,0:T(8,128)(2,1)S(1)}, bf16[168,256]{1,0:T(8,128)(2,1)S(1)}, u32[]{:S(2)}, u32[]{:S(2)}) collective-permute-start(bf16[168,256]{1,0:T(8,128)(2,1)S(1)} %fusion.28), channel_id=1, source_target_pairs={{0,8},{8,16},{16,24},{24,0},{1,9},{9,17},{17,25},{25,1},{2,10},{10... | collective-permute-start | bytes 258056 | tf_op jit(solution)/shard_map/ppermute | solution.py:21
  179.9 27.7 %collective-permute-start.21 = (bf16[168,256]{1,0:T(8,128)(2,1)S(1)}, bf16[168,256]{1,0:T(8,128)(2,1)S(1)}, u32[]{:S(2)}, u32[]{:S(2)}) collective-permute-start(bf16[168,256]{1,0:T(8,128)(2,1)S(1)} %get-tuple-element.8), channel_id=1, source_target_pairs={{0,24},{8,0},{16,8},{24,16},{1,25},{9,1},{17,9},{25,17},{2,26},{10... | collective-permute-start | bytes 258056 | tf_op jit(solution)/shard_map/ppermute | solution.py:21
  (10 other events, 41.7 us)

commit v9 on v5

--- a/solution.py
+++ b/solution.py
@@ -129,15 +129,17 @@
             query, key_band, value_band, grad_heads, query_start, query_start - reach * length
         )
         kv_parts = jnp.concatenate([key_parts, value_parts], axis=1)
-        kv_total = kv_parts[reach * length :].astype(jnp.float32)
+        core_index = lax.axis_index("core")
+        given = lax.dynamic_slice_in_dim(kv_parts, (1 - core_index) * dim, dim, 1)
+        pair = lax.dynamic_slice_in_dim(kv_parts, core_index * dim, dim, 1).astype(jnp.float32)
+        pair = (pair + shift(given, "core", n_core, 1).astype(jnp.float32)).astype(jnp.bfloat16)
+        total = pair[reach * length :].astype(jnp.float32)
         for distance in range(1, reach + 1):
             first = (reach - distance) * length
-            back = from_behind(kv_parts[first : first + length], "seq", -distance)
-            kv_total = kv_total + back.astype(jnp.float32)
-        kv_total = kv_total.astype(jnp.bfloat16)
-        grad_keys = kv_total[:, :dim]
-        grad_values = kv_total[:, dim:]
-        core_index = lax.axis_index("core")
+            back = from_behind(pair[first : first + length], "seq", -distance)
+            total = total + back.astype(jnp.float32)
+        grad_pair = total.astype(jnp.bfloat16)
+        w_pair = lax.select(core_index == 0, w_key, w_value)
 
         def project(index):
             def rows(w):
@@ -145,8 +147,7 @@
                 return lax.dynamic_index_in_dim(w, index, 2, keepdims=False).reshape(-1, dim)
 
             summed = dot_rows(rows(w_query), grad_query)
-            summed = summed + dot_rows(rows(w_key), grad_keys)
-            summed = summed + dot_rows(rows(w_value), grad_values)
+            summed = summed + dot_rows(rows(w_pair), grad_pair)
             return summed.astype(jnp.bfloat16).reshape(n_zhi, n_x, width, length)
 
         keep = project(core_index)

time: 201 us -> 204 us (1.015)
  the two profiles are of different devices: /device:TPU:166 before, /device:TPU:183 now
where the time goes in v9:
time: 204 us; the launch traced here: 203 us
  starting transfers between devices  117 us (57%)
  waiting for transfers between devices  59.8 us (29%)
  local copies, waits for them, and re-layouts  10.3 us (5%)
  matrix products  7.56 us (4%)
  other arithmetic  7.45 us (4%)
    ppermute x15, starting transfers between devices, shift(): lax.ppermute(block, axis, [(i, (i + step) % size) for i in range(size)])  90.9 us
    ppermute x15, waiting for transfers between devices, shift(): lax.ppermute(block, axis, [(i, (i + step) % size) for i in range(size)])  59.1 us
    ppermute x8, starting transfers between devices, from_behind(): return lax.ppermute(block, axis, route)  26.4 us
    unnamed x27, local copies, waits for them, and re-layouts  4.84 us
  transfers between devices with their start and end apart: 23, of which 13 were waited for; matrix products, arithmetic and copies ran while one was open for 7% of the time, Pallas kernels for 0%

profile of v9, /device:TPU:183, one launch (start us, length us, event | category | flops | bytes accessed | tf_op | source)
XLA Modules:
  0.0 203.2 jit_solution(8642132868504947865)
XLA Ops:
  0.0 15.6 %collective-permute-start.4 = (bf16[256,168]{0,1:T(8,128)(2,1)}, bf16[256,168]{0,1:T(8,128)(2,1)}, u32[]{:S(2)}, u32[]{:S(2)}) collective-permute-start(bf16[256,168]{0,1:T(8,128)(2,1)} %param.11), channel_id=1, source_target_pairs={{0,8},{8,16},{16,24},{24,0},{1,9},{9,17},{17,25},{25,1},{2,10},{10... | collective-permute-start | bytes 258056 | tf_op jit(solution)/shard_map/ppermute | solution.py:21
  15.6 3.5 %collective-permute-start.5 = (bf16[256,168]{0,1:T(8,128)(2,1)}, bf16[256,168]{0,1:T(8,128)(2,1)}, u32[]{:S(2)}, u32[]{:S(2)}) collective-permute-start(bf16[256,168]{0,1:T(8,128)(2,1)} %param.11), channel_id=1, source_target_pairs={{0,24},{8,0},{16,8},{24,16},{1,25},{9,1},{17,9},{25,17},{2,26},{10... | collective-permute-start | bytes 258056 | tf_op jit(solution)/shard_map/ppermute | solution.py:21
  22.1 2.6 %collective-permute-start = (bf16[256,256]{1,0:T(8,128)(2,1)}, bf16[256,256]{1,0:T(8,128)(2,1)S(1)}, u32[]{:S(2)}, u32[]{:S(2)}) collective-permute-start(bf16[256,256]{1,0:T(8,128)(2,1)} %constant_dynamic-update-slice_fusion), channel_id=1, source_target_pairs={{0,128},{32,160},{64,192},{96,224},{128,256},{160,288},{192,320},{... | collective-permute-start | bytes 393224 | tf_op jit(solution)/shard_map/ppermute | solution.py:17
  24.7 2.8 %collective-permute-start.1 = (bf16[256,256]{1,0:T(8,128)(2,1)}, bf16[256,256]{1,0:T(8,128)(2,1)S(1)}, u32[]{:S(2)}, u32[]{:S(2)}) collective-permute-start(bf16[256,256]{1,0:T(8,128)(2,1)} %constant_dynamic-update-slice_fusion), channel_id=1, source_target_pairs={{0,96},{32,128},{64,160},{96,192},{128,224},{160,256},{192,288},{2... | collective-permute-start | bytes 393224 | tf_op jit(solution)/shard_map/ppermute | solution.py:17
  27.5 4.5 %collective-permute-start.2 = (bf16[256,256]{1,0:T(8,128)(2,1)}, bf16[256,256]{1,0:T(8,128)(2,1)S(1)}, u32[]{:S(2)}, u32[]{:S(2)}) collective-permute-start(bf16[256,256]{1,0:T(8,128)(2,1)} %constant_dynamic-update-slice_fusion), channel_id=1, source_target_pairs={{0,64},{32,96},{64,128},{96,160},{128,192},{160,224},{192,256},{22... | collective-permute-start | bytes 393224 | tf_op jit(solution)/shard_map/ppermute | solution.py:17
  32.2 2.7 %copy.14 = bf16[128,5376]{0,1:T(8,128)(2,1)} copy(bf16[128,5376]{1,0:T(8,128)(2,1)} %param.12) | data formatting | bytes 2752512 | tf_op args[4]
  36.6 12.1 %collective-permute-start.6 = (bf16[256,168]{0,1:T(8,128)(2,1)}, bf16[256,168]{0,1:T(8,128)(2,1)S(1)}, u32[]{:S(2)}, u32[]{:S(2)}) collective-permute-start(bf16[256,168]{0,1:T(8,128)(2,1)} %collective-permute-done.4), channel_id=1, source_target_pairs={{0,8},{8,16},{16,24},{24,0},{1,9},{9,17},{17,25},{25,1},{2,10},{10... | collective-permute-start | bytes 258056 | tf_op jit(solution)/shard_map/ppermute | solution.py:21
  54.3 4.0 %collective-permute-start.8 = (bf16[4,256,168]{1,2,0:T(8,128)(2,1)S(1)}, bf16[4,256,168]{1,2,0:T(8,128)(2,1)S(1)}, u32[]{:S(2)}, u32[]{:S(2)}) collective-permute-start(bf16[4,256,168]{1,2,0:T(8,128)(2,1)S(1)} %bitcast_dynamic-update-slice_fusion.6), channel_id=1, source_target_pairs={{0,4},{2,6},{4,0},{6,2},{1,5},{3,7},{5,1},{7,3},{8,12},{10,14},{12... | collective-permute-start | bytes 1032200 | tf_op jit(solution)/shard_map/ppermute | solution.py:21
  60.5 2.4 %collective-permute-start.9 = (bf16[4,256,168]{1,2,0:T(8,128)(2,1)S(1)}, bf16[4,256,168]{1,2,0:T(8,128)(2,1)S(1)}, u32[]{:S(2)}, u32[]{:S(2)}) collective-permute-start(bf16[4,256,168]{1,2,0:T(8,128)(2,1)S(1)} %bitcast_dynamic-update-slice_fusion.6), channel_id=1, source_target_pairs={{0,6},{2,0},{4,2},{6,4},{1,7},{3,1},{5,3},{7,5},{8,14},{10,8},{12,... | collective-permute-start | bytes 1032200 | tf_op jit(solution)/shard_map/ppermute | solution.py:21
  66.0 3.6 %collective-permute-done.9 = bf16[4,256,168]{1,2,0:T(8,128)(2,1)S(1)} collective-permute-done((bf16[4,256,168]{1,2,0:T(8,128)(2,1)S(1)}, bf16[4,256,168]{1,2,0:T(8,128)(2,1)S(1)}, u32[]{:S(2)}, u32[]{:S(2)}) %collective-permute-start.9) | collective-permute-done | bytes 344096 | tf_op jit(solution)/shard_map/ppermute | solution.py:21
  69.7 16.2 %collective-permute-start.10 = (bf16[4,4,256,168]{2,3,1,0:T(8,128)(2,1)S(1)}, bf16[4,4,256,168]{2,3,1,0:T(8,128)(2,1)S(1)}, u32[]{:S(2)}, u32[]{:S(2)}) collective-permute-start(bf16[4,4,256,168]{2,3,1,0:T(8,128)(2,1)S(1)} %bitcast_dynamic-update-slice_fusion.2), channel_id=1, source_target_pairs={{0,1},{1,0},{2,3},{3,2},{4,5},{5,4},{6,7},{7,6},{8,9},{9,8},{10,11... | collective-permute-start | bytes 4128776 | tf_op jit(solution)/shard_map/ppermute | solution.py:21
  101.8 4.4 %collective-permute-start.13 = (bf16[256,128]{0,1:T(8,128)(2,1)S(1)}, bf16[256,128]{0,1:T(8,128)(2,1)S(1)}, u32[]{:S(2)}, u32[]{:S(2)}) collective-permute-start(bf16[256,128]{0,1:T(8,128)(2,1)S(1)} %get-tuple-element.17), channel_id=1, source_target_pairs={{64,0},{96,32},{128,64},{160,96},{192,128},{224,160},{256,192},{28... | collective-permute-start | bytes 196616 | tf_op jit(solution)/shard_map/ppermute | solution.py:17
  106.2 3.5 %collective-permute-start.14 = (bf16[256,128]{0,1:T(8,128)(2,1)S(1)}, bf16[256,128]{0,1:T(8,128)(2,1)S(1)}, u32[]{:S(2)}, u32[]{:S(2)}) collective-permute-start(bf16[256,128]{0,1:T(8,128)(2,1)S(1)} %get-tuple-element.16), channel_id=1, source_target_pairs={{96,0},{128,32},{160,64},{192,96},{224,128},{256,160},{288,192},{3... | collective-permute-start | bytes 196616 | tf_op jit(solution)/shard_map/ppermute | solution.py:17
  109.7 4.7 %collective-permute-start.15 = (bf16[256,128]{0,1:T(8,128)(2,1)S(1)}, bf16[256,128]{0,1:T(8,128)(2,1)S(1)}, u32[]{:S(2)}, u32[]{:S(2)}) collective-permute-start(bf16[256,128]{0,1:T(8,128)(2,1)S(1)} %get-tuple-element.15), channel_id=1, source_target_pairs={{128,0},{160,32},{192,64},{224,96},{256,128},{288,160},{320,192},{... | collective-permute-start | bytes 196616 | tf_op jit(solution)/shard_map/ppermute | solution.py:17
  116.4 4.0 %collective-permute-start.16 = (bf16[4,4,168,256]{3,2,0,1:T(8,128)(2,1)S(1)}, bf16[4,4,168,256]{3,2,0,1:T(8,128)(2,1)}, u32[]{:S(2)}, u32[]{:S(2)}) collective-permute-start(bf16[4,4,168,256]{3,2,0,1:T(8,128)(2,1)S(1)} %copy.18), channel_id=1, source_target_pairs={{0,1},{1,0},{2,3},{3,2},{4,5},{5,4},{6,7},{7,6},{8,9},{9,8},{10,11... | collective-permute-start | bytes 4128776 | tf_op jit(solution)/shard_map/ppermute | solution.py:21
  125.1 5.7 %collective-permute-start.17 = (bf16[4,168,256]{2,1,0:T(8,128)(2,1)S(1)}, bf16[4,168,256]{2,1,0:T(8,128)(2,1)S(1)}, u32[]{:S(2)}, u32[]{:S(2)}) collective-permute-start(bf16[4,168,256]{2,1,0:T(8,128)(2,1)S(1)} %get-tuple-element.5), channel_id=1, source_target_pairs={{0,2},{2,4},{4,6},{6,0},{1,3},{3,5},{5,7},{7,1},{8,10},{10,12},{12... | collective-permute-start | bytes 1032200 | tf_op jit(solution)/shard_map/ppermute | solution.py:21
  132.7 2.5 %collective-permute-start.19 = (bf16[4,168,256]{2,1,0:T(8,128)(2,1)S(1)}, bf16[4,168,256]{2,1,0:T(8,128)(2,1)S(1)}, u32[]{:S(2)}, u32[]{:S(2)}) collective-permute-start(bf16[4,168,256]{2,1,0:T(8,128)(2,1)S(1)} %get-tuple-element.6), channel_id=1, source_target_pairs={{0,6},{2,0},{4,2},{6,4},{1,7},{3,1},{5,3},{7,5},{8,14},{10,8},{12,... | collective-permute-start | bytes 1032200 | tf_op jit(solution)/shard_map/ppermute | solution.py:21
  135.2 9.9 %collective-permute-done.17 = bf16[4,168,256]{2,1,0:T(8,128)(2,1)S(1)} collective-permute-done((bf16[4,168,256]{2,1,0:T(8,128)(2,1)S(1)}, bf16[4,168,256]{2,1,0:T(8,128)(2,1)S(1)}, u32[]{:S(2)}, u32[]{:S(2)}) %collective-permute-start.17) | collective-permute-done | bytes 344096 | tf_op jit(solution)/shard_map/ppermute | solution.py:21
  145.1 6.5 %collective-permute-done.19 = bf16[4,168,256]{2,1,0:T(8,128)(2,1)S(1)} collective-permute-done((bf16[4,168,256]{2,1,0:T(8,128)(2,1)S(1)}, bf16[4,168,256]{2,1,0:T(8,128)(2,1)S(1)}, u32[]{:S(2)}, u32[]{:S(2)}) %collective-permute-start.19) | collective-permute-done | bytes 344096 | tf_op jit(solution)/shard_map/ppermute | solution.py:21
  151.8 10.6 %collective-permute-start.20 = (bf16[168,256]{1,0:T(8,128)(2,1)S(1)}, bf16[168,256]{1,0:T(8,128)(2,1)S(1)}, u32[]{:S(2)}, u32[]{:S(2)}) collective-permute-start(bf16[168,256]{1,0:T(8,128)(2,1)S(1)} %get-tuple-element.12), channel_id=1, source_target_pairs={{0,8},{8,16},{16,24},{24,0},{1,9},{9,17},{17,25},{25,1},{2,10},{10... | collective-permute-start | bytes 258056 | tf_op jit(solution)/shard_map/ppermute | solution.py:21
  162.4 4.4 %collective-permute-start.22 = (bf16[168,256]{1,0:T(8,128)(2,1)S(1)}, bf16[168,256]{1,0:T(8,128)(2,1)S(1)}, u32[]{:S(2)}, u32[]{:S(2)}) collective-permute-start(bf16[168,256]{1,0:T(8,128)(2,1)S(1)} %get-tuple-element.13), channel_id=1, source_target_pairs={{0,24},{8,0},{16,8},{24,16},{1,25},{9,1},{17,9},{25,17},{2,26},{10... | collective-permute-start | bytes 258056 | tf_op jit(solution)/shard_map/ppermute | solution.py:21
  166.8 14.4 %collective-permute-done.20 = bf16[168,256]{1,0:T(8,128)(2,1)S(1)} collective-permute-done((bf16[168,256]{1,0:T(8,128)(2,1)S(1)}, bf16[168,256]{1,0:T(8,128)(2,1)S(1)}, u32[]{:S(2)}, u32[]{:S(2)}) %collective-permute-start.20) | collective-permute-done | bytes 86048 | tf_op jit(solution)/shard_map/ppermute | solution.py:21
  181.3 3.9 %collective-permute-start.21 = (bf16[168,256]{1,0:T(8,128)(2,1)S(1)}, bf16[168,256]{1,0:T(8,128)(2,1)S(1)}, u32[]{:S(2)}, u32[]{:S(2)}) collective-permute-start(bf16[168,256]{1,0:T(8,128)(2,1)S(1)} %fusion.30), channel_id=1, source_target_pairs={{0,8},{8,16},{16,24},{24,0},{1,9},{9,17},{17,25},{25,1},{2,10},{10... | collective-permute-start | bytes 258056 | tf_op jit(solution)/shard_map/ppermute | solution.py:21
  185.6 17.0 %collective-permute-done.21 = bf16[168,256]{1,0:T(8,128)(2,1)S(1)} collective-permute-done((bf16[168,256]{1,0:T(8,128)(2,1)S(1)}, bf16[168,256]{1,0:T(8,128)(2,1)S(1)}, u32[]{:S(2)}, u32[]{:S(2)}) %collective-permute-start.21) | collective-permute-done | bytes 86048 | tf_op jit(solution)/shard_map/ppermute | solution.py:21
  (92 shorter events, 40.8 us)
Async XLA Ops:
  0.0 86.1 %copy-start = (bf16[256,128]{1,0:T(8,128)(2,1)S(1)}, bf16[256,128]{1,0:T(8,128)(2,1)}, u32[]{:S(2)}) copy-start(bf16[256,128]{1,0:T(8,128)(2,1)} %param.8) | copy-start | bytes 196612
  0.0 36.6 %collective-permute-start.4 = (bf16[256,168]{0,1:T(8,128)(2,1)}, bf16[256,168]{0,1:T(8,128)(2,1)}, u32[]{:S(2)}, u32[]{:S(2)}) collective-permute-start(bf16[256,168]{0,1:T(8,128)(2,1)} %param.11), channel_id=1, source_target_pairs={{0,8},{8,16},{16,24},{24,0},{1,9},{9,17},{17,25},{25,1},{2,10},{10... | collective-permute-start | bytes 258056 | tf_op jit(solution)/shard_map/ppermute | solution.py:21
  15.6 34.0 %collective-permute-start.5 = (bf16[256,168]{0,1:T(8,128)(2,1)}, bf16[256,168]{0,1:T(8,128)(2,1)}, u32[]{:S(2)}, u32[]{:S(2)}) collective-permute-start(bf16[256,168]{0,1:T(8,128)(2,1)} %param.11), channel_id=1, source_target_pairs={{0,24},{8,0},{16,8},{24,16},{1,25},{9,1},{17,9},{25,17},{2,26},{10... | collective-permute-start | bytes 258056 | tf_op jit(solution)/shard_map/ppermute | solution.py:21
  22.1 63.9 %collective-permute-start = (bf16[256,256]{1,0:T(8,128)(2,1)}, bf16[256,256]{1,0:T(8,128)(2,1)S(1)}, u32[]{:S(2)}, u32[]{:S(2)}) collective-permute-start(bf16[256,256]{1,0:T(8,128)(2,1)} %constant_dynamic-update-slice_fusion), channel_id=1, source_target_pairs={{0,128},{32,160},{64,192},{96,224},{128,256},{160,288},{192,320},{... | collective-permute-start | bytes 393224 | tf_op jit(solution)/shard_map/ppermute | solution.py:17
  24.7 61.3 %collective-permute-start.1 = (bf16[256,256]{1,0:T(8,128)(2,1)}, bf16[256,256]{1,0:T(8,128)(2,1)S(1)}, u32[]{:S(2)}, u32[]{:S(2)}) collective-permute-start(bf16[256,256]{1,0:T(8,128)(2,1)} %constant_dynamic-update-slice_fusion), channel_id=1, source_target_pairs={{0,96},{32,128},{64,160},{96,192},{128,224},{160,256},{192,288},{2... | collective-permute-start | bytes 393224 | tf_op jit(solution)/shard_map/ppermute | solution.py:17
  27.5 58.5 %collective-permute-start.2 = (bf16[256,256]{1,0:T(8,128)(2,1)}, bf16[256,256]{1,0:T(8,128)(2,1)S(1)}, u32[]{:S(2)}, u32[]{:S(2)}) collective-permute-start(bf16[256,256]{1,0:T(8,128)(2,1)} %constant_dynamic-update-slice_fusion), channel_id=1, source_target_pairs={{0,64},{32,96},{64,128},{96,160},{128,192},{160,224},{192,256},{22... | collective-permute-start | bytes 393224 | tf_op jit(solution)/shard_map/ppermute | solution.py:17
  36.6 15.6 %collective-permute-start.6 = (bf16[256,168]{0,1:T(8,128)(2,1)}, bf16[256,168]{0,1:T(8,128)(2,1)S(1)}, u32[]{:S(2)}, u32[]{:S(2)}) collective-permute-start(bf16[256,168]{0,1:T(8,128)(2,1)} %collective-permute-done.4), channel_id=1, source_target_pairs={{0,8},{8,16},{16,24},{24,0},{1,9},{9,17},{17,25},{25,1},{2,10},{10... | collective-permute-start | bytes 258056 | tf_op jit(solution)/shard_map/ppermute | solution.py:21
  52.2 8.3 %collective-permute-start.7 = (bf16[4,256,168]{1,2,0:T(8,128)(2,1)S(1)}, bf16[4,256,168]{1,2,0:T(8,128)(2,1)S(1)}, u32[]{:S(2)}, u32[]{:S(2)}) collective-permute-start(bf16[4,256,168]{1,2,0:T(8,128)(2,1)S(1)} %bitcast_dynamic-update-slice_fusion.6), channel_id=1, source_target_pairs={{0,2},{2,4},{4,6},{6,0},{1,3},{3,5},{5,7},{7,1},{8,10},{10,12},{12... | collective-permute-start | bytes 1032200 | tf_op jit(solution)/shard_map/ppermute | solution.py:21
  54.3 9.8 %collective-permute-start.8 = (bf16[4,256,168]{1,2,0:T(8,128)(2,1)S(1)}, bf16[4,256,168]{1,2,0:T(8,128)(2,1)S(1)}, u32[]{:S(2)}, u32[]{:S(2)}) collective-permute-start(bf16[4,256,168]{1,2,0:T(8,128)(2,1)S(1)} %bitcast_dynamic-update-slice_fusion.6), channel_id=1, source_target_pairs={{0,4},{2,6},{4,0},{6,2},{1,5},{3,7},{5,1},{7,3},{8,12},{10,14},{12... | collective-permute-start | bytes 1032200 | tf_op jit(solution)/shard_map/ppermute | solution.py:21
  60.5 9.2 %collective-permute-start.9 = (bf16[4,256,168]{1,2,0:T(8,128)(2,1)S(1)}, bf16[4,256,168]{1,2,0:T(8,128)(2,1)S(1)}, u32[]{:S(2)}, u32[]{:S(2)}) collective-permute-start(bf16[4,256,168]{1,2,0:T(8,128)(2,1)S(1)} %bitcast_dynamic-update-slice_fusion.6), channel_id=1, source_target_pairs={{0,6},{2,0},{4,2},{6,4},{1,7},{3,1},{5,3},{7,5},{8,14},{10,8},{12,... | collective-permute-start | bytes 1032200 | tf_op jit(solution)/shard_map/ppermute | solution.py:21
  64.1 21.9 %collective-permute-start.3 = (bf16[256,256]{1,0:T(8,128)(2,1)}, bf16[256,256]{1,0:T(8,128)(2,1)S(1)}, u32[]{:S(2)}, u32[]{:S(2)}) collective-permute-start(bf16[256,256]{1,0:T(8,128)(2,1)} %constant_dynamic-update-slice_fusion), channel_id=1, source_target_pairs={{0,32},{32,64},{64,96},{96,128},{128,160},{160,192},{192,224},{224... | collective-permute-start | bytes 393224 | tf_op jit(solution)/shard_map/ppermute | solution.py:17
  69.7 19.0 %collective-permute-start.10 = (bf16[4,4,256,168]{2,3,1,0:T(8,128)(2,1)S(1)}, bf16[4,4,256,168]{2,3,1,0:T(8,128)(2,1)S(1)}, u32[]{:S(2)}, u32[]{:S(2)}) collective-permute-start(bf16[4,4,256,168]{2,3,1,0:T(8,128)(2,1)S(1)} %bitcast_dynamic-update-slice_fusion.2), channel_id=1, source_target_pairs={{0,1},{1,0},{2,3},{3,2},{4,5},{5,4},{6,7},{7,6},{8,9},{9,8},{10,11... | collective-permute-start | bytes 4128776 | tf_op jit(solution)/shard_map/ppermute | solution.py:21
  94.8 3.9 %collective-permute-start.11 = (bf16[1280,128]{0,1:T(8,128)(2,1)}, bf16[1280,128]{0,1:T(8,128)(2,1)}, u32[]{:S(2)}, u32[]{:S(2)}) collective-permute-start(bf16[1280,128]{0,1:T(8,128)(2,1)} %fusion.24), channel_id=1, source_target_pairs={{0,1},{1,0},{2,3},{3,2},{4,5},{5,4},{6,7},{7,6},{8,9},{9,8},{10,11... | collective-permute-start | bytes 983048 | tf_op jit(solution)/shard_map/ppermute | solution.py:21
  99.8 15.1 %collective-permute-start.12 = (bf16[256,128]{0,1:T(8,128)(2,1)S(1)}, bf16[256,128]{0,1:T(8,128)(2,1)S(1)}, u32[]{:S(2)}, u32[]{:S(2)}) collective-permute-start(bf16[256,128]{0,1:T(8,128)(2,1)S(1)} %get-tuple-element.14), channel_id=1, source_target_pairs={{32,0},{64,32},{96,64},{128,96},{160,128},{192,160},{224,192},{256... | collective-permute-start | bytes 196616 | tf_op jit(solution)/shard_map/ppermute | solution.py:17
  101.8 13.2 %collective-permute-start.13 = (bf16[256,128]{0,1:T(8,128)(2,1)S(1)}, bf16[256,128]{0,1:T(8,128)(2,1)S(1)}, u32[]{:S(2)}, u32[]{:S(2)}) collective-permute-start(bf16[256,128]{0,1:T(8,128)(2,1)S(1)} %get-tuple-element.17), channel_id=1, source_target_pairs={{64,0},{96,32},{128,64},{160,96},{192,128},{224,160},{256,192},{28... | collective-permute-start | bytes 196616 | tf_op jit(solution)/shard_map/ppermute | solution.py:17
  106.2 8.8 %collective-permute-start.14 = (bf16[256,128]{0,1:T(8,128)(2,1)S(1)}, bf16[256,128]{0,1:T(8,128)(2,1)S(1)}, u32[]{:S(2)}, u32[]{:S(2)}) collective-permute-start(bf16[256,128]{0,1:T(8,128)(2,1)S(1)} %get-tuple-element.16), channel_id=1, source_target_pairs={{96,0},{128,32},{160,64},{192,96},{224,128},{256,160},{288,192},{3... | collective-permute-start | bytes 196616 | tf_op jit(solution)/shard_map/ppermute | solution.py:17
  109.7 6.0 %collective-permute-start.15 = (bf16[256,128]{0,1:T(8,128)(2,1)S(1)}, bf16[256,128]{0,1:T(8,128)(2,1)S(1)}, u32[]{:S(2)}, u32[]{:S(2)}) collective-permute-start(bf16[256,128]{0,1:T(8,128)(2,1)S(1)} %get-tuple-element.15), channel_id=1, source_target_pairs={{128,0},{160,32},{192,64},{224,96},{256,128},{288,160},{320,192},{... | collective-permute-start | bytes 196616 | tf_op jit(solution)/shard_map/ppermute | solution.py:17
  116.4 6.9 %collective-permute-start.16 = (bf16[4,4,168,256]{3,2,0,1:T(8,128)(2,1)S(1)}, bf16[4,4,168,256]{3,2,0,1:T(8,128)(2,1)}, u32[]{:S(2)}, u32[]{:S(2)}) collective-permute-start(bf16[4,4,168,256]{3,2,0,1:T(8,128)(2,1)S(1)} %copy.18), channel_id=1, source_target_pairs={{0,1},{1,0},{2,3},{3,2},{4,5},{5,4},{6,7},{7,6},{8,9},{9,8},{10,11... | collective-permute-start | bytes 4128776 | tf_op jit(solution)/shard_map/ppermute | solution.py:21
  125.1 20.0 %collective-permute-start.17 = (bf16[4,168,256]{2,1,0:T(8,128)(2,1)S(1)}, bf16[4,168,256]{2,1,0:T(8,128)(2,1)S(1)}, u32[]{:S(2)}, u32[]{:S(2)}) collective-permute-start(bf16[4,168,256]{2,1,0:T(8,128)(2,1)S(1)} %get-tuple-element.5), channel_id=1, source_target_pairs={{0,2},{2,4},{4,6},{6,0},{1,3},{3,5},{5,7},{7,1},{8,10},{10,12},{12... | collective-permute-start | bytes 1032200 | tf_op jit(solution)/shard_map/ppermute | solution.py:21
  130.8 14.3 %collective-permute-start.18 = (bf16[4,168,256]{2,1,0:T(8,128)(2,1)S(1)}, bf16[4,168,256]{2,1,0:T(8,128)(2,1)S(1)}, u32[]{:S(2)}, u32[]{:S(2)}) collective-permute-start(bf16[4,168,256]{2,1,0:T(8,128)(2,1)S(1)} %get-tuple-element.7), channel_id=1, source_target_pairs={{0,4},{2,6},{4,0},{6,2},{1,5},{3,7},{5,1},{7,3},{8,12},{10,14},{12... | collective-permute-start | bytes 1032200 | tf_op jit(solution)/shard_map/ppermute | solution.py:21
  132.7 18.8 %collective-permute-start.19 = (bf16[4,168,256]{2,1,0:T(8,128)(2,1)S(1)}, bf16[4,168,256]{2,1,0:T(8,128)(2,1)S(1)}, u32[]{:S(2)}, u32[]{:S(2)}) collective-permute-start(bf16[4,168,256]{2,1,0:T(8,128)(2,1)S(1)} %get-tuple-element.6), channel_id=1, source_target_pairs={{0,6},{2,0},{4,2},{6,4},{1,7},{3,1},{5,3},{7,5},{8,14},{10,8},{12,... | collective-permute-start | bytes 1032200 | tf_op jit(solution)/shard_map/ppermute | solution.py:21
  151.8 29.5 %collective-permute-start.20 = (bf16[168,256]{1,0:T(8,128)(2,1)S(1)}, bf16[168,256]{1,0:T(8,128)(2,1)S(1)}, u32[]{:S(2)}, u32[]{:S(2)}) collective-permute-start(bf16[168,256]{1,0:T(8,128)(2,1)S(1)} %get-tuple-element.12), channel_id=1, source_target_pairs={{0,8},{8,16},{16,24},{24,0},{1,9},{9,17},{17,25},{25,1},{2,10},{10... | collective-permute-start | bytes 258056 | tf_op jit(solution)/shard_map/ppermute | solution.py:21
  162.4 23.2 %collective-permute-start.22 = (bf16[168,256]{1,0:T(8,128)(2,1)S(1)}, bf16[168,256]{1,0:T(8,128)(2,1)S(1)}, u32[]{:S(2)}, u32[]{:S(2)}) collective-permute-start(bf16[168,256]{1,0:T(8,128)(2,1)S(1)} %get-tuple-element.13), channel_id=1, source_target_pairs={{0,24},{8,0},{16,8},{24,16},{1,25},{9,1},{17,9},{25,17},{2,26},{10... | collective-permute-start | bytes 258056 | tf_op jit(solution)/shard_map/ppermute | solution.py:21
  181.3 21.3 %collective-permute-start.21 = (bf16[168,256]{1,0:T(8,128)(2,1)S(1)}, bf16[168,256]{1,0:T(8,128)(2,1)S(1)}, u32[]{:S(2)}, u32[]{:S(2)}) collective-permute-start(bf16[168,256]{1,0:T(8,128)(2,1)S(1)} %fusion.30), channel_id=1, source_target_pairs={{0,8},{8,16},{16,24},{24,0},{1,9},{9,17},{17,25},{25,1},{2,10},{10... | collective-permute-start | bytes 258056 | tf_op jit(solution)/shard_map/ppermute | solution.py:21
  (9 other events, 89.8 us)

commit v10 on v6

--- a/solution.py
+++ b/solution.py
@@ -82,7 +82,7 @@
     )
 
 
-def band_backward(query_block, key_band, value_band, grad_block, query_start, key_start):
+def band_probs(query_block, key_band, query_start, key_start):
     length = query_block.shape[0]
     span = key_band.shape[0]
     query_pos = query_start + jnp.arange(length, dtype=jnp.int32)
@@ -94,6 +94,10 @@
     top = jnp.max(masked, axis=1, keepdims=True)
     weights = jnp.where(allowed, jnp.exp(masked - top), 0.0)
     probs = weights / jnp.sum(weights, axis=1, keepdims=True)
+    return probs
+
+
+def band_backward(query_block, key_band, value_band, grad_block, probs):
     probs_low = probs.astype(jnp.bfloat16)
     grad_probs = dot_rows(grad_block, value_band)
     delta = jnp.sum(probs * grad_probs, axis=1, keepdims=True)
@@ -112,22 +116,23 @@
         width = d_out.shape[1]
         seq_index = lax.axis_index("seq")
         stacked = gather_axis(d_out, "zhi", n_zhi, relay=True)
+        reach = NBR
         kv = jnp.concatenate([keys, values], axis=1)
-        stacked, kv = lax.optimization_barrier((stacked, kv))
+        kv_blocks = [from_behind(kv, "seq", distance) for distance in range(reach, 0, -1)]
+        kv_band = jnp.concatenate(kv_blocks + [kv], axis=0)
+        query_start = seq_index * length
+        probs = band_probs(query, kv_band[:, :dim], query_start, query_start - reach * length)
+        stacked, kv_band, probs = lax.optimization_barrier((stacked, kv_band, probs))
         stacked = gather_axis(stacked, "x", n_x)
         stacked = gather_axis(stacked, "core", n_core)
         out_rows = w_out.reshape(w_out.shape[0], n_zhi, n_x, n_core, width)
         grad_heads = jnp.einsum(
             "cxzti,hzxci->th", stacked, out_rows, preferred_element_type=jnp.float32
         ).astype(jnp.bfloat16)
-        reach = NBR
-        kv_blocks = [from_behind(kv, "seq", distance) for distance in range(reach, 0, -1)]
-        kv_band = jnp.concatenate(kv_blocks + [kv], axis=0)
         key_band = kv_band[:, :dim]
         value_band = kv_band[:, dim:]
-        query_start = seq_index * length
         grad_query, key_parts, value_parts = band_backward(
-            query, key_band, value_band, grad_heads, query_start, query_start - reach * length
+            query, key_band, value_band, grad_heads, probs
         )
         kv_parts = jnp.concatenate([key_parts, value_parts], axis=1)
         kv_total = kv_parts[reach * length :].astype(jnp.float32)

time: 210 us -> 201 us (0.957)
  the two profiles are of different devices: /device:TPU:131 before, /device:TPU:195 now
where the time goes in v10:
time: 201 us; the launch traced here: 200 us
  starting transfers between devices  125 us (62%)
  waiting for transfers between devices  49.8 us (25%)
  local copies, waits for them, and re-layouts  12.8 us (6%)
  matrix products  6.17 us (3%)
  other arithmetic  4.77 us (2%)
    ppermute x14, starting transfers between devices, shift(): lax.ppermute(block, axis, [(i, (i + step) % size) for i in range(size)])  89.7 us
    ppermute x14, waiting for transfers between devices, shift(): lax.ppermute(block, axis, [(i, (i + step) % size) for i in range(size)])  46.6 us
    ppermute x8, starting transfers between devices, from_behind(): return lax.ppermute(block, axis, route)  35.5 us
    unnamed x27, local copies, waits for them, and re-layouts  5.13 us
    dot_general x8, matrix products, dot_rows(): lax.dot_general(left, right, (((1,), (1,)), ((), ())), preferred_element_...  4.11 us
  transfers between devices with their start and end apart: 22, of which 10 were waited for; matrix products, arithmetic and copies ran while one was open for 7% of the time, Pallas kernels for 0%

profile of v10, /device:TPU:195, one launch (start us, length us, event | category | flops | bytes accessed | tf_op | source)
XLA Modules:
  0.0 199.5 jit_solution(16738453370234018400)
XLA Ops:
  0.0 15.6 %collective-permute-start = (bf16[256,168]{0,1:T(8,128)(2,1)}, bf16[256,168]{0,1:T(8,128)(2,1)S(1)}, u32[]{:S(2)}, u32[]{:S(2)}) collective-permute-start(bf16[256,168]{0,1:T(8,128)(2,1)} %param.11), channel_id=1, source_target_pairs={{0,8},{8,16},{16,24},{24,0},{1,9},{9,17},{17,25},{25,1},{2,10},{10... | collective-permute-start | bytes 258056 | tf_op jit(solution)/shard_map/ppermute | solution.py:21
  19.9 2.9 %collective-permute-start.3 = (bf16[256,256]{1,0:T(8,128)(2,1)S(1)}, bf16[256,256]{1,0:T(8,128)(2,1)S(1)}, u32[]{:S(2)}, u32[]{:S(2)}) collective-permute-start(bf16[256,256]{1,0:T(8,128)(2,1)S(1)} %constant_dynamic-update-slice_fusion), channel_id=1, source_target_pairs={{0,128},{32,160},{64,192},{96,224},{128,256},{160,288},{192,320},{... | collective-permute-start | bytes 393224 | tf_op jit(solution)/shard_map/ppermute | solution.py:17
  22.8 4.6 %collective-permute-start.4 = (bf16[256,256]{1,0:T(8,128)(2,1)S(1)}, bf16[256,256]{1,0:T(8,128)(2,1)S(1)}, u32[]{:S(2)}, u32[]{:S(2)}) collective-permute-start(bf16[256,256]{1,0:T(8,128)(2,1)S(1)} %constant_dynamic-update-slice_fusion), channel_id=1, source_target_pairs={{0,96},{32,128},{64,160},{96,192},{128,224},{160,256},{192,288},{2... | collective-permute-start | bytes 393224 | tf_op jit(solution)/shard_map/ppermute | solution.py:17
  30.6 2.8 %collective-permute-start.6 = (bf16[256,256]{1,0:T(8,128)(2,1)S(1)}, bf16[256,256]{1,0:T(8,128)(2,1)S(1)}, u32[]{:S(2)}, u32[]{:S(2)}) collective-permute-start(bf16[256,256]{1,0:T(8,128)(2,1)S(1)} %constant_dynamic-update-slice_fusion), channel_id=1, source_target_pairs={{0,32},{32,64},{64,96},{96,128},{128,160},{160,192},{192,224},{224... | collective-permute-start | bytes 393224 | tf_op jit(solution)/shard_map/ppermute | solution.py:17
  33.4 11.6 %collective-permute-start.2 = (bf16[256,168]{0,1:T(8,128)(2,1)S(1)}, bf16[256,168]{0,1:T(8,128)(2,1)S(1)}, u32[]{:S(2)}, u32[]{:S(2)}) collective-permute-start(bf16[256,168]{0,1:T(8,128)(2,1)S(1)} %collective-permute-done), channel_id=1, source_target_pairs={{0,8},{8,16},{16,24},{24,0},{1,9},{9,17},{17,25},{25,1},{2,10},{10... | collective-permute-start | bytes 258056 | tf_op jit(solution)/shard_map/ppermute | solution.py:21
  48.0 3.1 %collective-permute-start.7 = (bf16[4,256,168]{1,2,0:T(8,128)(2,1)S(1)}, bf16[4,256,168]{1,2,0:T(8,128)(2,1)S(1)}, u32[]{:S(2)}, u32[]{:S(2)}) collective-permute-start(bf16[4,256,168]{1,2,0:T(8,128)(2,1)S(1)} %bitcast_dynamic-update-slice_fusion.6), channel_id=1, source_target_pairs={{0,2},{2,4},{4,6},{6,0},{1,3},{3,5},{5,7},{7,1},{8,10},{10,12},{12... | collective-permute-start | bytes 1032200 | tf_op jit(solution)/shard_map/ppermute | solution.py:21
  51.2 2.7 %collective-permute-start.8 = (bf16[4,256,168]{1,2,0:T(8,128)(2,1)S(1)}, bf16[4,256,168]{1,2,0:T(8,128)(2,1)S(1)}, u32[]{:S(2)}, u32[]{:S(2)}) collective-permute-start(bf16[4,256,168]{1,2,0:T(8,128)(2,1)S(1)} %bitcast_dynamic-update-slice_fusion.6), channel_id=1, source_target_pairs={{0,4},{2,6},{4,0},{6,2},{1,5},{3,7},{5,1},{7,3},{8,12},{10,14},{12... | collective-permute-start | bytes 1032200 | tf_op jit(solution)/shard_map/ppermute | solution.py:21
  54.0 3.8 %collective-permute-start.9 = (bf16[4,256,168]{1,2,0:T(8,128)(2,1)S(1)}, bf16[4,256,168]{1,2,0:T(8,128)(2,1)S(1)}, u32[]{:S(2)}, u32[]{:S(2)}) collective-permute-start(bf16[4,256,168]{1,2,0:T(8,128)(2,1)S(1)} %bitcast_dynamic-update-slice_fusion.6), channel_id=1, source_target_pairs={{0,6},{2,0},{4,2},{6,4},{1,7},{3,1},{5,3},{7,5},{8,14},{10,8},{12,... | collective-permute-start | bytes 1032200 | tf_op jit(solution)/shard_map/ppermute | solution.py:21
  58.0 2.9 %collective-permute-done.8 = bf16[4,256,168]{1,2,0:T(8,128)(2,1)S(1)} collective-permute-done((bf16[4,256,168]{1,2,0:T(8,128)(2,1)S(1)}, bf16[4,256,168]{1,2,0:T(8,128)(2,1)S(1)}, u32[]{:S(2)}, u32[]{:S(2)}) %collective-permute-start.8) | collective-permute-done | bytes 344096 | tf_op jit(solution)/shard_map/ppermute | solution.py:21
  60.9 3.8 %collective-permute-done.9 = bf16[4,256,168]{1,2,0:T(8,128)(2,1)S(1)} collective-permute-done((bf16[4,256,168]{1,2,0:T(8,128)(2,1)S(1)}, bf16[4,256,168]{1,2,0:T(8,128)(2,1)S(1)}, u32[]{:S(2)}, u32[]{:S(2)}) %collective-permute-start.9) | collective-permute-done | bytes 344096 | tf_op jit(solution)/shard_map/ppermute | solution.py:21
  64.7 12.3 %collective-permute-start.10 = (bf16[4,4,256,168]{2,3,1,0:T(8,128)(2,1)S(1)}, bf16[4,4,256,168]{2,3,1,0:T(8,128)(2,1)}, u32[]{:S(2)}, u32[]{:S(2)}) collective-permute-start(bf16[4,4,256,168]{2,3,1,0:T(8,128)(2,1)S(1)} %bitcast_dynamic-update-slice_fusion.2), channel_id=1, source_target_pairs={{0,1},{1,0},{2,3},{3,2},{4,5},{5,4},{6,7},{7,6},{8,9},{9,8},{10,11... | collective-permute-start | bytes 4128776 | tf_op jit(solution)/shard_map/ppermute | solution.py:21
  88.6 10.5 %collective-permute-start.11 = (bf16[256,256]{0,1:T(8,128)(2,1)S(1)}, bf16[256,256]{0,1:T(8,128)(2,1)S(1)}, u32[]{:S(2)}, u32[]{:S(2)}) collective-permute-start(bf16[256,256]{0,1:T(8,128)(2,1)S(1)} %get-tuple-element.22), channel_id=1, source_target_pairs={{32,0},{64,32},{96,64},{128,96},{160,128},{192,160},{224,192},{256... | collective-permute-start | bytes 393224 | tf_op jit(solution)/shard_map/ppermute | solution.py:17
  99.1 3.0 %collective-permute-start.12 = (bf16[256,256]{0,1:T(8,128)(2,1)S(1)}, bf16[256,256]{0,1:T(8,128)(2,1)S(1)}, u32[]{:S(2)}, u32[]{:S(2)}) collective-permute-start(bf16[256,256]{0,1:T(8,128)(2,1)S(1)} %get-tuple-element.23), channel_id=1, source_target_pairs={{64,0},{96,32},{128,64},{160,96},{192,128},{224,160},{256,192},{28... | collective-permute-start | bytes 393224 | tf_op jit(solution)/shard_map/ppermute | solution.py:17
  102.1 6.9 %collective-permute-start.13 = (bf16[256,256]{0,1:T(8,128)(2,1)S(1)}, bf16[256,256]{0,1:T(8,128)(2,1)S(1)}, u32[]{:S(2)}, u32[]{:S(2)}) collective-permute-start(bf16[256,256]{0,1:T(8,128)(2,1)S(1)} %get-tuple-element.25), channel_id=1, source_target_pairs={{96,0},{128,32},{160,64},{192,96},{224,128},{256,160},{288,192},{3... | collective-permute-start | bytes 393224 | tf_op jit(solution)/shard_map/ppermute | solution.py:17
  109.0 2.7 %collective-permute-start.14 = (bf16[256,256]{0,1:T(8,128)(2,1)S(1)}, bf16[256,256]{0,1:T(8,128)(2,1)S(1)}, u32[]{:S(2)}, u32[]{:S(2)}) collective-permute-start(bf16[256,256]{0,1:T(8,128)(2,1)S(1)} %get-tuple-element.24), channel_id=1, source_target_pairs={{128,0},{160,32},{192,64},{224,96},{256,128},{288,160},{320,192},{... | collective-permute-start | bytes 393224 | tf_op jit(solution)/shard_map/ppermute | solution.py:17
  116.6 3.5 %collective-permute-start.15 = (bf16[4,4,168,256]{3,2,0,1:T(8,128)(2,1)S(1)}, bf16[4,4,168,256]{3,2,0,1:T(8,128)(2,1)}, u32[]{:S(2)}, u32[]{:S(2)}) collective-permute-start(bf16[4,4,168,256]{3,2,0,1:T(8,128)(2,1)S(1)} %copy.18), channel_id=1, source_target_pairs={{0,1},{1,0},{2,3},{3,2},{4,5},{5,4},{6,7},{7,6},{8,9},{9,8},{10,11... | collective-permute-start | bytes 4128776 | tf_op jit(solution)/shard_map/ppermute | solution.py:21
  127.0 2.8 %collective-permute-start.17 = (bf16[4,168,256]{2,1,0:T(8,128)(2,1)S(1)}, bf16[4,168,256]{2,1,0:T(8,128)(2,1)S(1)}, u32[]{:S(2)}, u32[]{:S(2)}) collective-permute-start(bf16[4,168,256]{2,1,0:T(8,128)(2,1)S(1)} %get-tuple-element.13), channel_id=1, source_target_pairs={{0,4},{2,6},{4,0},{6,2},{1,5},{3,7},{5,1},{7,3},{8,12},{10,14},{12... | collective-permute-start | bytes 1032200 | tf_op jit(solution)/shard_map/ppermute | solution.py:21
  129.7 3.6 %collective-permute-start.18 = (bf16[4,168,256]{2,1,0:T(8,128)(2,1)S(1)}, bf16[4,168,256]{2,1,0:T(8,128)(2,1)S(1)}, u32[]{:S(2)}, u32[]{:S(2)}) collective-permute-start(bf16[4,168,256]{2,1,0:T(8,128)(2,1)S(1)} %get-tuple-element.12), channel_id=1, source_target_pairs={{0,6},{2,0},{4,2},{6,4},{1,7},{3,1},{5,3},{7,5},{8,14},{10,8},{12,... | collective-permute-start | bytes 1032200 | tf_op jit(solution)/shard_map/ppermute | solution.py:21
  135.9 3.5 %collective-permute-done.17 = bf16[4,168,256]{2,1,0:T(8,128)(2,1)S(1)} collective-permute-done((bf16[4,168,256]{2,1,0:T(8,128)(2,1)S(1)}, bf16[4,168,256]{2,1,0:T(8,128)(2,1)S(1)}, u32[]{:S(2)}, u32[]{:S(2)}) %collective-permute-start.17) | collective-permute-done | bytes 344096 | tf_op jit(solution)/shard_map/ppermute | solution.py:21
  139.4 8.4 %collective-permute-done.18 = bf16[4,168,256]{2,1,0:T(8,128)(2,1)S(1)} collective-permute-done((bf16[4,168,256]{2,1,0:T(8,128)(2,1)S(1)}, bf16[4,168,256]{2,1,0:T(8,128)(2,1)S(1)}, u32[]{:S(2)}, u32[]{:S(2)}) %collective-permute-start.18) | collective-permute-done | bytes 344096 | tf_op jit(solution)/shard_map/ppermute | solution.py:21
  148.0 13.0 %collective-permute-start.19 = (bf16[168,256]{1,0:T(8,128)(2,1)S(1)}, bf16[168,256]{1,0:T(8,128)(2,1)S(1)}, u32[]{:S(2)}, u32[]{:S(2)}) collective-permute-start(bf16[168,256]{1,0:T(8,128)(2,1)S(1)} %get-tuple-element.20), channel_id=1, source_target_pairs={{0,8},{8,16},{16,24},{24,0},{1,9},{9,17},{17,25},{25,1},{2,10},{10... | collective-permute-start | bytes 258056 | tf_op jit(solution)/shard_map/ppermute | solution.py:21
  162.9 12.4 %collective-permute-done.19 = bf16[168,256]{1,0:T(8,128)(2,1)S(1)} collective-permute-done((bf16[168,256]{1,0:T(8,128)(2,1)S(1)}, bf16[168,256]{1,0:T(8,128)(2,1)S(1)}, u32[]{:S(2)}, u32[]{:S(2)}) %collective-permute-start.19) | collective-permute-done | bytes 86048 | tf_op jit(solution)/shard_map/ppermute | solution.py:21
  175.3 11.1 %collective-permute-start.20 = (bf16[168,256]{1,0:T(8,128)(2,1)S(1)}, bf16[168,256]{1,0:T(8,128)(2,1)S(1)}, u32[]{:S(2)}, u32[]{:S(2)}) collective-permute-start(bf16[168,256]{1,0:T(8,128)(2,1)S(1)} %fusion.28), channel_id=1, source_target_pairs={{0,8},{8,16},{16,24},{24,0},{1,9},{9,17},{17,25},{25,1},{2,10},{10... | collective-permute-start | bytes 258056 | tf_op jit(solution)/shard_map/ppermute | solution.py:21
  186.4 12.4 %collective-permute-done.20 = bf16[168,256]{1,0:T(8,128)(2,1)S(1)} collective-permute-done((bf16[168,256]{1,0:T(8,128)(2,1)S(1)}, bf16[168,256]{1,0:T(8,128)(2,1)S(1)}, u32[]{:S(2)}, u32[]{:S(2)}) %collective-permute-start.20) | collective-permute-done | bytes 86048 | tf_op jit(solution)/shard_map/ppermute | solution.py:21
  (91 shorter events, 39.0 us)
Async XLA Ops:
  0.0 45.2 %copy-start = (bf16[256,128]{1,0:T(8,128)(2,1)S(1)}, bf16[256,128]{1,0:T(8,128)(2,1)}, u32[]{:S(2)}) copy-start(bf16[256,128]{1,0:T(8,128)(2,1)} %param.8) | copy-start | bytes 196612
  0.0 45.2 %copy-start.9 = (bf16[256,128]{1,0:T(8,128)(2,1)S(1)}, bf16[256,128]{1,0:T(8,128)(2,1)}, u32[]{:S(2)}) copy-start(bf16[256,128]{1,0:T(8,128)(2,1)} %param.10) | copy-start | bytes 196612
  0.0 30.6 %collective-permute-start = (bf16[256,168]{0,1:T(8,128)(2,1)}, bf16[256,168]{0,1:T(8,128)(2,1)S(1)}, u32[]{:S(2)}, u32[]{:S(2)}) collective-permute-start(bf16[256,168]{0,1:T(8,128)(2,1)} %param.11), channel_id=1, source_target_pairs={{0,8},{8,16},{16,24},{24,0},{1,9},{9,17},{17,25},{25,1},{2,10},{10... | collective-permute-start | bytes 258056 | tf_op jit(solution)/shard_map/ppermute | solution.py:21
  15.6 17.8 %collective-permute-start.1 = (bf16[256,168]{0,1:T(8,128)(2,1)}, bf16[256,168]{0,1:T(8,128)(2,1)S(1)}, u32[]{:S(2)}, u32[]{:S(2)}) collective-permute-start(bf16[256,168]{0,1:T(8,128)(2,1)} %param.11), channel_id=1, source_target_pairs={{0,24},{8,0},{16,8},{24,16},{1,25},{9,1},{17,9},{25,17},{2,26},{10... | collective-permute-start | bytes 258056 | tf_op jit(solution)/shard_map/ppermute | solution.py:21
  19.9 25.1 %collective-permute-start.3 = (bf16[256,256]{1,0:T(8,128)(2,1)S(1)}, bf16[256,256]{1,0:T(8,128)(2,1)S(1)}, u32[]{:S(2)}, u32[]{:S(2)}) collective-permute-start(bf16[256,256]{1,0:T(8,128)(2,1)S(1)} %constant_dynamic-update-slice_fusion), channel_id=1, source_target_pairs={{0,128},{32,160},{64,192},{96,224},{128,256},{160,288},{192,320},{... | collective-permute-start | bytes 393224 | tf_op jit(solution)/shard_map/ppermute | solution.py:17
  22.8 22.3 %collective-permute-start.4 = (bf16[256,256]{1,0:T(8,128)(2,1)S(1)}, bf16[256,256]{1,0:T(8,128)(2,1)S(1)}, u32[]{:S(2)}, u32[]{:S(2)}) collective-permute-start(bf16[256,256]{1,0:T(8,128)(2,1)S(1)} %constant_dynamic-update-slice_fusion), channel_id=1, source_target_pairs={{0,96},{32,128},{64,160},{96,192},{128,224},{160,256},{192,288},{2... | collective-permute-start | bytes 393224 | tf_op jit(solution)/shard_map/ppermute | solution.py:17
  27.4 17.7 %collective-permute-start.5 = (bf16[256,256]{1,0:T(8,128)(2,1)S(1)}, bf16[256,256]{1,0:T(8,128)(2,1)S(1)}, u32[]{:S(2)}, u32[]{:S(2)}) collective-permute-start(bf16[256,256]{1,0:T(8,128)(2,1)S(1)} %constant_dynamic-update-slice_fusion), channel_id=1, source_target_pairs={{0,64},{32,96},{64,128},{96,160},{128,192},{160,224},{192,256},{22... | collective-permute-start | bytes 393224 | tf_op jit(solution)/shard_map/ppermute | solution.py:17
  30.6 14.5 %collective-permute-start.6 = (bf16[256,256]{1,0:T(8,128)(2,1)S(1)}, bf16[256,256]{1,0:T(8,128)(2,1)S(1)}, u32[]{:S(2)}, u32[]{:S(2)}) collective-permute-start(bf16[256,256]{1,0:T(8,128)(2,1)S(1)} %constant_dynamic-update-slice_fusion), channel_id=1, source_target_pairs={{0,32},{32,64},{64,96},{96,128},{128,160},{160,192},{192,224},{224... | collective-permute-start | bytes 393224 | tf_op jit(solution)/shard_map/ppermute | solution.py:17
  33.4 14.6 %collective-permute-start.2 = (bf16[256,168]{0,1:T(8,128)(2,1)S(1)}, bf16[256,168]{0,1:T(8,128)(2,1)S(1)}, u32[]{:S(2)}, u32[]{:S(2)}) collective-permute-start(bf16[256,168]{0,1:T(8,128)(2,1)S(1)} %collective-permute-done), channel_id=1, source_target_pairs={{0,8},{8,16},{16,24},{24,0},{1,9},{9,17},{17,25},{25,1},{2,10},{10... | collective-permute-start | bytes 258056 | tf_op jit(solution)/shard_map/ppermute | solution.py:21
  48.0 9.9 %collective-permute-start.7 = (bf16[4,256,168]{1,2,0:T(8,128)(2,1)S(1)}, bf16[4,256,168]{1,2,0:T(8,128)(2,1)S(1)}, u32[]{:S(2)}, u32[]{:S(2)}) collective-permute-start(bf16[4,256,168]{1,2,0:T(8,128)(2,1)S(1)} %bitcast_dynamic-update-slice_fusion.6), channel_id=1, source_target_pairs={{0,2},{2,4},{4,6},{6,0},{1,3},{3,5},{5,7},{7,1},{8,10},{10,12},{12... | collective-permute-start | bytes 1032200 | tf_op jit(solution)/shard_map/ppermute | solution.py:21
  51.2 9.6 %collective-permute-start.8 = (bf16[4,256,168]{1,2,0:T(8,128)(2,1)S(1)}, bf16[4,256,168]{1,2,0:T(8,128)(2,1)S(1)}, u32[]{:S(2)}, u32[]{:S(2)}) collective-permute-start(bf16[4,256,168]{1,2,0:T(8,128)(2,1)S(1)} %bitcast_dynamic-update-slice_fusion.6), channel_id=1, source_target_pairs={{0,4},{2,6},{4,0},{6,2},{1,5},{3,7},{5,1},{7,3},{8,12},{10,14},{12... | collective-permute-start | bytes 1032200 | tf_op jit(solution)/shard_map/ppermute | solution.py:21
  54.0 10.7 %collective-permute-start.9 = (bf16[4,256,168]{1,2,0:T(8,128)(2,1)S(1)}, bf16[4,256,168]{1,2,0:T(8,128)(2,1)S(1)}, u32[]{:S(2)}, u32[]{:S(2)}) collective-permute-start(bf16[4,256,168]{1,2,0:T(8,128)(2,1)S(1)} %bitcast_dynamic-update-slice_fusion.6), channel_id=1, source_target_pairs={{0,6},{2,0},{4,2},{6,4},{1,7},{3,1},{5,3},{7,5},{8,14},{10,8},{12,... | collective-permute-start | bytes 1032200 | tf_op jit(solution)/shard_map/ppermute | solution.py:21
  64.7 18.7 %collective-permute-start.10 = (bf16[4,4,256,168]{2,3,1,0:T(8,128)(2,1)S(1)}, bf16[4,4,256,168]{2,3,1,0:T(8,128)(2,1)}, u32[]{:S(2)}, u32[]{:S(2)}) collective-permute-start(bf16[4,4,256,168]{2,3,1,0:T(8,128)(2,1)S(1)} %bitcast_dynamic-update-slice_fusion.2), channel_id=1, source_target_pairs={{0,1},{1,0},{2,3},{3,2},{4,5},{5,4},{6,7},{7,6},{8,9},{9,8},{10,11... | collective-permute-start | bytes 4128776 | tf_op jit(solution)/shard_map/ppermute | solution.py:21
  88.6 23.6 %collective-permute-start.11 = (bf16[256,256]{0,1:T(8,128)(2,1)S(1)}, bf16[256,256]{0,1:T(8,128)(2,1)S(1)}, u32[]{:S(2)}, u32[]{:S(2)}) collective-permute-start(bf16[256,256]{0,1:T(8,128)(2,1)S(1)} %get-tuple-element.22), channel_id=1, source_target_pairs={{32,0},{64,32},{96,64},{128,96},{160,128},{192,160},{224,192},{256... | collective-permute-start | bytes 393224 | tf_op jit(solution)/shard_map/ppermute | solution.py:17
  99.1 13.1 %collective-permute-start.12 = (bf16[256,256]{0,1:T(8,128)(2,1)S(1)}, bf16[256,256]{0,1:T(8,128)(2,1)S(1)}, u32[]{:S(2)}, u32[]{:S(2)}) collective-permute-start(bf16[256,256]{0,1:T(8,128)(2,1)S(1)} %get-tuple-element.23), channel_id=1, source_target_pairs={{64,0},{96,32},{128,64},{160,96},{192,128},{224,160},{256,192},{28... | collective-permute-start | bytes 393224 | tf_op jit(solution)/shard_map/ppermute | solution.py:17
  102.1 11.0 %collective-permute-start.13 = (bf16[256,256]{0,1:T(8,128)(2,1)S(1)}, bf16[256,256]{0,1:T(8,128)(2,1)S(1)}, u32[]{:S(2)}, u32[]{:S(2)}) collective-permute-start(bf16[256,256]{0,1:T(8,128)(2,1)S(1)} %get-tuple-element.25), channel_id=1, source_target_pairs={{96,0},{128,32},{160,64},{192,96},{224,128},{256,160},{288,192},{3... | collective-permute-start | bytes 393224 | tf_op jit(solution)/shard_map/ppermute | solution.py:17
  109.0 6.4 %collective-permute-start.14 = (bf16[256,256]{0,1:T(8,128)(2,1)S(1)}, bf16[256,256]{0,1:T(8,128)(2,1)S(1)}, u32[]{:S(2)}, u32[]{:S(2)}) collective-permute-start(bf16[256,256]{0,1:T(8,128)(2,1)S(1)} %get-tuple-element.24), channel_id=1, source_target_pairs={{128,0},{160,32},{192,64},{224,96},{256,128},{288,160},{320,192},{... | collective-permute-start | bytes 393224 | tf_op jit(solution)/shard_map/ppermute | solution.py:17
  116.6 6.3 %collective-permute-start.15 = (bf16[4,4,168,256]{3,2,0,1:T(8,128)(2,1)S(1)}, bf16[4,4,168,256]{3,2,0,1:T(8,128)(2,1)}, u32[]{:S(2)}, u32[]{:S(2)}) collective-permute-start(bf16[4,4,168,256]{3,2,0,1:T(8,128)(2,1)S(1)} %copy.18), channel_id=1, source_target_pairs={{0,1},{1,0},{2,3},{3,2},{4,5},{5,4},{6,7},{7,6},{8,9},{9,8},{10,11... | collective-permute-start | bytes 4128776 | tf_op jit(solution)/shard_map/ppermute | solution.py:21
  124.7 11.2 %collective-permute-start.16 = (bf16[4,168,256]{2,1,0:T(8,128)(2,1)S(1)}, bf16[4,168,256]{2,1,0:T(8,128)(2,1)S(1)}, u32[]{:S(2)}, u32[]{:S(2)}) collective-permute-start(bf16[4,168,256]{2,1,0:T(8,128)(2,1)S(1)} %get-tuple-element.11), channel_id=1, source_target_pairs={{0,2},{2,4},{4,6},{6,0},{1,3},{3,5},{5,7},{7,1},{8,10},{10,12},{12... | collective-permute-start | bytes 1032200 | tf_op jit(solution)/shard_map/ppermute | solution.py:21
  127.0 12.4 %collective-permute-start.17 = (bf16[4,168,256]{2,1,0:T(8,128)(2,1)S(1)}, bf16[4,168,256]{2,1,0:T(8,128)(2,1)S(1)}, u32[]{:S(2)}, u32[]{:S(2)}) collective-permute-start(bf16[4,168,256]{2,1,0:T(8,128)(2,1)S(1)} %get-tuple-element.13), channel_id=1, source_target_pairs={{0,4},{2,6},{4,0},{6,2},{1,5},{3,7},{5,1},{7,3},{8,12},{10,14},{12... | collective-permute-start | bytes 1032200 | tf_op jit(solution)/shard_map/ppermute | solution.py:21
  129.7 18.0 %collective-permute-start.18 = (bf16[4,168,256]{2,1,0:T(8,128)(2,1)S(1)}, bf16[4,168,256]{2,1,0:T(8,128)(2,1)S(1)}, u32[]{:S(2)}, u32[]{:S(2)}) collective-permute-start(bf16[4,168,256]{2,1,0:T(8,128)(2,1)S(1)} %get-tuple-element.12), channel_id=1, source_target_pairs={{0,6},{2,0},{4,2},{6,4},{1,7},{3,1},{5,3},{7,5},{8,14},{10,8},{12,... | collective-permute-start | bytes 1032200 | tf_op jit(solution)/shard_map/ppermute | solution.py:21
  148.0 27.4 %collective-permute-start.19 = (bf16[168,256]{1,0:T(8,128)(2,1)S(1)}, bf16[168,256]{1,0:T(8,128)(2,1)S(1)}, u32[]{:S(2)}, u32[]{:S(2)}) collective-permute-start(bf16[168,256]{1,0:T(8,128)(2,1)S(1)} %get-tuple-element.20), channel_id=1, source_target_pairs={{0,8},{8,16},{16,24},{24,0},{1,9},{9,17},{17,25},{25,1},{2,10},{10... | collective-permute-start | bytes 258056 | tf_op jit(solution)/shard_map/ppermute | solution.py:21
  161.0 25.5 %collective-permute-start.21 = (bf16[168,256]{1,0:T(8,128)(2,1)S(1)}, bf16[168,256]{1,0:T(8,128)(2,1)S(1)}, u32[]{:S(2)}, u32[]{:S(2)}) collective-permute-start(bf16[168,256]{1,0:T(8,128)(2,1)S(1)} %get-tuple-element.21), channel_id=1, source_target_pairs={{0,24},{8,0},{16,8},{24,16},{1,25},{9,1},{17,9},{25,17},{2,26},{10... | collective-permute-start | bytes 258056 | tf_op jit(solution)/shard_map/ppermute | solution.py:21
  175.3 23.5 %collective-permute-start.20 = (bf16[168,256]{1,0:T(8,128)(2,1)S(1)}, bf16[168,256]{1,0:T(8,128)(2,1)S(1)}, u32[]{:S(2)}, u32[]{:S(2)}) collective-permute-start(bf16[168,256]{1,0:T(8,128)(2,1)S(1)} %fusion.28), channel_id=1, source_target_pairs={{0,8},{8,16},{16,24},{24,0},{1,9},{9,17},{17,25},{25,1},{2,10},{10... | collective-permute-start | bytes 258056 | tf_op jit(solution)/shard_map/ppermute | solution.py:21
  (8 other events, 58.4 us)

commit v11 on v10

--- a/solution.py
+++ b/solution.py
@@ -158,7 +158,7 @@
         keep = project(core_index)
         sent = shift(project((core_index + 1) % n_core), "core", n_core, 1)
         part = keep.astype(jnp.float32) + sent.astype(jnp.float32)
-        part = scatter_axis(part, "x", n_x, 1)
+        part = scatter_axis(part, "x", n_x, 1, relay=True)
         part = scatter_axis(part, "zhi", n_zhi, 0, relay=True)
         return part.T.astype(jnp.bfloat16)
 

time: 201 us -> 202 us (level)
  the two profiles are of different devices: /device:TPU:195 before, /device:TPU:193 now
where the time goes in v11:
time: 202 us; the launch traced here: 201 us
  starting transfers between devices  134 us (66%)
  waiting for transfers between devices  40.1 us (20%)
  local copies, waits for them, and re-layouts  12.8 us (6%)
  other arithmetic  6.81 us (3%)
  matrix products  6.17 us (3%)
    ppermute x14, starting transfers between devices, shift(): lax.ppermute(block, axis, [(i, (i + step) % size) for i in range(size)])  99.1 us
    ppermute x14, waiting for transfers between devices, shift(): lax.ppermute(block, axis, [(i, (i + step) % size) for i in range(size)])  36.9 us
    ppermute x8, starting transfers between devices, from_behind(): return lax.ppermute(block, axis, route)  35.1 us
    unnamed x27, local copies, waits for them, and re-layouts  5.14 us
    dot_general x8, matrix products, dot_rows(): lax.dot_general(left, right, (((1,), (1,)), ((), ())), preferred_element_...  4.11 us
  transfers between devices with their start and end apart: 22, of which 9 were waited for; matrix products, arithmetic and copies ran while one was open for 7% of the time, Pallas kernels for 0%

profile of v11, /device:TPU:193, one launch (start us, length us, event | category | flops | bytes accessed | tf_op | source)
XLA Modules:
  0.0 200.9 jit_solution(12412545006059094322)
XLA Ops:
  0.0 15.6 %collective-permute-start = (bf16[256,168]{0,1:T(8,128)(2,1)}, bf16[256,168]{0,1:T(8,128)(2,1)S(1)}, u32[]{:S(2)}, u32[]{:S(2)}) collective-permute-start(bf16[256,168]{0,1:T(8,128)(2,1)} %param.11), channel_id=1, source_target_pairs={{0,8},{8,16},{16,24},{24,0},{1,9},{9,17},{17,25},{25,1},{2,10},{10... | collective-permute-start | bytes 258056 | tf_op jit(solution)/shard_map/ppermute | solution.py:21
  15.6 2.6 %collective-permute-start.1 = (bf16[256,168]{0,1:T(8,128)(2,1)}, bf16[256,168]{0,1:T(8,128)(2,1)S(1)}, u32[]{:S(2)}, u32[]{:S(2)}) collective-permute-start(bf16[256,168]{0,1:T(8,128)(2,1)} %param.11), channel_id=1, source_target_pairs={{0,24},{8,0},{16,8},{24,16},{1,25},{9,1},{17,9},{25,17},{2,26},{10... | collective-permute-start | bytes 258056 | tf_op jit(solution)/shard_map/ppermute | solution.py:21
  19.9 2.9 %collective-permute-start.3 = (bf16[256,256]{1,0:T(8,128)(2,1)S(1)}, bf16[256,256]{1,0:T(8,128)(2,1)S(1)}, u32[]{:S(2)}, u32[]{:S(2)}) collective-permute-start(bf16[256,256]{1,0:T(8,128)(2,1)S(1)} %constant_dynamic-update-slice_fusion), channel_id=1, source_target_pairs={{0,128},{32,160},{64,192},{96,224},{128,256},{160,288},{192,320},{... | collective-permute-start | bytes 393224 | tf_op jit(solution)/shard_map/ppermute | solution.py:17
  22.8 4.6 %collective-permute-start.4 = (bf16[256,256]{1,0:T(8,128)(2,1)S(1)}, bf16[256,256]{1,0:T(8,128)(2,1)S(1)}, u32[]{:S(2)}, u32[]{:S(2)}) collective-permute-start(bf16[256,256]{1,0:T(8,128)(2,1)S(1)} %constant_dynamic-update-slice_fusion), channel_id=1, source_target_pairs={{0,96},{32,128},{64,160},{96,192},{128,224},{160,256},{192,288},{2... | collective-permute-start | bytes 393224 | tf_op jit(solution)/shard_map/ppermute | solution.py:17
  30.6 2.8 %collective-permute-start.6 = (bf16[256,256]{1,0:T(8,128)(2,1)S(1)}, bf16[256,256]{1,0:T(8,128)(2,1)S(1)}, u32[]{:S(2)}, u32[]{:S(2)}) collective-permute-start(bf16[256,256]{1,0:T(8,128)(2,1)S(1)} %constant_dynamic-update-slice_fusion), channel_id=1, source_target_pairs={{0,32},{32,64},{64,96},{96,128},{128,160},{160,192},{192,224},{224... | collective-permute-start | bytes 393224 | tf_op jit(solution)/shard_map/ppermute | solution.py:17
  33.4 11.6 %collective-permute-start.2 = (bf16[256,168]{0,1:T(8,128)(2,1)S(1)}, bf16[256,168]{0,1:T(8,128)(2,1)S(1)}, u32[]{:S(2)}, u32[]{:S(2)}) collective-permute-start(bf16[256,168]{0,1:T(8,128)(2,1)S(1)} %collective-permute-done), channel_id=1, source_target_pairs={{0,8},{8,16},{16,24},{24,0},{1,9},{9,17},{17,25},{25,1},{2,10},{10... | collective-permute-start | bytes 258056 | tf_op jit(solution)/shard_map/ppermute | solution.py:21
  48.0 3.1 %collective-permute-start.7 = (bf16[4,256,168]{1,2,0:T(8,128)(2,1)S(1)}, bf16[4,256,168]{1,2,0:T(8,128)(2,1)S(1)}, u32[]{:S(2)}, u32[]{:S(2)}) collective-permute-start(bf16[4,256,168]{1,2,0:T(8,128)(2,1)S(1)} %bitcast_dynamic-update-slice_fusion.6), channel_id=1, source_target_pairs={{0,2},{2,4},{4,6},{6,0},{1,3},{3,5},{5,7},{7,1},{8,10},{10,12},{12... | collective-permute-start | bytes 1032200 | tf_op jit(solution)/shard_map/ppermute | solution.py:21
  51.2 4.4 %collective-permute-start.8 = (bf16[4,256,168]{1,2,0:T(8,128)(2,1)S(1)}, bf16[4,256,168]{1,2,0:T(8,128)(2,1)S(1)}, u32[]{:S(2)}, u32[]{:S(2)}) collective-permute-start(bf16[4,256,168]{1,2,0:T(8,128)(2,1)S(1)} %bitcast_dynamic-update-slice_fusion.6), channel_id=1, source_target_pairs={{0,4},{2,6},{4,0},{6,2},{1,5},{3,7},{5,1},{7,3},{8,12},{10,14},{12... | collective-permute-start | bytes 1032200 | tf_op jit(solution)/shard_map/ppermute | solution.py:21
  55.6 3.1 %collective-permute-start.9 = (bf16[4,256,168]{1,2,0:T(8,128)(2,1)S(1)}, bf16[4,256,168]{1,2,0:T(8,128)(2,1)S(1)}, u32[]{:S(2)}, u32[]{:S(2)}) collective-permute-start(bf16[4,256,168]{1,2,0:T(8,128)(2,1)S(1)} %bitcast_dynamic-update-slice_fusion.6), channel_id=1, source_target_pairs={{0,6},{2,0},{4,2},{6,4},{1,7},{3,1},{5,3},{7,5},{8,14},{10,8},{12,... | collective-permute-start | bytes 1032200 | tf_op jit(solution)/shard_map/ppermute | solution.py:21
  58.9 3.1 %collective-permute-done.8 = bf16[4,256,168]{1,2,0:T(8,128)(2,1)S(1)} collective-permute-done((bf16[4,256,168]{1,2,0:T(8,128)(2,1)S(1)}, bf16[4,256,168]{1,2,0:T(8,128)(2,1)S(1)}, u32[]{:S(2)}, u32[]{:S(2)}) %collective-permute-start.8) | collective-permute-done | bytes 344096 | tf_op jit(solution)/shard_map/ppermute | solution.py:21
  63.9 12.6 %collective-permute-start.10 = (bf16[4,4,256,168]{2,3,1,0:T(8,128)(2,1)S(1)}, bf16[4,4,256,168]{2,3,1,0:T(8,128)(2,1)}, u32[]{:S(2)}, u32[]{:S(2)}) collective-permute-start(bf16[4,4,256,168]{2,3,1,0:T(8,128)(2,1)S(1)} %bitcast_dynamic-update-slice_fusion.2), channel_id=1, source_target_pairs={{0,1},{1,0},{2,3},{3,2},{4,5},{5,4},{6,7},{7,6},{8,9},{9,8},{10,11... | collective-permute-start | bytes 4128776 | tf_op jit(solution)/shard_map/ppermute | solution.py:21
  76.5 2.5 %copy.14 = bf16[128,5376]{0,1:T(8,128)(2,1)} copy(bf16[128,5376]{1,0:T(8,128)(2,1)} %param.12) | data formatting | bytes 2752512 | tf_op args[4]
  88.1 10.5 %collective-permute-start.11 = (bf16[256,256]{0,1:T(8,128)(2,1)S(1)}, bf16[256,256]{0,1:T(8,128)(2,1)S(1)}, u32[]{:S(2)}, u32[]{:S(2)}) collective-permute-start(bf16[256,256]{0,1:T(8,128)(2,1)S(1)} %get-tuple-element.21), channel_id=1, source_target_pairs={{32,0},{64,32},{96,64},{128,96},{160,128},{192,160},{224,192},{256... | collective-permute-start | bytes 393224 | tf_op jit(solution)/shard_map/ppermute | solution.py:17
  98.6 3.0 %collective-permute-start.12 = (bf16[256,256]{0,1:T(8,128)(2,1)S(1)}, bf16[256,256]{0,1:T(8,128)(2,1)S(1)}, u32[]{:S(2)}, u32[]{:S(2)}) collective-permute-start(bf16[256,256]{0,1:T(8,128)(2,1)S(1)} %get-tuple-element.22), channel_id=1, source_target_pairs={{64,0},{96,32},{128,64},{160,96},{192,128},{224,160},{256,192},{28... | collective-permute-start | bytes 393224 | tf_op jit(solution)/shard_map/ppermute | solution.py:17
  101.6 6.6 %collective-permute-start.13 = (bf16[256,256]{0,1:T(8,128)(2,1)S(1)}, bf16[256,256]{0,1:T(8,128)(2,1)S(1)}, u32[]{:S(2)}, u32[]{:S(2)}) collective-permute-start(bf16[256,256]{0,1:T(8,128)(2,1)S(1)} %get-tuple-element.24), channel_id=1, source_target_pairs={{96,0},{128,32},{160,64},{192,96},{224,128},{256,160},{288,192},{3... | collective-permute-start | bytes 393224 | tf_op jit(solution)/shard_map/ppermute | solution.py:17
  108.1 2.7 %collective-permute-start.14 = (bf16[256,256]{0,1:T(8,128)(2,1)S(1)}, bf16[256,256]{0,1:T(8,128)(2,1)S(1)}, u32[]{:S(2)}, u32[]{:S(2)}) collective-permute-start(bf16[256,256]{0,1:T(8,128)(2,1)S(1)} %get-tuple-element.23), channel_id=1, source_target_pairs={{128,0},{160,32},{192,64},{224,96},{256,128},{288,160},{320,192},{... | collective-permute-start | bytes 393224 | tf_op jit(solution)/shard_map/ppermute | solution.py:17
  115.7 3.5 %collective-permute-start.15 = (bf16[4,4,168,256]{3,2,0,1:T(8,128)(2,1)S(1)}, bf16[4,4,168,256]{3,2,0,1:T(8,128)(2,1)}, u32[]{:S(2)}, u32[]{:S(2)}) collective-permute-start(bf16[4,4,168,256]{3,2,0,1:T(8,128)(2,1)S(1)} %copy.18), channel_id=1, source_target_pairs={{0,1},{1,0},{2,3},{3,2},{4,5},{5,4},{6,7},{7,6},{8,9},{9,8},{10,11... | collective-permute-start | bytes 4128776 | tf_op jit(solution)/shard_map/ppermute | solution.py:21
  123.8 4.0 %collective-permute-start.16 = (bf16[4,168,256]{2,1,0:T(8,128)(2,1)S(1)}, bf16[4,168,256]{2,1,0:T(8,128)(2,1)}, u32[]{:S(2)}, u32[]{:S(2)}) collective-permute-start(bf16[4,168,256]{2,1,0:T(8,128)(2,1)S(1)} %get-tuple-element.11), channel_id=1, source_target_pairs={{0,2},{2,4},{4,6},{6,0},{1,3},{3,5},{5,7},{7,1},{8,10},{10,12},{12... | collective-permute-start | bytes 1032200 | tf_op jit(solution)/shard_map/ppermute | solution.py:21
  130.4 6.0 %collective-permute-done.16 = bf16[4,168,256]{2,1,0:T(8,128)(2,1)} collective-permute-done((bf16[4,168,256]{2,1,0:T(8,128)(2,1)S(1)}, bf16[4,168,256]{2,1,0:T(8,128)(2,1)}, u32[]{:S(2)}, u32[]{:S(2)}) %collective-permute-start.16) | collective-permute-done | bytes 344096 | tf_op jit(solution)/shard_map/ppermute | solution.py:21
  137.4 2.8 %collective-permute-start.17 = (bf16[4,168,256]{2,1,0:T(8,128)(2,1)S(1)}, bf16[4,168,256]{2,1,0:T(8,128)(2,1)}, u32[]{:S(2)}, u32[]{:S(2)}) collective-permute-start(bf16[4,168,256]{2,1,0:T(8,128)(2,1)S(1)} %fusion.18), channel_id=1, source_target_pairs={{0,2},{2,4},{4,6},{6,0},{1,3},{3,5},{5,7},{7,1},{8,10},{10,12},{12... | collective-permute-start | bytes 1032200 | tf_op jit(solution)/shard_map/ppermute | solution.py:21
  140.2 8.7 %collective-permute-done.17 = bf16[4,168,256]{2,1,0:T(8,128)(2,1)} collective-permute-done((bf16[4,168,256]{2,1,0:T(8,128)(2,1)S(1)}, bf16[4,168,256]{2,1,0:T(8,128)(2,1)}, u32[]{:S(2)}, u32[]{:S(2)}) %collective-permute-start.17) | collective-permute-done | bytes 344096 | tf_op jit(solution)/shard_map/ppermute | solution.py:21
  150.2 13.0 %collective-permute-start.19 = (bf16[168,256]{1,0:T(8,128)(2,1)S(1)}, bf16[168,256]{1,0:T(8,128)(2,1)S(1)}, u32[]{:S(2)}, u32[]{:S(2)}) collective-permute-start(bf16[168,256]{1,0:T(8,128)(2,1)S(1)} %get-tuple-element.19), channel_id=1, source_target_pairs={{0,8},{8,16},{16,24},{24,0},{1,9},{9,17},{17,25},{25,1},{2,10},{10... | collective-permute-start | bytes 258056 | tf_op jit(solution)/shard_map/ppermute | solution.py:21
  166.3 18.6 %collective-permute-start.20 = (bf16[168,256]{1,0:T(8,128)(2,1)S(1)}, bf16[168,256]{1,0:T(8,128)(2,1)S(1)}, u32[]{:S(2)}, u32[]{:S(2)}) collective-permute-start(bf16[168,256]{1,0:T(8,128)(2,1)S(1)} %fusion.27), channel_id=1, source_target_pairs={{0,8},{8,16},{16,24},{24,0},{1,9},{9,17},{17,25},{25,1},{2,10},{10... | collective-permute-start | bytes 258056 | tf_op jit(solution)/shard_map/ppermute | solution.py:21
  184.9 15.3 %collective-permute-done.20 = bf16[168,256]{1,0:T(8,128)(2,1)S(1)} collective-permute-done((bf16[168,256]{1,0:T(8,128)(2,1)S(1)}, bf16[168,256]{1,0:T(8,128)(2,1)S(1)}, u32[]{:S(2)}, u32[]{:S(2)}) %collective-permute-start.20) | collective-permute-done | bytes 86048 | tf_op jit(solution)/shard_map/ppermute | solution.py:21
  (92 shorter events, 36.8 us)
Async XLA Ops:
  0.0 45.2 %copy-start = (bf16[256,128]{1,0:T(8,128)(2,1)S(1)}, bf16[256,128]{1,0:T(8,128)(2,1)}, u32[]{:S(2)}) copy-start(bf16[256,128]{1,0:T(8,128)(2,1)} %param.8) | copy-start | bytes 196612
  0.0 45.2 %copy-start.9 = (bf16[256,128]{1,0:T(8,128)(2,1)S(1)}, bf16[256,128]{1,0:T(8,128)(2,1)}, u32[]{:S(2)}) copy-start(bf16[256,128]{1,0:T(8,128)(2,1)} %param.10) | copy-start | bytes 196612
  0.0 30.6 %collective-permute-start = (bf16[256,168]{0,1:T(8,128)(2,1)}, bf16[256,168]{0,1:T(8,128)(2,1)S(1)}, u32[]{:S(2)}, u32[]{:S(2)}) collective-permute-start(bf16[256,168]{0,1:T(8,128)(2,1)} %param.11), channel_id=1, source_target_pairs={{0,8},{8,16},{16,24},{24,0},{1,9},{9,17},{17,25},{25,1},{2,10},{10... | collective-permute-start | bytes 258056 | tf_op jit(solution)/shard_map/ppermute | solution.py:21
  15.6 17.8 %collective-permute-start.1 = (bf16[256,168]{0,1:T(8,128)(2,1)}, bf16[256,168]{0,1:T(8,128)(2,1)S(1)}, u32[]{:S(2)}, u32[]{:S(2)}) collective-permute-start(bf16[256,168]{0,1:T(8,128)(2,1)} %param.11), channel_id=1, source_target_pairs={{0,24},{8,0},{16,8},{24,16},{1,25},{9,1},{17,9},{25,17},{2,26},{10... | collective-permute-start | bytes 258056 | tf_op jit(solution)/shard_map/ppermute | solution.py:21
  19.9 25.1 %collective-permute-start.3 = (bf16[256,256]{1,0:T(8,128)(2,1)S(1)}, bf16[256,256]{1,0:T(8,128)(2,1)S(1)}, u32[]{:S(2)}, u32[]{:S(2)}) collective-permute-start(bf16[256,256]{1,0:T(8,128)(2,1)S(1)} %constant_dynamic-update-slice_fusion), channel_id=1, source_target_pairs={{0,128},{32,160},{64,192},{96,224},{128,256},{160,288},{192,320},{... | collective-permute-start | bytes 393224 | tf_op jit(solution)/shard_map/ppermute | solution.py:17
  22.8 22.3 %collective-permute-start.4 = (bf16[256,256]{1,0:T(8,128)(2,1)S(1)}, bf16[256,256]{1,0:T(8,128)(2,1)S(1)}, u32[]{:S(2)}, u32[]{:S(2)}) collective-permute-start(bf16[256,256]{1,0:T(8,128)(2,1)S(1)} %constant_dynamic-update-slice_fusion), channel_id=1, source_target_pairs={{0,96},{32,128},{64,160},{96,192},{128,224},{160,256},{192,288},{2... | collective-permute-start | bytes 393224 | tf_op jit(solution)/shard_map/ppermute | solution.py:17
  27.4 17.7 %collective-permute-start.5 = (bf16[256,256]{1,0:T(8,128)(2,1)S(1)}, bf16[256,256]{1,0:T(8,128)(2,1)S(1)}, u32[]{:S(2)}, u32[]{:S(2)}) collective-permute-start(bf16[256,256]{1,0:T(8,128)(2,1)S(1)} %constant_dynamic-update-slice_fusion), channel_id=1, source_target_pairs={{0,64},{32,96},{64,128},{96,160},{128,192},{160,224},{192,256},{22... | collective-permute-start | bytes 393224 | tf_op jit(solution)/shard_map/ppermute | solution.py:17
  30.6 14.5 %collective-permute-start.6 = (bf16[256,256]{1,0:T(8,128)(2,1)S(1)}, bf16[256,256]{1,0:T(8,128)(2,1)S(1)}, u32[]{:S(2)}, u32[]{:S(2)}) collective-permute-start(bf16[256,256]{1,0:T(8,128)(2,1)S(1)} %constant_dynamic-update-slice_fusion), channel_id=1, source_target_pairs={{0,32},{32,64},{64,96},{96,128},{128,160},{160,192},{192,224},{224... | collective-permute-start | bytes 393224 | tf_op jit(solution)/shard_map/ppermute | solution.py:17
  33.4 14.6 %collective-permute-start.2 = (bf16[256,168]{0,1:T(8,128)(2,1)S(1)}, bf16[256,168]{0,1:T(8,128)(2,1)S(1)}, u32[]{:S(2)}, u32[]{:S(2)}) collective-permute-start(bf16[256,168]{0,1:T(8,128)(2,1)S(1)} %collective-permute-done), channel_id=1, source_target_pairs={{0,8},{8,16},{16,24},{24,0},{1,9},{9,17},{17,25},{25,1},{2,10},{10... | collective-permute-start | bytes 258056 | tf_op jit(solution)/shard_map/ppermute | solution.py:21
  48.0 10.8 %collective-permute-start.7 = (bf16[4,256,168]{1,2,0:T(8,128)(2,1)S(1)}, bf16[4,256,168]{1,2,0:T(8,128)(2,1)S(1)}, u32[]{:S(2)}, u32[]{:S(2)}) collective-permute-start(bf16[4,256,168]{1,2,0:T(8,128)(2,1)S(1)} %bitcast_dynamic-update-slice_fusion.6), channel_id=1, source_target_pairs={{0,2},{2,4},{4,6},{6,0},{1,3},{3,5},{5,7},{7,1},{8,10},{10,12},{12... | collective-permute-start | bytes 1032200 | tf_op jit(solution)/shard_map/ppermute | solution.py:21
  51.2 10.7 %collective-permute-start.8 = (bf16[4,256,168]{1,2,0:T(8,128)(2,1)S(1)}, bf16[4,256,168]{1,2,0:T(8,128)(2,1)S(1)}, u32[]{:S(2)}, u32[]{:S(2)}) collective-permute-start(bf16[4,256,168]{1,2,0:T(8,128)(2,1)S(1)} %bitcast_dynamic-update-slice_fusion.6), channel_id=1, source_target_pairs={{0,4},{2,6},{4,0},{6,2},{1,5},{3,7},{5,1},{7,3},{8,12},{10,14},{12... | collective-permute-start | bytes 1032200 | tf_op jit(solution)/shard_map/ppermute | solution.py:21
  55.6 8.3 %collective-permute-start.9 = (bf16[4,256,168]{1,2,0:T(8,128)(2,1)S(1)}, bf16[4,256,168]{1,2,0:T(8,128)(2,1)S(1)}, u32[]{:S(2)}, u32[]{:S(2)}) collective-permute-start(bf16[4,256,168]{1,2,0:T(8,128)(2,1)S(1)} %bitcast_dynamic-update-slice_fusion.6), channel_id=1, source_target_pairs={{0,6},{2,0},{4,2},{6,4},{1,7},{3,1},{5,3},{7,5},{8,14},{10,8},{12,... | collective-permute-start | bytes 1032200 | tf_op jit(solution)/shard_map/ppermute | solution.py:21
  63.9 18.9 %collective-permute-start.10 = (bf16[4,4,256,168]{2,3,1,0:T(8,128)(2,1)S(1)}, bf16[4,4,256,168]{2,3,1,0:T(8,128)(2,1)}, u32[]{:S(2)}, u32[]{:S(2)}) collective-permute-start(bf16[4,4,256,168]{2,3,1,0:T(8,128)(2,1)S(1)} %bitcast_dynamic-update-slice_fusion.2), channel_id=1, source_target_pairs={{0,1},{1,0},{2,3},{3,2},{4,5},{5,4},{6,7},{7,6},{8,9},{9,8},{10,11... | collective-permute-start | bytes 4128776 | tf_op jit(solution)/shard_map/ppermute | solution.py:21
  88.1 23.3 %collective-permute-start.11 = (bf16[256,256]{0,1:T(8,128)(2,1)S(1)}, bf16[256,256]{0,1:T(8,128)(2,1)S(1)}, u32[]{:S(2)}, u32[]{:S(2)}) collective-permute-start(bf16[256,256]{0,1:T(8,128)(2,1)S(1)} %get-tuple-element.21), channel_id=1, source_target_pairs={{32,0},{64,32},{96,64},{128,96},{160,128},{192,160},{224,192},{256... | collective-permute-start | bytes 393224 | tf_op jit(solution)/shard_map/ppermute | solution.py:17
  98.6 12.8 %collective-permute-start.12 = (bf16[256,256]{0,1:T(8,128)(2,1)S(1)}, bf16[256,256]{0,1:T(8,128)(2,1)S(1)}, u32[]{:S(2)}, u32[]{:S(2)}) collective-permute-start(bf16[256,256]{0,1:T(8,128)(2,1)S(1)} %get-tuple-element.22), channel_id=1, source_target_pairs={{64,0},{96,32},{128,64},{160,96},{192,128},{224,160},{256,192},{28... | collective-permute-start | bytes 393224 | tf_op jit(solution)/shard_map/ppermute | solution.py:17
  101.6 11.1 %collective-permute-start.13 = (bf16[256,256]{0,1:T(8,128)(2,1)S(1)}, bf16[256,256]{0,1:T(8,128)(2,1)S(1)}, u32[]{:S(2)}, u32[]{:S(2)}) collective-permute-start(bf16[256,256]{0,1:T(8,128)(2,1)S(1)} %get-tuple-element.24), channel_id=1, source_target_pairs={{96,0},{128,32},{160,64},{192,96},{224,128},{256,160},{288,192},{3... | collective-permute-start | bytes 393224 | tf_op jit(solution)/shard_map/ppermute | solution.py:17
  108.1 6.4 %collective-permute-start.14 = (bf16[256,256]{0,1:T(8,128)(2,1)S(1)}, bf16[256,256]{0,1:T(8,128)(2,1)S(1)}, u32[]{:S(2)}, u32[]{:S(2)}) collective-permute-start(bf16[256,256]{0,1:T(8,128)(2,1)S(1)} %get-tuple-element.23), channel_id=1, source_target_pairs={{128,0},{160,32},{192,64},{224,96},{256,128},{288,160},{320,192},{... | collective-permute-start | bytes 393224 | tf_op jit(solution)/shard_map/ppermute | solution.py:17
  115.7 6.3 %collective-permute-start.15 = (bf16[4,4,168,256]{3,2,0,1:T(8,128)(2,1)S(1)}, bf16[4,4,168,256]{3,2,0,1:T(8,128)(2,1)}, u32[]{:S(2)}, u32[]{:S(2)}) collective-permute-start(bf16[4,4,168,256]{3,2,0,1:T(8,128)(2,1)S(1)} %copy.18), channel_id=1, source_target_pairs={{0,1},{1,0},{2,3},{3,2},{4,5},{5,4},{6,7},{7,6},{8,9},{9,8},{10,11... | collective-permute-start | bytes 4128776 | tf_op jit(solution)/shard_map/ppermute | solution.py:21
  123.8 12.5 %collective-permute-start.16 = (bf16[4,168,256]{2,1,0:T(8,128)(2,1)S(1)}, bf16[4,168,256]{2,1,0:T(8,128)(2,1)}, u32[]{:S(2)}, u32[]{:S(2)}) collective-permute-start(bf16[4,168,256]{2,1,0:T(8,128)(2,1)S(1)} %get-tuple-element.11), channel_id=1, source_target_pairs={{0,2},{2,4},{4,6},{6,0},{1,3},{3,5},{5,7},{7,1},{8,10},{10,12},{12... | collective-permute-start | bytes 1032200 | tf_op jit(solution)/shard_map/ppermute | solution.py:21
  127.9 12.3 %collective-permute-start.18 = (bf16[4,168,256]{2,1,0:T(8,128)(2,1)S(1)}, bf16[4,168,256]{2,1,0:T(8,128)(2,1)}, u32[]{:S(2)}, u32[]{:S(2)}) collective-permute-start(bf16[4,168,256]{2,1,0:T(8,128)(2,1)S(1)} %get-tuple-element.12), channel_id=1, source_target_pairs={{0,6},{2,0},{4,2},{6,4},{1,7},{3,1},{5,3},{7,5},{8,14},{10,8},{12,... | collective-permute-start | bytes 1032200 | tf_op jit(solution)/shard_map/ppermute | solution.py:21
  137.4 11.6 %collective-permute-start.17 = (bf16[4,168,256]{2,1,0:T(8,128)(2,1)S(1)}, bf16[4,168,256]{2,1,0:T(8,128)(2,1)}, u32[]{:S(2)}, u32[]{:S(2)}) collective-permute-start(bf16[4,168,256]{2,1,0:T(8,128)(2,1)S(1)} %fusion.18), channel_id=1, source_target_pairs={{0,2},{2,4},{4,6},{6,0},{1,3},{3,5},{5,7},{7,1},{8,10},{10,12},{12... | collective-permute-start | bytes 1032200 | tf_op jit(solution)/shard_map/ppermute | solution.py:21
  150.2 16.1 %collective-permute-start.19 = (bf16[168,256]{1,0:T(8,128)(2,1)S(1)}, bf16[168,256]{1,0:T(8,128)(2,1)S(1)}, u32[]{:S(2)}, u32[]{:S(2)}) collective-permute-start(bf16[168,256]{1,0:T(8,128)(2,1)S(1)} %get-tuple-element.19), channel_id=1, source_target_pairs={{0,8},{8,16},{16,24},{24,0},{1,9},{9,17},{17,25},{25,1},{2,10},{10... | collective-permute-start | bytes 258056 | tf_op jit(solution)/shard_map/ppermute | solution.py:21
  163.1 21.8 %collective-permute-start.21 = (bf16[168,256]{1,0:T(8,128)(2,1)S(1)}, bf16[168,256]{1,0:T(8,128)(2,1)S(1)}, u32[]{:S(2)}, u32[]{:S(2)}) collective-permute-start(bf16[168,256]{1,0:T(8,128)(2,1)S(1)} %get-tuple-element.20), channel_id=1, source_target_pairs={{0,24},{8,0},{16,8},{24,16},{1,25},{9,1},{17,9},{25,17},{2,26},{10... | collective-permute-start | bytes 258056 | tf_op jit(solution)/shard_map/ppermute | solution.py:21
  166.3 33.9 %collective-permute-start.20 = (bf16[168,256]{1,0:T(8,128)(2,1)S(1)}, bf16[168,256]{1,0:T(8,128)(2,1)S(1)}, u32[]{:S(2)}, u32[]{:S(2)}) collective-permute-start(bf16[168,256]{1,0:T(8,128)(2,1)S(1)} %fusion.27), channel_id=1, source_target_pairs={{0,8},{8,16},{16,24},{24,0},{1,9},{9,17},{17,25},{25,1},{2,10},{10... | collective-permute-start | bytes 258056 | tf_op jit(solution)/shard_map/ppermute | solution.py:21
  (8 other events, 58.4 us)

commit v12 on v10

--- a/solution.py
+++ b/solution.py
@@ -123,7 +123,7 @@
         query_start = seq_index * length
         probs = band_probs(query, kv_band[:, :dim], query_start, query_start - reach * length)
         stacked, kv_band, probs = lax.optimization_barrier((stacked, kv_band, probs))
-        stacked = gather_axis(stacked, "x", n_x)
+        stacked = gather_axis(stacked, "x", n_x, relay=True)
         stacked = gather_axis(stacked, "core", n_core)
         out_rows = w_out.reshape(w_out.shape[0], n_zhi, n_x, n_core, width)
         grad_heads = jnp.einsum(

time: 201 us -> 198 us (0.985)
  the two profiles are of different devices: /device:TPU:195 before, /device:TPU:199 now
where the time goes in v12:
time: 198 us
  starting transfers between devices  122 us (62%)
  waiting for transfers between devices  53.9 us (27%)
  local copies, waits for them, and re-layouts  11.1 us (6%)
  matrix products  6.17 us (3%)
  other arithmetic  3.38 us (2%)
    ppermute x14, starting transfers between devices, shift(): lax.ppermute(block, axis, [(i, (i + step) % size) for i in range(size)])  90.8 us
    ppermute x14, waiting for transfers between devices, shift(): lax.ppermute(block, axis, [(i, (i + step) % size) for i in range(size)])  51 us
    ppermute x8, starting transfers between devices, from_behind(): return lax.ppermute(block, axis, route)  31.5 us
    unnamed x23, local copies, waits for them, and re-layouts  5.15 us
    dot_general x8, matrix products, dot_rows(): lax.dot_general(left, right, (((1,), (1,)), ((), ())), preferred_element_...  4.11 us
  transfers between devices with their start and end apart: 22, of which 9 were waited for; matrix products, arithmetic and copies ran while one was open for 6% of the time, Pallas kernels for 0%

profile of v12, /device:TPU:199, one launch (start us, length us, event | category | flops | bytes accessed | tf_op | source)
XLA Modules:
  0.0 197.5 jit_solution(812201956795707993)
XLA Ops:
  0.0 15.6 %collective-permute-start = (bf16[256,168]{0,1:T(8,128)(2,1)}, bf16[256,168]{0,1:T(8,128)(2,1)S(1)}, u32[]{:S(2)}, u32[]{:S(2)}) collective-permute-start(bf16[256,168]{0,1:T(8,128)(2,1)} %param.11), channel_id=1, source_target_pairs={{0,8},{8,16},{16,24},{24,0},{1,9},{9,17},{17,25},{25,1},{2,10},{10... | collective-permute-start | bytes 258056 | tf_op jit(solution)/shard_map/ppermute | solution.py:21
  15.6 2.6 %collective-permute-start.1 = (bf16[256,168]{0,1:T(8,128)(2,1)}, bf16[256,168]{0,1:T(8,128)(2,1)S(1)}, u32[]{:S(2)}, u32[]{:S(2)}) collective-permute-start(bf16[256,168]{0,1:T(8,128)(2,1)} %param.11), channel_id=1, source_target_pairs={{0,24},{8,0},{16,8},{24,16},{1,25},{9,1},{17,9},{25,17},{2,26},{10... | collective-permute-start | bytes 258056 | tf_op jit(solution)/shard_map/ppermute | solution.py:21
  19.9 2.9 %collective-permute-start.3 = (bf16[256,256]{1,0:T(8,128)(2,1)S(1)}, bf16[256,256]{1,0:T(8,128)(2,1)S(1)}, u32[]{:S(2)}, u32[]{:S(2)}) collective-permute-start(bf16[256,256]{1,0:T(8,128)(2,1)S(1)} %constant_dynamic-update-slice_fusion), channel_id=1, source_target_pairs={{0,128},{32,160},{64,192},{96,224},{128,256},{160,288},{192,320},{... | collective-permute-start | bytes 393224 | tf_op jit(solution)/shard_map/ppermute | solution.py:17
  22.8 4.6 %collective-permute-start.4 = (bf16[256,256]{1,0:T(8,128)(2,1)S(1)}, bf16[256,256]{1,0:T(8,128)(2,1)S(1)}, u32[]{:S(2)}, u32[]{:S(2)}) collective-permute-start(bf16[256,256]{1,0:T(8,128)(2,1)S(1)} %constant_dynamic-update-slice_fusion), channel_id=1, source_target_pairs={{0,96},{32,128},{64,160},{96,192},{128,224},{160,256},{192,288},{2... | collective-permute-start | bytes 393224 | tf_op jit(solution)/shard_map/ppermute | solution.py:17
  30.6 2.8 %collective-permute-start.6 = (bf16[256,256]{1,0:T(8,128)(2,1)S(1)}, bf16[256,256]{1,0:T(8,128)(2,1)S(1)}, u32[]{:S(2)}, u32[]{:S(2)}) collective-permute-start(bf16[256,256]{1,0:T(8,128)(2,1)S(1)} %constant_dynamic-update-slice_fusion), channel_id=1, source_target_pairs={{0,32},{32,64},{64,96},{96,128},{128,160},{160,192},{192,224},{224... | collective-permute-start | bytes 393224 | tf_op jit(solution)/shard_map/ppermute | solution.py:17
  33.4 11.6 %collective-permute-start.2 = (bf16[256,168]{0,1:T(8,128)(2,1)S(1)}, bf16[256,168]{0,1:T(8,128)(2,1)S(1)}, u32[]{:S(2)}, u32[]{:S(2)}) collective-permute-start(bf16[256,168]{0,1:T(8,128)(2,1)S(1)} %collective-permute-done), channel_id=1, source_target_pairs={{0,8},{8,16},{16,24},{24,0},{1,9},{9,17},{17,25},{25,1},{2,10},{10... | collective-permute-start | bytes 258056 | tf_op jit(solution)/shard_map/ppermute | solution.py:21
  50.2 3.2 %collective-permute-start.8 = (bf16[4,256,168]{1,2,0:T(8,128)(2,1)S(1)}, bf16[4,256,168]{1,2,0:T(8,128)(2,1)S(1)}, u32[]{:S(2)}, u32[]{:S(2)}) collective-permute-start(bf16[4,256,168]{1,2,0:T(8,128)(2,1)S(1)} %bitcast_dynamic-update-slice_fusion.6), channel_id=1, source_target_pairs={{0,6},{2,0},{4,2},{6,4},{1,7},{3,1},{5,3},{7,5},{8,14},{10,8},{12,... | collective-permute-start | bytes 1032200 | tf_op jit(solution)/shard_map/ppermute | solution.py:21
  53.5 2.8 %collective-permute-done.7 = bf16[4,256,168]{1,2,0:T(8,128)(2,1)S(1)} collective-permute-done((bf16[4,256,168]{1,2,0:T(8,128)(2,1)S(1)}, bf16[4,256,168]{1,2,0:T(8,128)(2,1)S(1)}, u32[]{:S(2)}, u32[]{:S(2)}) %collective-permute-start.7) | collective-permute-done | bytes 344096 | tf_op jit(solution)/shard_map/ppermute | solution.py:21
  56.3 3.0 %collective-permute-start.9 = (bf16[4,256,168]{1,2,0:T(8,128)(2,1)S(1)}, bf16[4,256,168]{1,2,0:T(8,128)(2,1)S(1)}, u32[]{:S(2)}, u32[]{:S(2)}) collective-permute-start(bf16[4,256,168]{1,2,0:T(8,128)(2,1)S(1)} %collective-permute-done.7), channel_id=1, source_target_pairs={{0,2},{2,4},{4,6},{6,0},{1,3},{3,5},{5,7},{7,1},{8,10},{10,12},{12... | collective-permute-start | bytes 1032200 | tf_op jit(solution)/shard_map/ppermute | solution.py:21
  59.4 7.4 %collective-permute-done.9 = bf16[4,256,168]{1,2,0:T(8,128)(2,1)S(1)} collective-permute-done((bf16[4,256,168]{1,2,0:T(8,128)(2,1)S(1)}, bf16[4,256,168]{1,2,0:T(8,128)(2,1)S(1)}, u32[]{:S(2)}, u32[]{:S(2)}) %collective-permute-start.9) | collective-permute-done | bytes 344096 | tf_op jit(solution)/shard_map/ppermute | solution.py:21
  66.8 13.0 %collective-permute-start.10 = (bf16[4,4,256,168]{2,3,1,0:T(8,128)(2,1)S(1)}, bf16[4,4,256,168]{2,3,1,0:T(8,128)(2,1)}, u32[]{:S(2)}, u32[]{:S(2)}) collective-permute-start(bf16[4,4,256,168]{2,3,1,0:T(8,128)(2,1)S(1)} %bitcast_dynamic-update-slice_fusion.2), channel_id=1, source_target_pairs={{0,1},{1,0},{2,3},{3,2},{4,5},{5,4},{6,7},{7,6},{8,9},{9,8},{10,11... | collective-permute-start | bytes 4128776 | tf_op jit(solution)/shard_map/ppermute | solution.py:21
  79.9 2.5 %copy.14 = bf16[128,5376]{0,1:T(8,128)(2,1)} copy(bf16[128,5376]{1,0:T(8,128)(2,1)} %param.12) | data formatting | bytes 2752512 | tf_op args[4]
  90.4 8.1 %collective-permute-start.11 = (bf16[256,256]{0,1:T(8,128)(2,1)S(1)}, bf16[256,256]{0,1:T(8,128)(2,1)S(1)}, u32[]{:S(2)}, u32[]{:S(2)}) collective-permute-start(bf16[256,256]{0,1:T(8,128)(2,1)S(1)} %get-tuple-element.22), channel_id=1, source_target_pairs={{32,0},{64,32},{96,64},{128,96},{160,128},{192,160},{224,192},{256... | collective-permute-start | bytes 393224 | tf_op jit(solution)/shard_map/ppermute | solution.py:17
  98.5 3.0 %collective-permute-start.12 = (bf16[256,256]{0,1:T(8,128)(2,1)S(1)}, bf16[256,256]{0,1:T(8,128)(2,1)S(1)}, u32[]{:S(2)}, u32[]{:S(2)}) collective-permute-start(bf16[256,256]{0,1:T(8,128)(2,1)S(1)} %get-tuple-element.23), channel_id=1, source_target_pairs={{64,0},{96,32},{128,64},{160,96},{192,128},{224,160},{256,192},{28... | collective-permute-start | bytes 393224 | tf_op jit(solution)/shard_map/ppermute | solution.py:17
  101.5 5.0 %collective-permute-start.13 = (bf16[256,256]{0,1:T(8,128)(2,1)S(1)}, bf16[256,256]{0,1:T(8,128)(2,1)S(1)}, u32[]{:S(2)}, u32[]{:S(2)}) collective-permute-start(bf16[256,256]{0,1:T(8,128)(2,1)S(1)} %get-tuple-element.25), channel_id=1, source_target_pairs={{96,0},{128,32},{160,64},{192,96},{224,128},{256,160},{288,192},{3... | collective-permute-start | bytes 393224 | tf_op jit(solution)/shard_map/ppermute | solution.py:17
  106.5 3.0 %collective-permute-start.14 = (bf16[256,256]{0,1:T(8,128)(2,1)S(1)}, bf16[256,256]{0,1:T(8,128)(2,1)S(1)}, u32[]{:S(2)}, u32[]{:S(2)}) collective-permute-start(bf16[256,256]{0,1:T(8,128)(2,1)S(1)} %get-tuple-element.24), channel_id=1, source_target_pairs={{128,0},{160,32},{192,64},{224,96},{256,128},{288,160},{320,192},{... | collective-permute-start | bytes 393224 | tf_op jit(solution)/shard_map/ppermute | solution.py:17
  114.1 3.3 %collective-permute-start.15 = (bf16[4,4,168,256]{3,2,0,1:T(8,128)(2,1)S(1)}, bf16[4,4,168,256]{3,2,0,1:T(8,128)(2,1)S(1)}, u32[]{:S(2)}, u32[]{:S(2)}) collective-permute-start(bf16[4,4,168,256]{3,2,0,1:T(8,128)(2,1)S(1)} %copy.18), channel_id=1, source_target_pairs={{0,1},{1,0},{2,3},{3,2},{4,5},{5,4},{6,7},{7,6},{8,9},{9,8},{10,11... | collective-permute-start | bytes 4128776 | tf_op jit(solution)/shard_map/ppermute | solution.py:21
  120.6 4.6 %collective-permute-start.16 = (bf16[4,168,256]{2,1,0:T(8,128)(2,1)S(1)}, bf16[4,168,256]{2,1,0:T(8,128)(2,1)S(1)}, u32[]{:S(2)}, u32[]{:S(2)}) collective-permute-start(bf16[4,168,256]{2,1,0:T(8,128)(2,1)S(1)} %get-tuple-element.11), channel_id=1, source_target_pairs={{0,2},{2,4},{4,6},{6,0},{1,3},{3,5},{5,7},{7,1},{8,10},{10,12},{12... | collective-permute-start | bytes 1032200 | tf_op jit(solution)/shard_map/ppermute | solution.py:21
  129.7 9.9 %collective-permute-done.16 = bf16[4,168,256]{2,1,0:T(8,128)(2,1)S(1)} collective-permute-done((bf16[4,168,256]{2,1,0:T(8,128)(2,1)S(1)}, bf16[4,168,256]{2,1,0:T(8,128)(2,1)S(1)}, u32[]{:S(2)}, u32[]{:S(2)}) %collective-permute-start.16) | collective-permute-done | bytes 344096 | tf_op jit(solution)/shard_map/ppermute | solution.py:21
  139.5 6.5 %collective-permute-done.18 = bf16[4,168,256]{2,1,0:T(8,128)(2,1)S(1)} collective-permute-done((bf16[4,168,256]{2,1,0:T(8,128)(2,1)S(1)}, bf16[4,168,256]{2,1,0:T(8,128)(2,1)S(1)}, u32[]{:S(2)}, u32[]{:S(2)}) %collective-permute-start.18) | collective-permute-done | bytes 344096 | tf_op jit(solution)/shard_map/ppermute | solution.py:21
  146.2 12.9 %collective-permute-start.19 = (bf16[168,256]{1,0:T(8,128)(2,1)S(1)}, bf16[168,256]{1,0:T(8,128)(2,1)S(1)}, u32[]{:S(2)}, u32[]{:S(2)}) collective-permute-start(bf16[168,256]{1,0:T(8,128)(2,1)S(1)} %get-tuple-element.20), channel_id=1, source_target_pairs={{0,8},{8,16},{16,24},{24,0},{1,9},{9,17},{17,25},{25,1},{2,10},{10... | collective-permute-start | bytes 258056 | tf_op jit(solution)/shard_map/ppermute | solution.py:21
  161.1 12.5 %collective-permute-start.20 = (bf16[168,256]{1,0:T(8,128)(2,1)S(1)}, bf16[168,256]{1,0:T(8,128)(2,1)S(1)}, u32[]{:S(2)}, u32[]{:S(2)}) collective-permute-start(bf16[168,256]{1,0:T(8,128)(2,1)S(1)} %fusion.28), channel_id=1, source_target_pairs={{0,8},{8,16},{16,24},{24,0},{1,9},{9,17},{17,25},{25,1},{2,10},{10... | collective-permute-start | bytes 258056 | tf_op jit(solution)/shard_map/ppermute | solution.py:21
  173.6 3.6 %collective-permute-done.21 = bf16[168,256]{1,0:T(8,128)(2,1)S(1)} collective-permute-done((bf16[168,256]{1,0:T(8,128)(2,1)S(1)}, bf16[168,256]{1,0:T(8,128)(2,1)S(1)}, u32[]{:S(2)}, u32[]{:S(2)}) %collective-permute-start.21) | collective-permute-done | bytes 86048 | tf_op jit(solution)/shard_map/ppermute | solution.py:21
  177.3 19.6 %collective-permute-done.20 = bf16[168,256]{1,0:T(8,128)(2,1)S(1)} collective-permute-done((bf16[168,256]{1,0:T(8,128)(2,1)S(1)}, bf16[168,256]{1,0:T(8,128)(2,1)S(1)}, u32[]{:S(2)}, u32[]{:S(2)}) %collective-permute-start.20) | collective-permute-done | bytes 86048 | tf_op jit(solution)/shard_map/ppermute | solution.py:21
  (87 shorter events, 32.8 us)
Async XLA Ops:
  0.0 45.2 %copy-start = (bf16[256,128]{1,0:T(8,128)(2,1)S(1)}, bf16[256,128]{1,0:T(8,128)(2,1)}, u32[]{:S(2)}) copy-start(bf16[256,128]{1,0:T(8,128)(2,1)} %param.8) | copy-start | bytes 196612
  0.0 45.2 %copy-start.7 = (bf16[256,128]{1,0:T(8,128)(2,1)S(1)}, bf16[256,128]{1,0:T(8,128)(2,1)}, u32[]{:S(2)}) copy-start(bf16[256,128]{1,0:T(8,128)(2,1)} %param.10) | copy-start | bytes 196612
  0.0 30.6 %collective-permute-start = (bf16[256,168]{0,1:T(8,128)(2,1)}, bf16[256,168]{0,1:T(8,128)(2,1)S(1)}, u32[]{:S(2)}, u32[]{:S(2)}) collective-permute-start(bf16[256,168]{0,1:T(8,128)(2,1)} %param.11), channel_id=1, source_target_pairs={{0,8},{8,16},{16,24},{24,0},{1,9},{9,17},{17,25},{25,1},{2,10},{10... | collective-permute-start | bytes 258056 | tf_op jit(solution)/shard_map/ppermute | solution.py:21
  15.6 17.8 %collective-permute-start.1 = (bf16[256,168]{0,1:T(8,128)(2,1)}, bf16[256,168]{0,1:T(8,128)(2,1)S(1)}, u32[]{:S(2)}, u32[]{:S(2)}) collective-permute-start(bf16[256,168]{0,1:T(8,128)(2,1)} %param.11), channel_id=1, source_target_pairs={{0,24},{8,0},{16,8},{24,16},{1,25},{9,1},{17,9},{25,17},{2,26},{10... | collective-permute-start | bytes 258056 | tf_op jit(solution)/shard_map/ppermute | solution.py:21
  19.9 25.1 %collective-permute-start.3 = (bf16[256,256]{1,0:T(8,128)(2,1)S(1)}, bf16[256,256]{1,0:T(8,128)(2,1)S(1)}, u32[]{:S(2)}, u32[]{:S(2)}) collective-permute-start(bf16[256,256]{1,0:T(8,128)(2,1)S(1)} %constant_dynamic-update-slice_fusion), channel_id=1, source_target_pairs={{0,128},{32,160},{64,192},{96,224},{128,256},{160,288},{192,320},{... | collective-permute-start | bytes 393224 | tf_op jit(solution)/shard_map/ppermute | solution.py:17
  22.8 22.3 %collective-permute-start.4 = (bf16[256,256]{1,0:T(8,128)(2,1)S(1)}, bf16[256,256]{1,0:T(8,128)(2,1)S(1)}, u32[]{:S(2)}, u32[]{:S(2)}) collective-permute-start(bf16[256,256]{1,0:T(8,128)(2,1)S(1)} %constant_dynamic-update-slice_fusion), channel_id=1, source_target_pairs={{0,96},{32,128},{64,160},{96,192},{128,224},{160,256},{192,288},{2... | collective-permute-start | bytes 393224 | tf_op jit(solution)/shard_map/ppermute | solution.py:17
  27.4 17.7 %collective-permute-start.5 = (bf16[256,256]{1,0:T(8,128)(2,1)S(1)}, bf16[256,256]{1,0:T(8,128)(2,1)S(1)}, u32[]{:S(2)}, u32[]{:S(2)}) collective-permute-start(bf16[256,256]{1,0:T(8,128)(2,1)S(1)} %constant_dynamic-update-slice_fusion), channel_id=1, source_target_pairs={{0,64},{32,96},{64,128},{96,160},{128,192},{160,224},{192,256},{22... | collective-permute-start | bytes 393224 | tf_op jit(solution)/shard_map/ppermute | solution.py:17
  30.6 14.5 %collective-permute-start.6 = (bf16[256,256]{1,0:T(8,128)(2,1)S(1)}, bf16[256,256]{1,0:T(8,128)(2,1)S(1)}, u32[]{:S(2)}, u32[]{:S(2)}) collective-permute-start(bf16[256,256]{1,0:T(8,128)(2,1)S(1)} %constant_dynamic-update-slice_fusion), channel_id=1, source_target_pairs={{0,32},{32,64},{64,96},{96,128},{128,160},{160,192},{192,224},{224... | collective-permute-start | bytes 393224 | tf_op jit(solution)/shard_map/ppermute | solution.py:17
  33.4 14.6 %collective-permute-start.2 = (bf16[256,168]{0,1:T(8,128)(2,1)S(1)}, bf16[256,168]{0,1:T(8,128)(2,1)S(1)}, u32[]{:S(2)}, u32[]{:S(2)}) collective-permute-start(bf16[256,168]{0,1:T(8,128)(2,1)S(1)} %collective-permute-done), channel_id=1, source_target_pairs={{0,8},{8,16},{16,24},{24,0},{1,9},{9,17},{17,25},{25,1},{2,10},{10... | collective-permute-start | bytes 258056 | tf_op jit(solution)/shard_map/ppermute | solution.py:21
  48.0 8.3 %collective-permute-start.7 = (bf16[4,256,168]{1,2,0:T(8,128)(2,1)S(1)}, bf16[4,256,168]{1,2,0:T(8,128)(2,1)S(1)}, u32[]{:S(2)}, u32[]{:S(2)}) collective-permute-start(bf16[4,256,168]{1,2,0:T(8,128)(2,1)S(1)} %bitcast_dynamic-update-slice_fusion.6), channel_id=1, source_target_pairs={{0,2},{2,4},{4,6},{6,0},{1,3},{3,5},{5,7},{7,1},{8,10},{10,12},{12... | collective-permute-start | bytes 1032200 | tf_op jit(solution)/shard_map/ppermute | solution.py:21
  50.2 9.2 %collective-permute-start.8 = (bf16[4,256,168]{1,2,0:T(8,128)(2,1)S(1)}, bf16[4,256,168]{1,2,0:T(8,128)(2,1)S(1)}, u32[]{:S(2)}, u32[]{:S(2)}) collective-permute-start(bf16[4,256,168]{1,2,0:T(8,128)(2,1)S(1)} %bitcast_dynamic-update-slice_fusion.6), channel_id=1, source_target_pairs={{0,6},{2,0},{4,2},{6,4},{1,7},{3,1},{5,3},{7,5},{8,14},{10,8},{12,... | collective-permute-start | bytes 1032200 | tf_op jit(solution)/shard_map/ppermute | solution.py:21
  56.3 10.5 %collective-permute-start.9 = (bf16[4,256,168]{1,2,0:T(8,128)(2,1)S(1)}, bf16[4,256,168]{1,2,0:T(8,128)(2,1)S(1)}, u32[]{:S(2)}, u32[]{:S(2)}) collective-permute-start(bf16[4,256,168]{1,2,0:T(8,128)(2,1)S(1)} %collective-permute-done.7), channel_id=1, source_target_pairs={{0,2},{2,4},{4,6},{6,0},{1,3},{3,5},{5,7},{7,1},{8,10},{10,12},{12... | collective-permute-start | bytes 1032200 | tf_op jit(solution)/shard_map/ppermute | solution.py:21
  66.8 18.4 %collective-permute-start.10 = (bf16[4,4,256,168]{2,3,1,0:T(8,128)(2,1)S(1)}, bf16[4,4,256,168]{2,3,1,0:T(8,128)(2,1)}, u32[]{:S(2)}, u32[]{:S(2)}) collective-permute-start(bf16[4,4,256,168]{2,3,1,0:T(8,128)(2,1)S(1)} %bitcast_dynamic-update-slice_fusion.2), channel_id=1, source_target_pairs={{0,1},{1,0},{2,3},{3,2},{4,5},{5,4},{6,7},{7,6},{8,9},{9,8},{10,11... | collective-permute-start | bytes 4128776 | tf_op jit(solution)/shard_map/ppermute | solution.py:21
  90.4 19.6 %collective-permute-start.11 = (bf16[256,256]{0,1:T(8,128)(2,1)S(1)}, bf16[256,256]{0,1:T(8,128)(2,1)S(1)}, u32[]{:S(2)}, u32[]{:S(2)}) collective-permute-start(bf16[256,256]{0,1:T(8,128)(2,1)S(1)} %get-tuple-element.22), channel_id=1, source_target_pairs={{32,0},{64,32},{96,64},{128,96},{160,128},{192,160},{224,192},{256... | collective-permute-start | bytes 393224 | tf_op jit(solution)/shard_map/ppermute | solution.py:17
  98.5 11.5 %collective-permute-start.12 = (bf16[256,256]{0,1:T(8,128)(2,1)S(1)}, bf16[256,256]{0,1:T(8,128)(2,1)S(1)}, u32[]{:S(2)}, u32[]{:S(2)}) collective-permute-start(bf16[256,256]{0,1:T(8,128)(2,1)S(1)} %get-tuple-element.23), channel_id=1, source_target_pairs={{64,0},{96,32},{128,64},{160,96},{192,128},{224,160},{256,192},{28... | collective-permute-start | bytes 393224 | tf_op jit(solution)/shard_map/ppermute | solution.py:17
  101.5 10.2 %collective-permute-start.13 = (bf16[256,256]{0,1:T(8,128)(2,1)S(1)}, bf16[256,256]{0,1:T(8,128)(2,1)S(1)}, u32[]{:S(2)}, u32[]{:S(2)}) collective-permute-start(bf16[256,256]{0,1:T(8,128)(2,1)S(1)} %get-tuple-element.25), channel_id=1, source_target_pairs={{96,0},{128,32},{160,64},{192,96},{224,128},{256,160},{288,192},{3... | collective-permute-start | bytes 393224 | tf_op jit(solution)/shard_map/ppermute | solution.py:17
  106.5 6.4 %collective-permute-start.14 = (bf16[256,256]{0,1:T(8,128)(2,1)S(1)}, bf16[256,256]{0,1:T(8,128)(2,1)S(1)}, u32[]{:S(2)}, u32[]{:S(2)}) collective-permute-start(bf16[256,256]{0,1:T(8,128)(2,1)S(1)} %get-tuple-element.24), channel_id=1, source_target_pairs={{128,0},{160,32},{192,64},{224,96},{256,128},{288,160},{320,192},{... | collective-permute-start | bytes 393224 | tf_op jit(solution)/shard_map/ppermute | solution.py:17
  114.1 6.1 %collective-permute-start.15 = (bf16[4,4,168,256]{3,2,0,1:T(8,128)(2,1)S(1)}, bf16[4,4,168,256]{3,2,0,1:T(8,128)(2,1)S(1)}, u32[]{:S(2)}, u32[]{:S(2)}) collective-permute-start(bf16[4,4,168,256]{3,2,0,1:T(8,128)(2,1)S(1)} %copy.18), channel_id=1, source_target_pairs={{0,1},{1,0},{2,3},{3,2},{4,5},{5,4},{6,7},{7,6},{8,9},{9,8},{10,11... | collective-permute-start | bytes 4128776 | tf_op jit(solution)/shard_map/ppermute | solution.py:21
  120.6 18.9 %collective-permute-start.16 = (bf16[4,168,256]{2,1,0:T(8,128)(2,1)S(1)}, bf16[4,168,256]{2,1,0:T(8,128)(2,1)S(1)}, u32[]{:S(2)}, u32[]{:S(2)}) collective-permute-start(bf16[4,168,256]{2,1,0:T(8,128)(2,1)S(1)} %get-tuple-element.11), channel_id=1, source_target_pairs={{0,2},{2,4},{4,6},{6,0},{1,3},{3,5},{5,7},{7,1},{8,10},{10,12},{12... | collective-permute-start | bytes 1032200 | tf_op jit(solution)/shard_map/ppermute | solution.py:21
  125.2 14.3 %collective-permute-start.17 = (bf16[4,168,256]{2,1,0:T(8,128)(2,1)S(1)}, bf16[4,168,256]{2,1,0:T(8,128)(2,1)S(1)}, u32[]{:S(2)}, u32[]{:S(2)}) collective-permute-start(bf16[4,168,256]{2,1,0:T(8,128)(2,1)S(1)} %get-tuple-element.13), channel_id=1, source_target_pairs={{0,4},{2,6},{4,0},{6,2},{1,5},{3,7},{5,1},{7,3},{8,12},{10,14},{12... | collective-permute-start | bytes 1032200 | tf_op jit(solution)/shard_map/ppermute | solution.py:21
  127.2 18.8 %collective-permute-start.18 = (bf16[4,168,256]{2,1,0:T(8,128)(2,1)S(1)}, bf16[4,168,256]{2,1,0:T(8,128)(2,1)S(1)}, u32[]{:S(2)}, u32[]{:S(2)}) collective-permute-start(bf16[4,168,256]{2,1,0:T(8,128)(2,1)S(1)} %get-tuple-element.12), channel_id=1, source_target_pairs={{0,6},{2,0},{4,2},{6,4},{1,7},{3,1},{5,3},{7,5},{8,14},{10,8},{12,... | collective-permute-start | bytes 1032200 | tf_op jit(solution)/shard_map/ppermute | solution.py:21
  146.2 14.9 %collective-permute-start.19 = (bf16[168,256]{1,0:T(8,128)(2,1)S(1)}, bf16[168,256]{1,0:T(8,128)(2,1)S(1)}, u32[]{:S(2)}, u32[]{:S(2)}) collective-permute-start(bf16[168,256]{1,0:T(8,128)(2,1)S(1)} %get-tuple-element.20), channel_id=1, source_target_pairs={{0,8},{8,16},{16,24},{24,0},{1,9},{9,17},{17,25},{25,1},{2,10},{10... | collective-permute-start | bytes 258056 | tf_op jit(solution)/shard_map/ppermute | solution.py:21
  159.2 18.1 %collective-permute-start.21 = (bf16[168,256]{1,0:T(8,128)(2,1)S(1)}, bf16[168,256]{1,0:T(8,128)(2,1)S(1)}, u32[]{:S(2)}, u32[]{:S(2)}) collective-permute-start(bf16[168,256]{1,0:T(8,128)(2,1)S(1)} %get-tuple-element.21), channel_id=1, source_target_pairs={{0,24},{8,0},{16,8},{24,16},{1,25},{9,1},{17,9},{25,17},{2,26},{10... | collective-permute-start | bytes 258056 | tf_op jit(solution)/shard_map/ppermute | solution.py:21
  161.1 35.7 %collective-permute-start.20 = (bf16[168,256]{1,0:T(8,128)(2,1)S(1)}, bf16[168,256]{1,0:T(8,128)(2,1)S(1)}, u32[]{:S(2)}, u32[]{:S(2)}) collective-permute-start(bf16[168,256]{1,0:T(8,128)(2,1)S(1)} %fusion.28), channel_id=1, source_target_pairs={{0,8},{8,16},{16,24},{24,0},{1,9},{9,17},{17,25},{25,1},{2,10},{10... | collective-permute-start | bytes 258056 | tf_op jit(solution)/shard_map/ppermute | solution.py:21
  (6 other events, 52.8 us)
